TPU v7x, 512 devices: a whole 4x8x8 slice. The times are simulated.
512 devices in a mesh: wide: 64 (over y, x, core), narrow: 8 (over z).
Axes of the slice: x: 4, y: 8, z: 8, core: 2. Of those that a mesh axis runs over, the one named last changes fastest.
Arguments:
- point_owner: int32 [524288, 1], P(('wide', 'narrow')), may hold values from 0 to 63; in each aligned block of 1024 rows (0 to 1023, 1024 to 2047, ...) at most 32 rows name the same one
- point_cell: int32 [524288], P(('wide', 'narrow')), may hold values from 0 to 8191
- normals: float32 [3, 524288], P(None, ('wide', 'narrow')), may hold values from -6 to 6
- strip_count: int32 [512], P(('wide', 'narrow')), may hold values from 1 to 1024, 458752 in all
- neighbours: int32 [64, 8, 2, 27], P('wide', 'narrow'), may hold values from 0 to 18, as said below
Outputs:
- solution: float32 [64, 8, 2, 4096], P('wide', 'narrow')
- residual: float32 [64, 8, 2, 4096], P('wide', 'narrow')
Inputs may be any that keep to these rules, and one draw needn't show every extreme that they name: `point_owner`: the points of one device name each wide index at most 32 times, and some wide index exactly 32 times. `strip_count`: some device has exactly 1024 live points. `neighbours`: entries follow the encoding of the steps; dw and dn are -1, 0 or 1; the relation is mutual (b sees c in a direction exactly when c sees b in the opposite one); entry 13 names the brick itself.
All inputs are finite; a program needn't handle non-finite values.
Results may differ from a plain program's by a relative error of at most 0.0003.
Values sent between devices are 32-bit elements; how exact they have to be, the bound alone decides.
No kernel may reach another device: no remote copies, remote signals or barrier semaphores. Data moves between devices by JAX's collectives and lax.ppermute only.
A program may use at most 64 MiB of HBM per device.

v0:
```python
import math

import jax
import jax.numpy as jnp
from jax import lax
from jax.sharding import PartitionSpec as P

ITERS = 3


WEIGHTS = (0.0, 1.0, 0.5, 0.25)
DIRECTIONS = tuple(((a, b, c) for a in (-1, 0, 1) for b in (-1, 0, 1) for c in (-1, 0, 1)))
HIGHEST = lax.Precision.HIGHEST


def padded_2(array, sides, width):
    for axis, dim in sides:
        peers, length = (lax.axis_size(axis), array.shape[dim])
        up = [(i, (i + 1) % peers) for i in range(peers - 1)]
        down = [(j, i) for i, j in up]
        last = lax.slice_in_dim(array, length - width, length, axis=dim)
        leading = lax.slice_in_dim(array, 0, width, axis=dim)
        before = lax.ppermute(last, axis, up)
        after = lax.ppermute(leading, axis, down)
        array = jnp.concatenate([before, array, after], axis=dim)
    return array


def cell_span(shift_by):
    if shift_by == -1:
        return (15, 16)
    if shift_by == 1:
        return (0, 1)
    return (0, 16)


def fetch_piece(source, layout, brick_table, step_x, step_y, step_z):
    column = (step_x + 1) * 9 + (step_y + 1) * 3 + (step_z + 1)
    low_x, high_x = cell_span(step_x)
    low_y, high_y = cell_span(step_y)
    low_z, high_z = cell_span(step_z)
    piece = source[:, low_x:high_x, low_y:high_y, low_z:high_z]
    return jnp.take(piece, brick_table[:, column], axis=0)


def make_source(rim_data):
    row_width = rim_data.shape[-1]
    flat_rows = rim_data.reshape(-1, row_width)
    flat_rows = jnp.concatenate([flat_rows, jnp.zeros((1, row_width), flat_rows.dtype)], 0)
    return flat_rows.reshape(-1, 16, 16, 16)


def stencil(source, layout, brick_table, values, diagonal):
    brick_count = values.shape[0]
    own_cube = values.reshape(brick_count, 16, 16, 16)
    planes = []
    for step_x in (-1, 0, 1):
        row_parts = []
        for step_y in (-1, 0, 1):
            col_parts = []
            for step_z in (-1, 0, 1):
                if step_x == 0 and step_y == 0 and (step_z == 0):
                    col_parts.append(own_cube)
                else:
                    col_parts.append(
                        fetch_piece(source, layout, brick_table, step_x, step_y, step_z)
                    )
            row_parts.append(jnp.concatenate(col_parts, 3))
        planes.append(jnp.concatenate(row_parts, 2))
    padded = jnp.concatenate(planes, 1)
    summed = jnp.zeros_like(own_cube)
    for step_x, step_y, step_z in DIRECTIONS:
        reach = abs(step_x) + abs(step_y) + abs(step_z)
        if reach > 0:
            summed = (
                summed
                + WEIGHTS[reach]
                * padded[
                    :, 1 + step_x : 17 + step_x, 1 + step_y : 17 + step_y, 1 + step_z : 17 + step_z
                ]
            )
    return diagonal * values - summed.reshape(brick_count, 4096)


def divergence(sources, layout, brick_table, vector_field):
    brick_count = vector_field.shape[1]
    summed = jnp.zeros((brick_count, 16, 16, 16), vector_field.dtype)
    for direction in range(3):
        upper_step = [0, 0, 0]
        upper_step[direction] = 1
        lower_step = [0, 0, 0]
        lower_step[direction] = -1
        lower_piece = fetch_piece(sources[direction], layout, brick_table, *lower_step)
        upper_piece = fetch_piece(sources[direction], layout, brick_table, *upper_step)
        own_cube = vector_field[direction].reshape(brick_count, 16, 16, 16)
        extended = jnp.concatenate([lower_piece, own_cube, upper_piece], direction + 1)
        change = lax.slice_in_dim(extended, 2, 18, axis=direction + 1) - lax.slice_in_dim(
            extended, 0, 16, axis=direction + 1
        )
        summed = summed + change
    return -4.0 * summed.reshape(brick_count, 4096)


def shards(point_owner, point_cell, normals, strip_count, neighbours):
    owners = lax.axis_size("wide")
    point_total = point_cell.shape[0]
    brick_table = neighbours[0, 0]
    brick_count = brick_table.shape[0]
    brick_cells = brick_count * 4096
    capacity = 2 * point_total // owners
    target_owner = point_owner[:, 0]
    is_live = jnp.arange(point_total, dtype=jnp.int32) < strip_count[0]
    target = jnp.where(is_live, point_cell, brick_cells)
    sort_order = jnp.argsort(target_owner, stable=True)
    sorted_owner = target_owner[sort_order]
    owner_ids = jnp.arange(owners, dtype=jnp.int32)
    per_owner = jnp.sum((target_owner[:, None] == owner_ids[None, :]).astype(jnp.int32), axis=0)
    first_slot = jnp.cumsum(per_owner) - per_owner
    sorted_marks = (sorted_owner[:, None] == owner_ids[None, :]).astype(jnp.int32)
    slot_rank = jnp.arange(point_total, dtype=jnp.int32) - jnp.sum(
        sorted_marks * first_slot[None, :], axis=1
    )
    send_index = (
        jnp.full((owners, capacity), brick_cells, jnp.int32)
        .at[sorted_owner, slot_rank]
        .set(target[sort_order])
    )
    send_vectors = (
        jnp.zeros((owners, 3, capacity), jnp.float32)
        .at[sorted_owner, :, slot_rank]
        .set(normals[:, sort_order].T)
    )
    got_index, got_vectors = (
        lax.all_to_all(send_index, "wide", split_axis=0, concat_axis=0, tiled=True),
        lax.all_to_all(send_vectors, "wide", split_axis=0, concat_axis=0, tiled=True),
    )
    slot_total = owners * capacity
    block_rows = math.gcd(slot_total, 2048)
    flat_index = got_index.reshape(slot_total // block_rows, block_rows)
    flat_vectors = got_vectors.transpose(0, 2, 1).reshape(slot_total // block_rows, block_rows, 3)
    columns_high = jnp.arange(brick_count * 64, dtype=jnp.int32)
    columns_low = jnp.arange(64, dtype=jnp.int32)

    def splat_step(summed, pieces):
        indices, vectors = pieces
        brick_hot = (indices[:, None] // 64 == columns_high[None, :]).astype(jnp.float32)
        cell_hot = (indices[:, None] % 64 == columns_low[None, :]).astype(jnp.float32)
        weighted = jnp.concatenate(
            [
                cell_hot * vectors[:, 0:1],
                cell_hot * vectors[:, 1:2],
                cell_hot * vectors[:, 2:3],
                cell_hot,
            ],
            1,
        )
        return (
            summed
            + jnp.einsum(
                "pa,pb->ab",
                brick_hot,
                weighted,
                precision=HIGHEST,
                preferred_element_type=jnp.float32,
            ),
            None,
        )

    splatted, leftover = lax.scan(
        splat_step, jnp.zeros((brick_count * 64, 256), jnp.float32), (flat_index, flat_vectors)
    )
    vector_field = jnp.stack(
        [splatted[:, c * 64 : (c + 1) * 64].reshape(brick_count, 4096) for c in range(3)]
    )
    density = splatted[:, 192:256].reshape(brick_count, 4096)
    diagonal = 14.5 + 2.0 * density
    vector_rim = padded_2(vector_field[None, None], (("wide", 0), ("narrow", 1)), 1)
    layout = "whole"
    sources = [make_source(vector_rim[:, :, c]) for c in range(3)]
    right_side = divergence(sources, layout, brick_table, vector_field)

    def global_squares(values):
        return lax.psum(jnp.sum(values * values), ("wide", "narrow"))

    solution = jnp.zeros_like(right_side)
    residual = right_side
    direction = right_side
    norm_now = global_squares(residual)
    for iteration in range(ITERS):
        field_rim = padded_2(direction[None, None], (("wide", 0), ("narrow", 1)), 1)
        image_field = stencil(make_source(field_rim), layout, brick_table, direction, diagonal)
        step_size = norm_now / lax.psum(jnp.sum(direction * image_field), ("wide", "narrow"))
        solution = solution + step_size * direction
        residual = residual - step_size * image_field
        norm_next = global_squares(residual)
        direction = residual + norm_next / norm_now * direction
        norm_now = norm_next
    return (solution.reshape(1, 1, brick_count, 4096), residual.reshape(1, 1, brick_count, 4096))


def solution(mesh):
    return jax.shard_map(
        shards,
        mesh=mesh,
        in_specs=(
            P(("wide", "narrow"), None),
            P(("wide", "narrow")),
            P(None, ("wide", "narrow")),
            P(("wide", "narrow")),
            P("wide", "narrow", None, None),
        ),
        out_specs=(P("wide", "narrow", None, None), P("wide", "narrow", None, None)),
        check_vma=False,
    )
```

profile of v0, /device:TPU:1, one launch (start us, length us, event | category | flops | bytes accessed | tf_op | source)
XLA Modules:
  0.0 918.0 jit_solution(15576321594947085789)
XLA Ops:
  2.1 5.1 sort.17
  7.2 1.9 slice_reduce_fusion.43
  9.8 4.5 gather_fusion
  14.4 4.5 gather_fusion.1
  19.6 4.3 scatter_custom_fusion
  24.7 11.6 %all-to-all-start = ((s32[64,1,32]{2,1,0:T(1,128)}), s32[64,1,32]{2,1,0:T(1,128)S(1)}, u32[]{:S(2)}, u32[]{:S(2)}) async-start(s32[64,1,32]{2,1,0:T(1,128)} %copy.664), calls=%async_computation | async-start | bytes 65536 | tf_op jit(solution)/shard_map/all_to_all | solution.py:134
  47.0 6.9 scatter_custom_fusion.1
  55.2 10.6 %all-to-all-start.1 = ((f32[64,3,32]{2,1,0:T(4,128)}), f32[64,3,32]{2,1,0:T(4,128)S(1)}, u32[]{:S(2)}, u32[]{:S(2)}) async-start(f32[64,3,32]{2,1,0:T(4,128)} %bitcast.8), calls=%async_computation.1 | async-start | bytes 262144 | tf_op jit(solution)/shard_map/all_to_all | solution.py:135
  67.5 9.3 %all-to-all-done.1 = f32[64,3,32]{2,1,0:T(4,128)S(1)} async-done(((f32[64,3,32]{2,1,0:T(4,128)}), f32[64,3,32]{2,1,0:T(4,128)S(1)}, u32[]{:S(2)}, u32[]{:S(2)}) %all-to-all-start.1) | async-done | bytes 24608 | tf_op jit(solution)/shard_map/all_to_all | solution.py:135
  78.1 2.2 fusion
  80.8 2.3 collective-permute-start.1
  83.1 3.3 collective-permute-start
  89.4 4.6 collective-permute-start.2
  98.0 1.8 collective-permute-done.2
  101.8 1.9 reshape.561
  105.4 2.3 reshape.560
  107.7 1.7 slice_bitcast_fusion.7
  109.4 3.1 fusion.114
  112.4 3.7 copy.848
  116.1 1.8 copy.849
  125.9 3.7 collective-permute-start.4
  130.2 1.9 collective-permute-start.5
  132.2 3.3 collective-permute-done.5
  136.7 4.7 collective-permute-start.6
  144.2 1.9 reshape.564
  151.4 3.1 fusion.112
  178.5 1.6 gather_fusion.29
  187.0 1.7 copy.859
  188.8 1.7 copy.858
  190.5 1.7 copy.851
  200.9 1.7 copy.857
  202.7 1.7 copy.856
  212.8 3.5 copy.854
  218.4 1.8 copy.855
  239.1 2.0 multiply_reduce_fusion.4
  241.3 109.3 %all-reduce.6 = (f32[]{:T(128)}, f32[]{:T(128)}) all-reduce(f32[]{:T(128)} %get-tuple-element.54, f32[]{:T(128)} %get-tuple-element.53), channel_id=1, replica_groups=mesh['wide'=64,'narrow'=8] {'wide','narrow'}, use_global_device_ids=true, to_apply=%region_7.11 | all-reduce | flops 2 | bytes 16 | tf_op jit(solution)/shard_map/psum | solution.py:183
  353.4 94.9 %psum.44 = f32[]{:T(128)} all-reduce(f32[]{:T(128)} %get-tuple-element.93), channel_id=1, replica_groups=mesh['wide'=64,'narrow'=8] {'wide','narrow'}, use_global_device_ids=true, to_apply=%region_11.19 | all-reduce | flops 1 | bytes 8 | tf_op jit(solution)/shard_map/psum | solution.py:183
  449.9 3.0 collective-permute-start.9
  452.8 3.6 collective-permute-start.8
  458.8 4.0 collective-permute-start.10
  463.0 1.8 collective-permute-done.10
  469.2 1.6 fusion.105
  470.8 3.1 fusion.107
  492.7 1.6 gather_fusion.55
  494.3 1.6 gather_fusion.44
  496.0 1.6 gather_fusion.49
  520.3 3.5 copy.864
  525.4 1.8 copy.865
  529.9 2.0 multiply_reduce_fusion.2
  531.9 102.2 %psum.45 = f32[]{:T(128)} all-reduce(f32[]{:T(128)} %get-tuple-element.89), channel_id=1, replica_groups=mesh['wide'=64,'narrow'=8] {'wide','narrow'}, use_global_device_ids=true, to_apply=%region_13.21 | all-reduce | flops 1 | bytes 8 | tf_op jit(solution)/shard_map/psum | solution.py:192
  636.3 95.7 %psum.46 = f32[]{:T(128)} all-reduce(f32[]{:T(128)} %get-tuple-element.87), channel_id=1, replica_groups=mesh['wide'=64,'narrow'=8] {'wide','narrow'}, use_global_device_ids=true, to_apply=%region_15.23 | all-reduce | flops 1 | bytes 8 | tf_op jit(solution)/shard_map/psum | solution.py:183
  733.5 2.6 collective-permute-start.13
  736.0 3.0 collective-permute-start.12
  741.4 4.2 collective-permute-start.14
  746.2 1.7 collective-permute-done.14
  749.1 1.9 reshape.570
  755.7 3.1 fusion.102
  777.5 1.6 gather_fusion.81
  779.2 1.6 gather_fusion.70
  780.8 1.6 gather_fusion.75
  799.8 3.5 copy.874
  804.1 1.8 copy.875
  811.3 2.0 multiply_reduce_fusion
  813.3 102.3 %psum.47 = f32[]{:T(128)} all-reduce(f32[]{:T(128)} %get-tuple-element.83), channel_id=1, replica_groups=mesh['wide'=64,'narrow'=8] {'wide','narrow'}, use_global_device_ids=true, to_apply=%region_17.25 | all-reduce | flops 1 | bytes 8 | tf_op jit(solution)/shard_map/psum | solution.py:192
  (653 shorter events, 222.0 us)
Async XLA Ops:
  9.1 32.8 %copy-start.74 = (s32[2]{0:T(128)}, s32[2]{0:T(128)S(1)}, u32[]{:S(2)}) copy-start(s32[2]{0:T(128)S(1)} %get-tuple-element.55) | copy-start | bytes 28
  9.1 32.8 %copy-start.72 = (s32[2]{0:T(128)}, s32[2]{0:T(128)S(1)}, u32[]{:S(2)}) copy-start(s32[2]{0:T(128)S(1)} %get-tuple-element.58) | copy-start | bytes 28
  9.1 33.3 %copy-start.73 = (s32[2]{0:T(128)}, s32[2]{0:T(128)S(1)}, u32[]{:S(2)}) copy-start(s32[2]{0:T(128)S(1)} %get-tuple-element.61) | copy-start | bytes 28
  9.1 33.3 %copy-start.71 = (s32[2]{0:T(128)}, s32[2]{0:T(128)S(1)}, u32[]{:S(2)}) copy-start(s32[2]{0:T(128)S(1)} %get-tuple-element.63) | copy-start | bytes 28
  9.1 33.3 %copy-start.69 = (s32[2]{0:T(128)}, s32[2]{0:T(128)S(1)}, u32[]{:S(2)}) copy-start(s32[2]{0:T(128)S(1)} %get-tuple-element.68) | copy-start | bytes 28
  9.1 33.3 %copy-start.65 = (s32[2]{0:T(128)}, s32[2]{0:T(128)S(1)}, u32[]{:S(2)}) copy-start(s32[2]{0:T(128)S(1)} %get-tuple-element.70) | copy-start | bytes 28
  9.2 33.4 %copy-start.63 = (s32[2]{0:T(128)}, s32[2]{0:T(128)S(1)}, u32[]{:S(2)}) copy-start(s32[2]{0:T(128)S(1)} %get-tuple-element.73) | copy-start | bytes 28
  14.3 22.0 %copy-start.9 = (s32[1,1,2,27]{3,2,1,0:T(2,128)S(1)}, s32[1,1,2,27]{3,2,1,0:T(2,128)}, u32[]{:S(2)}) copy-start(s32[1,1,2,27]{3,2,1,0:T(2,128)} %param.23) | copy-start | bytes 652
  14.4 32.5 %copy-start.15 = (f32[3,1024]{1,0:T(4,128)S(1)}, f32[3,1024]{1,0:T(4,128)}, u32[]{:S(2)}) copy-start(f32[3,1024]{1,0:T(4,128)} %param.21) | copy-start | bytes 36868
  24.7 30.5 %all-to-all-start = ((s32[64,1,32]{2,1,0:T(1,128)}), s32[64,1,32]{2,1,0:T(1,128)S(1)}, u32[]{:S(2)}, u32[]{:S(2)}) async-start(s32[64,1,32]{2,1,0:T(1,128)} %copy.664), calls=%async_computation | async-start | bytes 65536 | tf_op jit(solution)/shard_map/all_to_all | solution.py:134
  36.6 86.7 %copy-start.39 = (pred[2]{0:T(512)(128)(4,1)}, pred[2]{0:T(512)(128)(4,1)S(1)}, u32[]{:S(2)}) copy-start(pred[2]{0:T(512)(128)(4,1)S(1)} %compare_and_fusion.25) | copy-start | bytes 10
  37.3 86.8 %copy-start.20 = (pred[2]{0:T(512)(128)(4,1)}, pred[2]{0:T(512)(128)(4,1)S(1)}, u32[]{:S(2)}) copy-start(pred[2]{0:T(512)(128)(4,1)S(1)} %get-tuple-element.231) | copy-start | bytes 10
  37.3 84.5 %copy-start.23 = (pred[2]{0:T(512)(128)(4,1)}, pred[2]{0:T(512)(128)(4,1)S(1)}, u32[]{:S(2)}) copy-start(pred[2]{0:T(512)(128)(4,1)S(1)} %get-tuple-element.233) | copy-start | bytes 10
  37.3 86.9 %copy-start.16 = (pred[2]{0:T(512)(128)(4,1)}, pred[2]{0:T(512)(128)(4,1)S(1)}, u32[]{:S(2)}) copy-start(pred[2]{0:T(512)(128)(4,1)S(1)} %get-tuple-element.232) | copy-start | bytes 10
  37.3 83.8 %copy-start.27 = (pred[2]{0:T(512)(128)(4,1)}, pred[2]{0:T(512)(128)(4,1)S(1)}, u32[]{:S(2)}) copy-start(pred[2]{0:T(512)(128)(4,1)S(1)} %get-tuple-element.234) | copy-start | bytes 10
  37.4 141.0 %copy-start.30 = (pred[2]{0:T(512)(128)(4,1)}, pred[2]{0:T(512)(128)(4,1)S(1)}, u32[]{:S(2)}) copy-start(pred[2]{0:T(512)(128)(4,1)S(1)} %get-tuple-element.235) | copy-start | bytes 10
  42.5 77.1 %copy-start.34 = (s32[1024]{0:T(1024)}, s32[1024]{0:T(1024)S(1)}, u32[]{:S(2)}) copy-start(s32[1024]{0:T(1024)S(1)} %get-tuple-element.228) | copy-start | bytes 12292
  42.6 80.9 %copy-start.36 = (s32[1024]{0:T(1024)}, s32[1024]{0:T(1024)S(1)}, u32[]{:S(2)}) copy-start(s32[1024]{0:T(1024)S(1)} %get-tuple-element.229) | copy-start | bytes 12292
  42.6 76.2 %copy-start.33 = (s32[1024]{0:T(1024)}, s32[1024]{0:T(1024)S(1)}, u32[]{:S(2)}) copy-start(s32[1024]{0:T(1024)S(1)} %get-tuple-element.226) | copy-start | bytes 12292
  42.6 78.6 %copy-start.35 = (s32[1024]{0:T(1024)}, s32[1024]{0:T(1024)S(1)}, u32[]{:S(2)}) copy-start(s32[1024]{0:T(1024)S(1)} %get-tuple-element.227) | copy-start | bytes 12292
  55.2 21.6 %all-to-all-start.1 = ((f32[64,3,32]{2,1,0:T(4,128)}), f32[64,3,32]{2,1,0:T(4,128)S(1)}, u32[]{:S(2)}, u32[]{:S(2)}) async-start(f32[64,3,32]{2,1,0:T(4,128)} %bitcast.8), calls=%async_computation.1 | async-start | bytes 262144 | tf_op jit(solution)/shard_map/all_to_all | solution.py:135
  80.8 6.2 collective-permute-start.1
  83.1 4.9 collective-permute-start
  86.9 31.1 %copy-start.37 = (s32[1024]{0:T(1024)}, s32[1024]{0:T(1024)S(1)}, u32[]{:S(2)}) copy-start(s32[1024]{0:T(1024)S(1)} %get-tuple-element.225) | copy-start | bytes 12292
  88.1 9.9 %collective-permute-start.3 = (f32[3,1,3,2,4096]{4,3,2,1,0:T(2,128)S(1)}, f32[3,1,3,2,4096]{4,3,2,1,0:T(2,128)S(1)}, u32[]{:S(2)}, u32[]{:S(2)}) collective-permute-start(f32[3,1,3,2,4096]{4,3,2,1,0:T(2,128)S(1)} %pad_maximum_fusion.7), channel_id=1, source_target_pairs={{1,0},{2,1},{3,2},{4,3},{5,4},{6,5},{7,6},{9,8},{10,9},{11,10},{12... | collective-permute-start | bytes 884744 | tf_op jit(solution)/shard_map/ppermute | solution.py:24
  89.4 10.4 %collective-permute-start.2 = (f32[3,1,3,2,4096]{4,3,2,1,0:T(2,128)S(1)}, f32[3,1,3,2,4096]{4,3,2,1,0:T(2,128)S(1)}, u32[]{:S(2)}, u32[]{:S(2)}) collective-permute-start(f32[3,1,3,2,4096]{4,3,2,1,0:T(2,128)S(1)} %pad_maximum_fusion.7), channel_id=1, source_target_pairs={{0,1},{1,2},{2,3},{3,4},{4,5},{5,6},{6,7},{8,9},{9,10},{10,11},{11... | collective-permute-start | bytes 884744 | tf_op jit(solution)/shard_map/ppermute | solution.py:23
  94.1 27.8 %copy-start.38 = (s32[1024]{0:T(1024)}, s32[1024]{0:T(1024)S(1)}, u32[]{:S(2)}) copy-start(s32[1024]{0:T(1024)S(1)} %pad_clamp_fusion.25) | copy-start | bytes 12292
  118.0 23.5 %copy-start.91 = (s32[2]{0:T(128)S(1)}, s32[2]{0:T(128)}, u32[]{:S(2)}) copy-start(s32[2]{0:T(128)} %compare_select_fusion.4) | copy-start | bytes 28
  118.0 23.5 %copy-start.92 = (s32[2]{0:T(128)S(1)}, s32[2]{0:T(128)}, u32[]{:S(2)}) copy-start(s32[2]{0:T(128)} %compare_select_fusion.5) | copy-start | bytes 28
  125.9 6.2 collective-permute-start.4
  130.2 5.2 collective-permute-start.5
  135.4 6.9 collective-permute-start.7
  136.7 6.4 collective-permute-start.6
  154.4 21.2 %copy-start.13 = (f32[19,1,1,16]{3,2,1,0:T(1,128)S(1)}, f32[19,1,1,16]{3,2,1,0:T(1,128)}, u32[]{:S(2)}) copy-start(f32[19,1,1,16]{3,2,1,0:T(1,128)} %get-tuple-element.152) | copy-start | bytes 3652
  154.4 27.9 %copy-start.24 = (pred[2]{0:T(512)(128)(4,1)S(1)}, pred[2]{0:T(512)(128)(4,1)}, u32[]{:S(2)}) copy-start(pred[2]{0:T(512)(128)(4,1)} %copy-done.23) | copy-start | bytes 10
  170.8 46.8 %copy-start.21 = (pred[2]{0:T(512)(128)(4,1)S(1)}, pred[2]{0:T(512)(128)(4,1)}, u32[]{:S(2)}) copy-start(pred[2]{0:T(512)(128)(4,1)} %copy-done.20) | copy-start | bytes 10
  171.7 46.7 %copy-start.3 = (f32[19,16,16,1]{3,2,1,0:T(8,128)S(1)}, f32[19,16,16,1]{3,2,1,0:T(8,128)}, u32[]{:S(2)}) copy-start(f32[19,16,16,1]{3,2,1,0:T(8,128)} %get-tuple-element.167) | copy-start | bytes 58372
  241.2 223.7 %copy-start.10 = (f32[1,1,2,4096]{3,2,1,0:T(2,128)}, f32[1,1,2,4096]{3,2,1,0:T(2,128)S(1)}, u32[]{:S(2)}) copy-start(f32[1,1,2,4096]{3,2,1,0:T(2,128)S(1)} %reshape.565) | copy-start | bytes 98308
  353.4 111.8 %copy-start.5 = (f32[2,16,16,16]{3,2,1,0:T(8,128)}, f32[2,16,16,16]{3,2,1,0:T(8,128)S(1)}, u32[]{:S(2)}) copy-start(f32[2,16,16,16]{3,2,1,0:T(8,128)S(1)} %get-tuple-element.94) | copy-start | bytes 98308
  449.9 6.6 collective-permute-start.9
  452.8 4.6 collective-permute-start.8
  457.5 5.5 collective-permute-start.11
  458.8 6.0 collective-permute-start.10
  473.9 22.0 %copy-start.25 = (pred[2]{0:T(512)(128)(4,1)S(1)}, pred[2]{0:T(512)(128)(4,1)}, u32[]{:S(2)}) copy-start(pred[2]{0:T(512)(128)(4,1)} %copy-done.23) | copy-start | bytes 10
  473.9 23.7 %copy-start.28 = (pred[2]{0:T(512)(128)(4,1)S(1)}, pred[2]{0:T(512)(128)(4,1)}, u32[]{:S(2)}) copy-start(pred[2]{0:T(512)(128)(4,1)} %copy-done.27) | copy-start | bytes 10
  475.4 32.3 %copy-start.44 = (pred[2]{0:T(512)(128)(4,1)S(1)}, pred[2]{0:T(512)(128)(4,1)}, u32[]{:S(2)}) copy-start(pred[2]{0:T(512)(128)(4,1)} %get-tuple-element.237) | copy-start | bytes 10
  486.8 38.5 %copy-start.2 = (f32[19,16,16,1]{3,2,1,0:T(8,128)S(1)}, f32[19,16,16,1]{3,2,1,0:T(8,128)}, u32[]{:S(2)}) copy-start(f32[19,16,16,1]{3,2,1,0:T(8,128)} %get-tuple-element.149) | copy-start | bytes 58372
  529.9 105.7 %copy-start.6 = (f32[2,16,16,16]{3,2,1,0:T(8,128)S(1)}, f32[2,16,16,16]{3,2,1,0:T(8,128)}, u32[]{:S(2)}) copy-start(f32[2,16,16,16]{3,2,1,0:T(8,128)} %copy-done.5) | copy-start | bytes 98308
  529.9 203.5 %copy-start.11 = (f32[1,1,2,4096]{3,2,1,0:T(2,128)S(1)}, f32[1,1,2,4096]{3,2,1,0:T(2,128)}, u32[]{:S(2)}) copy-start(f32[1,1,2,4096]{3,2,1,0:T(2,128)} %copy-done.10) | copy-start | bytes 98308
  529.9 209.1 %copy-start.7 = (f32[2,16,16,16]{3,2,1,0:T(8,128)S(1)}, f32[2,16,16,16]{3,2,1,0:T(8,128)}, u32[]{:S(2)}) copy-start(f32[2,16,16,16]{3,2,1,0:T(8,128)} %get-tuple-element.189) | copy-start | bytes 98308
  733.5 5.8 collective-permute-start.13
  736.0 4.0 collective-permute-start.12
  740.1 6.1 collective-permute-start.15
  741.4 6.6 collective-permute-start.14
  758.8 21.9 %copy-start.26 = (pred[2]{0:T(512)(128)(4,1)S(1)}, pred[2]{0:T(512)(128)(4,1)}, u32[]{:S(2)}) copy-start(pred[2]{0:T(512)(128)(4,1)} %copy-done.23) | copy-start | bytes 10
  758.8 23.6 %copy-start.29 = (pred[2]{0:T(512)(128)(4,1)S(1)}, pred[2]{0:T(512)(128)(4,1)}, u32[]{:S(2)}) copy-start(pred[2]{0:T(512)(128)(4,1)} %copy-done.27) | copy-start | bytes 10
  759.6 30.2 %copy-start.47 = (pred[2]{0:T(512)(128)(4,1)S(1)}, pred[2]{0:T(512)(128)(4,1)}, u32[]{:S(2)}) copy-start(pred[2]{0:T(512)(128)(4,1)} %get-tuple-element.245) | copy-start | bytes 10
  759.6 30.4 %copy-start.46 = (pred[2]{0:T(512)(128)(4,1)S(1)}, pred[2]{0:T(512)(128)(4,1)}, u32[]{:S(2)}) copy-start(pred[2]{0:T(512)(128)(4,1)} %get-tuple-element.238) | copy-start | bytes 10
  759.6 30.5 %copy-start.45 = (pred[2]{0:T(512)(128)(4,1)S(1)}, pred[2]{0:T(512)(128)(4,1)}, u32[]{:S(2)}) copy-start(pred[2]{0:T(512)(128)(4,1)} %get-tuple-element.237) | copy-start | bytes 10
  759.6 30.7 %copy-start.56 = (pred[2]{0:T(512)(128)(4,1)S(1)}, pred[2]{0:T(512)(128)(4,1)}, u32[]{:S(2)}) copy-start(pred[2]{0:T(512)(128)(4,1)} %compare_and_fusion.16) | copy-start | bytes 10
  761.2 35.6 %copy-start.43 = (pred[2]{0:T(512)(128)(4,1)S(1)}, pred[2]{0:T(512)(128)(4,1)}, u32[]{:S(2)}) copy-start(pred[2]{0:T(512)(128)(4,1)} %get-tuple-element.242) | copy-start | bytes 10
  761.2 36.5 %copy-start.42 = (pred[2]{0:T(512)(128)(4,1)S(1)}, pred[2]{0:T(512)(128)(4,1)}, u32[]{:S(2)}) copy-start(pred[2]{0:T(512)(128)(4,1)} %get-tuple-element.240) | copy-start | bytes 10
  770.2 33.8 %copy-start.22 = (pred[2]{0:T(512)(128)(4,1)S(1)}, pred[2]{0:T(512)(128)(4,1)}, u32[]{:S(2)}) copy-start(pred[2]{0:T(512)(128)(4,1)} %copy-done.20) | copy-start | bytes 10
  771.7 32.4 %copy-start.1 = (f32[19,16,16,1]{3,2,1,0:T(8,128)S(1)}, f32[19,16,16,1]{3,2,1,0:T(8,128)}, u32[]{:S(2)}) copy-start(f32[19,16,16,1]{3,2,1,0:T(8,128)} %get-tuple-element.131) | copy-start | bytes 58372
  (67 other events, 670.0 us)
where the time goes:
time: 929 us; the launch traced here: 918 us
  blocking collectives  504 us (54%)
  local copies, waits for them, and re-layouts  233 us (25%)
  other arithmetic  76.8 us (8%)
  starting transfers between devices  68.2 us (7%)
  waiting for transfers between devices  23.2 us (2%)
  between operations  10.6 us (1%)
    psum x3, blocking collectives, global_squares(): return lax.psum(jnp.sum(values * values), ('wide', 'narrow'))  300 us
    psum x2, blocking collectives, shards(): lax.psum(jnp.sum(direction * image_field), ('wide', 'narrow'))  204 us
    gather x110, local copies, waits for them, and re-layouts, fetch_piece(): return jnp.take(piece, brick_table[:, column], axis=0)  91 us
    another operation x36, local copies, waits for them, and re-layouts, fetch_piece(): return jnp.take(piece, brick_table[:, column], axis=0)  52 us
    select_n x110, other arithmetic, fetch_piece(): return jnp.take(piece, brick_table[:, column], axis=0)  38 us
    ppermute x8, starting transfers between devices, padded_2(): before = lax.ppermute(last, axis, up)  31 us
    slice x20, local copies, waits for them, and re-layouts, fetch_piece(): piece = source[:, low_x:high_x, low_y:high_y, low_z:high_z]  25.5 us
  transfers between devices with their start and end apart: 18, of which 12 were waited for; matrix products, arithmetic and copies ran while one was open for 3% of the time, Pallas kernels for 0%

commit v1 on v0

--- a/solution.py
+++ b/solution.py
@@ -103,6 +103,7 @@
 
 def shards(point_owner, point_cell, normals, strip_count, neighbours):
     owners = lax.axis_size("wide")
+    devices = owners * lax.axis_size("narrow")
     point_total = point_cell.shape[0]
     brick_table = neighbours[0, 0]
     brick_count = brick_table.shape[0]
@@ -179,8 +180,14 @@
     sources = [make_source(vector_rim[:, :, c]) for c in range(3)]
     right_side = divergence(sources, layout, brick_table, vector_field)
 
+    def global_sum(parts):
+        stacked = jnp.stack(parts)[None, :]
+        spread = jnp.broadcast_to(stacked, (devices, stacked.shape[1]))
+        gathered = lax.all_to_all(spread, ("wide", "narrow"), 0, 0, tiled=True)
+        return jnp.sum(gathered, axis=0)
+
     def global_squares(values):
-        return lax.psum(jnp.sum(values * values), ("wide", "narrow"))
+        return global_sum([jnp.sum(values * values)])[0]
 
     solution = jnp.zeros_like(right_side)
     residual = right_side
@@ -189,7 +196,7 @@
     for iteration in range(ITERS):
         field_rim = padded_2(direction[None, None], (("wide", 0), ("narrow", 1)), 1)
         image_field = stencil(make_source(field_rim), layout, brick_table, direction, diagonal)
-        step_size = norm_now / lax.psum(jnp.sum(direction * image_field), ("wide", "narrow"))
+        step_size = norm_now / global_sum([jnp.sum(direction * image_field)])[0]
         solution = solution + step_size * direction
         residual = residual - step_size * image_field
         norm_next = global_squares(residual)

time: 929 us -> 623 us (0.67)
  blocking collectives: 504 us -> 77.9 us
  waiting for transfers between devices: 23.2 us -> 89.2 us
  starting transfers between devices: 68.2 us -> 111 us
    psum x5 -> x0, blocking collectives: 504 us -> none  [the longest x3 300 us: global_squares(): return lax.psum(jnp.sum(values * values), ('wide', 'narrow'))]
    all_to_all x0 -> x2, blocking collectives: none -> 77.9 us  [global_sum(): gathered = lax.all_to_all(spread, ('wide', 'narrow'), 0, 0, tiled=True)]
    all_to_all x0 -> x4, waiting for transfers between devices: none -> 67.5 us  [global_sum(): gathered = lax.all_to_all(spread, ('wide', 'narrow'), 0, 0, tiled=True)]
    all_to_all x0 -> x4, starting transfers between devices: none -> 42.8 us  [global_sum(): gathered = lax.all_to_all(spread, ('wide', 'narrow'), 0, 0, tiled=True)]
  transfers between devices with their start and end apart: 18 -> 22, of which waited for: 12 -> 14; matrix products, arithmetic and copies ran while one was open for 3% -> 5% of each run, Pallas kernels for 0% -> 0%
where the time goes in v1:
time: 623 us; the launch traced here: 612 us
  local copies, waits for them, and re-layouts  241 us (39%)
  starting transfers between devices  111 us (18%)
  waiting for transfers between devices  89.2 us (14%)
  other arithmetic  80.7 us (13%)
  blocking collectives  77.9 us (13%)
  between operations  10.5 us (2%)
    gather x110, local copies, waits for them, and re-layouts, fetch_piece(): return jnp.take(piece, brick_table[:, column], axis=0)  93.4 us
    all_to_all x2, blocking collectives, global_sum(): gathered = lax.all_to_all(spread, ('wide', 'narrow'), 0, 0, tiled=True)  77.9 us
    all_to_all x4, waiting for transfers between devices, global_sum(): gathered = lax.all_to_all(spread, ('wide', 'narrow'), 0, 0, tiled=True)  67.5 us
    another operation x36, local copies, waits for them, and re-layouts, fetch_piece(): return jnp.take(piece, brick_table[:, column], axis=0)  50.8 us
    all_to_all x4, starting transfers between devices, global_sum(): gathered = lax.all_to_all(spread, ('wide', 'narrow'), 0, 0, tiled=True)  42.8 us
    select_n x110, other arithmetic, fetch_piece(): return jnp.take(piece, brick_table[:, column], axis=0)  34.4 us
    ppermute x8, starting transfers between devices, padded_2(): before = lax.ppermute(last, axis, up)  32.2 us
    slice x20, local copies, waits for them, and re-layouts, fetch_piece(): piece = source[:, low_x:high_x, low_y:high_y, low_z:high_z]  25.5 us
  transfers between devices with their start and end apart: 22, of which 14 were waited for; matrix products, arithmetic and copies ran while one was open for 5% of the time, Pallas kernels for 0%

profile of v1, /device:TPU:1, one launch (start us, length us, event | category | flops | bytes accessed | tf_op | source)
XLA Modules:
  0.0 611.8 jit_solution(11333270151844790405)
XLA Ops:
  2.1 5.1 sort.17
  7.2 1.9 slice_reduce_fusion.43
  9.8 4.5 gather_fusion
  14.4 4.5 gather_fusion.1
  19.6 4.3 scatter_custom_fusion
  24.7 11.6 %all-to-all-start = ((s32[64,1,32]{2,1,0:T(1,128)}), s32[64,1,32]{2,1,0:T(1,128)S(1)}, u32[]{:S(2)}, u32[]{:S(2)}) async-start(s32[64,1,32]{2,1,0:T(1,128)} %copy.849), calls=%async_computation | async-start | bytes 65536 | tf_op jit(solution)/shard_map/all_to_all | solution.py:135
  48.1 6.9 %scatter_custom_fusion.1 = f32[3,2048]{0,1:T(8,128)S(1)} fusion(s32[1024]{0:T(1024)S(1)} %broadcast_select_fusion.28, f32[3,1024]{0,1:T(8,128)S(1)} %copy.850, s32[1024]{0:T(1024)S(1)} %get-tuple-element.202, f32[]{:T(128)} %constant.111.clone.1), kind=kCustom, calls=%fused_computation.104 | custom fusion | bytes 24580
  56.2 10.9 %all-to-all-start.1 = ((f32[64,3,32]{2,1,0:T(4,128)}), f32[64,3,32]{2,1,0:T(4,128)S(1)}, u32[]{:S(2)}, u32[]{:S(2)}) async-start(f32[64,3,32]{2,1,0:T(4,128)} %bitcast.8), calls=%async_computation.1 | async-start | bytes 262144 | tf_op jit(solution)/shard_map/all_to_all | solution.py:136
  68.8 9.3 %all-to-all-done.1 = f32[64,3,32]{2,1,0:T(4,128)S(1)} async-done(((f32[64,3,32]{2,1,0:T(4,128)}), f32[64,3,32]{2,1,0:T(4,128)S(1)}, u32[]{:S(2)}, u32[]{:S(2)}) %all-to-all-start.1) | async-done | bytes 24608 | tf_op jit(solution)/shard_map/all_to_all | solution.py:136
  79.4 2.2 fusion
  82.1 2.3 collective-permute-start.1
  84.4 3.3 collective-permute-start
  90.7 4.6 collective-permute-start.2
  99.3 1.8 collective-permute-done.2
  103.1 1.9 reshape.603
  106.7 2.3 reshape.602
  109.0 1.7 slice_bitcast_fusion.7
  110.7 3.1 fusion.114
  113.7 3.7 copy.1039
  117.4 1.8 copy.1040
  123.2 1.6 gather_fusion.2
  127.5 3.6 collective-permute-start.4
  131.7 1.9 collective-permute-start.5
  133.7 3.3 collective-permute-done.5
  138.3 4.7 collective-permute-start.6
  145.8 1.9 reshape.606
  152.9 3.1 fusion.112
  190.2 1.7 copy.1049
  191.9 1.7 copy.1042
  193.7 2.0 gather_fusion.13
  197.0 1.9 gather_fusion.28
  206.5 1.7 copy.1047
  215.9 3.5 copy.1045
  221.5 1.8 copy.1046
  242.3 2.1 multiply_reduce_fusion.4
  245.2 42.7 %all_to_all.50 = f32[512,1,1]{2,1,0:T(1,128)S(1)} all-to-all(f32[512,1,1]{2,1,0:T(1,128)S(1)} %broadcast_in_dim.134), channel_id=1, replica_groups=mesh['wide'=64,'narrow'=8] {'wide','narrow'}, dimensions={0} | all-to-all | bytes 4096 | tf_op jit(solution)/shard_map/all_to_all | solution.py:186
  289.4 8.4 %all-to-all-start.2 = ((f32[512,1,1]{2,1,0:T(1,128)}), f32[512,1,1]{2,1,0:T(1,128)S(1)}, u32[]{:S(2)}, u32[]{:S(2)}) async-start(f32[512,1,1]{2,1,0:T(1,128)} %broadcast_in_dim.133), calls=%async_computation.2 | async-start | bytes 524288 | tf_op jit(solution)/shard_map/all_to_all | solution.py:186
  299.0 16.2 %all-to-all-done.2 = f32[512,1,1]{2,1,0:T(1,128)S(1)} async-done(((f32[512,1,1]{2,1,0:T(1,128)}), f32[512,1,1]{2,1,0:T(1,128)S(1)}, u32[]{:S(2)}, u32[]{:S(2)}) %all-to-all-start.2) | async-done | bytes 2080 | tf_op jit(solution)/shard_map/all_to_all | solution.py:186
  320.6 8.3 %all-to-all-start.4 = ((f32[512,1,1]{2,1,0:T(1,128)}), f32[512,1,1]{2,1,0:T(1,128)S(1)}, u32[]{:S(2)}, u32[]{:S(2)}) async-start(f32[512,1,1]{2,1,0:T(1,128)} %broadcast_in_dim.135), calls=%async_computation.4 | async-start | bytes 524288 | tf_op jit(solution)/shard_map/all_to_all | solution.py:186
  329.2 17.0 %all-to-all-done.4 = f32[512,1,1]{2,1,0:T(1,128)S(1)} async-done(((f32[512,1,1]{2,1,0:T(1,128)}), f32[512,1,1]{2,1,0:T(1,128)S(1)}, u32[]{:S(2)}, u32[]{:S(2)}) %all-to-all-start.4) | async-done | bytes 2080 | tf_op jit(solution)/shard_map/all_to_all | solution.py:186
  348.9 1.9 collective-permute-start.9
  350.9 3.6 collective-permute-start.8
  356.9 4.4 collective-permute-start.10
  367.2 1.6 fusion.105
  368.8 3.1 fusion.107
  390.7 1.6 gather_fusion.55
  392.3 1.6 gather_fusion.44
  416.5 3.5 copy.1055
  420.9 1.8 copy.1056
  425.4 2.0 multiply_reduce_fusion.2
  428.2 35.2 %all_to_all.51 = f32[512,1,1]{2,1,0:T(1,128)S(1)} all-to-all(f32[512,1,1]{2,1,0:T(1,128)S(1)} %broadcast_in_dim.136), channel_id=1, replica_groups=mesh['wide'=64,'narrow'=8] {'wide','narrow'}, dimensions={0} | all-to-all | bytes 4096 | tf_op jit(solution)/shard_map/all_to_all | solution.py:186
  468.1 8.3 %all-to-all-start.6 = ((f32[512,1,1]{2,1,0:T(1,128)}), f32[512,1,1]{2,1,0:T(1,128)S(1)}, u32[]{:S(2)}, u32[]{:S(2)}) async-start(f32[512,1,1]{2,1,0:T(1,128)} %broadcast_in_dim.137), calls=%async_computation.6 | async-start | bytes 524288 | tf_op jit(solution)/shard_map/all_to_all | solution.py:186
  476.5 17.1 %all-to-all-done.6 = f32[512,1,1]{2,1,0:T(1,128)S(1)} async-done(((f32[512,1,1]{2,1,0:T(1,128)}), f32[512,1,1]{2,1,0:T(1,128)S(1)}, u32[]{:S(2)}, u32[]{:S(2)}) %all-to-all-start.6) | async-done | bytes 2080 | tf_op jit(solution)/shard_map/all_to_all | solution.py:186
  496.2 1.9 collective-permute-start.13
  498.1 3.6 collective-permute-start.12
  504.1 4.2 collective-permute-start.14
  508.4 1.7 collective-permute-done.14
  511.2 1.9 reshape.612
  517.8 3.1 fusion.102
  559.5 3.5 copy.1065
  563.8 1.8 copy.1066
  569.6 2.0 multiply_reduce_fusion
  573.1 17.8 %all-to-all-start.7 = ((f32[512,1,1]{2,1,0:T(1,128)}), f32[512,1,1]{2,1,0:T(1,128)S(1)}, u32[]{:S(2)}, u32[]{:S(2)}) async-start(f32[512,1,1]{2,1,0:T(1,128)} %broadcast_in_dim.138), calls=%async_computation.7 | async-start | bytes 524288 | tf_op jit(solution)/shard_map/all_to_all | solution.py:186
  591.2 17.2 %all-to-all-done.7 = f32[512,1,1]{2,1,0:T(1,128)S(1)} async-done(((f32[512,1,1]{2,1,0:T(1,128)}), f32[512,1,1]{2,1,0:T(1,128)S(1)}, u32[]{:S(2)}, u32[]{:S(2)}) %all-to-all-start.7) | async-done | bytes 2080 | tf_op jit(solution)/shard_map/all_to_all | solution.py:186
  (670 shorter events, 240.0 us)
Async XLA Ops:
  9.1 33.3 %copy-start.74 = (s32[2]{0:T(128)}, s32[2]{0:T(128)S(1)}, u32[]{:S(2)}) copy-start(s32[2]{0:T(128)S(1)} %get-tuple-element.55) | copy-start | bytes 28
  9.1 33.3 %copy-start.72 = (s32[2]{0:T(128)}, s32[2]{0:T(128)S(1)}, u32[]{:S(2)}) copy-start(s32[2]{0:T(128)S(1)} %get-tuple-element.58) | copy-start | bytes 28
  9.1 33.8 %copy-start.73 = (s32[2]{0:T(128)}, s32[2]{0:T(128)S(1)}, u32[]{:S(2)}) copy-start(s32[2]{0:T(128)S(1)} %get-tuple-element.61) | copy-start | bytes 28
  9.1 33.8 %copy-start.71 = (s32[2]{0:T(128)}, s32[2]{0:T(128)S(1)}, u32[]{:S(2)}) copy-start(s32[2]{0:T(128)S(1)} %get-tuple-element.63) | copy-start | bytes 28
  9.1 33.8 %copy-start.69 = (s32[2]{0:T(128)}, s32[2]{0:T(128)S(1)}, u32[]{:S(2)}) copy-start(s32[2]{0:T(128)S(1)} %get-tuple-element.68) | copy-start | bytes 28
  9.1 33.8 %copy-start.65 = (s32[2]{0:T(128)}, s32[2]{0:T(128)S(1)}, u32[]{:S(2)}) copy-start(s32[2]{0:T(128)S(1)} %get-tuple-element.70) | copy-start | bytes 28
  9.2 33.8 %copy-start.63 = (s32[2]{0:T(128)}, s32[2]{0:T(128)S(1)}, u32[]{:S(2)}) copy-start(s32[2]{0:T(128)S(1)} %get-tuple-element.73) | copy-start | bytes 28
  14.4 33.5 %copy-start.17 = (f32[3,1024]{1,0:T(4,128)S(1)}, f32[3,1024]{1,0:T(4,128)}, u32[]{:S(2)}) copy-start(f32[3,1024]{1,0:T(4,128)} %param.21) | copy-start | bytes 36868
  24.7 31.5 %all-to-all-start = ((s32[64,1,32]{2,1,0:T(1,128)}), s32[64,1,32]{2,1,0:T(1,128)S(1)}, u32[]{:S(2)}, u32[]{:S(2)}) async-start(s32[64,1,32]{2,1,0:T(1,128)} %copy.849), calls=%async_computation | async-start | bytes 65536 | tf_op jit(solution)/shard_map/all_to_all | solution.py:135
  37.8 87.8 %copy-start.21 = (pred[2]{0:T(512)(128)(4,1)}, pred[2]{0:T(512)(128)(4,1)S(1)}, u32[]{:S(2)}) copy-start(pred[2]{0:T(512)(128)(4,1)S(1)} %get-tuple-element.229) | copy-start | bytes 10
  37.8 85.3 %copy-start.24 = (pred[2]{0:T(512)(128)(4,1)}, pred[2]{0:T(512)(128)(4,1)S(1)}, u32[]{:S(2)}) copy-start(pred[2]{0:T(512)(128)(4,1)S(1)} %get-tuple-element.231) | copy-start | bytes 10
  37.8 87.9 %copy-start.18 = (pred[2]{0:T(512)(128)(4,1)}, pred[2]{0:T(512)(128)(4,1)S(1)}, u32[]{:S(2)}) copy-start(pred[2]{0:T(512)(128)(4,1)S(1)} %get-tuple-element.230) | copy-start | bytes 10
  37.9 84.6 %copy-start.26 = (pred[2]{0:T(512)(128)(4,1)}, pred[2]{0:T(512)(128)(4,1)S(1)}, u32[]{:S(2)}) copy-start(pred[2]{0:T(512)(128)(4,1)S(1)} %get-tuple-element.232) | copy-start | bytes 10
  37.9 87.7 %copy-start.28 = (pred[2]{0:T(512)(128)(4,1)}, pred[2]{0:T(512)(128)(4,1)S(1)}, u32[]{:S(2)}) copy-start(pred[2]{0:T(512)(128)(4,1)S(1)} %get-tuple-element.233) | copy-start | bytes 10
  43.6 77.3 %copy-start.32 = (s32[1024]{0:T(1024)}, s32[1024]{0:T(1024)S(1)}, u32[]{:S(2)}) copy-start(s32[1024]{0:T(1024)S(1)} %get-tuple-element.226) | copy-start | bytes 12292
  43.6 76.5 %copy-start.31 = (s32[1024]{0:T(1024)}, s32[1024]{0:T(1024)S(1)}, u32[]{:S(2)}) copy-start(s32[1024]{0:T(1024)S(1)} %get-tuple-element.224) | copy-start | bytes 12292
  43.6 78.9 %copy-start.33 = (s32[1024]{0:T(1024)}, s32[1024]{0:T(1024)S(1)}, u32[]{:S(2)}) copy-start(s32[1024]{0:T(1024)S(1)} %get-tuple-element.225) | copy-start | bytes 12292
  56.2 21.9 %all-to-all-start.1 = ((f32[64,3,32]{2,1,0:T(4,128)}), f32[64,3,32]{2,1,0:T(4,128)S(1)}, u32[]{:S(2)}, u32[]{:S(2)}) async-start(f32[64,3,32]{2,1,0:T(4,128)} %bitcast.8), calls=%async_computation.1 | async-start | bytes 262144 | tf_op jit(solution)/shard_map/all_to_all | solution.py:136
  82.1 6.2 %collective-permute-start.1 = (f32[1,1,3,2,4096]{4,3,2,1,0:T(2,128)S(1)}, f32[1,1,3,2,4096]{4,3,2,1,0:T(2,128)S(1)}, u32[]{:S(2)}, u32[]{:S(2)}) collective-permute-start(f32[1,1,3,2,4096]{4,3,2,1,0:T(2,128)S(1)} %maximum_bitcast_fusion), channel_id=1, source_target_pairs={{8,0},{16,8},{24,16},{32,24},{40,32},{48,40},{56,48},{64,56},{72,6... | collective-permute-start | bytes 294920 | tf_op jit(solution)/shard_map/ppermute | solution.py:24
  84.4 4.9 collective-permute-start
  88.2 31.1 %copy-start.34 = (s32[1024]{0:T(1024)}, s32[1024]{0:T(1024)S(1)}, u32[]{:S(2)}) copy-start(s32[1024]{0:T(1024)S(1)} %get-tuple-element.223) | copy-start | bytes 12292
  89.4 9.9 %collective-permute-start.3 = (f32[3,1,3,2,4096]{4,3,2,1,0:T(2,128)S(1)}, f32[3,1,3,2,4096]{4,3,2,1,0:T(2,128)S(1)}, u32[]{:S(2)}, u32[]{:S(2)}) collective-permute-start(f32[3,1,3,2,4096]{4,3,2,1,0:T(2,128)S(1)} %pad_maximum_fusion.7), channel_id=1, source_target_pairs={{1,0},{2,1},{3,2},{4,3},{5,4},{6,5},{7,6},{9,8},{10,9},{11,10},{12... | collective-permute-start | bytes 884744 | tf_op jit(solution)/shard_map/ppermute | solution.py:24
  90.7 10.4 %collective-permute-start.2 = (f32[3,1,3,2,4096]{4,3,2,1,0:T(2,128)S(1)}, f32[3,1,3,2,4096]{4,3,2,1,0:T(2,128)S(1)}, u32[]{:S(2)}, u32[]{:S(2)}) collective-permute-start(f32[3,1,3,2,4096]{4,3,2,1,0:T(2,128)S(1)} %pad_maximum_fusion.7), channel_id=1, source_target_pairs={{0,1},{1,2},{2,3},{3,4},{4,5},{5,6},{6,7},{8,9},{9,10},{10,11},{11... | collective-permute-start | bytes 884744 | tf_op jit(solution)/shard_map/ppermute | solution.py:23
  119.3 23.7 %copy-start.91 = (s32[2]{0:T(128)S(1)}, s32[2]{0:T(128)}, u32[]{:S(2)}) copy-start(s32[2]{0:T(128)} %compare_select_fusion.4) | copy-start | bytes 28
  119.3 23.7 %copy-start.92 = (s32[2]{0:T(128)S(1)}, s32[2]{0:T(128)}, u32[]{:S(2)}) copy-start(s32[2]{0:T(128)} %compare_select_fusion.5) | copy-start | bytes 28
  127.5 6.2 %collective-permute-start.4 = (f32[1,1,2,4096]{3,2,1,0:T(2,128)S(1)}, f32[1,1,2,4096]{3,2,1,0:T(2,128)S(1)}, u32[]{:S(2)}, u32[]{:S(2)}) collective-permute-start(f32[1,1,2,4096]{3,2,1,0:T(2,128)S(1)} %mul.592), channel_id=1, source_target_pairs={{0,8},{8,16},{16,24},{24,32},{32,40},{40,48},{48,56},{56,64},{64,7... | collective-permute-start | bytes 98312 | tf_op jit(solution)/shard_map/ppermute | solution.py:23
  131.7 5.2 collective-permute-start.5
  137.0 6.8 %collective-permute-start.7 = (f32[3,1,2,4096]{3,2,1,0:T(2,128)S(1)}, f32[3,1,2,4096]{3,2,1,0:T(2,128)S(1)}, u32[]{:S(2)}, u32[]{:S(2)}) collective-permute-start(f32[3,1,2,4096]{3,2,1,0:T(2,128)S(1)} %constant_dynamic-update-slice_fusion), channel_id=1, source_target_pairs={{1,0},{2,1},{3,2},{4,3},{5,4},{6,5},{7,6},{9,8},{10,9},{11,10},{12... | collective-permute-start | bytes 294920 | tf_op jit(solution)/shard_map/ppermute | solution.py:24
  138.3 6.4 %collective-permute-start.6 = (f32[3,1,2,4096]{3,2,1,0:T(2,128)S(1)}, f32[3,1,2,4096]{3,2,1,0:T(2,128)S(1)}, u32[]{:S(2)}, u32[]{:S(2)}) collective-permute-start(f32[3,1,2,4096]{3,2,1,0:T(2,128)S(1)} %constant_dynamic-update-slice_fusion), channel_id=1, source_target_pairs={{0,1},{1,2},{2,3},{3,4},{4,5},{5,6},{6,7},{8,9},{9,10},{10,11},{11... | collective-permute-start | bytes 294920 | tf_op jit(solution)/shard_map/ppermute | solution.py:23
  173.1 48.4 %copy-start.3 = (f32[19,16,16,1]{3,2,1,0:T(8,128)S(1)}, f32[19,16,16,1]{3,2,1,0:T(8,128)}, u32[]{:S(2)}) copy-start(f32[19,16,16,1]{3,2,1,0:T(8,128)} %get-tuple-element.165) | copy-start | bytes 58372
  289.4 59.5 %copy-start.11 = (f32[1,1,2,4096]{3,2,1,0:T(2,128)S(1)}, f32[1,1,2,4096]{3,2,1,0:T(2,128)}, u32[]{:S(2)}) copy-start(f32[1,1,2,4096]{3,2,1,0:T(2,128)} %copy-done.10) | copy-start | bytes 98308
  289.4 25.7 %all-to-all-start.2 = ((f32[512,1,1]{2,1,0:T(1,128)}), f32[512,1,1]{2,1,0:T(1,128)S(1)}, u32[]{:S(2)}, u32[]{:S(2)}) async-start(f32[512,1,1]{2,1,0:T(1,128)} %broadcast_in_dim.133), calls=%async_computation.2 | async-start | bytes 524288 | tf_op jit(solution)/shard_map/all_to_all | solution.py:186
  319.1 44.1 %copy-start.5 = (f32[2,16,16,16]{3,2,1,0:T(8,128)}, f32[2,16,16,16]{3,2,1,0:T(8,128)S(1)}, u32[]{:S(2)}) copy-start(f32[2,16,16,16]{3,2,1,0:T(8,128)S(1)} %get-tuple-element.92) | copy-start | bytes 98308
  320.6 25.6 %all-to-all-start.4 = ((f32[512,1,1]{2,1,0:T(1,128)}), f32[512,1,1]{2,1,0:T(1,128)S(1)}, u32[]{:S(2)}, u32[]{:S(2)}) async-start(f32[512,1,1]{2,1,0:T(1,128)} %broadcast_in_dim.135), calls=%async_computation.4 | async-start | bytes 524288 | tf_op jit(solution)/shard_map/all_to_all | solution.py:186
  329.0 34.0 %copy-start.13 = (f32[1,1,2,4096]{3,2,1,0:T(2,128)}, f32[1,1,2,4096]{3,2,1,0:T(2,128)S(1)}, u32[]{:S(2)}) copy-start(f32[1,1,2,4096]{3,2,1,0:T(2,128)S(1)} %add.457) | copy-start | bytes 98308
  348.9 5.6 collective-permute-start.9
  350.9 4.7 collective-permute-start.8
  355.6 5.7 collective-permute-start.11
  356.9 5.9 collective-permute-start.10
  371.9 22.0 %copy-start.25 = (pred[2]{0:T(512)(128)(4,1)S(1)}, pred[2]{0:T(512)(128)(4,1)}, u32[]{:S(2)}) copy-start(pred[2]{0:T(512)(128)(4,1)} %copy-done.24) | copy-start | bytes 10
  371.9 23.7 %copy-start.27 = (pred[2]{0:T(512)(128)(4,1)S(1)}, pred[2]{0:T(512)(128)(4,1)}, u32[]{:S(2)}) copy-start(pred[2]{0:T(512)(128)(4,1)} %copy-done.26) | copy-start | bytes 10
  372.7 30.9 %copy-start.46 = (pred[2]{0:T(512)(128)(4,1)S(1)}, pred[2]{0:T(512)(128)(4,1)}, u32[]{:S(2)}) copy-start(pred[2]{0:T(512)(128)(4,1)} %get-tuple-element.243) | copy-start | bytes 10
  372.7 31.0 %copy-start.44 = (pred[2]{0:T(512)(128)(4,1)S(1)}, pred[2]{0:T(512)(128)(4,1)}, u32[]{:S(2)}) copy-start(pred[2]{0:T(512)(128)(4,1)} %get-tuple-element.236) | copy-start | bytes 10
  373.4 30.5 %copy-start.42 = (pred[2]{0:T(512)(128)(4,1)S(1)}, pred[2]{0:T(512)(128)(4,1)}, u32[]{:S(2)}) copy-start(pred[2]{0:T(512)(128)(4,1)} %get-tuple-element.235) | copy-start | bytes 10
  384.8 36.0 %copy-start.2 = (f32[19,16,16,1]{3,2,1,0:T(8,128)S(1)}, f32[19,16,16,1]{3,2,1,0:T(8,128)}, u32[]{:S(2)}) copy-start(f32[19,16,16,1]{3,2,1,0:T(8,128)} %get-tuple-element.147) | copy-start | bytes 58372
  425.4 40.5 %copy-start.6 = (f32[2,16,16,16]{3,2,1,0:T(8,128)S(1)}, f32[2,16,16,16]{3,2,1,0:T(8,128)}, u32[]{:S(2)}) copy-start(f32[2,16,16,16]{3,2,1,0:T(8,128)} %copy-done.5) | copy-start | bytes 98308
  427.4 68.7 %copy-start.12 = (f32[1,1,2,4096]{3,2,1,0:T(2,128)S(1)}, f32[1,1,2,4096]{3,2,1,0:T(2,128)}, u32[]{:S(2)}) copy-start(f32[1,1,2,4096]{3,2,1,0:T(2,128)} %copy-done.10) | copy-start | bytes 98308
  427.4 68.7 %copy-start.14 = (f32[1,1,2,4096]{3,2,1,0:T(2,128)S(1)}, f32[1,1,2,4096]{3,2,1,0:T(2,128)}, u32[]{:S(2)}) copy-start(f32[1,1,2,4096]{3,2,1,0:T(2,128)} %copy-done.13) | copy-start | bytes 98308
  468.1 25.6 %all-to-all-start.6 = ((f32[512,1,1]{2,1,0:T(1,128)}), f32[512,1,1]{2,1,0:T(1,128)S(1)}, u32[]{:S(2)}, u32[]{:S(2)}) async-start(f32[512,1,1]{2,1,0:T(1,128)} %broadcast_in_dim.137), calls=%async_computation.6 | async-start | bytes 524288 | tf_op jit(solution)/shard_map/all_to_all | solution.py:186
  496.2 5.6 collective-permute-start.13
  498.1 4.7 collective-permute-start.12
  502.8 5.6 collective-permute-start.15
  504.1 5.9 collective-permute-start.14
  521.7 30.3 %copy-start.47 = (pred[2]{0:T(512)(128)(4,1)S(1)}, pred[2]{0:T(512)(128)(4,1)}, u32[]{:S(2)}) copy-start(pred[2]{0:T(512)(128)(4,1)} %get-tuple-element.243) | copy-start | bytes 10
  521.7 30.4 %copy-start.45 = (pred[2]{0:T(512)(128)(4,1)S(1)}, pred[2]{0:T(512)(128)(4,1)}, u32[]{:S(2)}) copy-start(pred[2]{0:T(512)(128)(4,1)} %get-tuple-element.236) | copy-start | bytes 10
  521.7 30.6 %copy-start.43 = (pred[2]{0:T(512)(128)(4,1)S(1)}, pred[2]{0:T(512)(128)(4,1)}, u32[]{:S(2)}) copy-start(pred[2]{0:T(512)(128)(4,1)} %get-tuple-element.235) | copy-start | bytes 10
  521.7 30.7 %copy-start.56 = (pred[2]{0:T(512)(128)(4,1)S(1)}, pred[2]{0:T(512)(128)(4,1)}, u32[]{:S(2)}) copy-start(pred[2]{0:T(512)(128)(4,1)} %compare_and_fusion.16) | copy-start | bytes 10
  523.2 35.7 %copy-start.41 = (pred[2]{0:T(512)(128)(4,1)S(1)}, pred[2]{0:T(512)(128)(4,1)}, u32[]{:S(2)}) copy-start(pred[2]{0:T(512)(128)(4,1)} %get-tuple-element.240) | copy-start | bytes 10
  523.2 35.8 %copy-start.40 = (pred[2]{0:T(512)(128)(4,1)S(1)}, pred[2]{0:T(512)(128)(4,1)}, u32[]{:S(2)}) copy-start(pred[2]{0:T(512)(128)(4,1)} %get-tuple-element.239) | copy-start | bytes 10
  523.2 36.0 %copy-start.38 = (pred[2]{0:T(512)(128)(4,1)S(1)}, pred[2]{0:T(512)(128)(4,1)}, u32[]{:S(2)}) copy-start(pred[2]{0:T(512)(128)(4,1)} %get-tuple-element.238) | copy-start | bytes 10
  523.2 36.1 %copy-start.39 = (pred[2]{0:T(512)(128)(4,1)S(1)}, pred[2]{0:T(512)(128)(4,1)}, u32[]{:S(2)}) copy-start(pred[2]{0:T(512)(128)(4,1)} %get-tuple-element.241) | copy-start | bytes 10
  532.3 31.4 %copy-start.23 = (pred[2]{0:T(512)(128)(4,1)S(1)}, pred[2]{0:T(512)(128)(4,1)}, u32[]{:S(2)}) copy-start(pred[2]{0:T(512)(128)(4,1)} %copy-done.21) | copy-start | bytes 10
  533.8 30.0 %copy-start.1 = (f32[19,16,16,1]{3,2,1,0:T(8,128)S(1)}, f32[19,16,16,1]{3,2,1,0:T(8,128)}, u32[]{:S(2)}) copy-start(f32[19,16,16,1]{3,2,1,0:T(8,128)} %get-tuple-element.129) | copy-start | bytes 58372
  573.1 35.4 %all-to-all-start.7 = ((f32[512,1,1]{2,1,0:T(1,128)}), f32[512,1,1]{2,1,0:T(1,128)S(1)}, u32[]{:S(2)}, u32[]{:S(2)}) async-start(f32[512,1,1]{2,1,0:T(1,128)} %broadcast_in_dim.138), calls=%async_computation.7 | async-start | bytes 524288 | tf_op jit(solution)/shard_map/all_to_all | solution.py:186
  (71 other events, 753.7 us)

commit v2 on v1

v2 whole, which is shorter than its diff:
```python
import math

import jax
import jax.numpy as jnp
from jax import lax
from jax.experimental import pallas as pl
from jax.experimental.pallas import tpu as pltpu
from jax.sharding import PartitionSpec as P

ITERS = 3
CAP = 32
HIGHEST = lax.Precision.HIGHEST
ROWS, LANES = 16, 256


def _masks():
    shape = (ROWS, LANES)
    lane = lax.broadcasted_iota(jnp.int32, shape, 1)
    row = lax.broadcasted_iota(jnp.int32, shape, 0)
    return row, lane >> 4, lane & 15


def _neighbour_x(c, m, p, row):
    lo = jnp.where(row == 0, pltpu.roll(m, 1, 0), pltpu.roll(c, 1, 0))
    hi = jnp.where(row == ROWS - 1, pltpu.roll(p, ROWS - 1, 0), pltpu.roll(c, ROWS - 1, 0))
    return lo, hi


def _neighbour_y(c, m, p, y):
    lo = jnp.where(y == 0, pltpu.roll(m, 16, 1), pltpu.roll(c, 16, 1))
    hi = jnp.where(y == 15, pltpu.roll(p, LANES - 16, 1), pltpu.roll(c, LANES - 16, 1))
    return lo, hi


def _neighbour_z(c, m, p, z):
    lo = jnp.where(z == 0, pltpu.roll(m, LANES - 15, 1), pltpu.roll(c, 1, 1))
    hi = jnp.where(z == 15, pltpu.roll(p, 15, 1), pltpu.roll(c, LANES - 1, 1))
    return lo, hi


def _column(ex, ey, ez):
    return (ex + 1) * 9 + (ey + 1) * 3 + (ez + 1)


def _stencil_kernel(tab_ref, src_ref, diag_ref, out_ref):
    row, y, z = _masks()
    bricks = out_ref.shape[0]
    for b in range(bricks):
        own = src_ref[4 * bricks + b]

        def brick(ex, ey, ez):
            if ex == 0 and ey == 0 and ez == 0:
                return own
            return src_ref[tab_ref[b * 27 + _column(ex, ey, ez)]]

        planes = {}
        for ex in (-1, 0, 1):
            lines = {}
            for ey in (-1, 0, 1):
                c = brick(ex, ey, 0)
                lo, hi = _neighbour_z(c, brick(ex, ey, -1), brick(ex, ey, 1), z)
                lines[ey] = c + 0.5 * (lo + hi)
            lo, hi = _neighbour_y(lines[0], lines[-1], lines[1], y)
            planes[ex] = lines[0] + 0.5 * (lo + hi)
        lo, hi = _neighbour_x(planes[0], planes[-1], planes[1], row)
        smoothed = planes[0] + 0.5 * (lo + hi)
        out_ref[b] = (diag_ref[b] + 2.0) * own - 2.0 * smoothed


def _divergence_kernel(tab_ref, src_ref, out_ref):
    row, y, z = _masks()
    bricks = out_ref.shape[0]
    for b in range(bricks):

        def brick(k, ex, ey, ez):
            if ex == 0 and ey == 0 and ez == 0:
                return src_ref[k, 4 * bricks + b]
            return src_ref[k, tab_ref[b * 27 + _column(ex, ey, ez)]]

        lo, hi = _neighbour_x(brick(0, 0, 0, 0), brick(0, -1, 0, 0), brick(0, 1, 0, 0), row)
        change_x = hi - lo
        lo, hi = _neighbour_y(brick(1, 0, 0, 0), brick(1, 0, -1, 0), brick(1, 0, 1, 0), y)
        change_y = hi - lo
        lo, hi = _neighbour_z(brick(2, 0, 0, 0), brick(2, 0, 0, -1), brick(2, 0, 0, 1), z)
        change_z = hi - lo
        out_ref[b] = -4.0 * ((change_x + change_y) + change_z)


def _local_call(kernel, out_shape, operands, flops):
    spaces = [pltpu.SMEM] + [pltpu.VMEM] * (len(operands) - 1)
    moved = sum(int(a.size) * 4 for a in operands) + math.prod(out_shape) * 4
    return pl.pallas_call(
        kernel,
        out_shape=jax.ShapeDtypeStruct(out_shape, jnp.float32),
        in_specs=[pl.BlockSpec(memory_space=s) for s in spaces],
        out_specs=pl.BlockSpec(memory_space=pltpu.VMEM),
        cost_estimate=pl.CostEstimate(flops=flops, bytes_accessed=moved, transcendentals=0),
    )(*operands)


def halo(field):
    n_wide, n_narrow = lax.axis_size("wide"), lax.axis_size("narrow")
    pieces = []
    for dw in (-1, 0, 1):
        for dn in (-1, 0, 1):
            if dw == 0 and dn == 0:
                pieces.append(field)
                continue
            pairs = [
                ((w + dw) * n_narrow + n + dn, w * n_narrow + n)
                for w in range(n_wide)
                for n in range(n_narrow)
                if 0 <= w + dw < n_wide and 0 <= n + dn < n_narrow
            ]
            pieces.append(lax.ppermute(field, ("wide", "narrow"), pairs))
    zero_shape = field.shape[:-3] + (1,) + field.shape[-2:]
    pieces.append(jnp.zeros(zero_shape, field.dtype))
    return jnp.concatenate(pieces, axis=-3)


def shards(point_owner, point_cell, normals, strip_count, neighbours):
    owners = lax.axis_size("wide")
    devices = owners * lax.axis_size("narrow")
    point_total = point_cell.shape[0]
    bricks = neighbours.shape[2]
    table = neighbours.reshape(bricks * 27)

    owner = point_owner[:, 0]
    slots = jnp.arange(point_total, dtype=jnp.int32)
    is_live = slots < strip_count[0]
    code = jnp.where(is_live, point_cell + 1, 0).astype(jnp.float32)
    owner_hot = (owner[:, None] == jnp.arange(owners, dtype=jnp.int32)[None, :]).astype(jnp.bfloat16)
    earlier = (slots[None, :] < slots[:, None]).astype(jnp.bfloat16)
    before = jnp.dot(earlier, owner_hot, preferred_element_type=jnp.float32)
    rank = jnp.sum(before * owner_hot.astype(jnp.float32), axis=1).astype(jnp.int32)
    dest = owner * CAP + rank
    payload = jnp.concatenate([code[:, None], normals.T], axis=1)
    place_hot = (jnp.arange(owners * CAP, dtype=jnp.int32)[:, None] == dest[None, :]).astype(jnp.float32)
    send = jnp.dot(place_hot, payload, precision=HIGHEST, preferred_element_type=jnp.float32)
    got = lax.all_to_all(send.reshape(owners, CAP, 4), "wide", 0, 0, tiled=True).reshape(owners * CAP, 4)

    cell = got[:, 0].astype(jnp.int32) - 1
    brick_x = cell >> 8
    cell_yz = cell & (LANES - 1)
    bx_hot = (brick_x[:, None] == jnp.arange(bricks * ROWS, dtype=jnp.int32)[None, :]).astype(jnp.float32)
    yz_hot = (cell_yz[:, None] == jnp.arange(LANES, dtype=jnp.int32)[None, :]).astype(jnp.float32)
    weighted = jnp.concatenate([bx_hot * got[:, 1:2], bx_hot * got[:, 2:3], bx_hot * got[:, 3:4], bx_hot], axis=1)
    splatted = jnp.einsum("pa,pb->ab", weighted, yz_hot, precision=HIGHEST, preferred_element_type=jnp.float32)
    splatted = splatted.reshape(4, bricks, ROWS, LANES)
    vector_field = splatted[:3]
    diagonal = 14.5 + 2.0 * splatted[3]

    shape = (bricks, ROWS, LANES)
    right_side = _local_call(_divergence_kernel, shape, [table, halo(vector_field)], 20 * bricks * 4096)

    def global_sum(parts):
        stacked = jnp.stack(parts)[None, :]
        spread = jnp.broadcast_to(stacked, (devices, stacked.shape[1]))
        gathered = lax.all_to_all(spread, ("wide", "narrow"), 0, 0, tiled=True)
        return jnp.sum(gathered, axis=0)

    residual = right_side
    solution = jnp.zeros_like(right_side)
    for iteration in range(ITERS):
        image_r = _local_call(_stencil_kernel, shape, [table, halo(residual), diagonal], 60 * bricks * 4096)
        sums = global_sum([jnp.sum(residual * residual), jnp.sum(residual * image_r)])
        norm_now, curvature = sums[0], sums[1]
        if iteration == 0:
            step_size = norm_now / curvature
            direction, image_field = residual, image_r
        else:
            ratio = norm_now / norm_before
            step_size = norm_now / (curvature - ratio * norm_now / step_before)
            direction = residual + ratio * direction
            image_field = image_r + ratio * image_field
        solution = solution + step_size * direction
        residual = residual - step_size * image_field
        norm_before, step_before = norm_now, step_size
    out = (1, 1, bricks, ROWS * LANES)
    return solution.reshape(out), residual.reshape(out)


def solution(mesh):
    return jax.shard_map(
        shards,
        mesh=mesh,
        in_specs=(
            P(("wide", "narrow"), None),
            P(("wide", "narrow")),
            P(None, ("wide", "narrow")),
            P(("wide", "narrow")),
            P("wide", "narrow", None, None),
        ),
        out_specs=(P("wide", "narrow", None, None), P("wide", "narrow", None, None)),
        check_vma=False,
    )
```

time: 623 us -> 283 us (0.45); the launches traced: 612 us -> 282 us
  local copies, waits for them, and re-layouts: 241 us -> 9.42 us
  other arithmetic: 80.7 us -> 13 us
  waiting for transfers between devices: 89.2 us -> 23.4 us
  blocking collectives: 77.9 us -> 122 us
  starting transfers between devices: 111 us -> 85.6 us
  Pallas kernels: 0 us -> 9.01 us
    gather x112 -> x0, local copies, waits for them, and re-layouts: 102 us -> none  [the longest x110 93.4 us: fetch_piece(): return jnp.take(piece, brick_table[:, column], axis=0)]
    all_to_all x6 -> x0, waiting for transfers between devices: 76.8 us -> none  [the longest x4 67.5 us: global_sum(): gathered = lax.all_to_all(spread, ('wide', 'narrow'), 0, 0, tiled=True)]
    all_to_all x6 -> x0, starting transfers between devices: 65.3 us -> none  [the longest x4 42.8 us: global_sum(): gathered = lax.all_to_all(spread, ('wide', 'narrow'), 0, 0, tiled=True)]
    another operation x46 -> x0, local copies, waits for them, and re-layouts: 54.3 us -> none  [the longest x36 50.8 us: fetch_piece(): return jnp.take(piece, brick_table[:, column], axis=0)]
    ppermute x16 -> x32, starting transfers between devices: 45.4 us -> 85.6 us  [halo(): pieces.append(lax.ppermute(field, ('wide', 'narrow'), pairs))]
    select_n x114 -> x0, other arithmetic: 34.4 us -> none  [the longest x110 34.4 us: fetch_piece(): return jnp.take(piece, brick_table[:, column], axis=0)]
    slice x24 -> x5, local copies, waits for them, and re-layouts: 27.7 us -> 1.82 us  [the longest x3 1.79 us: shards(): norm_now, curvature = (sums[0], sums[1])]
    all_to_all x2 -> x3, blocking collectives: 77.9 us -> 101 us  [global_sum(): gathered = lax.all_to_all(spread, ('wide', 'narrow'), 0, 0, tiled=True)]
  transfers between devices with their start and end apart: 22 -> 32, of which waited for: 14 -> 8; matrix products, arithmetic and copies ran while one was open for 5% -> 1% of each run, Pallas kernels for 0% -> 0%
where the time goes in v2:
time: 283 us; the launch traced here: 282 us
  blocking collectives  122 us (43%)
  starting transfers between devices  85.6 us (30%)
  waiting for transfers between devices  23.4 us (8%)
  other arithmetic  13 us (5%)
  between operations  11.7 us (4%)
  local copies, waits for them, and re-layouts  9.42 us (3%)
  Pallas kernels  9.01 us (3%)
  matrix products  7.35 us (3%)
    all_to_all x3, blocking collectives, global_sum(): gathered = lax.all_to_all(spread, ('wide', 'narrow'), 0, 0, tiled=True)  101 us
    ppermute x32, starting transfers between devices, halo(): pieces.append(lax.ppermute(field, ('wide', 'narrow'), pairs))  85.6 us
    ppermute x32, waiting for transfers between devices, halo(): pieces.append(lax.ppermute(field, ('wide', 'narrow'), pairs))  23.4 us
    all_to_all x1, blocking collectives, shards(): lax.all_to_all(send.reshape(owners, CAP, 4), 'wide', 0, 0, tiled=True)  20.8 us
    pallas_call x4, Pallas kernels, _local_call(): pl.pallas_call(kernel, out_shape=jax.ShapeDtypeStruct(out_shape, jnp.floa...  9.01 us
  transfers between devices with their start and end apart: 32, of which 8 were waited for; matrix products, arithmetic and copies ran while one was open for 1% of the time, Pallas kernels for 0%

profile of v2, /device:TPU:1, one launch (start us, length us, event | category | flops | bytes accessed | tf_op | source)
XLA Modules:
  0.0 281.6 jit_solution(9966058144808812894)
XLA Ops:
  0.7 1.4 fusion.5
  2.7 3.7 %fusion = f32[2048,4]{0,1:T(4,128)S(1)} fusion(s32[1024]{0:T(1024)S(1)} %convert_add_fusion, f32[1024,3]{0,1:T(4,128)S(1)} %bitcast.55, f32[1024,1]{0,1:T(1,128)S(1)} %bitcast.54), kind=kOutput, calls=%fused_computation.1 | convolution fusion | flops 102764544 | bytes 53248 | tf_op jit(solution)/shard_map/dot_general | solution.py:139
  6.8 20.8 %all_to_all.23 = f32[64,1,128]{2,1,0:T(1,128)S(1)} all-to-all(f32[64,1,128]{2,1,0:T(1,128)S(1)} %reshape.59), channel_id=1, replica_groups=mesh['wide'=64,'narrow'=8] {'wide'}, dimensions={0} | all-to-all | bytes 65536 | tf_op jit(solution)/shard_map/all_to_all | solution.py:140
  28.1 0.7 reduce.3
  29.5 1.1 fusion.17
  30.7 2.2 fusion.3
  33.0 4.6 %collective-permute-start = (f32[3,2,16,256]{3,2,1,0:T(8,128)S(1)}, f32[3,2,16,256]{3,2,1,0:T(8,128)S(1)}, u32[]{:S(2)}, u32[]{:S(2)}) collective-permute-start(f32[3,2,16,256]{3,2,1,0:T(8,128)S(1)} %bitcast.37), channel_id=1, source_target_pairs={{0,9},{1,10},{2,11},{3,12},{4,13},{5,14},{6,15},{8,17},{9,18},{10,... | collective-permute-start | bytes 294920 | tf_op jit(solution)/shard_map/ppermute | solution.py:115
  38.2 1.9 collective-permute-start.1
  40.1 1.3 collective-permute-start.2
  41.4 4.6 %collective-permute-start.3 = (f32[3,2,16,256]{3,2,1,0:T(8,128)S(1)}, f32[3,2,16,256]{3,2,1,0:T(8,128)S(1)}, u32[]{:S(2)}, u32[]{:S(2)}) collective-permute-start(f32[3,2,16,256]{3,2,1,0:T(8,128)S(1)} %bitcast.40), channel_id=1, source_target_pairs={{0,1},{1,2},{2,3},{3,4},{4,5},{5,6},{6,7},{8,9},{9,10},{10,11},{11... | collective-permute-start | bytes 294920 | tf_op jit(solution)/shard_map/ppermute | solution.py:115
  46.1 1.3 collective-permute-start.4
  47.4 4.7 %collective-permute-start.5 = (f32[3,2,16,256]{3,2,1,0:T(8,128)S(1)}, f32[3,2,16,256]{3,2,1,0:T(8,128)S(1)}, u32[]{:S(2)}, u32[]{:S(2)}) collective-permute-start(f32[3,2,16,256]{3,2,1,0:T(8,128)S(1)} %bitcast.42), channel_id=1, source_target_pairs={{8,1},{9,2},{10,3},{11,4},{12,5},{13,6},{14,7},{16,9},{17,10},{18,... | collective-permute-start | bytes 294920 | tf_op jit(solution)/shard_map/ppermute | solution.py:115
  52.1 1.9 collective-permute-start.6
  54.0 1.3 collective-permute-start.7
  55.5 2.6 collective-permute-done.6
  58.0 5.5 %collective-permute-done.7 = f32[3,2,16,256]{3,2,1,0:T(8,128)S(1)} collective-permute-done((f32[3,2,16,256]{3,2,1,0:T(8,128)S(1)}, f32[3,2,16,256]{3,2,1,0:T(8,128)S(1)}, u32[]{:S(2)}, u32[]{:S(2)}) %collective-permute-start.7) | collective-permute-done | bytes 98336 | tf_op jit(solution)/shard_map/ppermute | solution.py:115
  63.6 0.9 copy-done
  64.5 1.9 shard_map.68
  66.5 5.2 %collective-permute-start.8 = (f32[2,16,256]{2,1,0:T(8,128)}, f32[2,16,256]{2,1,0:T(8,128)S(1)}, u32[]{:S(2)}, u32[]{:S(2)}) collective-permute-start(f32[2,16,256]{2,1,0:T(8,128)} %shard_map.68), channel_id=1, source_target_pairs={{0,9},{1,10},{2,11},{3,12},{4,13},{5,14},{6,15},{8,17},{9,18},{10,... | collective-permute-start | bytes 98312 | tf_op jit(solution)/shard_map/ppermute | solution.py:115
  72.3 3.2 %collective-permute-start.9 = (f32[2,16,256]{2,1,0:T(8,128)}, f32[2,16,256]{2,1,0:T(8,128)S(1)}, u32[]{:S(2)}, u32[]{:S(2)}) collective-permute-start(f32[2,16,256]{2,1,0:T(8,128)} %shard_map.68), channel_id=1, source_target_pairs={{0,8},{1,9},{2,10},{3,11},{4,12},{5,13},{6,14},{7,15},{8,16},{9,17... | collective-permute-start | bytes 98312 | tf_op jit(solution)/shard_map/ppermute | solution.py:115
  75.4 1.3 collective-permute-start.10
  76.7 5.2 %collective-permute-start.11 = (f32[2,16,256]{2,1,0:T(8,128)}, f32[2,16,256]{2,1,0:T(8,128)S(1)}, u32[]{:S(2)}, u32[]{:S(2)}) collective-permute-start(f32[2,16,256]{2,1,0:T(8,128)} %shard_map.68), channel_id=1, source_target_pairs={{0,1},{1,2},{2,3},{3,4},{4,5},{5,6},{6,7},{8,9},{9,10},{10,11},{11... | collective-permute-start | bytes 98312 | tf_op jit(solution)/shard_map/ppermute | solution.py:115
  81.9 1.3 collective-permute-start.12
  83.2 5.1 %collective-permute-start.13 = (f32[2,16,256]{2,1,0:T(8,128)}, f32[2,16,256]{2,1,0:T(8,128)S(1)}, u32[]{:S(2)}, u32[]{:S(2)}) collective-permute-start(f32[2,16,256]{2,1,0:T(8,128)} %shard_map.68), channel_id=1, source_target_pairs={{8,1},{9,2},{10,3},{11,4},{12,5},{13,6},{14,7},{16,9},{17,10},{18,... | collective-permute-start | bytes 98312 | tf_op jit(solution)/shard_map/ppermute | solution.py:115
  88.3 1.9 collective-permute-start.14
  90.3 1.3 collective-permute-start.15
  91.6 0.8 constant_dynamic-update-slice_fusion.15
  92.4 1.4 collective-permute-done.14
  93.8 3.8 %collective-permute-done.15 = f32[2,16,256]{2,1,0:T(8,128)S(1)} collective-permute-done((f32[2,16,256]{2,1,0:T(8,128)}, f32[2,16,256]{2,1,0:T(8,128)S(1)}, u32[]{:S(2)}, u32[]{:S(2)}) %collective-permute-start.15) | collective-permute-done | bytes 32800 | tf_op jit(solution)/shard_map/ppermute | solution.py:115
  97.6 0.7 copy-done.4
  98.3 2.3 shard_map.69
  100.7 1.5 multiply_reduce_fusion.5
  102.2 1.3 pad_maximum_fusion
  103.6 36.7 %all_to_all.24 = f32[512,1,2]{2,1,0:T(1,128)S(1)} all-to-all(f32[512,1,2]{2,1,0:T(1,128)S(1)} %broadcast_in_dim.17), channel_id=1, replica_groups=mesh['wide'=64,'narrow'=8] {'wide','narrow'}, dimensions={0} | all-to-all | bytes 8192 | tf_op jit(solution)/shard_map/all_to_all | solution.py:159
  142.8 2.7 collective-permute-start.16
  145.5 2.6 collective-permute-start.17
  148.0 1.3 collective-permute-start.18
  149.3 4.1 %collective-permute-start.19 = (f32[2,16,256]{2,1,0:T(8,128)S(1)}, f32[2,16,256]{2,1,0:T(8,128)S(1)}, u32[]{:S(2)}, u32[]{:S(2)}) collective-permute-start(f32[2,16,256]{2,1,0:T(8,128)S(1)} %multiply_subtract_fusion.2), channel_id=1, source_target_pairs={{0,1},{1,2},{2,3},{3,4},{4,5},{5,6},{6,7},{8,9},{9,10},{10,11},{11... | collective-permute-start | bytes 98312 | tf_op jit(solution)/shard_map/ppermute | solution.py:115
  153.4 1.3 collective-permute-start.20
  154.7 4.7 %collective-permute-start.21 = (f32[2,16,256]{2,1,0:T(8,128)S(1)}, f32[2,16,256]{2,1,0:T(8,128)S(1)}, u32[]{:S(2)}, u32[]{:S(2)}) collective-permute-start(f32[2,16,256]{2,1,0:T(8,128)S(1)} %multiply_subtract_fusion.2), channel_id=1, source_target_pairs={{8,1},{9,2},{10,3},{11,4},{12,5},{13,6},{14,7},{16,9},{17,10},{18,... | collective-permute-start | bytes 98312 | tf_op jit(solution)/shard_map/ppermute | solution.py:115
  159.5 1.9 collective-permute-start.22
  161.4 1.3 collective-permute-start.23
  162.8 1.9 collective-permute-done.22
  164.7 3.2 %collective-permute-done.23 = f32[2,16,256]{2,1,0:T(8,128)S(1)} collective-permute-done((f32[2,16,256]{2,1,0:T(8,128)S(1)}, f32[2,16,256]{2,1,0:T(8,128)S(1)}, u32[]{:S(2)}, u32[]{:S(2)}) %collective-permute-start.23) | collective-permute-done | bytes 32800 | tf_op jit(solution)/shard_map/ppermute | solution.py:115
  167.9 0.7 copy-done.5
  168.6 2.4 shard_map.70
  171.0 1.5 multiply_reduce_fusion.3
  172.5 1.3 pad_maximum_fusion.1
  174.0 32.3 %all_to_all.25 = f32[512,1,2]{2,1,0:T(1,128)S(1)} all-to-all(f32[512,1,2]{2,1,0:T(1,128)S(1)} %broadcast_in_dim.18), channel_id=1, replica_groups=mesh['wide'=64,'narrow'=8] {'wide','narrow'}, dimensions={0} | all-to-all | bytes 8192 | tf_op jit(solution)/shard_map/all_to_all | solution.py:159
  211.8 2.7 collective-permute-start.24
  214.5 2.6 collective-permute-start.25
  217.1 1.3 collective-permute-start.26
  218.4 4.1 %collective-permute-start.27 = (f32[2,16,256]{2,1,0:T(8,128)S(1)}, f32[2,16,256]{2,1,0:T(8,128)S(1)}, u32[]{:S(2)}, u32[]{:S(2)}) collective-permute-start(f32[2,16,256]{2,1,0:T(8,128)S(1)} %multiply_subtract_fusion.1), channel_id=1, source_target_pairs={{0,1},{1,2},{2,3},{3,4},{4,5},{5,6},{6,7},{8,9},{9,10},{10,11},{11... | collective-permute-start | bytes 98312 | tf_op jit(solution)/shard_map/ppermute | solution.py:115
  222.5 1.3 collective-permute-start.28
  223.8 4.7 %collective-permute-start.29 = (f32[2,16,256]{2,1,0:T(8,128)S(1)}, f32[2,16,256]{2,1,0:T(8,128)S(1)}, u32[]{:S(2)}, u32[]{:S(2)}) collective-permute-start(f32[2,16,256]{2,1,0:T(8,128)S(1)} %multiply_subtract_fusion.1), channel_id=1, source_target_pairs={{8,1},{9,2},{10,3},{11,4},{12,5},{13,6},{14,7},{16,9},{17,10},{18,... | collective-permute-start | bytes 98312 | tf_op jit(solution)/shard_map/ppermute | solution.py:115
  228.5 1.9 collective-permute-start.30
  230.5 1.3 collective-permute-start.31
  231.9 1.9 collective-permute-done.30
  233.8 3.2 %collective-permute-done.31 = f32[2,16,256]{2,1,0:T(8,128)S(1)} collective-permute-done((f32[2,16,256]{2,1,0:T(8,128)S(1)}, f32[2,16,256]{2,1,0:T(8,128)S(1)}, u32[]{:S(2)}, u32[]{:S(2)}) %collective-permute-start.31) | collective-permute-done | bytes 32800 | tf_op jit(solution)/shard_map/ppermute | solution.py:115
  237.0 0.7 copy-done.6
  237.7 2.4 shard_map.71
  240.0 1.5 multiply_reduce_fusion.1
  241.5 1.3 pad_maximum_fusion.2
  243.0 32.3 %all_to_all.26 = f32[512,1,2]{2,1,0:T(1,128)S(1)} all-to-all(f32[512,1,2]{2,1,0:T(1,128)S(1)} %broadcast_in_dim.19), channel_id=1, replica_groups=mesh['wide'=64,'narrow'=8] {'wide','narrow'}, dimensions={0} | all-to-all | bytes 8192 | tf_op jit(solution)/shard_map/all_to_all | solution.py:159
  (112 shorter events, 8.3 us)
Async XLA Ops:
  0.6 1.4 copy-start.8
  0.6 2.1 copy-start.9
  0.6 2.1 copy-start.10
  30.7 6.9 %copy-start.11 = (s32[1,1,2,27]{3,2,1,0:T(2,128)S(1)}, s32[1,1,2,27]{3,2,1,0:T(2,128)}, u32[]{:S(2)}) copy-start(s32[1,1,2,27]{3,2,1,0:T(2,128)} %param.9) | copy-start | bytes 652
  33.0 14.4 %collective-permute-start = (f32[3,2,16,256]{3,2,1,0:T(8,128)S(1)}, f32[3,2,16,256]{3,2,1,0:T(8,128)S(1)}, u32[]{:S(2)}, u32[]{:S(2)}) collective-permute-start(f32[3,2,16,256]{3,2,1,0:T(8,128)S(1)} %bitcast.37), channel_id=1, source_target_pairs={{0,9},{1,10},{2,11},{3,12},{4,13},{5,14},{6,15},{8,17},{9,18},{10,... | collective-permute-start | bytes 294920 | tf_op jit(solution)/shard_map/ppermute | solution.py:115
  38.2 13.9 %collective-permute-start.1 = (f32[3,2,16,256]{3,2,1,0:T(8,128)S(1)}, f32[3,2,16,256]{3,2,1,0:T(8,128)S(1)}, u32[]{:S(2)}, u32[]{:S(2)}) collective-permute-start(f32[3,2,16,256]{3,2,1,0:T(8,128)S(1)} %bitcast.38), channel_id=1, source_target_pairs={{0,8},{1,9},{2,10},{3,11},{4,12},{5,13},{6,14},{7,15},{8,16},{9,17... | collective-permute-start | bytes 294920 | tf_op jit(solution)/shard_map/ppermute | solution.py:115
  40.1 13.9 %collective-permute-start.2 = (f32[3,2,16,256]{3,2,1,0:T(8,128)S(1)}, f32[3,2,16,256]{3,2,1,0:T(8,128)S(1)}, u32[]{:S(2)}, u32[]{:S(2)}) collective-permute-start(f32[3,2,16,256]{3,2,1,0:T(8,128)S(1)} %bitcast.39), channel_id=1, source_target_pairs={{1,8},{2,9},{3,10},{4,11},{5,12},{6,13},{7,14},{9,16},{10,17},{11,... | collective-permute-start | bytes 294920 | tf_op jit(solution)/shard_map/ppermute | solution.py:115
  41.4 13.9 %collective-permute-start.3 = (f32[3,2,16,256]{3,2,1,0:T(8,128)S(1)}, f32[3,2,16,256]{3,2,1,0:T(8,128)S(1)}, u32[]{:S(2)}, u32[]{:S(2)}) collective-permute-start(f32[3,2,16,256]{3,2,1,0:T(8,128)S(1)} %bitcast.40), channel_id=1, source_target_pairs={{0,1},{1,2},{2,3},{3,4},{4,5},{5,6},{6,7},{8,9},{9,10},{10,11},{11... | collective-permute-start | bytes 294920 | tf_op jit(solution)/shard_map/ppermute | solution.py:115
  46.1 9.3 %collective-permute-start.4 = (f32[3,2,16,256]{3,2,1,0:T(8,128)S(1)}, f32[3,2,16,256]{3,2,1,0:T(8,128)S(1)}, u32[]{:S(2)}, u32[]{:S(2)}) collective-permute-start(f32[3,2,16,256]{3,2,1,0:T(8,128)S(1)} %bitcast.41), channel_id=1, source_target_pairs={{1,0},{2,1},{3,2},{4,3},{5,4},{6,5},{7,6},{9,8},{10,9},{11,10},{12... | collective-permute-start | bytes 294920 | tf_op jit(solution)/shard_map/ppermute | solution.py:115
  47.4 8.0 %collective-permute-start.5 = (f32[3,2,16,256]{3,2,1,0:T(8,128)S(1)}, f32[3,2,16,256]{3,2,1,0:T(8,128)S(1)}, u32[]{:S(2)}, u32[]{:S(2)}) collective-permute-start(f32[3,2,16,256]{3,2,1,0:T(8,128)S(1)} %bitcast.42), channel_id=1, source_target_pairs={{8,1},{9,2},{10,3},{11,4},{12,5},{13,6},{14,7},{16,9},{17,10},{18,... | collective-permute-start | bytes 294920 | tf_op jit(solution)/shard_map/ppermute | solution.py:115
  52.1 5.9 %collective-permute-start.6 = (f32[3,2,16,256]{3,2,1,0:T(8,128)S(1)}, f32[3,2,16,256]{3,2,1,0:T(8,128)S(1)}, u32[]{:S(2)}, u32[]{:S(2)}) collective-permute-start(f32[3,2,16,256]{3,2,1,0:T(8,128)S(1)} %bitcast.43), channel_id=1, source_target_pairs={{8,0},{9,1},{10,2},{11,3},{12,4},{13,5},{14,6},{15,7},{16,8},{17,9... | collective-permute-start | bytes 294920 | tf_op jit(solution)/shard_map/ppermute | solution.py:115
  54.0 9.5 %collective-permute-start.7 = (f32[3,2,16,256]{3,2,1,0:T(8,128)S(1)}, f32[3,2,16,256]{3,2,1,0:T(8,128)S(1)}, u32[]{:S(2)}, u32[]{:S(2)}) collective-permute-start(f32[3,2,16,256]{3,2,1,0:T(8,128)S(1)} %bitcast.44), channel_id=1, source_target_pairs={{9,0},{10,1},{11,2},{12,3},{13,4},{14,5},{15,6},{17,8},{18,9},{19,... | collective-permute-start | bytes 294920 | tf_op jit(solution)/shard_map/ppermute | solution.py:115
  63.6 0.9 copy-start
  66.5 34.2 %copy-start.1 = (f32[2,16,256]{2,1,0:T(8,128)S(1)}, f32[2,16,256]{2,1,0:T(8,128)}, u32[]{:S(2)}) copy-start(f32[2,16,256]{2,1,0:T(8,128)} %shard_map.68) | copy-start | bytes 98308
  66.5 16.8 %collective-permute-start.8 = (f32[2,16,256]{2,1,0:T(8,128)}, f32[2,16,256]{2,1,0:T(8,128)S(1)}, u32[]{:S(2)}, u32[]{:S(2)}) collective-permute-start(f32[2,16,256]{2,1,0:T(8,128)} %shard_map.68), channel_id=1, source_target_pairs={{0,9},{1,10},{2,11},{3,12},{4,13},{5,14},{6,15},{8,17},{9,18},{10,... | collective-permute-start | bytes 98312 | tf_op jit(solution)/shard_map/ppermute | solution.py:115
  72.3 16.1 %collective-permute-start.9 = (f32[2,16,256]{2,1,0:T(8,128)}, f32[2,16,256]{2,1,0:T(8,128)S(1)}, u32[]{:S(2)}, u32[]{:S(2)}) collective-permute-start(f32[2,16,256]{2,1,0:T(8,128)} %shard_map.68), channel_id=1, source_target_pairs={{0,8},{1,9},{2,10},{3,11},{4,12},{5,13},{6,14},{7,15},{8,16},{9,17... | collective-permute-start | bytes 98312 | tf_op jit(solution)/shard_map/ppermute | solution.py:115
  75.4 14.9 %collective-permute-start.10 = (f32[2,16,256]{2,1,0:T(8,128)}, f32[2,16,256]{2,1,0:T(8,128)S(1)}, u32[]{:S(2)}, u32[]{:S(2)}) collective-permute-start(f32[2,16,256]{2,1,0:T(8,128)} %shard_map.68), channel_id=1, source_target_pairs={{1,8},{2,9},{3,10},{4,11},{5,12},{6,13},{7,14},{9,16},{10,17},{11,... | collective-permute-start | bytes 98312 | tf_op jit(solution)/shard_map/ppermute | solution.py:115
  76.7 14.9 %collective-permute-start.11 = (f32[2,16,256]{2,1,0:T(8,128)}, f32[2,16,256]{2,1,0:T(8,128)S(1)}, u32[]{:S(2)}, u32[]{:S(2)}) collective-permute-start(f32[2,16,256]{2,1,0:T(8,128)} %shard_map.68), channel_id=1, source_target_pairs={{0,1},{1,2},{2,3},{3,4},{4,5},{5,6},{6,7},{8,9},{9,10},{10,11},{11... | collective-permute-start | bytes 98312 | tf_op jit(solution)/shard_map/ppermute | solution.py:115
  81.9 10.5 %collective-permute-start.12 = (f32[2,16,256]{2,1,0:T(8,128)}, f32[2,16,256]{2,1,0:T(8,128)S(1)}, u32[]{:S(2)}, u32[]{:S(2)}) collective-permute-start(f32[2,16,256]{2,1,0:T(8,128)} %shard_map.68), channel_id=1, source_target_pairs={{1,0},{2,1},{3,2},{4,3},{5,4},{6,5},{7,6},{9,8},{10,9},{11,10},{12... | collective-permute-start | bytes 98312 | tf_op jit(solution)/shard_map/ppermute | solution.py:115
  83.2 9.2 %collective-permute-start.13 = (f32[2,16,256]{2,1,0:T(8,128)}, f32[2,16,256]{2,1,0:T(8,128)S(1)}, u32[]{:S(2)}, u32[]{:S(2)}) collective-permute-start(f32[2,16,256]{2,1,0:T(8,128)} %shard_map.68), channel_id=1, source_target_pairs={{8,1},{9,2},{10,3},{11,4},{12,5},{13,6},{14,7},{16,9},{17,10},{18,... | collective-permute-start | bytes 98312 | tf_op jit(solution)/shard_map/ppermute | solution.py:115
  88.3 5.4 %collective-permute-start.14 = (f32[2,16,256]{2,1,0:T(8,128)}, f32[2,16,256]{2,1,0:T(8,128)S(1)}, u32[]{:S(2)}, u32[]{:S(2)}) collective-permute-start(f32[2,16,256]{2,1,0:T(8,128)} %shard_map.68), channel_id=1, source_target_pairs={{8,0},{9,1},{10,2},{11,3},{12,4},{13,5},{14,6},{15,7},{16,8},{17,9... | collective-permute-start | bytes 98312 | tf_op jit(solution)/shard_map/ppermute | solution.py:115
  90.3 7.3 %collective-permute-start.15 = (f32[2,16,256]{2,1,0:T(8,128)}, f32[2,16,256]{2,1,0:T(8,128)S(1)}, u32[]{:S(2)}, u32[]{:S(2)}) collective-permute-start(f32[2,16,256]{2,1,0:T(8,128)} %shard_map.68), channel_id=1, source_target_pairs={{9,0},{10,1},{11,2},{12,3},{13,4},{14,5},{15,6},{17,8},{18,9},{19,... | collective-permute-start | bytes 98312 | tf_op jit(solution)/shard_map/ppermute | solution.py:115
  97.6 0.7 copy-start.4
  100.7 42.1 %copy-start.2 = (f32[2,16,256]{2,1,0:T(8,128)S(1)}, f32[2,16,256]{2,1,0:T(8,128)}, u32[]{:S(2)}) copy-start(f32[2,16,256]{2,1,0:T(8,128)} %shard_map.69) | copy-start | bytes 98308
  142.8 11.9 %collective-permute-start.16 = (f32[2,16,256]{2,1,0:T(8,128)S(1)}, f32[2,16,256]{2,1,0:T(8,128)S(1)}, u32[]{:S(2)}, u32[]{:S(2)}) collective-permute-start(f32[2,16,256]{2,1,0:T(8,128)S(1)} %multiply_subtract_fusion.2), channel_id=1, source_target_pairs={{0,9},{1,10},{2,11},{3,12},{4,13},{5,14},{6,15},{8,17},{9,18},{10,... | collective-permute-start | bytes 98312 | tf_op jit(solution)/shard_map/ppermute | solution.py:115
  145.5 14.0 %collective-permute-start.17 = (f32[2,16,256]{2,1,0:T(8,128)S(1)}, f32[2,16,256]{2,1,0:T(8,128)S(1)}, u32[]{:S(2)}, u32[]{:S(2)}) collective-permute-start(f32[2,16,256]{2,1,0:T(8,128)S(1)} %multiply_subtract_fusion.2), channel_id=1, source_target_pairs={{0,8},{1,9},{2,10},{3,11},{4,12},{5,13},{6,14},{7,15},{8,16},{9,17... | collective-permute-start | bytes 98312 | tf_op jit(solution)/shard_map/ppermute | solution.py:115
  148.0 13.4 %collective-permute-start.18 = (f32[2,16,256]{2,1,0:T(8,128)S(1)}, f32[2,16,256]{2,1,0:T(8,128)S(1)}, u32[]{:S(2)}, u32[]{:S(2)}) collective-permute-start(f32[2,16,256]{2,1,0:T(8,128)S(1)} %multiply_subtract_fusion.2), channel_id=1, source_target_pairs={{1,8},{2,9},{3,10},{4,11},{5,12},{6,13},{7,14},{9,16},{10,17},{11,... | collective-permute-start | bytes 98312 | tf_op jit(solution)/shard_map/ppermute | solution.py:115
  149.3 13.4 %collective-permute-start.19 = (f32[2,16,256]{2,1,0:T(8,128)S(1)}, f32[2,16,256]{2,1,0:T(8,128)S(1)}, u32[]{:S(2)}, u32[]{:S(2)}) collective-permute-start(f32[2,16,256]{2,1,0:T(8,128)S(1)} %multiply_subtract_fusion.2), channel_id=1, source_target_pairs={{0,1},{1,2},{2,3},{3,4},{4,5},{5,6},{6,7},{8,9},{9,10},{10,11},{11... | collective-permute-start | bytes 98312 | tf_op jit(solution)/shard_map/ppermute | solution.py:115
  153.4 9.4 %collective-permute-start.20 = (f32[2,16,256]{2,1,0:T(8,128)S(1)}, f32[2,16,256]{2,1,0:T(8,128)S(1)}, u32[]{:S(2)}, u32[]{:S(2)}) collective-permute-start(f32[2,16,256]{2,1,0:T(8,128)S(1)} %multiply_subtract_fusion.2), channel_id=1, source_target_pairs={{1,0},{2,1},{3,2},{4,3},{5,4},{6,5},{7,6},{9,8},{10,9},{11,10},{12... | collective-permute-start | bytes 98312 | tf_op jit(solution)/shard_map/ppermute | solution.py:115
  154.7 8.1 %collective-permute-start.21 = (f32[2,16,256]{2,1,0:T(8,128)S(1)}, f32[2,16,256]{2,1,0:T(8,128)S(1)}, u32[]{:S(2)}, u32[]{:S(2)}) collective-permute-start(f32[2,16,256]{2,1,0:T(8,128)S(1)} %multiply_subtract_fusion.2), channel_id=1, source_target_pairs={{8,1},{9,2},{10,3},{11,4},{12,5},{13,6},{14,7},{16,9},{17,10},{18,... | collective-permute-start | bytes 98312 | tf_op jit(solution)/shard_map/ppermute | solution.py:115
  159.5 5.2 %collective-permute-start.22 = (f32[2,16,256]{2,1,0:T(8,128)S(1)}, f32[2,16,256]{2,1,0:T(8,128)S(1)}, u32[]{:S(2)}, u32[]{:S(2)}) collective-permute-start(f32[2,16,256]{2,1,0:T(8,128)S(1)} %multiply_subtract_fusion.2), channel_id=1, source_target_pairs={{8,0},{9,1},{10,2},{11,3},{12,4},{13,5},{14,6},{15,7},{16,8},{17,9... | collective-permute-start | bytes 98312 | tf_op jit(solution)/shard_map/ppermute | solution.py:115
  161.4 6.5 %collective-permute-start.23 = (f32[2,16,256]{2,1,0:T(8,128)S(1)}, f32[2,16,256]{2,1,0:T(8,128)S(1)}, u32[]{:S(2)}, u32[]{:S(2)}) collective-permute-start(f32[2,16,256]{2,1,0:T(8,128)S(1)} %multiply_subtract_fusion.2), channel_id=1, source_target_pairs={{9,0},{10,1},{11,2},{12,3},{13,4},{14,5},{15,6},{17,8},{18,9},{19,... | collective-permute-start | bytes 98312 | tf_op jit(solution)/shard_map/ppermute | solution.py:115
  167.9 0.7 copy-start.5
  171.0 40.8 %copy-start.3 = (f32[2,16,256]{2,1,0:T(8,128)S(1)}, f32[2,16,256]{2,1,0:T(8,128)}, u32[]{:S(2)}) copy-start(f32[2,16,256]{2,1,0:T(8,128)} %shard_map.70) | copy-start | bytes 98308
  211.8 11.9 %collective-permute-start.24 = (f32[2,16,256]{2,1,0:T(8,128)S(1)}, f32[2,16,256]{2,1,0:T(8,128)S(1)}, u32[]{:S(2)}, u32[]{:S(2)}) collective-permute-start(f32[2,16,256]{2,1,0:T(8,128)S(1)} %multiply_subtract_fusion.1), channel_id=1, source_target_pairs={{0,9},{1,10},{2,11},{3,12},{4,13},{5,14},{6,15},{8,17},{9,18},{10,... | collective-permute-start | bytes 98312 | tf_op jit(solution)/shard_map/ppermute | solution.py:115
  214.5 14.0 %collective-permute-start.25 = (f32[2,16,256]{2,1,0:T(8,128)S(1)}, f32[2,16,256]{2,1,0:T(8,128)S(1)}, u32[]{:S(2)}, u32[]{:S(2)}) collective-permute-start(f32[2,16,256]{2,1,0:T(8,128)S(1)} %multiply_subtract_fusion.1), channel_id=1, source_target_pairs={{0,8},{1,9},{2,10},{3,11},{4,12},{5,13},{6,14},{7,15},{8,16},{9,17... | collective-permute-start | bytes 98312 | tf_op jit(solution)/shard_map/ppermute | solution.py:115
  217.1 13.4 %collective-permute-start.26 = (f32[2,16,256]{2,1,0:T(8,128)S(1)}, f32[2,16,256]{2,1,0:T(8,128)S(1)}, u32[]{:S(2)}, u32[]{:S(2)}) collective-permute-start(f32[2,16,256]{2,1,0:T(8,128)S(1)} %multiply_subtract_fusion.1), channel_id=1, source_target_pairs={{1,8},{2,9},{3,10},{4,11},{5,12},{6,13},{7,14},{9,16},{10,17},{11,... | collective-permute-start | bytes 98312 | tf_op jit(solution)/shard_map/ppermute | solution.py:115
  218.4 13.4 %collective-permute-start.27 = (f32[2,16,256]{2,1,0:T(8,128)S(1)}, f32[2,16,256]{2,1,0:T(8,128)S(1)}, u32[]{:S(2)}, u32[]{:S(2)}) collective-permute-start(f32[2,16,256]{2,1,0:T(8,128)S(1)} %multiply_subtract_fusion.1), channel_id=1, source_target_pairs={{0,1},{1,2},{2,3},{3,4},{4,5},{5,6},{6,7},{8,9},{9,10},{10,11},{11... | collective-permute-start | bytes 98312 | tf_op jit(solution)/shard_map/ppermute | solution.py:115
  222.5 9.4 %collective-permute-start.28 = (f32[2,16,256]{2,1,0:T(8,128)S(1)}, f32[2,16,256]{2,1,0:T(8,128)S(1)}, u32[]{:S(2)}, u32[]{:S(2)}) collective-permute-start(f32[2,16,256]{2,1,0:T(8,128)S(1)} %multiply_subtract_fusion.1), channel_id=1, source_target_pairs={{1,0},{2,1},{3,2},{4,3},{5,4},{6,5},{7,6},{9,8},{10,9},{11,10},{12... | collective-permute-start | bytes 98312 | tf_op jit(solution)/shard_map/ppermute | solution.py:115
  223.8 8.1 %collective-permute-start.29 = (f32[2,16,256]{2,1,0:T(8,128)S(1)}, f32[2,16,256]{2,1,0:T(8,128)S(1)}, u32[]{:S(2)}, u32[]{:S(2)}) collective-permute-start(f32[2,16,256]{2,1,0:T(8,128)S(1)} %multiply_subtract_fusion.1), channel_id=1, source_target_pairs={{8,1},{9,2},{10,3},{11,4},{12,5},{13,6},{14,7},{16,9},{17,10},{18,... | collective-permute-start | bytes 98312 | tf_op jit(solution)/shard_map/ppermute | solution.py:115
  228.5 5.2 %collective-permute-start.30 = (f32[2,16,256]{2,1,0:T(8,128)S(1)}, f32[2,16,256]{2,1,0:T(8,128)S(1)}, u32[]{:S(2)}, u32[]{:S(2)}) collective-permute-start(f32[2,16,256]{2,1,0:T(8,128)S(1)} %multiply_subtract_fusion.1), channel_id=1, source_target_pairs={{8,0},{9,1},{10,2},{11,3},{12,4},{13,5},{14,6},{15,7},{16,8},{17,9... | collective-permute-start | bytes 98312 | tf_op jit(solution)/shard_map/ppermute | solution.py:115
  230.5 6.5 %collective-permute-start.31 = (f32[2,16,256]{2,1,0:T(8,128)S(1)}, f32[2,16,256]{2,1,0:T(8,128)S(1)}, u32[]{:S(2)}, u32[]{:S(2)}) collective-permute-start(f32[2,16,256]{2,1,0:T(8,128)S(1)} %multiply_subtract_fusion.1), channel_id=1, source_target_pairs={{9,0},{10,1},{11,2},{12,3},{13,4},{14,5},{15,6},{17,8},{18,9},{19,... | collective-permute-start | bytes 98312 | tf_op jit(solution)/shard_map/ppermute | solution.py:115
  237.0 0.7 copy-start.6
  240.0 40.2 %copy-start.7 = (f32[2,16,256]{2,1,0:T(8,128)S(1)}, f32[2,16,256]{2,1,0:T(8,128)}, u32[]{:S(2)}) copy-start(f32[2,16,256]{2,1,0:T(8,128)} %shard_map.71) | copy-start | bytes 98308

commit v3 on v2

--- a/solution.py
+++ b/solution.py
@@ -1,3 +1,4 @@
+import functools
 import math
 
 import jax
@@ -11,6 +12,23 @@
 CAP = 32
 HIGHEST = lax.Precision.HIGHEST
 ROWS, LANES = 16, 256
+SHIFT, SPAN = 8.5, 8.0
+
+
+def _solve(matrix, rhs):
+    n = len(rhs)
+    m = [list(r) + [v] for r, v in zip(matrix, rhs)]
+    for k in range(n):
+        for i in range(k + 1, n):
+            f = m[i][k] / m[k][k]
+            m[i] = [m[i][j] - f * m[k][j] if j > k else m[i][j] for j in range(n + 1)]
+    x = [None] * n
+    for i in reversed(range(n)):
+        acc = m[i][n]
+        for j in range(i + 1, n):
+            acc = acc - m[i][j] * x[j]
+        x[i] = acc / m[i][i]
+    return x
 
 
 def _masks():
@@ -42,7 +60,7 @@
     return (ex + 1) * 9 + (ey + 1) * 3 + (ez + 1)
 
 
-def _stencil_kernel(tab_ref, src_ref, diag_ref, out_ref):
+def _stencil_kernel(tab_ref, src_ref, diag_ref, out_ref, shift=0.0, scale=1.0):
     row, y, z = _masks()
     bricks = out_ref.shape[0]
     for b in range(bricks):
@@ -64,7 +82,7 @@
             planes[ex] = lines[0] + 0.5 * (lo + hi)
         lo, hi = _neighbour_x(planes[0], planes[-1], planes[1], row)
         smoothed = planes[0] + 0.5 * (lo + hi)
-        out_ref[b] = (diag_ref[b] + 2.0) * own - 2.0 * smoothed
+        out_ref[b] = ((diag_ref[b] + (2.0 - shift)) * own - 2.0 * smoothed) * scale
 
 
 def _divergence_kernel(tab_ref, src_ref, out_ref):
@@ -98,24 +116,19 @@
     )(*operands)
 
 
+def _shift(field, axis, step):
+    size = lax.axis_size(axis)
+    pairs = [(i + step, i) for i in range(size) if 0 <= i + step < size]
+    return lax.ppermute(field, axis, pairs)
+
+
 def halo(field):
-    n_wide, n_narrow = lax.axis_size("wide"), lax.axis_size("narrow")
-    pieces = []
-    for dw in (-1, 0, 1):
-        for dn in (-1, 0, 1):
-            if dw == 0 and dn == 0:
-                pieces.append(field)
-                continue
-            pairs = [
-                ((w + dw) * n_narrow + n + dn, w * n_narrow + n)
-                for w in range(n_wide)
-                for n in range(n_narrow)
-                if 0 <= w + dw < n_wide and 0 <= n + dn < n_narrow
-            ]
-            pieces.append(lax.ppermute(field, ("wide", "narrow"), pairs))
-    zero_shape = field.shape[:-3] + (1,) + field.shape[-2:]
-    pieces.append(jnp.zeros(zero_shape, field.dtype))
-    return jnp.concatenate(pieces, axis=-3)
+    lead, bricks = field.shape[:-3], field.shape[-3]
+    column = jnp.stack([_shift(field, "wide", -1), field, _shift(field, "wide", 1)], axis=-4)
+    block = jnp.stack([_shift(column, "narrow", -1), column, _shift(column, "narrow", 1)], axis=-4)
+    block = block.reshape(lead + (9 * bricks,) + field.shape[-2:])
+    zero = jnp.zeros(lead + (1,) + field.shape[-2:], field.dtype)
+    return jnp.concatenate([block, zero], axis=-3)
 
 
 def shards(point_owner, point_cell, normals, strip_count, neighbours):
@@ -159,23 +172,39 @@
         gathered = lax.all_to_all(spread, ("wide", "narrow"), 0, 0, tiled=True)
         return jnp.sum(gathered, axis=0)
 
-    residual = right_side
-    solution = jnp.zeros_like(right_side)
-    for iteration in range(ITERS):
-        image_r = _local_call(_stencil_kernel, shape, [table, halo(residual), diagonal], 60 * bricks * 4096)
-        sums = global_sum([jnp.sum(residual * residual), jnp.sum(residual * image_r)])
-        norm_now, curvature = sums[0], sums[1]
-        if iteration == 0:
-            step_size = norm_now / curvature
-            direction, image_field = residual, image_r
+    basis = [right_side]
+    kernel = functools.partial(_stencil_kernel, shift=SHIFT, scale=1.0 / SPAN)
+    for k in range(ITERS):
+        image = _local_call(kernel, shape, [table, halo(basis[-1]), diagonal], 60 * bricks * 4096)
+        basis.append(image if k == 0 else 2.0 * image - basis[-2])
+    lift = [[0.0] * ITERS for _ in range(ITERS + 1)]
+    for k in range(ITERS):
+        lift[k][k] = SHIFT
+        if k == 0:
+            lift[1][0] = SPAN
         else:
-            ratio = norm_now / norm_before
-            step_size = norm_now / (curvature - ratio * norm_now / step_before)
-            direction = residual + ratio * direction
-            image_field = image_r + ratio * image_field
-        solution = solution + step_size * direction
-        residual = residual - step_size * image_field
-        norm_before, step_before = norm_now, step_size
+            lift[k - 1][k] = lift[k + 1][k] = 0.5 * SPAN
+    pairs = [(i, j) for i in range(ITERS + 1) for j in range(i, ITERS + 1)]
+    sums = global_sum([jnp.sum(basis[i] * basis[j]) for i, j in pairs])
+    gram = [[None] * (ITERS + 1) for _ in range(ITERS + 1)]
+    for k, (i, j) in enumerate(pairs):
+        gram[i][j] = gram[j][i] = sums[k]
+
+    def lifted(i, j):
+        terms = [lift[k][j] * gram[i][k] for k in range(ITERS + 1) if lift[k][j] != 0.0]
+        return sum(terms[1:], terms[0])
+
+    coeff = _solve([[lifted(i, j) for j in range(ITERS)] for i in range(ITERS)], [gram[i][0] for i in range(ITERS)])
+    solution = coeff[0] * basis[0]
+    for j in range(1, ITERS):
+        solution = solution + coeff[j] * basis[j]
+    weights = []
+    for k in range(ITERS + 1):
+        terms = [lift[k][j] * coeff[j] for j in range(ITERS) if lift[k][j] != 0.0]
+        weights.append((1.0 if k == 0 else 0.0) - sum(terms[1:], terms[0]))
+    residual = weights[0] * basis[0]
+    for k in range(1, ITERS + 1):
+        residual = residual + weights[k] * basis[k]
     out = (1, 1, bricks, ROWS * LANES)
     return solution.reshape(out), residual.reshape(out)
 

time: 283 us -> 191 us (0.67)
  blocking collectives: 122 us -> 57.7 us
  starting transfers between devices: 85.6 us -> 44.1 us
  waiting for transfers between devices: 23.4 us -> 34.7 us
  other arithmetic: 13 us -> 7.49 us
  between operations: 11.7 us -> 16.2 us
  local copies, waits for them, and re-layouts: 9.42 us -> 13.4 us
    all_to_all x3 -> x1, blocking collectives: 101 us -> 36.9 us  [global_sum(): gathered = lax.all_to_all(spread, ('wide', 'narrow'), 0, 0, tiled=True)]
    ppermute x32 -> x16, starting transfers between devices: 85.6 us -> 44.1 us  [_shift(): return lax.ppermute(field, axis, pairs)]
    ppermute x32 -> x16, waiting for transfers between devices: 23.4 us -> 34.7 us  [_shift(): return lax.ppermute(field, axis, pairs)]
    another operation x0 -> x4, local copies, waits for them, and re-layouts: none -> 6.33 us  [the longest x1 6.27 us: global_sum(): stacked = jnp.stack(parts)[None, :]]
    unnamed x62 -> x16, local copies, waits for them, and re-layouts: 4.38 us -> 0.28 us
    concatenate x4, local copies, waits for them, and re-layouts: 0.01 us -> 3.22 us  [halo(): return jnp.concatenate([block, zero], axis=-3)]
    reduce_sum x3 -> x1, other arithmetic: 4.39 us -> 1.56 us  [shards(): sums = global_sum([jnp.sum(basis[i] * basis[j]) for i, j in pairs])]
  transfers between devices with their start and end apart: 32 -> 16, of which waited for: 8 -> 11; matrix products, arithmetic and copies ran while one was open for 1% -> 1% of each run, Pallas kernels for 0% -> 0%
where the time goes in v3:
time: 191 us; the launch traced here: 190 us
  blocking collectives  57.7 us (30%)
  starting transfers between devices  44.1 us (23%)
  waiting for transfers between devices  34.7 us (18%)
  between operations  16.2 us (8%)
  local copies, waits for them, and re-layouts  13.4 us (7%)
  Pallas kernels  9.02 us (5%)
  other arithmetic  7.49 us (4%)
  matrix products  7.35 us (4%)
    ppermute x16, starting transfers between devices, _shift(): return lax.ppermute(field, axis, pairs)  44.1 us
    all_to_all x1, blocking collectives, global_sum(): gathered = lax.all_to_all(spread, ('wide', 'narrow'), 0, 0, tiled=True)  36.9 us
    ppermute x16, waiting for transfers between devices, _shift(): return lax.ppermute(field, axis, pairs)  34.7 us
    all_to_all x1, blocking collectives, shards(): lax.all_to_all(send.reshape(owners, CAP, 4), 'wide', 0, 0, tiled=True)  20.8 us
    pallas_call x4, Pallas kernels, _local_call(): pl.pallas_call(kernel, out_shape=jax.ShapeDtypeStruct(out_shape, jnp.floa...  9.02 us
    another operation x1, local copies, waits for them, and re-layouts, global_sum(): stacked = jnp.stack(parts)[None, :]  6.27 us
  transfers between devices with their start and end apart: 16, of which 11 were waited for; matrix products, arithmetic and copies ran while one was open for 1% of the time, Pallas kernels for 0%

profile of v3, /device:TPU:1, one launch (start us, length us, event | category | flops | bytes accessed | tf_op | source)
XLA Modules:
  0.0 190.1 jit_solution(15376583707170455953)
XLA Ops:
  0.7 1.4 fusion.5
  2.7 3.7 %fusion = f32[2048,4]{0,1:T(4,128)S(1)} fusion(s32[1024]{0:T(1024)S(1)} %convert_add_fusion, f32[1024,3]{0,1:T(4,128)S(1)} %bitcast.124, f32[1024,1]{0,1:T(1,128)S(1)} %bitcast.123), kind=kOutput, calls=%fused_computation.1 | convolution fusion | flops 102764544 | bytes 53248 | tf_op jit(solution)/shard_map/dot_general | solution.py:152
  6.5 0.1 reshape.78
  6.6 0.1 copy.70
  6.7 0.1 reshape.86
  6.8 20.8 %all_to_all.11 = f32[64,1,128]{2,1,0:T(1,128)S(1)} all-to-all(f32[64,1,128]{2,1,0:T(1,128)S(1)} %reshape.86), channel_id=1, replica_groups=mesh['wide'=64,'narrow'=8] {'wide'}, dimensions={0} | all-to-all | bytes 65536 | tf_op jit(solution)/shard_map/all_to_all | solution.py:153
  27.6 0.5 broadcast.62
  28.1 0.7 reduce.1
  28.9 0.1 reshape.87
  29.0 0.1 reshape.79
  29.2 0.3 fusion.14
  29.5 1.1 fusion.17
  30.7 2.2 %fusion.3 = f32[128,256]{1,0:T(8,128)S(1)} fusion(f32[2048,32]{1,0:T(8,128)S(1)} %fusion.14, f32[2048,32]{1,0:T(8,128)S(1)} %get-tuple-element.28, f32[2048,32]{1,0:T(8,128)S(1)} %get-tuple-element.29, f32[2048,32]{1,0:T(8,128)S(1)} %get-tuple-element.27, s32[2048]{0:T(1024)S(1)} %bitcast.111), kind=kOutput, calls=%fused_computation.6 | convolution fusion | flops 806617088 | bytes 1187840 | tf_op jit(solution)/shard_map/pa,pb->ab/dot_general | solution.py:161
  32.9 0.0 copy-start.6
  33.0 2.8 %collective-permute-start = (f32[3,2,16,256]{3,2,1,0:T(8,128)S(1)}, f32[3,2,16,256]{3,2,1,0:T(8,128)S(1)}, u32[]{:S(2)}, u32[]{:S(2)}) collective-permute-start(f32[3,2,16,256]{3,2,1,0:T(8,128)S(1)} %bitcast.96), channel_id=1, source_target_pairs={{0,8},{8,16},{16,24},{24,32},{32,40},{40,48},{48,56},{56,64},{64,7... | collective-permute-start | bytes 294920 | tf_op jit(solution)/shard_map/ppermute | solution.py:122
  35.7 1.9 %collective-permute-start.1 = (f32[3,2,16,256]{3,2,1,0:T(8,128)S(1)}, f32[3,2,16,256]{3,2,1,0:T(8,128)S(1)}, u32[]{:S(2)}, u32[]{:S(2)}) collective-permute-start(f32[3,2,16,256]{3,2,1,0:T(8,128)S(1)} %bitcast.97), channel_id=1, source_target_pairs={{8,0},{16,8},{24,16},{32,24},{40,32},{48,40},{56,48},{64,56},{72,6... | collective-permute-start | bytes 294920 | tf_op jit(solution)/shard_map/ppermute | solution.py:122
  37.7 4.0 %collective-permute-done.1 = f32[3,2,16,256]{3,2,1,0:T(8,128)S(1)} collective-permute-done((f32[3,2,16,256]{3,2,1,0:T(8,128)S(1)}, f32[3,2,16,256]{3,2,1,0:T(8,128)S(1)}, u32[]{:S(2)}, u32[]{:S(2)}) %collective-permute-start.1) | collective-permute-done | bytes 98336 | tf_op jit(solution)/shard_map/ppermute | solution.py:122
  41.7 0.1 fusion.30
  41.7 4.0 %collective-permute-start.2 = (f32[3,3,2,16,256]{4,3,2,1,0:T(8,128)S(1)}, f32[3,3,2,16,256]{4,3,2,1,0:T(8,128)S(1)}, u32[]{:S(2)}, u32[]{:S(2)}) collective-permute-start(f32[3,3,2,16,256]{4,3,2,1,0:T(8,128)S(1)} %get-tuple-element.13), channel_id=1, source_target_pairs={{0,1},{1,2},{2,3},{3,4},{4,5},{5,6},{6,7},{8,9},{9,10},{10,11},{11... | collective-permute-start | bytes 884744 | tf_op jit(solution)/shard_map/ppermute | solution.py:122
  45.7 1.3 collective-permute-start.3
  47.1 0.7 reshape.77.tab_ref
  47.7 2.6 %collective-permute-done.2 = f32[3,3,2,16,256]{4,3,2,1,0:T(8,128)S(1)} collective-permute-done((f32[3,3,2,16,256]{4,3,2,1,0:T(8,128)S(1)}, f32[3,3,2,16,256]{4,3,2,1,0:T(8,128)S(1)}, u32[]{:S(2)}, u32[]{:S(2)}) %collective-permute-start.2) | collective-permute-done | bytes 294944 | tf_op jit(solution)/shard_map/ppermute | solution.py:122
  50.3 4.5 %collective-permute-done.3 = f32[3,3,2,16,256]{4,3,2,1,0:T(8,128)S(1)} collective-permute-done((f32[3,3,2,16,256]{4,3,2,1,0:T(8,128)S(1)}, f32[3,3,2,16,256]{4,3,2,1,0:T(8,128)S(1)}, u32[]{:S(2)}, u32[]{:S(2)}) %collective-permute-start.3) | collective-permute-done | bytes 294944 | tf_op jit(solution)/shard_map/ppermute | solution.py:122
  54.7 0.1 pad_maximum_fusion
  54.8 1.0 concatenate.20.src_ref
  55.8 1.9 %shard_map.68 = f32[2,16,256]{2,1,0:T(8,128)} custom-call(s32[54]{0:T(128)} %reshape.77.tab_ref, f32[3,19,16,256]{3,2,1,0:T(8,128)} %concatenate.20.src_ref), custom_call_target="tpu_custom_call" | custom-call | flops 163840 | bytes 966872 | tf_op jit(solution)/shard_map/pallas_call | solution.py:110
  57.8 5.1 %collective-permute-start.4 = (f32[2,16,256]{2,1,0:T(8,128)}, f32[2,16,256]{2,1,0:T(8,128)S(1)}, u32[]{:S(2)}, u32[]{:S(2)}) collective-permute-start(f32[2,16,256]{2,1,0:T(8,128)} %shard_map.68), channel_id=1, source_target_pairs={{0,8},{8,16},{16,24},{24,32},{32,40},{40,48},{48,56},{56,64},{64,7... | collective-permute-start | bytes 98312 | tf_op jit(solution)/shard_map/ppermute | solution.py:122
  62.9 1.9 %collective-permute-start.5 = (f32[2,16,256]{2,1,0:T(8,128)}, f32[2,16,256]{2,1,0:T(8,128)S(1)}, u32[]{:S(2)}, u32[]{:S(2)}) collective-permute-start(f32[2,16,256]{2,1,0:T(8,128)} %shard_map.68), channel_id=1, source_target_pairs={{8,0},{16,8},{24,16},{32,24},{40,32},{48,40},{56,48},{64,56},{72,6... | collective-permute-start | bytes 98312 | tf_op jit(solution)/shard_map/ppermute | solution.py:122
  64.8 3.5 %collective-permute-done.5 = f32[2,16,256]{2,1,0:T(8,128)S(1)} collective-permute-done((f32[2,16,256]{2,1,0:T(8,128)}, f32[2,16,256]{2,1,0:T(8,128)S(1)}, u32[]{:S(2)}, u32[]{:S(2)}) %collective-permute-start.5) | collective-permute-done | bytes 32800 | tf_op jit(solution)/shard_map/ppermute | solution.py:122
  68.3 0.8 fusion.29
  69.1 4.0 %collective-permute-start.6 = (f32[3,2,16,256]{3,2,1,0:T(8,128)S(1)}, f32[3,2,16,256]{3,2,1,0:T(8,128)S(1)}, u32[]{:S(2)}, u32[]{:S(2)}) collective-permute-start(f32[3,2,16,256]{3,2,1,0:T(8,128)S(1)} %get-tuple-element.21), channel_id=1, source_target_pairs={{0,1},{1,2},{2,3},{3,4},{4,5},{5,6},{6,7},{8,9},{9,10},{10,11},{11... | collective-permute-start | bytes 294920 | tf_op jit(solution)/shard_map/ppermute | solution.py:122
  73.1 1.3 collective-permute-start.7
  74.4 0.6 fusion.20
  75.0 5.3 %collective-permute-done.7 = f32[3,2,16,256]{3,2,1,0:T(8,128)S(1)} collective-permute-done((f32[3,2,16,256]{3,2,1,0:T(8,128)S(1)}, f32[3,2,16,256]{3,2,1,0:T(8,128)S(1)}, u32[]{:S(2)}, u32[]{:S(2)}) %collective-permute-start.7) | collective-permute-done | bytes 98336 | tf_op jit(solution)/shard_map/ppermute | solution.py:122
  80.3 0.7 concatenate.21.src_ref
  81.1 2.4 %shard_map.69 = f32[2,16,256]{2,1,0:T(8,128)} custom-call(s32[54]{0:T(128)} %reshape.77.tab_ref, f32[19,16,256]{2,1,0:T(8,128)} %concatenate.21.src_ref, f32[2,16,256]{2,1,0:T(8,128)} %bitcast.89), custom_call_target="tpu_custom_call" | custom-call | flops 491520 | bytes 377048 | tf_op jit(solution)/shard_map/pallas_call | solution.py:110
  83.4 3.6 %collective-permute-start.8 = (f32[2,16,256]{2,1,0:T(8,128)}, f32[2,16,256]{2,1,0:T(8,128)S(1)}, u32[]{:S(2)}, u32[]{:S(2)}) collective-permute-start(f32[2,16,256]{2,1,0:T(8,128)} %shard_map.69), channel_id=1, source_target_pairs={{0,8},{8,16},{16,24},{24,32},{32,40},{40,48},{48,56},{56,64},{64,7... | collective-permute-start | bytes 98312 | tf_op jit(solution)/shard_map/ppermute | solution.py:122
  87.0 1.9 %collective-permute-start.9 = (f32[2,16,256]{2,1,0:T(8,128)}, f32[2,16,256]{2,1,0:T(8,128)S(1)}, u32[]{:S(2)}, u32[]{:S(2)}) collective-permute-start(f32[2,16,256]{2,1,0:T(8,128)} %shard_map.69), channel_id=1, source_target_pairs={{8,0},{16,8},{24,16},{32,24},{40,32},{48,40},{56,48},{64,56},{72,6... | collective-permute-start | bytes 98312 | tf_op jit(solution)/shard_map/ppermute | solution.py:122
  88.9 3.5 %collective-permute-done.9 = f32[2,16,256]{2,1,0:T(8,128)S(1)} collective-permute-done((f32[2,16,256]{2,1,0:T(8,128)}, f32[2,16,256]{2,1,0:T(8,128)S(1)}, u32[]{:S(2)}, u32[]{:S(2)}) %collective-permute-start.9) | collective-permute-done | bytes 32800 | tf_op jit(solution)/shard_map/ppermute | solution.py:122
  92.5 0.8 fusion.28
  93.2 5.1 %collective-permute-start.10 = (f32[3,2,16,256]{3,2,1,0:T(8,128)S(1)}, f32[3,2,16,256]{3,2,1,0:T(8,128)S(1)}, u32[]{:S(2)}, u32[]{:S(2)}) collective-permute-start(f32[3,2,16,256]{3,2,1,0:T(8,128)S(1)} %get-tuple-element.19), channel_id=1, source_target_pairs={{0,1},{1,2},{2,3},{3,4},{4,5},{5,6},{6,7},{8,9},{9,10},{10,11},{11... | collective-permute-start | bytes 294920 | tf_op jit(solution)/shard_map/ppermute | solution.py:122
  98.3 1.3 collective-permute-start.11
  99.6 0.3 collective-permute-done.10
  99.9 3.7 %collective-permute-done.11 = f32[3,2,16,256]{3,2,1,0:T(8,128)S(1)} collective-permute-done((f32[3,2,16,256]{3,2,1,0:T(8,128)S(1)}, f32[3,2,16,256]{3,2,1,0:T(8,128)S(1)}, u32[]{:S(2)}, u32[]{:S(2)}) %collective-permute-start.11) | collective-permute-done | bytes 98336 | tf_op jit(solution)/shard_map/ppermute | solution.py:122
  103.7 0.7 concatenate.22.src_ref
  104.4 2.4 %shard_map.70 = f32[2,16,256]{2,1,0:T(8,128)} custom-call(s32[54]{0:T(128)} %reshape.77.tab_ref, f32[19,16,256]{2,1,0:T(8,128)} %concatenate.22.src_ref, f32[2,16,256]{2,1,0:T(8,128)} %bitcast.90), custom_call_target="tpu_custom_call" | custom-call | flops 491520 | bytes 377048 | tf_op jit(solution)/shard_map/pallas_call | solution.py:110
  106.8 0.8 multiply_subtract_fusion.1
  107.6 3.4 %collective-permute-start.12 = (f32[2,16,256]{2,1,0:T(8,128)S(1)}, f32[2,16,256]{2,1,0:T(8,128)S(1)}, u32[]{:S(2)}, u32[]{:S(2)}) collective-permute-start(f32[2,16,256]{2,1,0:T(8,128)S(1)} %multiply_subtract_fusion.1), channel_id=1, source_target_pairs={{0,8},{8,16},{16,24},{24,32},{32,40},{40,48},{48,56},{56,64},{64,7... | collective-permute-start | bytes 98312 | tf_op jit(solution)/shard_map/ppermute | solution.py:122
  111.0 1.9 %collective-permute-start.13 = (f32[2,16,256]{2,1,0:T(8,128)S(1)}, f32[2,16,256]{2,1,0:T(8,128)S(1)}, u32[]{:S(2)}, u32[]{:S(2)}) collective-permute-start(f32[2,16,256]{2,1,0:T(8,128)S(1)} %multiply_subtract_fusion.1), channel_id=1, source_target_pairs={{8,0},{16,8},{24,16},{32,24},{40,32},{48,40},{56,48},{64,56},{72,6... | collective-permute-start | bytes 98312 | tf_op jit(solution)/shard_map/ppermute | solution.py:122
  112.9 3.3 %collective-permute-done.13 = f32[2,16,256]{2,1,0:T(8,128)S(1)} collective-permute-done((f32[2,16,256]{2,1,0:T(8,128)S(1)}, f32[2,16,256]{2,1,0:T(8,128)S(1)}, u32[]{:S(2)}, u32[]{:S(2)}) %collective-permute-start.13) | collective-permute-done | bytes 32800 | tf_op jit(solution)/shard_map/ppermute | solution.py:122
  116.3 3.4 %collective-permute-start.14 = (f32[3,2,16,256]{3,2,1,0:T(8,128)S(1)}, f32[3,2,16,256]{3,2,1,0:T(8,128)S(1)}, u32[]{:S(2)}, u32[]{:S(2)}) collective-permute-start(f32[3,2,16,256]{3,2,1,0:T(8,128)S(1)} %get-tuple-element.17), channel_id=1, source_target_pairs={{0,1},{1,2},{2,3},{3,4},{4,5},{5,6},{6,7},{8,9},{9,10},{10,11},{11... | collective-permute-start | bytes 294920 | tf_op jit(solution)/shard_map/ppermute | solution.py:122
  119.6 1.3 collective-permute-start.15
  120.9 0.3 collective-permute-done.14
  121.2 3.7 %collective-permute-done.15 = f32[3,2,16,256]{3,2,1,0:T(8,128)S(1)} collective-permute-done((f32[3,2,16,256]{3,2,1,0:T(8,128)S(1)}, f32[3,2,16,256]{3,2,1,0:T(8,128)S(1)}, u32[]{:S(2)}, u32[]{:S(2)}) %collective-permute-start.15) | collective-permute-done | bytes 98336 | tf_op jit(solution)/shard_map/ppermute | solution.py:122
  125.0 0.7 concatenate.23.src_ref
  125.8 2.4 %shard_map.71 = f32[2,16,256]{2,1,0:T(8,128)} custom-call(s32[54]{0:T(128)} %reshape.77.tab_ref, f32[19,16,256]{2,1,0:T(8,128)} %concatenate.23.src_ref, f32[2,16,256]{2,1,0:T(8,128)} %bitcast.91), custom_call_target="tpu_custom_call" | custom-call | flops 491520 | bytes 377048 | tf_op jit(solution)/shard_map/pallas_call | solution.py:110
  128.1 1.6 multiply_reduce_fusion
  129.7 6.3 %stack.171 = f32[10]{0:T(128)S(1)} concatenate(f32[1]{0:T(128)} %bitcast.21, f32[1]{0:T(128)} %bitcast.30, f32[1]{0:T(128)} %bitcast.38, f32[1]{0:T(128)} %bitcast.46, f32[1]{0:T(128)} %bitcast.47, f32[1]{0:T(128)} %bitcast.48, f32[1]{0:T(128)} %bitcast.49, f32[1]{0:T(128)} %bitcast.50, f32[1]{0:T(128)} %bitcast.51, f32[1]{0:T(128)} %bitcast.52), dimensions={0} | concatenate | bytes 80 | tf_op jit(solution)/shard_map/stack | solution.py:170
  136.0 0.1 broadcast_in_dim.10
  136.1 36.9 %all_to_all.12 = f32[512,1,10]{2,1,0:T(1,128)S(1)} all-to-all(f32[512,1,10]{2,1,0:T(1,128)S(1)} %broadcast_in_dim.10), channel_id=1, replica_groups=mesh['wide'=64,'narrow'=8] {'wide','narrow'}, dimensions={0} | all-to-all | bytes 40960 | tf_op jit(solution)/shard_map/all_to_all | solution.py:172
  173.1 0.6 reduce_sum.119
  173.6 0.7 fusion.32
  188.8 0.6 reshape.84
  189.5 0.6 reshape.85
  (32 shorter events, 0.3 us)
Async XLA Ops:
  0.6 1.4 copy-start.3
  0.6 2.1 %copy-start.4 = (s32[1024]{0:T(1024)S(1)}, s32[1024]{0:T(1024)}, u32[]{:S(2)}) copy-start(s32[1024]{0:T(1024)} %param.6) | copy-start | bytes 12292
  0.6 2.1 %copy-start.5 = (f32[3,1024]{1,0:T(4,128)S(1)}, f32[3,1024]{1,0:T(4,128)}, u32[]{:S(2)}) copy-start(f32[3,1024]{1,0:T(4,128)} %param.7) | copy-start | bytes 36868
  32.9 14.1 %copy-start.6 = (s32[1,1,2,27]{3,2,1,0:T(2,128)S(1)}, s32[1,1,2,27]{3,2,1,0:T(2,128)}, u32[]{:S(2)}) copy-start(s32[1,1,2,27]{3,2,1,0:T(2,128)} %param.9) | copy-start | bytes 652
  33.0 4.7 %collective-permute-start = (f32[3,2,16,256]{3,2,1,0:T(8,128)S(1)}, f32[3,2,16,256]{3,2,1,0:T(8,128)S(1)}, u32[]{:S(2)}, u32[]{:S(2)}) collective-permute-start(f32[3,2,16,256]{3,2,1,0:T(8,128)S(1)} %bitcast.96), channel_id=1, source_target_pairs={{0,8},{8,16},{16,24},{24,32},{32,40},{40,48},{48,56},{56,64},{64,7... | collective-permute-start | bytes 294920 | tf_op jit(solution)/shard_map/ppermute | solution.py:122
  35.7 5.9 %collective-permute-start.1 = (f32[3,2,16,256]{3,2,1,0:T(8,128)S(1)}, f32[3,2,16,256]{3,2,1,0:T(8,128)S(1)}, u32[]{:S(2)}, u32[]{:S(2)}) collective-permute-start(f32[3,2,16,256]{3,2,1,0:T(8,128)S(1)} %bitcast.97), channel_id=1, source_target_pairs={{8,0},{16,8},{24,16},{32,24},{40,32},{48,40},{56,48},{64,56},{72,6... | collective-permute-start | bytes 294920 | tf_op jit(solution)/shard_map/ppermute | solution.py:122
  41.7 8.5 %collective-permute-start.2 = (f32[3,3,2,16,256]{4,3,2,1,0:T(8,128)S(1)}, f32[3,3,2,16,256]{4,3,2,1,0:T(8,128)S(1)}, u32[]{:S(2)}, u32[]{:S(2)}) collective-permute-start(f32[3,3,2,16,256]{4,3,2,1,0:T(8,128)S(1)} %get-tuple-element.13), channel_id=1, source_target_pairs={{0,1},{1,2},{2,3},{3,4},{4,5},{5,6},{6,7},{8,9},{9,10},{10,11},{11... | collective-permute-start | bytes 884744 | tf_op jit(solution)/shard_map/ppermute | solution.py:122
  45.7 9.0 %collective-permute-start.3 = (f32[3,3,2,16,256]{4,3,2,1,0:T(8,128)S(1)}, f32[3,3,2,16,256]{4,3,2,1,0:T(8,128)S(1)}, u32[]{:S(2)}, u32[]{:S(2)}) collective-permute-start(f32[3,3,2,16,256]{4,3,2,1,0:T(8,128)S(1)} %get-tuple-element.13), channel_id=1, source_target_pairs={{1,0},{2,1},{3,2},{4,3},{5,4},{6,5},{7,6},{9,8},{10,9},{11,10},{12... | collective-permute-start | bytes 884744 | tf_op jit(solution)/shard_map/ppermute | solution.py:122
  57.8 7.0 %collective-permute-start.4 = (f32[2,16,256]{2,1,0:T(8,128)}, f32[2,16,256]{2,1,0:T(8,128)S(1)}, u32[]{:S(2)}, u32[]{:S(2)}) collective-permute-start(f32[2,16,256]{2,1,0:T(8,128)} %shard_map.68), channel_id=1, source_target_pairs={{0,8},{8,16},{16,24},{24,32},{32,40},{40,48},{48,56},{56,64},{64,7... | collective-permute-start | bytes 98312 | tf_op jit(solution)/shard_map/ppermute | solution.py:122
  62.9 5.4 %collective-permute-start.5 = (f32[2,16,256]{2,1,0:T(8,128)}, f32[2,16,256]{2,1,0:T(8,128)S(1)}, u32[]{:S(2)}, u32[]{:S(2)}) collective-permute-start(f32[2,16,256]{2,1,0:T(8,128)} %shard_map.68), channel_id=1, source_target_pairs={{8,0},{16,8},{24,16},{32,24},{40,32},{48,40},{56,48},{64,56},{72,6... | collective-permute-start | bytes 98312 | tf_op jit(solution)/shard_map/ppermute | solution.py:122
  69.1 5.9 %collective-permute-start.6 = (f32[3,2,16,256]{3,2,1,0:T(8,128)S(1)}, f32[3,2,16,256]{3,2,1,0:T(8,128)S(1)}, u32[]{:S(2)}, u32[]{:S(2)}) collective-permute-start(f32[3,2,16,256]{3,2,1,0:T(8,128)S(1)} %get-tuple-element.21), channel_id=1, source_target_pairs={{0,1},{1,2},{2,3},{3,4},{4,5},{5,6},{6,7},{8,9},{9,10},{10,11},{11... | collective-permute-start | bytes 294920 | tf_op jit(solution)/shard_map/ppermute | solution.py:122
  73.1 7.2 %collective-permute-start.7 = (f32[3,2,16,256]{3,2,1,0:T(8,128)S(1)}, f32[3,2,16,256]{3,2,1,0:T(8,128)S(1)}, u32[]{:S(2)}, u32[]{:S(2)}) collective-permute-start(f32[3,2,16,256]{3,2,1,0:T(8,128)S(1)} %get-tuple-element.21), channel_id=1, source_target_pairs={{1,0},{2,1},{3,2},{4,3},{5,4},{6,5},{7,6},{9,8},{10,9},{11,10},{12... | collective-permute-start | bytes 294920 | tf_op jit(solution)/shard_map/ppermute | solution.py:122
  83.4 5.5 %collective-permute-start.8 = (f32[2,16,256]{2,1,0:T(8,128)}, f32[2,16,256]{2,1,0:T(8,128)S(1)}, u32[]{:S(2)}, u32[]{:S(2)}) collective-permute-start(f32[2,16,256]{2,1,0:T(8,128)} %shard_map.69), channel_id=1, source_target_pairs={{0,8},{8,16},{16,24},{24,32},{32,40},{40,48},{48,56},{56,64},{64,7... | collective-permute-start | bytes 98312 | tf_op jit(solution)/shard_map/ppermute | solution.py:122
  87.0 5.4 %collective-permute-start.9 = (f32[2,16,256]{2,1,0:T(8,128)}, f32[2,16,256]{2,1,0:T(8,128)S(1)}, u32[]{:S(2)}, u32[]{:S(2)}) collective-permute-start(f32[2,16,256]{2,1,0:T(8,128)} %shard_map.69), channel_id=1, source_target_pairs={{8,0},{16,8},{24,16},{32,24},{40,32},{48,40},{56,48},{64,56},{72,6... | collective-permute-start | bytes 98312 | tf_op jit(solution)/shard_map/ppermute | solution.py:122
  93.2 6.7 %collective-permute-start.10 = (f32[3,2,16,256]{3,2,1,0:T(8,128)S(1)}, f32[3,2,16,256]{3,2,1,0:T(8,128)S(1)}, u32[]{:S(2)}, u32[]{:S(2)}) collective-permute-start(f32[3,2,16,256]{3,2,1,0:T(8,128)S(1)} %get-tuple-element.19), channel_id=1, source_target_pairs={{0,1},{1,2},{2,3},{3,4},{4,5},{5,6},{6,7},{8,9},{9,10},{10,11},{11... | collective-permute-start | bytes 294920 | tf_op jit(solution)/shard_map/ppermute | solution.py:122
  98.3 5.4 %collective-permute-start.11 = (f32[3,2,16,256]{3,2,1,0:T(8,128)S(1)}, f32[3,2,16,256]{3,2,1,0:T(8,128)S(1)}, u32[]{:S(2)}, u32[]{:S(2)}) collective-permute-start(f32[3,2,16,256]{3,2,1,0:T(8,128)S(1)} %get-tuple-element.19), channel_id=1, source_target_pairs={{1,0},{2,1},{3,2},{4,3},{5,4},{6,5},{7,6},{9,8},{10,9},{11,10},{12... | collective-permute-start | bytes 294920 | tf_op jit(solution)/shard_map/ppermute | solution.py:122
  103.7 3.1 %copy-start = (f32[2,16,256]{2,1,0:T(8,128)S(1)}, f32[2,16,256]{2,1,0:T(8,128)}, u32[]{:S(2)}) copy-start(f32[2,16,256]{2,1,0:T(8,128)} %shard_map.68) | copy-start | bytes 98308
  107.6 5.4 %collective-permute-start.12 = (f32[2,16,256]{2,1,0:T(8,128)S(1)}, f32[2,16,256]{2,1,0:T(8,128)S(1)}, u32[]{:S(2)}, u32[]{:S(2)}) collective-permute-start(f32[2,16,256]{2,1,0:T(8,128)S(1)} %multiply_subtract_fusion.1), channel_id=1, source_target_pairs={{0,8},{8,16},{16,24},{24,32},{32,40},{40,48},{48,56},{56,64},{64,7... | collective-permute-start | bytes 98312 | tf_op jit(solution)/shard_map/ppermute | solution.py:122
  111.0 5.2 %collective-permute-start.13 = (f32[2,16,256]{2,1,0:T(8,128)S(1)}, f32[2,16,256]{2,1,0:T(8,128)S(1)}, u32[]{:S(2)}, u32[]{:S(2)}) collective-permute-start(f32[2,16,256]{2,1,0:T(8,128)S(1)} %multiply_subtract_fusion.1), channel_id=1, source_target_pairs={{8,0},{16,8},{24,16},{32,24},{40,32},{48,40},{56,48},{64,56},{72,6... | collective-permute-start | bytes 98312 | tf_op jit(solution)/shard_map/ppermute | solution.py:122
  116.3 5.0 %collective-permute-start.14 = (f32[3,2,16,256]{3,2,1,0:T(8,128)S(1)}, f32[3,2,16,256]{3,2,1,0:T(8,128)S(1)}, u32[]{:S(2)}, u32[]{:S(2)}) collective-permute-start(f32[3,2,16,256]{3,2,1,0:T(8,128)S(1)} %get-tuple-element.17), channel_id=1, source_target_pairs={{0,1},{1,2},{2,3},{3,4},{4,5},{5,6},{6,7},{8,9},{9,10},{10,11},{11... | collective-permute-start | bytes 294920 | tf_op jit(solution)/shard_map/ppermute | solution.py:122
  119.6 5.4 %collective-permute-start.15 = (f32[3,2,16,256]{3,2,1,0:T(8,128)S(1)}, f32[3,2,16,256]{3,2,1,0:T(8,128)S(1)}, u32[]{:S(2)}, u32[]{:S(2)}) collective-permute-start(f32[3,2,16,256]{3,2,1,0:T(8,128)S(1)} %get-tuple-element.17), channel_id=1, source_target_pairs={{1,0},{2,1},{3,2},{4,3},{5,4},{6,5},{7,6},{9,8},{10,9},{11,10},{12... | collective-permute-start | bytes 294920 | tf_op jit(solution)/shard_map/ppermute | solution.py:122
  125.0 3.1 %copy-start.1 = (f32[2,16,256]{2,1,0:T(8,128)S(1)}, f32[2,16,256]{2,1,0:T(8,128)}, u32[]{:S(2)}) copy-start(f32[2,16,256]{2,1,0:T(8,128)} %shard_map.69) | copy-start | bytes 98308
  128.1 60.7 %copy-start.2 = (f32[2,16,256]{2,1,0:T(8,128)S(1)}, f32[2,16,256]{2,1,0:T(8,128)}, u32[]{:S(2)}) copy-start(f32[2,16,256]{2,1,0:T(8,128)} %shard_map.71) | copy-start | bytes 98308

commit v4 on v2

--- a/solution.py
+++ b/solution.py
@@ -98,24 +98,19 @@
     )(*operands)
 
 
+def _shift(field, axis, step):
+    size = lax.axis_size(axis)
+    pairs = [(i + step, i) for i in range(size) if 0 <= i + step < size]
+    return lax.ppermute(field, axis, pairs)
+
+
 def halo(field):
-    n_wide, n_narrow = lax.axis_size("wide"), lax.axis_size("narrow")
-    pieces = []
-    for dw in (-1, 0, 1):
-        for dn in (-1, 0, 1):
-            if dw == 0 and dn == 0:
-                pieces.append(field)
-                continue
-            pairs = [
-                ((w + dw) * n_narrow + n + dn, w * n_narrow + n)
-                for w in range(n_wide)
-                for n in range(n_narrow)
-                if 0 <= w + dw < n_wide and 0 <= n + dn < n_narrow
-            ]
-            pieces.append(lax.ppermute(field, ("wide", "narrow"), pairs))
-    zero_shape = field.shape[:-3] + (1,) + field.shape[-2:]
-    pieces.append(jnp.zeros(zero_shape, field.dtype))
-    return jnp.concatenate(pieces, axis=-3)
+    lead, bricks = field.shape[:-3], field.shape[-3]
+    column = jnp.stack([_shift(field, "wide", -1), field, _shift(field, "wide", 1)], axis=-4)
+    block = jnp.stack([_shift(column, "narrow", -1), column, _shift(column, "narrow", 1)], axis=-4)
+    block = block.reshape(lead + (9 * bricks,) + field.shape[-2:])
+    zero = jnp.zeros(lead + (1,) + field.shape[-2:], field.dtype)
+    return jnp.concatenate([block, zero], axis=-3)
 
 
 def shards(point_owner, point_cell, normals, strip_count, neighbours):

time: 283 us -> 238 us (0.84)
  starting transfers between devices: 85.6 us -> 39.4 us
  waiting for transfers between devices: 23.4 us -> 33.5 us
  blocking collectives: 122 us -> 114 us
    ppermute x32 -> x16, starting transfers between devices: 85.6 us -> 39.4 us  [_shift(): return lax.ppermute(field, axis, pairs)]
    ppermute x32 -> x16, waiting for transfers between devices: 23.4 us -> 33.5 us  [_shift(): return lax.ppermute(field, axis, pairs)]
    all_to_all x3, blocking collectives: 101 us -> 92.9 us  [global_sum(): gathered = lax.all_to_all(spread, ('wide', 'narrow'), 0, 0, tiled=True)]
    unnamed x62 -> x18, local copies, waits for them, and re-layouts: 4.38 us -> 0.29 us
    concatenate x4, local copies, waits for them, and re-layouts: 0.01 us -> 3.24 us  [halo(): return jnp.concatenate([block, zero], axis=-3)]
  transfers between devices with their start and end apart: 32 -> 16, of which waited for: 8 -> 11; matrix products, arithmetic and copies ran while one was open for 1% -> 1% of each run, Pallas kernels for 0% -> 0%
where the time goes in v4:
time: 238 us; the launch traced here: 237 us
  blocking collectives  114 us (48%)
  starting transfers between devices  39.4 us (17%)
  waiting for transfers between devices  33.5 us (14%)
  other arithmetic  13.8 us (6%)
  between operations  11.3 us (5%)
  Pallas kernels  9.03 us (4%)
  local copies, waits for them, and re-layouts  8.67 us (4%)
  matrix products  7.35 us (3%)
    all_to_all x3, blocking collectives, global_sum(): gathered = lax.all_to_all(spread, ('wide', 'narrow'), 0, 0, tiled=True)  92.9 us
    ppermute x16, starting transfers between devices, _shift(): return lax.ppermute(field, axis, pairs)  39.4 us
    ppermute x16, waiting for transfers between devices, _shift(): return lax.ppermute(field, axis, pairs)  33.5 us
    all_to_all x1, blocking collectives, shards(): lax.all_to_all(send.reshape(owners, CAP, 4), 'wide', 0, 0, tiled=True)  20.8 us
    pallas_call x4, Pallas kernels, _local_call(): pl.pallas_call(kernel, out_shape=jax.ShapeDtypeStruct(out_shape, jnp.floa...  9.03 us
  transfers between devices with their start and end apart: 16, of which 11 were waited for; matrix products, arithmetic and copies ran while one was open for 1% of the time, Pallas kernels for 0%

profile of v4, /device:TPU:1, one launch (start us, length us, event | category | flops | bytes accessed | tf_op | source)
XLA Modules:
  0.0 236.7 jit_solution(5799519303294554115)
XLA Ops:
  0.7 1.4 fusion.5
  2.7 3.7 %fusion = f32[2048,4]{0,1:T(4,128)S(1)} fusion(s32[1024]{0:T(1024)S(1)} %convert_add_fusion, f32[1024,3]{0,1:T(4,128)S(1)} %bitcast.112, f32[1024,1]{0,1:T(1,128)S(1)} %bitcast.111), kind=kOutput, calls=%fused_computation.1 | convolution fusion | flops 102764544 | bytes 53248 | tf_op jit(solution)/shard_map/dot_general | solution.py:134
  6.8 20.8 %all_to_all.23 = f32[64,1,128]{2,1,0:T(1,128)S(1)} all-to-all(f32[64,1,128]{2,1,0:T(1,128)S(1)} %reshape.76), channel_id=1, replica_groups=mesh['wide'=64,'narrow'=8] {'wide'}, dimensions={0} | all-to-all | bytes 65536 | tf_op jit(solution)/shard_map/all_to_all | solution.py:135
  27.6 0.5 broadcast.48
  28.1 0.7 reduce.3
  29.2 0.3 fusion.14
  29.5 1.1 fusion.17
  30.7 2.2 fusion.3
  33.0 2.8 %collective-permute-start = (f32[3,2,16,256]{3,2,1,0:T(8,128)S(1)}, f32[3,2,16,256]{3,2,1,0:T(8,128)S(1)}, u32[]{:S(2)}, u32[]{:S(2)}) collective-permute-start(f32[3,2,16,256]{3,2,1,0:T(8,128)S(1)} %bitcast.84), channel_id=1, source_target_pairs={{0,8},{8,16},{16,24},{24,32},{32,40},{40,48},{48,56},{56,64},{64,7... | collective-permute-start | bytes 294920 | tf_op jit(solution)/shard_map/ppermute | solution.py:104
  35.7 1.9 collective-permute-start.1
  37.7 4.0 %collective-permute-done.1 = f32[3,2,16,256]{3,2,1,0:T(8,128)S(1)} collective-permute-done((f32[3,2,16,256]{3,2,1,0:T(8,128)S(1)}, f32[3,2,16,256]{3,2,1,0:T(8,128)S(1)}, u32[]{:S(2)}, u32[]{:S(2)}) %collective-permute-start.1) | collective-permute-done | bytes 98336 | tf_op jit(solution)/shard_map/ppermute | solution.py:104
  41.7 4.0 %collective-permute-start.2 = (f32[3,3,2,16,256]{4,3,2,1,0:T(8,128)S(1)}, f32[3,3,2,16,256]{4,3,2,1,0:T(8,128)S(1)}, u32[]{:S(2)}, u32[]{:S(2)}) collective-permute-start(f32[3,3,2,16,256]{4,3,2,1,0:T(8,128)S(1)} %get-tuple-element.9), channel_id=1, source_target_pairs={{0,1},{1,2},{2,3},{3,4},{4,5},{5,6},{6,7},{8,9},{9,10},{10,11},{11... | collective-permute-start | bytes 884744 | tf_op jit(solution)/shard_map/ppermute | solution.py:104
  45.7 1.3 collective-permute-start.3
  47.1 0.7 reshape.67.tab_ref
  47.7 2.5 %collective-permute-done.2 = f32[3,3,2,16,256]{4,3,2,1,0:T(8,128)S(1)} collective-permute-done((f32[3,3,2,16,256]{4,3,2,1,0:T(8,128)S(1)}, f32[3,3,2,16,256]{4,3,2,1,0:T(8,128)S(1)}, u32[]{:S(2)}, u32[]{:S(2)}) %collective-permute-start.2) | collective-permute-done | bytes 294944 | tf_op jit(solution)/shard_map/ppermute | solution.py:104
  50.3 4.5 %collective-permute-done.3 = f32[3,3,2,16,256]{4,3,2,1,0:T(8,128)S(1)} collective-permute-done((f32[3,3,2,16,256]{4,3,2,1,0:T(8,128)S(1)}, f32[3,3,2,16,256]{4,3,2,1,0:T(8,128)S(1)}, u32[]{:S(2)}, u32[]{:S(2)}) %collective-permute-start.3) | collective-permute-done | bytes 294944 | tf_op jit(solution)/shard_map/ppermute | solution.py:104
  54.8 1.0 concatenate.20.src_ref
  55.8 1.9 shard_map.68
  57.8 5.1 %collective-permute-start.4 = (f32[2,16,256]{2,1,0:T(8,128)}, f32[2,16,256]{2,1,0:T(8,128)S(1)}, u32[]{:S(2)}, u32[]{:S(2)}) collective-permute-start(f32[2,16,256]{2,1,0:T(8,128)} %shard_map.68), channel_id=1, source_target_pairs={{0,8},{8,16},{16,24},{24,32},{32,40},{40,48},{48,56},{56,64},{64,7... | collective-permute-start | bytes 98312 | tf_op jit(solution)/shard_map/ppermute | solution.py:104
  62.9 1.9 collective-permute-start.5
  64.8 3.5 %collective-permute-done.5 = f32[2,16,256]{2,1,0:T(8,128)S(1)} collective-permute-done((f32[2,16,256]{2,1,0:T(8,128)}, f32[2,16,256]{2,1,0:T(8,128)S(1)}, u32[]{:S(2)}, u32[]{:S(2)}) %collective-permute-start.5) | collective-permute-done | bytes 32800 | tf_op jit(solution)/shard_map/ppermute | solution.py:104
  68.3 0.8 fusion.29
  69.1 4.0 %collective-permute-start.6 = (f32[3,2,16,256]{3,2,1,0:T(8,128)S(1)}, f32[3,2,16,256]{3,2,1,0:T(8,128)S(1)}, u32[]{:S(2)}, u32[]{:S(2)}) collective-permute-start(f32[3,2,16,256]{3,2,1,0:T(8,128)S(1)} %get-tuple-element.15), channel_id=1, source_target_pairs={{0,1},{1,2},{2,3},{3,4},{4,5},{5,6},{6,7},{8,9},{9,10},{10,11},{11... | collective-permute-start | bytes 294920 | tf_op jit(solution)/shard_map/ppermute | solution.py:104
  73.1 1.3 collective-permute-start.7
  74.4 0.6 fusion.20
  75.0 5.3 %collective-permute-done.7 = f32[3,2,16,256]{3,2,1,0:T(8,128)S(1)} collective-permute-done((f32[3,2,16,256]{3,2,1,0:T(8,128)S(1)}, f32[3,2,16,256]{3,2,1,0:T(8,128)S(1)}, u32[]{:S(2)}, u32[]{:S(2)}) %collective-permute-start.7) | collective-permute-done | bytes 98336 | tf_op jit(solution)/shard_map/ppermute | solution.py:104
  80.4 0.7 concatenate.21.src_ref
  81.1 2.4 shard_map.69
  83.5 1.4 multiply_reduce_fusion.5
  84.9 1.3 pad_maximum_fusion.8
  86.2 0.1 broadcast_in_dim.14
  86.3 32.7 %all_to_all.24 = f32[512,1,2]{2,1,0:T(1,128)S(1)} all-to-all(f32[512,1,2]{2,1,0:T(1,128)S(1)} %broadcast_in_dim.14), channel_id=1, replica_groups=mesh['wide'=64,'narrow'=8] {'wide','narrow'}, dimensions={0} | all-to-all | bytes 8192 | tf_op jit(solution)/shard_map/all_to_all | solution.py:154
  119.0 0.6 reduce_sum.93
  119.6 0.6 fusion.34
  121.5 1.9 collective-permute-start.8
  123.4 2.4 %collective-permute-start.9 = (f32[2,16,256]{2,1,0:T(8,128)S(1)}, f32[2,16,256]{2,1,0:T(8,128)S(1)}, u32[]{:S(2)}, u32[]{:S(2)}) collective-permute-start(f32[2,16,256]{2,1,0:T(8,128)S(1)} %multiply_subtract_fusion.2), channel_id=1, source_target_pairs={{8,0},{16,8},{24,16},{32,24},{40,32},{48,40},{56,48},{64,56},{72,6... | collective-permute-start | bytes 98312 | tf_op jit(solution)/shard_map/ppermute | solution.py:104
  125.8 2.8 %collective-permute-done.9 = f32[2,16,256]{2,1,0:T(8,128)S(1)} collective-permute-done((f32[2,16,256]{2,1,0:T(8,128)S(1)}, f32[2,16,256]{2,1,0:T(8,128)S(1)}, u32[]{:S(2)}, u32[]{:S(2)}) %collective-permute-start.9) | collective-permute-done | bytes 32800 | tf_op jit(solution)/shard_map/ppermute | solution.py:104
  128.6 2.9 %collective-permute-start.10 = (f32[3,2,16,256]{3,2,1,0:T(8,128)S(1)}, f32[3,2,16,256]{3,2,1,0:T(8,128)S(1)}, u32[]{:S(2)}, u32[]{:S(2)}) collective-permute-start(f32[3,2,16,256]{3,2,1,0:T(8,128)S(1)} %get-tuple-element.13), channel_id=1, source_target_pairs={{0,1},{1,2},{2,3},{3,4},{4,5},{5,6},{6,7},{8,9},{9,10},{10,11},{11... | collective-permute-start | bytes 294920 | tf_op jit(solution)/shard_map/ppermute | solution.py:104
  131.6 1.3 collective-permute-start.11
  132.9 0.3 collective-permute-done.10
  133.2 3.7 %collective-permute-done.11 = f32[3,2,16,256]{3,2,1,0:T(8,128)S(1)} collective-permute-done((f32[3,2,16,256]{3,2,1,0:T(8,128)S(1)}, f32[3,2,16,256]{3,2,1,0:T(8,128)S(1)}, u32[]{:S(2)}, u32[]{:S(2)}) %collective-permute-start.11) | collective-permute-done | bytes 98336 | tf_op jit(solution)/shard_map/ppermute | solution.py:104
  137.0 0.7 concatenate.22.src_ref
  137.7 2.4 shard_map.70
  140.1 1.5 multiply_reduce_fusion.3
  141.6 1.3 pad_maximum_fusion.9
  143.1 30.1 %all_to_all.25 = f32[512,1,2]{2,1,0:T(1,128)S(1)} all-to-all(f32[512,1,2]{2,1,0:T(1,128)S(1)} %broadcast_in_dim.15), channel_id=1, replica_groups=mesh['wide'=64,'narrow'=8] {'wide','narrow'}, dimensions={0} | all-to-all | bytes 8192 | tf_op jit(solution)/shard_map/all_to_all | solution.py:154
  173.2 0.6 reduce_sum.96
  173.7 0.7 fusion.33
  179.0 1.9 collective-permute-start.12
  180.9 2.4 %collective-permute-start.13 = (f32[2,16,256]{2,1,0:T(8,128)S(1)}, f32[2,16,256]{2,1,0:T(8,128)S(1)}, u32[]{:S(2)}, u32[]{:S(2)}) collective-permute-start(f32[2,16,256]{2,1,0:T(8,128)S(1)} %multiply_subtract_fusion.1), channel_id=1, source_target_pairs={{8,0},{16,8},{24,16},{32,24},{40,32},{48,40},{56,48},{64,56},{72,6... | collective-permute-start | bytes 98312 | tf_op jit(solution)/shard_map/ppermute | solution.py:104
  183.4 2.8 %collective-permute-done.13 = f32[2,16,256]{2,1,0:T(8,128)S(1)} collective-permute-done((f32[2,16,256]{2,1,0:T(8,128)S(1)}, f32[2,16,256]{2,1,0:T(8,128)S(1)}, u32[]{:S(2)}, u32[]{:S(2)}) %collective-permute-start.13) | collective-permute-done | bytes 32800 | tf_op jit(solution)/shard_map/ppermute | solution.py:104
  186.2 2.9 %collective-permute-start.14 = (f32[3,2,16,256]{3,2,1,0:T(8,128)S(1)}, f32[3,2,16,256]{3,2,1,0:T(8,128)S(1)}, u32[]{:S(2)}, u32[]{:S(2)}) collective-permute-start(f32[3,2,16,256]{3,2,1,0:T(8,128)S(1)} %get-tuple-element.11), channel_id=1, source_target_pairs={{0,1},{1,2},{2,3},{3,4},{4,5},{5,6},{6,7},{8,9},{9,10},{10,11},{11... | collective-permute-start | bytes 294920 | tf_op jit(solution)/shard_map/ppermute | solution.py:104
  189.1 1.3 collective-permute-start.15
  190.4 0.3 collective-permute-done.14
  190.7 3.7 %collective-permute-done.15 = f32[3,2,16,256]{3,2,1,0:T(8,128)S(1)} collective-permute-done((f32[3,2,16,256]{3,2,1,0:T(8,128)S(1)}, f32[3,2,16,256]{3,2,1,0:T(8,128)S(1)}, u32[]{:S(2)}, u32[]{:S(2)}) %collective-permute-start.15) | collective-permute-done | bytes 98336 | tf_op jit(solution)/shard_map/ppermute | solution.py:104
  194.5 0.7 concatenate.23.src_ref
  195.3 2.4 shard_map.71
  197.6 1.4 multiply_reduce_fusion.1
  199.1 1.3 pad_maximum_fusion.10
  200.5 30.1 %all_to_all.26 = f32[512,1,2]{2,1,0:T(1,128)S(1)} all-to-all(f32[512,1,2]{2,1,0:T(1,128)S(1)} %broadcast_in_dim.16), channel_id=1, replica_groups=mesh['wide'=64,'narrow'=8] {'wide','narrow'}, dimensions={0} | all-to-all | bytes 8192 | tf_op jit(solution)/shard_map/all_to_all | solution.py:154
  230.6 0.6 reduce_sum.99
  231.2 0.6 fusion.32
  235.5 0.6 reshape.74
  236.1 0.6 reshape.75
  (47 shorter events, 1.3 us)
Async XLA Ops:
  0.6 1.4 copy-start.4
  0.6 2.1 copy-start.5
  0.6 2.1 copy-start.6
  32.9 14.1 %copy-start.7 = (s32[1,1,2,27]{3,2,1,0:T(2,128)S(1)}, s32[1,1,2,27]{3,2,1,0:T(2,128)}, u32[]{:S(2)}) copy-start(s32[1,1,2,27]{3,2,1,0:T(2,128)} %param.9) | copy-start | bytes 652
  33.0 4.7 %collective-permute-start = (f32[3,2,16,256]{3,2,1,0:T(8,128)S(1)}, f32[3,2,16,256]{3,2,1,0:T(8,128)S(1)}, u32[]{:S(2)}, u32[]{:S(2)}) collective-permute-start(f32[3,2,16,256]{3,2,1,0:T(8,128)S(1)} %bitcast.84), channel_id=1, source_target_pairs={{0,8},{8,16},{16,24},{24,32},{32,40},{40,48},{48,56},{56,64},{64,7... | collective-permute-start | bytes 294920 | tf_op jit(solution)/shard_map/ppermute | solution.py:104
  35.7 5.9 %collective-permute-start.1 = (f32[3,2,16,256]{3,2,1,0:T(8,128)S(1)}, f32[3,2,16,256]{3,2,1,0:T(8,128)S(1)}, u32[]{:S(2)}, u32[]{:S(2)}) collective-permute-start(f32[3,2,16,256]{3,2,1,0:T(8,128)S(1)} %bitcast.85), channel_id=1, source_target_pairs={{8,0},{16,8},{24,16},{32,24},{40,32},{48,40},{56,48},{64,56},{72,6... | collective-permute-start | bytes 294920 | tf_op jit(solution)/shard_map/ppermute | solution.py:104
  41.7 8.5 %collective-permute-start.2 = (f32[3,3,2,16,256]{4,3,2,1,0:T(8,128)S(1)}, f32[3,3,2,16,256]{4,3,2,1,0:T(8,128)S(1)}, u32[]{:S(2)}, u32[]{:S(2)}) collective-permute-start(f32[3,3,2,16,256]{4,3,2,1,0:T(8,128)S(1)} %get-tuple-element.9), channel_id=1, source_target_pairs={{0,1},{1,2},{2,3},{3,4},{4,5},{5,6},{6,7},{8,9},{9,10},{10,11},{11... | collective-permute-start | bytes 884744 | tf_op jit(solution)/shard_map/ppermute | solution.py:104
  45.7 9.0 %collective-permute-start.3 = (f32[3,3,2,16,256]{4,3,2,1,0:T(8,128)S(1)}, f32[3,3,2,16,256]{4,3,2,1,0:T(8,128)S(1)}, u32[]{:S(2)}, u32[]{:S(2)}) collective-permute-start(f32[3,3,2,16,256]{4,3,2,1,0:T(8,128)S(1)} %get-tuple-element.9), channel_id=1, source_target_pairs={{1,0},{2,1},{3,2},{4,3},{5,4},{6,5},{7,6},{9,8},{10,9},{11,10},{12... | collective-permute-start | bytes 884744 | tf_op jit(solution)/shard_map/ppermute | solution.py:104
  57.8 7.0 %collective-permute-start.4 = (f32[2,16,256]{2,1,0:T(8,128)}, f32[2,16,256]{2,1,0:T(8,128)S(1)}, u32[]{:S(2)}, u32[]{:S(2)}) collective-permute-start(f32[2,16,256]{2,1,0:T(8,128)} %shard_map.68), channel_id=1, source_target_pairs={{0,8},{8,16},{16,24},{24,32},{32,40},{40,48},{48,56},{56,64},{64,7... | collective-permute-start | bytes 98312 | tf_op jit(solution)/shard_map/ppermute | solution.py:104
  62.9 5.4 %collective-permute-start.5 = (f32[2,16,256]{2,1,0:T(8,128)}, f32[2,16,256]{2,1,0:T(8,128)S(1)}, u32[]{:S(2)}, u32[]{:S(2)}) collective-permute-start(f32[2,16,256]{2,1,0:T(8,128)} %shard_map.68), channel_id=1, source_target_pairs={{8,0},{16,8},{24,16},{32,24},{40,32},{48,40},{56,48},{64,56},{72,6... | collective-permute-start | bytes 98312 | tf_op jit(solution)/shard_map/ppermute | solution.py:104
  69.1 5.9 %collective-permute-start.6 = (f32[3,2,16,256]{3,2,1,0:T(8,128)S(1)}, f32[3,2,16,256]{3,2,1,0:T(8,128)S(1)}, u32[]{:S(2)}, u32[]{:S(2)}) collective-permute-start(f32[3,2,16,256]{3,2,1,0:T(8,128)S(1)} %get-tuple-element.15), channel_id=1, source_target_pairs={{0,1},{1,2},{2,3},{3,4},{4,5},{5,6},{6,7},{8,9},{9,10},{10,11},{11... | collective-permute-start | bytes 294920 | tf_op jit(solution)/shard_map/ppermute | solution.py:104
  73.1 7.2 %collective-permute-start.7 = (f32[3,2,16,256]{3,2,1,0:T(8,128)S(1)}, f32[3,2,16,256]{3,2,1,0:T(8,128)S(1)}, u32[]{:S(2)}, u32[]{:S(2)}) collective-permute-start(f32[3,2,16,256]{3,2,1,0:T(8,128)S(1)} %get-tuple-element.15), channel_id=1, source_target_pairs={{1,0},{2,1},{3,2},{4,3},{5,4},{6,5},{7,6},{9,8},{10,9},{11,10},{12... | collective-permute-start | bytes 294920 | tf_op jit(solution)/shard_map/ppermute | solution.py:104
  80.3 3.2 %copy-start = (f32[2,16,256]{2,1,0:T(8,128)S(1)}, f32[2,16,256]{2,1,0:T(8,128)}, u32[]{:S(2)}) copy-start(f32[2,16,256]{2,1,0:T(8,128)} %shard_map.68) | copy-start | bytes 98308
  83.5 38.0 %copy-start.1 = (f32[2,16,256]{2,1,0:T(8,128)S(1)}, f32[2,16,256]{2,1,0:T(8,128)}, u32[]{:S(2)}) copy-start(f32[2,16,256]{2,1,0:T(8,128)} %shard_map.69) | copy-start | bytes 98308
  121.5 4.3 %collective-permute-start.8 = (f32[2,16,256]{2,1,0:T(8,128)S(1)}, f32[2,16,256]{2,1,0:T(8,128)S(1)}, u32[]{:S(2)}, u32[]{:S(2)}) collective-permute-start(f32[2,16,256]{2,1,0:T(8,128)S(1)} %multiply_subtract_fusion.2), channel_id=1, source_target_pairs={{0,8},{8,16},{16,24},{24,32},{32,40},{40,48},{48,56},{56,64},{64,7... | collective-permute-start | bytes 98312 | tf_op jit(solution)/shard_map/ppermute | solution.py:104
  123.4 5.2 %collective-permute-start.9 = (f32[2,16,256]{2,1,0:T(8,128)S(1)}, f32[2,16,256]{2,1,0:T(8,128)S(1)}, u32[]{:S(2)}, u32[]{:S(2)}) collective-permute-start(f32[2,16,256]{2,1,0:T(8,128)S(1)} %multiply_subtract_fusion.2), channel_id=1, source_target_pairs={{8,0},{16,8},{24,16},{32,24},{40,32},{48,40},{56,48},{64,56},{72,6... | collective-permute-start | bytes 98312 | tf_op jit(solution)/shard_map/ppermute | solution.py:104
  128.6 4.6 %collective-permute-start.10 = (f32[3,2,16,256]{3,2,1,0:T(8,128)S(1)}, f32[3,2,16,256]{3,2,1,0:T(8,128)S(1)}, u32[]{:S(2)}, u32[]{:S(2)}) collective-permute-start(f32[3,2,16,256]{3,2,1,0:T(8,128)S(1)} %get-tuple-element.13), channel_id=1, source_target_pairs={{0,1},{1,2},{2,3},{3,4},{4,5},{5,6},{6,7},{8,9},{9,10},{10,11},{11... | collective-permute-start | bytes 294920 | tf_op jit(solution)/shard_map/ppermute | solution.py:104
  131.6 5.4 %collective-permute-start.11 = (f32[3,2,16,256]{3,2,1,0:T(8,128)S(1)}, f32[3,2,16,256]{3,2,1,0:T(8,128)S(1)}, u32[]{:S(2)}, u32[]{:S(2)}) collective-permute-start(f32[3,2,16,256]{3,2,1,0:T(8,128)S(1)} %get-tuple-element.13), channel_id=1, source_target_pairs={{1,0},{2,1},{3,2},{4,3},{5,4},{6,5},{7,6},{9,8},{10,9},{11,10},{12... | collective-permute-start | bytes 294920 | tf_op jit(solution)/shard_map/ppermute | solution.py:104
  140.1 38.9 %copy-start.2 = (f32[2,16,256]{2,1,0:T(8,128)S(1)}, f32[2,16,256]{2,1,0:T(8,128)}, u32[]{:S(2)}) copy-start(f32[2,16,256]{2,1,0:T(8,128)} %shard_map.70) | copy-start | bytes 98308
  179.0 4.3 %collective-permute-start.12 = (f32[2,16,256]{2,1,0:T(8,128)S(1)}, f32[2,16,256]{2,1,0:T(8,128)S(1)}, u32[]{:S(2)}, u32[]{:S(2)}) collective-permute-start(f32[2,16,256]{2,1,0:T(8,128)S(1)} %multiply_subtract_fusion.1), channel_id=1, source_target_pairs={{0,8},{8,16},{16,24},{24,32},{32,40},{40,48},{48,56},{56,64},{64,7... | collective-permute-start | bytes 98312 | tf_op jit(solution)/shard_map/ppermute | solution.py:104
  180.9 5.2 %collective-permute-start.13 = (f32[2,16,256]{2,1,0:T(8,128)S(1)}, f32[2,16,256]{2,1,0:T(8,128)S(1)}, u32[]{:S(2)}, u32[]{:S(2)}) collective-permute-start(f32[2,16,256]{2,1,0:T(8,128)S(1)} %multiply_subtract_fusion.1), channel_id=1, source_target_pairs={{8,0},{16,8},{24,16},{32,24},{40,32},{48,40},{56,48},{64,56},{72,6... | collective-permute-start | bytes 98312 | tf_op jit(solution)/shard_map/ppermute | solution.py:104
  186.2 4.6 %collective-permute-start.14 = (f32[3,2,16,256]{3,2,1,0:T(8,128)S(1)}, f32[3,2,16,256]{3,2,1,0:T(8,128)S(1)}, u32[]{:S(2)}, u32[]{:S(2)}) collective-permute-start(f32[3,2,16,256]{3,2,1,0:T(8,128)S(1)} %get-tuple-element.11), channel_id=1, source_target_pairs={{0,1},{1,2},{2,3},{3,4},{4,5},{5,6},{6,7},{8,9},{9,10},{10,11},{11... | collective-permute-start | bytes 294920 | tf_op jit(solution)/shard_map/ppermute | solution.py:104
  189.1 5.4 %collective-permute-start.15 = (f32[3,2,16,256]{3,2,1,0:T(8,128)S(1)}, f32[3,2,16,256]{3,2,1,0:T(8,128)S(1)}, u32[]{:S(2)}, u32[]{:S(2)}) collective-permute-start(f32[3,2,16,256]{3,2,1,0:T(8,128)S(1)} %get-tuple-element.11), channel_id=1, source_target_pairs={{1,0},{2,1},{3,2},{4,3},{5,4},{6,5},{7,6},{9,8},{10,9},{11,10},{12... | collective-permute-start | bytes 294920 | tf_op jit(solution)/shard_map/ppermute | solution.py:104
  197.6 37.8 %copy-start.3 = (f32[2,16,256]{2,1,0:T(8,128)S(1)}, f32[2,16,256]{2,1,0:T(8,128)}, u32[]{:S(2)}) copy-start(f32[2,16,256]{2,1,0:T(8,128)} %shard_map.71) | copy-start | bytes 98308

commit v5 on v3

--- a/solution.py
+++ b/solution.py
@@ -12,7 +12,7 @@
 CAP = 32
 HIGHEST = lax.Precision.HIGHEST
 ROWS, LANES = 16, 256
-SHIFT, SPAN = 8.5, 8.0
+SHIFT, SPAN = 8.0, 8.0
 
 
 def _solve(matrix, rhs):
@@ -31,6 +31,116 @@
     return x
 
 
+def _two_sum(a, b):
+    total = a + b
+    part = total - a
+    return total, (a - (total - part)) + (b - part)
+
+
+def _split(a):
+    scaled = a * 4097.0
+    high = scaled - (scaled - a)
+    return high, a - high
+
+
+def _two_prod(a, b):
+    product = a * b
+    ah, al = _split(a)
+    bh, bl = _split(b)
+    return product, ((ah * bh - product) + ah * bl + al * bh) + al * bl
+
+
+def _halve(s, e, axis, stop):
+    while s.shape[axis] > stop:
+        h = s.shape[axis] // 2
+        first = lax.slice_in_dim(s, 0, h, axis=axis)
+        second = lax.slice_in_dim(s, h, 2 * h, axis=axis)
+        s, err = _two_sum(first, second)
+        e = lax.slice_in_dim(e, 0, h, axis=axis) + lax.slice_in_dim(e, h, 2 * h, axis=axis) + err
+    return s, e
+
+
+def _spread(s, e, axis):
+    k = s.shape[axis] // 2
+    while k >= 1:
+        s, err = _two_sum(s, pltpu.roll(s, k, axis))
+        e = e + pltpu.roll(e, k, axis) + err
+        k //= 2
+    return s, e
+
+
+def _dd_add(x, y):
+    s, e = _two_sum(x[0], y[0])
+    return _two_sum(s, e + (x[1] + y[1]))
+
+
+def _gram_kernel(basis_ref, out_ref):
+    row = lax.broadcasted_iota(jnp.int32, out_ref.shape, 0)
+    lane = lax.broadcasted_iota(jnp.int32, out_ref.shape, 1)
+    count = basis_ref.shape[0]
+    acc = jnp.zeros(out_ref.shape, jnp.float32)
+    k = 0
+    for i in range(count):
+        for j in range(i, count):
+            s, e = _two_prod(basis_ref[i], basis_ref[j])
+            s, e = _halve(s, e, 0, 8)
+            s, e = _halve(s, e, 1, 128)
+            s, e = _spread(s, e, 0)
+            s, e = _spread(s, e, 1)
+            high, low = _two_sum(s, e)
+            acc = jnp.where((row == 0) & (lane == k), high, acc)
+            acc = jnp.where((row == 1) & (lane == k), low, acc)
+            k += 1
+    out_ref[...] = acc
+
+
+def _galerkin_kernel(parts_ref, out_ref, lift=None):
+    half = parts_ref.shape[0] // 2
+    s, e = _halve(parts_ref[0:half, :], parts_ref[half:, :], 1, 128)
+    s, e = _spread(s, e, 1)
+    high, low = _two_sum(s, e)
+    rows = lax.broadcasted_iota(jnp.int32, high.shape, 0)
+
+    def pick(values, k):
+        return jnp.sum(jnp.where(rows == k, values, 0.0), axis=0, keepdims=True)
+
+    size = len(lift)
+    pairs = [(i, j) for i in range(size) for j in range(i, size)]
+    gram = {}
+    for k, (i, j) in enumerate(pairs):
+        gram[i, j] = gram[j, i] = (pick(high, k), pick(low, k))
+    n = size - 1
+    matrix = [[None] * n for _ in range(n)]
+    for i in range(n):
+        for j in range(n):
+            entry = None
+            for k in range(size):
+                if lift[k][j] != 0.0:
+                    term = (lift[k][j] * gram[i, k][0], lift[k][j] * gram[i, k][1])
+                    entry = term if entry is None else _dd_add(entry, term)
+            matrix[i][j] = entry
+    wanted = [gram[i, 0] for i in range(n)]
+    top = [[matrix[i][j][0] for j in range(n)] for i in range(n)]
+    coeff = _solve(top, [w[0] for w in wanted])
+    misfit = []
+    for i in range(n):
+        acc = wanted[i]
+        for j in range(n):
+            p, pe = _two_prod(matrix[i][j][0], coeff[j])
+            acc = _dd_add(acc, (-p, -(pe + matrix[i][j][1] * coeff[j])))
+        misfit.append(acc[0] + acc[1])
+    coeff = [c + d for c, d in zip(coeff, _solve(top, misfit))]
+    values = list(coeff)
+    for k in range(size):
+        terms = [lift[k][j] * coeff[j] for j in range(n) if lift[k][j] != 0.0]
+        values.append((1.0 if k == 0 else 0.0) - sum(terms[1:], terms[0]))
+    out_rows = lax.broadcasted_iota(jnp.int32, out_ref.shape, 0)
+    out = jnp.zeros(out_ref.shape, jnp.float32)
+    for k, v in enumerate(values):
+        out = jnp.where(out_rows == k, v, out)
+    out_ref[...] = out
+
+
 def _masks():
     shape = (ROWS, LANES)
     lane = lax.broadcasted_iota(jnp.int32, shape, 1)
@@ -166,12 +276,6 @@
     shape = (bricks, ROWS, LANES)
     right_side = _local_call(_divergence_kernel, shape, [table, halo(vector_field)], 20 * bricks * 4096)
 
-    def global_sum(parts):
-        stacked = jnp.stack(parts)[None, :]
-        spread = jnp.broadcast_to(stacked, (devices, stacked.shape[1]))
-        gathered = lax.all_to_all(spread, ("wide", "narrow"), 0, 0, tiled=True)
-        return jnp.sum(gathered, axis=0)
-
     basis = [right_side]
     kernel = functools.partial(_stencil_kernel, shift=SHIFT, scale=1.0 / SPAN)
     for k in range(ITERS):
@@ -184,24 +288,24 @@
             lift[1][0] = SPAN
         else:
             lift[k - 1][k] = lift[k + 1][k] = 0.5 * SPAN
-    pairs = [(i, j) for i in range(ITERS + 1) for j in range(i, ITERS + 1)]
-    sums = global_sum([jnp.sum(basis[i] * basis[j]) for i, j in pairs])
-    gram = [[None] * (ITERS + 1) for _ in range(ITERS + 1)]
-    for k, (i, j) in enumerate(pairs):
-        gram[i][j] = gram[j][i] = sums[k]
-
-    def lifted(i, j):
-        terms = [lift[k][j] * gram[i][k] for k in range(ITERS + 1) if lift[k][j] != 0.0]
-        return sum(terms[1:], terms[0])
-
-    coeff = _solve([[lifted(i, j) for j in range(ITERS)] for i in range(ITERS)], [gram[i][0] for i in range(ITERS)])
+    vmem = pl.BlockSpec(memory_space=pltpu.VMEM)
+    stacked = jnp.stack(basis).reshape(ITERS + 1, bricks * ROWS, LANES)
+    partial_sums = pl.pallas_call(
+        _gram_kernel, out_shape=jax.ShapeDtypeStruct((8, 128), jnp.float32), in_specs=[vmem], out_specs=vmem
+    )(stacked)
+    payload = partial_sums[0:2, 0:16].reshape(1, 32)
+    gathered = lax.all_to_all(jnp.broadcast_to(payload, (devices, 32)), ("wide", "narrow"), 0, 0, tiled=True)
+    found = pl.pallas_call(
+        functools.partial(_galerkin_kernel, lift=lift),
+        out_shape=jax.ShapeDtypeStruct((8, 128), jnp.float32),
+        in_specs=[vmem],
+        out_specs=vmem,
+    )(jnp.pad(gathered.T, ((0, 0), (0, max(0, 128 - devices)))))
+    coeff = [found[k, 0] for k in range(ITERS)]
+    weights = [found[ITERS + k, 0] for k in range(ITERS + 1)]
     solution = coeff[0] * basis[0]
     for j in range(1, ITERS):
         solution = solution + coeff[j] * basis[j]
-    weights = []
-    for k in range(ITERS + 1):
-        terms = [lift[k][j] * coeff[j] for j in range(ITERS) if lift[k][j] != 0.0]
-        weights.append((1.0 if k == 0 else 0.0) - sum(terms[1:], terms[0]))
     residual = weights[0] * basis[0]
     for k in range(1, ITERS + 1):
         residual = residual + weights[k] * basis[k]

time: 191 us -> 181 us (0.948)
  between operations: 16.2 us -> 1.71 us
  Pallas kernels: 9.02 us -> 13.3 us
  local copies, waits for them, and re-layouts: 13.4 us -> 9.56 us
  other arithmetic: 7.49 us -> 11.3 us
    another operation x1 -> x0, local copies, waits for them, and re-layouts: 6.27 us -> none  [global_sum(): stacked = jnp.stack(parts)[None, :]]
    add x1, other arithmetic: 0.02 us -> 4.44 us  [shards(): residual = residual + weights[k] * basis[k]]
    pallas_call x0 -> x2, Pallas kernels: none -> 4.29 us  [the longest x1 2.23 us: shards(): pl.pallas_call(_gram_kernel, out_shape=jax.ShapeDtypeStruct((8, 128), jnp...]
    reduce_sum x2 -> x0, other arithmetic: 2.12 us -> none  [the longest x1 1.56 us: shards(): sums = global_sum([jnp.sum(basis[i] * basis[j]) for i, j in pairs])]
where the time goes in v5:
time: 181 us; the launch traced here: 180 us
  blocking collectives  57.7 us (32%)
  starting transfers between devices  44.3 us (24%)
  waiting for transfers between devices  34.6 us (19%)
  Pallas kernels  13.3 us (7%)
  other arithmetic  11.3 us (6%)
  local copies, waits for them, and re-layouts  9.56 us (5%)
  matrix products  7.35 us (4%)
    ppermute x16, starting transfers between devices, _shift(): return lax.ppermute(field, axis, pairs)  44.3 us
    all_to_all x1, blocking collectives, shards(): lax.all_to_all(jnp.broadcast_to(payload, (devices, 32)), ('wide', 'narrow...  36.9 us
    ppermute x16, waiting for transfers between devices, _shift(): return lax.ppermute(field, axis, pairs)  34.6 us
    all_to_all x1, blocking collectives, shards(): lax.all_to_all(send.reshape(owners, CAP, 4), 'wide', 0, 0, tiled=True)  20.8 us
    pallas_call x4, Pallas kernels, _local_call(): pl.pallas_call(kernel, out_shape=jax.ShapeDtypeStruct(out_shape, jnp.floa...  8.99 us
    add x1, other arithmetic, shards(): residual = residual + weights[k] * basis[k]  4.44 us
    dot_general x1, matrix products, shards(): jnp.dot(place_hot, payload, precision=HIGHEST, preferred_element_type=jnp...  3.74 us
  transfers between devices with their start and end apart: 16, of which 11 were waited for; matrix products, arithmetic and copies ran while one was open for 1% of the time, Pallas kernels for 0%

profile of v5, /device:TPU:1, one launch (start us, length us, event | category | flops | bytes accessed | tf_op | source)
XLA Modules:
  0.0 179.8 jit_solution(10703888655040743411)
XLA Ops:
  0.7 1.4 fusion.5
  2.7 3.7 %fusion = f32[2048,4]{0,1:T(4,128)S(1)} fusion(s32[1024]{0:T(1024)S(1)} %convert_add_fusion, f32[1024,3]{0,1:T(4,128)S(1)} %bitcast.119, f32[1024,1]{0,1:T(1,128)S(1)} %bitcast.118), kind=kOutput, calls=%fused_computation.1 | convolution fusion | flops 102764544 | bytes 53248 | tf_op jit(solution)/shard_map/dot_general | solution.py:262
  6.5 0.1 reshape.68
  6.7 0.1 reshape.76
  6.8 20.8 %all_to_all.14 = f32[64,1,128]{2,1,0:T(1,128)S(1)} all-to-all(f32[64,1,128]{2,1,0:T(1,128)S(1)} %reshape.76), channel_id=1, replica_groups=mesh['wide'=64,'narrow'=8] {'wide'}, dimensions={0} | all-to-all | bytes 65536 | tf_op jit(solution)/shard_map/all_to_all | solution.py:263
  27.6 0.5 broadcast.54
  28.1 0.7 reduce
  28.9 0.1 reshape.77
  29.0 0.1 reshape.69
  29.2 0.3 fusion.14
  29.5 1.1 fusion.17
  30.7 2.2 %fusion.3 = f32[128,256]{1,0:T(8,128)S(1)} fusion(f32[2048,32]{1,0:T(8,128)S(1)} %fusion.14, f32[2048,32]{1,0:T(8,128)S(1)} %get-tuple-element.18, f32[2048,32]{1,0:T(8,128)S(1)} %get-tuple-element.19, f32[2048,32]{1,0:T(8,128)S(1)} %get-tuple-element.17, s32[2048]{0:T(1024)S(1)} %bitcast.106), kind=kOutput, calls=%fused_computation.6 | convolution fusion | flops 806617088 | bytes 1187840 | tf_op jit(solution)/shard_map/pa,pb->ab/dot_general | solution.py:271
  33.0 2.8 %collective-permute-start = (f32[3,2,16,256]{3,2,1,0:T(8,128)S(1)}, f32[3,2,16,256]{3,2,1,0:T(8,128)S(1)}, u32[]{:S(2)}, u32[]{:S(2)}) collective-permute-start(f32[3,2,16,256]{3,2,1,0:T(8,128)S(1)} %bitcast.89), channel_id=1, source_target_pairs={{0,8},{8,16},{16,24},{24,32},{32,40},{40,48},{48,56},{56,64},{64,7... | collective-permute-start | bytes 294920 | tf_op jit(solution)/shard_map/ppermute | solution.py:232
  35.7 1.9 %collective-permute-start.1 = (f32[3,2,16,256]{3,2,1,0:T(8,128)S(1)}, f32[3,2,16,256]{3,2,1,0:T(8,128)S(1)}, u32[]{:S(2)}, u32[]{:S(2)}) collective-permute-start(f32[3,2,16,256]{3,2,1,0:T(8,128)S(1)} %bitcast.90), channel_id=1, source_target_pairs={{8,0},{16,8},{24,16},{32,24},{40,32},{48,40},{56,48},{64,56},{72,6... | collective-permute-start | bytes 294920 | tf_op jit(solution)/shard_map/ppermute | solution.py:232
  37.7 4.0 %collective-permute-done.1 = f32[3,2,16,256]{3,2,1,0:T(8,128)S(1)} collective-permute-done((f32[3,2,16,256]{3,2,1,0:T(8,128)S(1)}, f32[3,2,16,256]{3,2,1,0:T(8,128)S(1)}, u32[]{:S(2)}, u32[]{:S(2)}) %collective-permute-start.1) | collective-permute-done | bytes 98336 | tf_op jit(solution)/shard_map/ppermute | solution.py:232
  41.7 4.0 %collective-permute-start.2 = (f32[3,3,2,16,256]{4,3,2,1,0:T(8,128)S(1)}, f32[3,3,2,16,256]{4,3,2,1,0:T(8,128)S(1)}, u32[]{:S(2)}, u32[]{:S(2)}) collective-permute-start(f32[3,3,2,16,256]{4,3,2,1,0:T(8,128)S(1)} %get-tuple-element.3), channel_id=1, source_target_pairs={{0,1},{1,2},{2,3},{3,4},{4,5},{5,6},{6,7},{8,9},{9,10},{10,11},{11... | collective-permute-start | bytes 884744 | tf_op jit(solution)/shard_map/ppermute | solution.py:232
  45.7 1.3 collective-permute-start.3
  47.1 0.6 reshape.67.tab_ref
  47.7 2.6 %collective-permute-done.2 = f32[3,3,2,16,256]{4,3,2,1,0:T(8,128)S(1)} collective-permute-done((f32[3,3,2,16,256]{4,3,2,1,0:T(8,128)S(1)}, f32[3,3,2,16,256]{4,3,2,1,0:T(8,128)S(1)}, u32[]{:S(2)}, u32[]{:S(2)}) %collective-permute-start.2) | collective-permute-done | bytes 294944 | tf_op jit(solution)/shard_map/ppermute | solution.py:232
  50.3 4.5 %collective-permute-done.3 = f32[3,3,2,16,256]{4,3,2,1,0:T(8,128)S(1)} collective-permute-done((f32[3,3,2,16,256]{4,3,2,1,0:T(8,128)S(1)}, f32[3,3,2,16,256]{4,3,2,1,0:T(8,128)S(1)}, u32[]{:S(2)}, u32[]{:S(2)}) %collective-permute-start.3) | collective-permute-done | bytes 294944 | tf_op jit(solution)/shard_map/ppermute | solution.py:232
  54.8 1.0 concatenate.21.src_ref
  55.8 1.9 %shard_map.68 = f32[2,16,256]{2,1,0:T(8,128)} custom-call(s32[54]{0:T(128)} %reshape.67.tab_ref, f32[3,19,16,256]{3,2,1,0:T(8,128)} %concatenate.21.src_ref), custom_call_target="tpu_custom_call" | custom-call | flops 163840 | bytes 966872 | tf_op jit(solution)/shard_map/pallas_call | solution.py:220
  57.8 5.1 %collective-permute-start.4 = (f32[2,16,256]{2,1,0:T(8,128)}, f32[2,16,256]{2,1,0:T(8,128)S(1)}, u32[]{:S(2)}, u32[]{:S(2)}) collective-permute-start(f32[2,16,256]{2,1,0:T(8,128)} %shard_map.68), channel_id=1, source_target_pairs={{0,8},{8,16},{16,24},{24,32},{32,40},{40,48},{48,56},{56,64},{64,7... | collective-permute-start | bytes 98312 | tf_op jit(solution)/shard_map/ppermute | solution.py:232
  62.9 1.9 %collective-permute-start.5 = (f32[2,16,256]{2,1,0:T(8,128)}, f32[2,16,256]{2,1,0:T(8,128)S(1)}, u32[]{:S(2)}, u32[]{:S(2)}) collective-permute-start(f32[2,16,256]{2,1,0:T(8,128)} %shard_map.68), channel_id=1, source_target_pairs={{8,0},{16,8},{24,16},{32,24},{40,32},{48,40},{56,48},{64,56},{72,6... | collective-permute-start | bytes 98312 | tf_op jit(solution)/shard_map/ppermute | solution.py:232
  64.8 3.5 %collective-permute-done.5 = f32[2,16,256]{2,1,0:T(8,128)S(1)} collective-permute-done((f32[2,16,256]{2,1,0:T(8,128)}, f32[2,16,256]{2,1,0:T(8,128)S(1)}, u32[]{:S(2)}, u32[]{:S(2)}) %collective-permute-start.5) | collective-permute-done | bytes 32800 | tf_op jit(solution)/shard_map/ppermute | solution.py:232
  68.3 0.8 fusion.29
  69.1 4.0 %collective-permute-start.6 = (f32[3,2,16,256]{3,2,1,0:T(8,128)S(1)}, f32[3,2,16,256]{3,2,1,0:T(8,128)S(1)}, u32[]{:S(2)}, u32[]{:S(2)}) collective-permute-start(f32[3,2,16,256]{3,2,1,0:T(8,128)S(1)} %get-tuple-element.11), channel_id=1, source_target_pairs={{0,1},{1,2},{2,3},{3,4},{4,5},{5,6},{6,7},{8,9},{9,10},{10,11},{11... | collective-permute-start | bytes 294920 | tf_op jit(solution)/shard_map/ppermute | solution.py:232
  73.1 1.3 collective-permute-start.7
  74.4 0.6 fusion.20
  75.0 5.3 %collective-permute-done.7 = f32[3,2,16,256]{3,2,1,0:T(8,128)S(1)} collective-permute-done((f32[3,2,16,256]{3,2,1,0:T(8,128)S(1)}, f32[3,2,16,256]{3,2,1,0:T(8,128)S(1)}, u32[]{:S(2)}, u32[]{:S(2)}) %collective-permute-start.7) | collective-permute-done | bytes 98336 | tf_op jit(solution)/shard_map/ppermute | solution.py:232
  80.4 0.7 concatenate.22.src_ref
  81.1 2.3 %shard_map.69 = f32[2,16,256]{2,1,0:T(8,128)} custom-call(s32[54]{0:T(128)} %reshape.67.tab_ref, f32[19,16,256]{2,1,0:T(8,128)} %concatenate.22.src_ref, f32[2,16,256]{2,1,0:T(8,128)} %bitcast.82), custom_call_target="tpu_custom_call" | custom-call | flops 491520 | bytes 377048 | tf_op jit(solution)/shard_map/pallas_call | solution.py:220
  83.4 3.6 %collective-permute-start.8 = (f32[2,16,256]{2,1,0:T(8,128)}, f32[2,16,256]{2,1,0:T(8,128)S(1)}, u32[]{:S(2)}, u32[]{:S(2)}) collective-permute-start(f32[2,16,256]{2,1,0:T(8,128)} %shard_map.69), channel_id=1, source_target_pairs={{0,8},{8,16},{16,24},{24,32},{32,40},{40,48},{48,56},{56,64},{64,7... | collective-permute-start | bytes 98312 | tf_op jit(solution)/shard_map/ppermute | solution.py:232
  87.0 1.9 %collective-permute-start.9 = (f32[2,16,256]{2,1,0:T(8,128)}, f32[2,16,256]{2,1,0:T(8,128)S(1)}, u32[]{:S(2)}, u32[]{:S(2)}) collective-permute-start(f32[2,16,256]{2,1,0:T(8,128)} %shard_map.69), channel_id=1, source_target_pairs={{8,0},{16,8},{24,16},{32,24},{40,32},{48,40},{56,48},{64,56},{72,6... | collective-permute-start | bytes 98312 | tf_op jit(solution)/shard_map/ppermute | solution.py:232
  88.9 3.5 %collective-permute-done.9 = f32[2,16,256]{2,1,0:T(8,128)S(1)} collective-permute-done((f32[2,16,256]{2,1,0:T(8,128)}, f32[2,16,256]{2,1,0:T(8,128)S(1)}, u32[]{:S(2)}, u32[]{:S(2)}) %collective-permute-start.9) | collective-permute-done | bytes 32800 | tf_op jit(solution)/shard_map/ppermute | solution.py:232
  92.5 0.8 fusion.28
  93.2 5.1 %collective-permute-start.10 = (f32[3,2,16,256]{3,2,1,0:T(8,128)S(1)}, f32[3,2,16,256]{3,2,1,0:T(8,128)S(1)}, u32[]{:S(2)}, u32[]{:S(2)}) collective-permute-start(f32[3,2,16,256]{3,2,1,0:T(8,128)S(1)} %get-tuple-element.9), channel_id=1, source_target_pairs={{0,1},{1,2},{2,3},{3,4},{4,5},{5,6},{6,7},{8,9},{9,10},{10,11},{11... | collective-permute-start | bytes 294920 | tf_op jit(solution)/shard_map/ppermute | solution.py:232
  98.3 1.3 collective-permute-start.11
  99.6 0.3 collective-permute-done.10
  99.9 3.7 %collective-permute-done.11 = f32[3,2,16,256]{3,2,1,0:T(8,128)S(1)} collective-permute-done((f32[3,2,16,256]{3,2,1,0:T(8,128)S(1)}, f32[3,2,16,256]{3,2,1,0:T(8,128)S(1)}, u32[]{:S(2)}, u32[]{:S(2)}) %collective-permute-start.11) | collective-permute-done | bytes 98336 | tf_op jit(solution)/shard_map/ppermute | solution.py:232
  103.7 0.7 concatenate.23.src_ref
  104.5 2.3 %shard_map.70 = f32[2,16,256]{2,1,0:T(8,128)} custom-call(s32[54]{0:T(128)} %reshape.67.tab_ref, f32[19,16,256]{2,1,0:T(8,128)} %concatenate.23.src_ref, f32[2,16,256]{2,1,0:T(8,128)} %bitcast.83), custom_call_target="tpu_custom_call" | custom-call | flops 491520 | bytes 377048 | tf_op jit(solution)/shard_map/pallas_call | solution.py:220
  106.8 0.8 multiply_subtract_fusion.1
  107.6 3.4 %collective-permute-start.12 = (f32[2,16,256]{2,1,0:T(8,128)S(1)}, f32[2,16,256]{2,1,0:T(8,128)S(1)}, u32[]{:S(2)}, u32[]{:S(2)}) collective-permute-start(f32[2,16,256]{2,1,0:T(8,128)S(1)} %multiply_subtract_fusion.1), channel_id=1, source_target_pairs={{0,8},{8,16},{16,24},{24,32},{32,40},{40,48},{48,56},{56,64},{64,7... | collective-permute-start | bytes 98312 | tf_op jit(solution)/shard_map/ppermute | solution.py:232
  111.0 1.9 %collective-permute-start.13 = (f32[2,16,256]{2,1,0:T(8,128)S(1)}, f32[2,16,256]{2,1,0:T(8,128)S(1)}, u32[]{:S(2)}, u32[]{:S(2)}) collective-permute-start(f32[2,16,256]{2,1,0:T(8,128)S(1)} %multiply_subtract_fusion.1), channel_id=1, source_target_pairs={{8,0},{16,8},{24,16},{32,24},{40,32},{48,40},{56,48},{64,56},{72,6... | collective-permute-start | bytes 98312 | tf_op jit(solution)/shard_map/ppermute | solution.py:232
  112.9 3.3 %collective-permute-done.13 = f32[2,16,256]{2,1,0:T(8,128)S(1)} collective-permute-done((f32[2,16,256]{2,1,0:T(8,128)S(1)}, f32[2,16,256]{2,1,0:T(8,128)S(1)}, u32[]{:S(2)}, u32[]{:S(2)}) %collective-permute-start.13) | collective-permute-done | bytes 32800 | tf_op jit(solution)/shard_map/ppermute | solution.py:232
  116.3 3.4 %collective-permute-start.14 = (f32[3,2,16,256]{3,2,1,0:T(8,128)S(1)}, f32[3,2,16,256]{3,2,1,0:T(8,128)S(1)}, u32[]{:S(2)}, u32[]{:S(2)}) collective-permute-start(f32[3,2,16,256]{3,2,1,0:T(8,128)S(1)} %get-tuple-element.7), channel_id=1, source_target_pairs={{0,1},{1,2},{2,3},{3,4},{4,5},{5,6},{6,7},{8,9},{9,10},{10,11},{11... | collective-permute-start | bytes 294920 | tf_op jit(solution)/shard_map/ppermute | solution.py:232
  119.6 1.5 collective-permute-start.15
  121.1 0.1 collective-permute-done.14
  121.2 3.7 %collective-permute-done.15 = f32[3,2,16,256]{3,2,1,0:T(8,128)S(1)} collective-permute-done((f32[3,2,16,256]{3,2,1,0:T(8,128)S(1)}, f32[3,2,16,256]{3,2,1,0:T(8,128)S(1)}, u32[]{:S(2)}, u32[]{:S(2)}) %collective-permute-start.15) | collective-permute-done | bytes 98336 | tf_op jit(solution)/shard_map/ppermute | solution.py:232
  125.0 0.7 concatenate.24.src_ref
  125.8 2.4 %shard_map.71 = f32[2,16,256]{2,1,0:T(8,128)} custom-call(s32[54]{0:T(128)} %reshape.67.tab_ref, f32[19,16,256]{2,1,0:T(8,128)} %concatenate.24.src_ref, f32[2,16,256]{2,1,0:T(8,128)} %bitcast.84), custom_call_target="tpu_custom_call" | custom-call | flops 491520 | bytes 377048 | tf_op jit(solution)/shard_map/pallas_call | solution.py:220
  128.1 0.8 multiply_subtract_fusion
  129.0 0.7 pad_maximum_fusion.5.basis_ref
  129.6 2.2 %shard_map.72 = f32[8,128]{1,0:T(8,128)} custom-call(f32[4,32,256]{2,1,0:T(8,128)} %pad_maximum_fusion.5.basis_ref), custom_call_target="tpu_custom_call" | custom-call | tf_op jit(solution)/shard_map/pallas_call | solution.py:293
  131.9 0.7 slice.53
  132.7 0.1 broadcast_in_dim.13
  132.8 36.9 %all_to_all.15 = f32[512,1,32]{2,1,0:T(1,128)S(1)} all-to-all(f32[512,1,32]{2,1,0:T(1,128)S(1)} %broadcast_in_dim.13), channel_id=1, replica_groups=mesh['wide'=64,'narrow'=8] {'wide','narrow'}, dimensions={0} | all-to-all | bytes 131072 | tf_op jit(solution)/shard_map/all_to_all | solution.py:297
  169.7 0.7 copy.30
  170.5 2.1 %shard_map.73 = f32[8,128]{1,0:T(8,128)} custom-call(f32[32,512]{1,0:T(8,128)} %bitcast.94), custom_call_target="tpu_custom_call" | custom-call | tf_op jit(solution)/shard_map/pallas_call | solution.py:298
  172.5 1.6 fusion.32
  174.1 4.4 %multiply_add_fusion = (f32[2,16,256]{2,1,0:T(8,128)S(1)}, f32[2,16,256]{2,1,0:T(8,128)S(1)}) fusion(f32[2,16,256]{2,1,0:T(8,128)S(1)} %multiply_subtract_fusion.1, f32[2,16,256]{2,1,0:T(8,128)S(1)} %copy-done.1, f32[2,16,256]{2,1,0:T(8,128)S(1)} %copy-done, f32[]{:T(128)} %bitcast.55, f32[]{:T(128)} %bitcast.54, f32[]{:T(128)} %bitcast.53, f32[]{:T(128)} %bitcast.52, ...), kind=kLoop, calls=%fused_computation.36 | loop fusion | flops 114688 | bytes 196636 | tf_op jit(solution)/shard_map/add | solution.py:311
  178.5 0.6 reshape.74
  179.2 0.6 reshape.75
  (36 shorter events, 0.5 us)
Async XLA Ops:
  0.6 1.4 copy-start.3
  0.6 2.1 %copy-start.4 = (s32[1024]{0:T(1024)S(1)}, s32[1024]{0:T(1024)}, u32[]{:S(2)}) copy-start(s32[1024]{0:T(1024)} %param.6) | copy-start | bytes 12292
  0.6 2.1 %copy-start.5 = (f32[3,1024]{1,0:T(4,128)S(1)}, f32[3,1024]{1,0:T(4,128)}, u32[]{:S(2)}) copy-start(f32[3,1024]{1,0:T(4,128)} %param.7) | copy-start | bytes 36868
  32.9 14.1 %copy-start.6 = (s32[1,1,2,27]{3,2,1,0:T(2,128)S(1)}, s32[1,1,2,27]{3,2,1,0:T(2,128)}, u32[]{:S(2)}) copy-start(s32[1,1,2,27]{3,2,1,0:T(2,128)} %param.9) | copy-start | bytes 652
  33.0 4.7 %collective-permute-start = (f32[3,2,16,256]{3,2,1,0:T(8,128)S(1)}, f32[3,2,16,256]{3,2,1,0:T(8,128)S(1)}, u32[]{:S(2)}, u32[]{:S(2)}) collective-permute-start(f32[3,2,16,256]{3,2,1,0:T(8,128)S(1)} %bitcast.89), channel_id=1, source_target_pairs={{0,8},{8,16},{16,24},{24,32},{32,40},{40,48},{48,56},{56,64},{64,7... | collective-permute-start | bytes 294920 | tf_op jit(solution)/shard_map/ppermute | solution.py:232
  35.7 5.9 %collective-permute-start.1 = (f32[3,2,16,256]{3,2,1,0:T(8,128)S(1)}, f32[3,2,16,256]{3,2,1,0:T(8,128)S(1)}, u32[]{:S(2)}, u32[]{:S(2)}) collective-permute-start(f32[3,2,16,256]{3,2,1,0:T(8,128)S(1)} %bitcast.90), channel_id=1, source_target_pairs={{8,0},{16,8},{24,16},{32,24},{40,32},{48,40},{56,48},{64,56},{72,6... | collective-permute-start | bytes 294920 | tf_op jit(solution)/shard_map/ppermute | solution.py:232
  41.7 8.5 %collective-permute-start.2 = (f32[3,3,2,16,256]{4,3,2,1,0:T(8,128)S(1)}, f32[3,3,2,16,256]{4,3,2,1,0:T(8,128)S(1)}, u32[]{:S(2)}, u32[]{:S(2)}) collective-permute-start(f32[3,3,2,16,256]{4,3,2,1,0:T(8,128)S(1)} %get-tuple-element.3), channel_id=1, source_target_pairs={{0,1},{1,2},{2,3},{3,4},{4,5},{5,6},{6,7},{8,9},{9,10},{10,11},{11... | collective-permute-start | bytes 884744 | tf_op jit(solution)/shard_map/ppermute | solution.py:232
  45.7 9.0 %collective-permute-start.3 = (f32[3,3,2,16,256]{4,3,2,1,0:T(8,128)S(1)}, f32[3,3,2,16,256]{4,3,2,1,0:T(8,128)S(1)}, u32[]{:S(2)}, u32[]{:S(2)}) collective-permute-start(f32[3,3,2,16,256]{4,3,2,1,0:T(8,128)S(1)} %get-tuple-element.3), channel_id=1, source_target_pairs={{1,0},{2,1},{3,2},{4,3},{5,4},{6,5},{7,6},{9,8},{10,9},{11,10},{12... | collective-permute-start | bytes 884744 | tf_op jit(solution)/shard_map/ppermute | solution.py:232
  57.8 7.0 %collective-permute-start.4 = (f32[2,16,256]{2,1,0:T(8,128)}, f32[2,16,256]{2,1,0:T(8,128)S(1)}, u32[]{:S(2)}, u32[]{:S(2)}) collective-permute-start(f32[2,16,256]{2,1,0:T(8,128)} %shard_map.68), channel_id=1, source_target_pairs={{0,8},{8,16},{16,24},{24,32},{32,40},{40,48},{48,56},{56,64},{64,7... | collective-permute-start | bytes 98312 | tf_op jit(solution)/shard_map/ppermute | solution.py:232
  62.9 5.4 %collective-permute-start.5 = (f32[2,16,256]{2,1,0:T(8,128)}, f32[2,16,256]{2,1,0:T(8,128)S(1)}, u32[]{:S(2)}, u32[]{:S(2)}) collective-permute-start(f32[2,16,256]{2,1,0:T(8,128)} %shard_map.68), channel_id=1, source_target_pairs={{8,0},{16,8},{24,16},{32,24},{40,32},{48,40},{56,48},{64,56},{72,6... | collective-permute-start | bytes 98312 | tf_op jit(solution)/shard_map/ppermute | solution.py:232
  69.1 5.9 %collective-permute-start.6 = (f32[3,2,16,256]{3,2,1,0:T(8,128)S(1)}, f32[3,2,16,256]{3,2,1,0:T(8,128)S(1)}, u32[]{:S(2)}, u32[]{:S(2)}) collective-permute-start(f32[3,2,16,256]{3,2,1,0:T(8,128)S(1)} %get-tuple-element.11), channel_id=1, source_target_pairs={{0,1},{1,2},{2,3},{3,4},{4,5},{5,6},{6,7},{8,9},{9,10},{10,11},{11... | collective-permute-start | bytes 294920 | tf_op jit(solution)/shard_map/ppermute | solution.py:232
  73.1 7.2 %collective-permute-start.7 = (f32[3,2,16,256]{3,2,1,0:T(8,128)S(1)}, f32[3,2,16,256]{3,2,1,0:T(8,128)S(1)}, u32[]{:S(2)}, u32[]{:S(2)}) collective-permute-start(f32[3,2,16,256]{3,2,1,0:T(8,128)S(1)} %get-tuple-element.11), channel_id=1, source_target_pairs={{1,0},{2,1},{3,2},{4,3},{5,4},{6,5},{7,6},{9,8},{10,9},{11,10},{12... | collective-permute-start | bytes 294920 | tf_op jit(solution)/shard_map/ppermute | solution.py:232
  83.4 5.5 %collective-permute-start.8 = (f32[2,16,256]{2,1,0:T(8,128)}, f32[2,16,256]{2,1,0:T(8,128)S(1)}, u32[]{:S(2)}, u32[]{:S(2)}) collective-permute-start(f32[2,16,256]{2,1,0:T(8,128)} %shard_map.69), channel_id=1, source_target_pairs={{0,8},{8,16},{16,24},{24,32},{32,40},{40,48},{48,56},{56,64},{64,7... | collective-permute-start | bytes 98312 | tf_op jit(solution)/shard_map/ppermute | solution.py:232
  87.0 5.4 %collective-permute-start.9 = (f32[2,16,256]{2,1,0:T(8,128)}, f32[2,16,256]{2,1,0:T(8,128)S(1)}, u32[]{:S(2)}, u32[]{:S(2)}) collective-permute-start(f32[2,16,256]{2,1,0:T(8,128)} %shard_map.69), channel_id=1, source_target_pairs={{8,0},{16,8},{24,16},{32,24},{40,32},{48,40},{56,48},{64,56},{72,6... | collective-permute-start | bytes 98312 | tf_op jit(solution)/shard_map/ppermute | solution.py:232
  93.2 6.7 %collective-permute-start.10 = (f32[3,2,16,256]{3,2,1,0:T(8,128)S(1)}, f32[3,2,16,256]{3,2,1,0:T(8,128)S(1)}, u32[]{:S(2)}, u32[]{:S(2)}) collective-permute-start(f32[3,2,16,256]{3,2,1,0:T(8,128)S(1)} %get-tuple-element.9), channel_id=1, source_target_pairs={{0,1},{1,2},{2,3},{3,4},{4,5},{5,6},{6,7},{8,9},{9,10},{10,11},{11... | collective-permute-start | bytes 294920 | tf_op jit(solution)/shard_map/ppermute | solution.py:232
  98.3 5.4 %collective-permute-start.11 = (f32[3,2,16,256]{3,2,1,0:T(8,128)S(1)}, f32[3,2,16,256]{3,2,1,0:T(8,128)S(1)}, u32[]{:S(2)}, u32[]{:S(2)}) collective-permute-start(f32[3,2,16,256]{3,2,1,0:T(8,128)S(1)} %get-tuple-element.9), channel_id=1, source_target_pairs={{1,0},{2,1},{3,2},{4,3},{5,4},{6,5},{7,6},{9,8},{10,9},{11,10},{12... | collective-permute-start | bytes 294920 | tf_op jit(solution)/shard_map/ppermute | solution.py:232
  103.7 3.1 %copy-start = (f32[2,16,256]{2,1,0:T(8,128)S(1)}, f32[2,16,256]{2,1,0:T(8,128)}, u32[]{:S(2)}) copy-start(f32[2,16,256]{2,1,0:T(8,128)} %shard_map.68) | copy-start | bytes 98308
  107.6 5.4 %collective-permute-start.12 = (f32[2,16,256]{2,1,0:T(8,128)S(1)}, f32[2,16,256]{2,1,0:T(8,128)S(1)}, u32[]{:S(2)}, u32[]{:S(2)}) collective-permute-start(f32[2,16,256]{2,1,0:T(8,128)S(1)} %multiply_subtract_fusion.1), channel_id=1, source_target_pairs={{0,8},{8,16},{16,24},{24,32},{32,40},{40,48},{48,56},{56,64},{64,7... | collective-permute-start | bytes 98312 | tf_op jit(solution)/shard_map/ppermute | solution.py:232
  111.0 5.2 %collective-permute-start.13 = (f32[2,16,256]{2,1,0:T(8,128)S(1)}, f32[2,16,256]{2,1,0:T(8,128)S(1)}, u32[]{:S(2)}, u32[]{:S(2)}) collective-permute-start(f32[2,16,256]{2,1,0:T(8,128)S(1)} %multiply_subtract_fusion.1), channel_id=1, source_target_pairs={{8,0},{16,8},{24,16},{32,24},{40,32},{48,40},{56,48},{64,56},{72,6... | collective-permute-start | bytes 98312 | tf_op jit(solution)/shard_map/ppermute | solution.py:232
  116.3 5.0 %collective-permute-start.14 = (f32[3,2,16,256]{3,2,1,0:T(8,128)S(1)}, f32[3,2,16,256]{3,2,1,0:T(8,128)S(1)}, u32[]{:S(2)}, u32[]{:S(2)}) collective-permute-start(f32[3,2,16,256]{3,2,1,0:T(8,128)S(1)} %get-tuple-element.7), channel_id=1, source_target_pairs={{0,1},{1,2},{2,3},{3,4},{4,5},{5,6},{6,7},{8,9},{9,10},{10,11},{11... | collective-permute-start | bytes 294920 | tf_op jit(solution)/shard_map/ppermute | solution.py:232
  119.6 5.4 %collective-permute-start.15 = (f32[3,2,16,256]{3,2,1,0:T(8,128)S(1)}, f32[3,2,16,256]{3,2,1,0:T(8,128)S(1)}, u32[]{:S(2)}, u32[]{:S(2)}) collective-permute-start(f32[3,2,16,256]{3,2,1,0:T(8,128)S(1)} %get-tuple-element.7), channel_id=1, source_target_pairs={{1,0},{2,1},{3,2},{4,3},{5,4},{6,5},{7,6},{9,8},{10,9},{11,10},{12... | collective-permute-start | bytes 294920 | tf_op jit(solution)/shard_map/ppermute | solution.py:232
  125.0 3.2 %copy-start.1 = (f32[2,16,256]{2,1,0:T(8,128)S(1)}, f32[2,16,256]{2,1,0:T(8,128)}, u32[]{:S(2)}) copy-start(f32[2,16,256]{2,1,0:T(8,128)} %shard_map.69) | copy-start | bytes 98308
  128.1 45.9 %copy-start.2 = (f32[2,16,256]{2,1,0:T(8,128)S(1)}, f32[2,16,256]{2,1,0:T(8,128)}, u32[]{:S(2)}) copy-start(f32[2,16,256]{2,1,0:T(8,128)} %shard_map.71) | copy-start | bytes 98308

commit v6 on v5

--- a/solution.py
+++ b/solution.py
@@ -94,7 +94,7 @@
     out_ref[...] = acc
 
 
-def _galerkin_kernel(parts_ref, out_ref, lift=None):
+def _galerkin_kernel(parts_ref, basis_ref, solution_ref, residual_ref, lift=None):
     half = parts_ref.shape[0] // 2
     s, e = _halve(parts_ref[0:half, :], parts_ref[half:, :], 1, 128)
     s, e = _spread(s, e, 1)
@@ -130,15 +130,24 @@
             acc = _dd_add(acc, (-p, -(pe + matrix[i][j][1] * coeff[j])))
         misfit.append(acc[0] + acc[1])
     coeff = [c + d for c, d in zip(coeff, _solve(top, misfit))]
-    values = list(coeff)
+    weights = []
     for k in range(size):
         terms = [lift[k][j] * coeff[j] for j in range(n) if lift[k][j] != 0.0]
-        values.append((1.0 if k == 0 else 0.0) - sum(terms[1:], terms[0]))
-    out_rows = lax.broadcasted_iota(jnp.int32, out_ref.shape, 0)
-    out = jnp.zeros(out_ref.shape, jnp.float32)
-    for k, v in enumerate(values):
-        out = jnp.where(out_rows == k, v, out)
-    out_ref[...] = out
+        weights.append((1.0 if k == 0 else 0.0) - sum(terms[1:], terms[0]))
+    shape = solution_ref.shape
+
+    def wide(v):
+        v = jnp.broadcast_to(v, (shape[0], v.shape[1]))
+        return jnp.concatenate([v] * (shape[1] // v.shape[1]), axis=1)
+
+    total = wide(coeff[0]) * basis_ref[0]
+    for j in range(1, n):
+        total = total + wide(coeff[j]) * basis_ref[j]
+    solution_ref[...] = total
+    total = wide(weights[0]) * basis_ref[0]
+    for k in range(1, size):
+        total = total + wide(weights[k]) * basis_ref[k]
+    residual_ref[...] = total
 
 
 def _masks():
@@ -295,20 +304,13 @@
     )(stacked)
     payload = partial_sums[0:2, 0:16].reshape(1, 32)
     gathered = lax.all_to_all(jnp.broadcast_to(payload, (devices, 32)), ("wide", "narrow"), 0, 0, tiled=True)
-    found = pl.pallas_call(
+    flat = jax.ShapeDtypeStruct((bricks * ROWS, LANES), jnp.float32)
+    solution, residual = pl.pallas_call(
         functools.partial(_galerkin_kernel, lift=lift),
-        out_shape=jax.ShapeDtypeStruct((8, 128), jnp.float32),
-        in_specs=[vmem],
-        out_specs=vmem,
-    )(jnp.pad(gathered.T, ((0, 0), (0, max(0, 128 - devices)))))
-    coeff = [found[k, 0] for k in range(ITERS)]
-    weights = [found[ITERS + k, 0] for k in range(ITERS + 1)]
-    solution = coeff[0] * basis[0]
-    for j in range(1, ITERS):
-        solution = solution + coeff[j] * basis[j]
-    residual = weights[0] * basis[0]
-    for k in range(1, ITERS + 1):
-        residual = residual + weights[k] * basis[k]
+        out_shape=(flat, flat),
+        in_specs=[vmem, vmem],
+        out_specs=(vmem, vmem),
+    )(jnp.pad(gathered.T, ((0, 0), (0, max(0, 128 - devices)))), stacked)
     out = (1, 1, bricks, ROWS * LANES)
     return solution.reshape(out), residual.reshape(out)
 

time: 181 us -> 177 us (0.978)
  other arithmetic: 11.3 us -> 6.76 us
    add x1 -> x0, other arithmetic: 4.44 us -> none  [shards(): residual = residual + weights[k] * basis[k]]
where the time goes in v6:
time: 177 us; the launch traced here: 175 us
  blocking collectives  57.7 us (33%)
  starting transfers between devices  44.3 us (25%)
  waiting for transfers between devices  34.6 us (20%)
  Pallas kernels  13.4 us (8%)
  local copies, waits for them, and re-layouts  9.57 us (5%)
  matrix products  7.35 us (4%)
  other arithmetic  6.76 us (4%)
    ppermute x16, starting transfers between devices, _shift(): return lax.ppermute(field, axis, pairs)  44.3 us
    all_to_all x1, blocking collectives, shards(): lax.all_to_all(jnp.broadcast_to(payload, (devices, 32)), ('wide', 'narrow...  36.9 us
    ppermute x16, waiting for transfers between devices, _shift(): return lax.ppermute(field, axis, pairs)  34.6 us
    all_to_all x1, blocking collectives, shards(): lax.all_to_all(send.reshape(owners, CAP, 4), 'wide', 0, 0, tiled=True)  20.8 us
    pallas_call x4, Pallas kernels, _local_call(): pl.pallas_call(kernel, out_shape=jax.ShapeDtypeStruct(out_shape, jnp.floa...  8.99 us
    dot_general x1, matrix products, shards(): jnp.dot(place_hot, payload, precision=HIGHEST, preferred_element_type=jnp...  3.74 us
  transfers between devices with their start and end apart: 16, of which 11 were waited for; matrix products, arithmetic and copies ran while one was open for 1% of the time, Pallas kernels for 0%

profile of v6, /device:TPU:1, one launch (start us, length us, event | category | flops | bytes accessed | tf_op | source)
XLA Modules:
  0.0 175.4 jit_solution(11277930791619361456)
XLA Ops:
  0.7 1.4 fusion.5
  2.7 3.7 %fusion = f32[2048,4]{0,1:T(4,128)S(1)} fusion(s32[1024]{0:T(1024)S(1)} %convert_add_fusion, f32[1024,3]{0,1:T(4,128)S(1)} %bitcast.112, f32[1024,1]{0,1:T(1,128)S(1)} %bitcast.111), kind=kOutput, calls=%fused_computation.1 | convolution fusion | flops 102764544 | bytes 53248 | tf_op jit(solution)/shard_map/dot_general | solution.py:271
  6.5 0.1 reshape.68
  6.6 0.1 copy.32
  6.7 0.1 reshape.76
  6.8 20.8 %all_to_all.14 = f32[64,1,128]{2,1,0:T(1,128)S(1)} all-to-all(f32[64,1,128]{2,1,0:T(1,128)S(1)} %reshape.76), channel_id=1, replica_groups=mesh['wide'=64,'narrow'=8] {'wide'}, dimensions={0} | all-to-all | bytes 65536 | tf_op jit(solution)/shard_map/all_to_all | solution.py:272
  27.6 0.5 broadcast.52
  28.1 0.7 reduce
  28.9 0.1 reshape.77
  29.0 0.1 reshape.69
  29.2 0.3 fusion.14
  29.5 1.1 fusion.17
  30.7 2.2 %fusion.3 = f32[128,256]{1,0:T(8,128)S(1)} fusion(f32[2048,32]{1,0:T(8,128)S(1)} %fusion.14, f32[2048,32]{1,0:T(8,128)S(1)} %get-tuple-element.20, f32[2048,32]{1,0:T(8,128)S(1)} %get-tuple-element.21, f32[2048,32]{1,0:T(8,128)S(1)} %get-tuple-element.19, s32[2048]{0:T(1024)S(1)} %bitcast.99), kind=kOutput, calls=%fused_computation.6 | convolution fusion | flops 806617088 | bytes 1187840 | tf_op jit(solution)/shard_map/pa,pb->ab/dot_general | solution.py:280
  33.0 2.8 %collective-permute-start = (f32[3,2,16,256]{3,2,1,0:T(8,128)S(1)}, f32[3,2,16,256]{3,2,1,0:T(8,128)S(1)}, u32[]{:S(2)}, u32[]{:S(2)}) collective-permute-start(f32[3,2,16,256]{3,2,1,0:T(8,128)S(1)} %bitcast.80), channel_id=1, source_target_pairs={{0,8},{8,16},{16,24},{24,32},{32,40},{40,48},{48,56},{56,64},{64,7... | collective-permute-start | bytes 294920 | tf_op jit(solution)/shard_map/ppermute | solution.py:241
  35.7 1.9 %collective-permute-start.1 = (f32[3,2,16,256]{3,2,1,0:T(8,128)S(1)}, f32[3,2,16,256]{3,2,1,0:T(8,128)S(1)}, u32[]{:S(2)}, u32[]{:S(2)}) collective-permute-start(f32[3,2,16,256]{3,2,1,0:T(8,128)S(1)} %bitcast.81), channel_id=1, source_target_pairs={{8,0},{16,8},{24,16},{32,24},{40,32},{48,40},{56,48},{64,56},{72,6... | collective-permute-start | bytes 294920 | tf_op jit(solution)/shard_map/ppermute | solution.py:241
  37.7 4.0 %collective-permute-done.1 = f32[3,2,16,256]{3,2,1,0:T(8,128)S(1)} collective-permute-done((f32[3,2,16,256]{3,2,1,0:T(8,128)S(1)}, f32[3,2,16,256]{3,2,1,0:T(8,128)S(1)}, u32[]{:S(2)}, u32[]{:S(2)}) %collective-permute-start.1) | collective-permute-done | bytes 98336 | tf_op jit(solution)/shard_map/ppermute | solution.py:241
  41.7 4.0 %collective-permute-start.2 = (f32[3,3,2,16,256]{4,3,2,1,0:T(8,128)S(1)}, f32[3,3,2,16,256]{4,3,2,1,0:T(8,128)S(1)}, u32[]{:S(2)}, u32[]{:S(2)}) collective-permute-start(f32[3,3,2,16,256]{4,3,2,1,0:T(8,128)S(1)} %get-tuple-element.7), channel_id=1, source_target_pairs={{0,1},{1,2},{2,3},{3,4},{4,5},{5,6},{6,7},{8,9},{9,10},{10,11},{11... | collective-permute-start | bytes 884744 | tf_op jit(solution)/shard_map/ppermute | solution.py:241
  45.7 1.3 collective-permute-start.3
  47.1 0.7 reshape.67.tab_ref
  47.7 2.6 %collective-permute-done.2 = f32[3,3,2,16,256]{4,3,2,1,0:T(8,128)S(1)} collective-permute-done((f32[3,3,2,16,256]{4,3,2,1,0:T(8,128)S(1)}, f32[3,3,2,16,256]{4,3,2,1,0:T(8,128)S(1)}, u32[]{:S(2)}, u32[]{:S(2)}) %collective-permute-start.2) | collective-permute-done | bytes 294944 | tf_op jit(solution)/shard_map/ppermute | solution.py:241
  50.3 4.5 %collective-permute-done.3 = f32[3,3,2,16,256]{4,3,2,1,0:T(8,128)S(1)} collective-permute-done((f32[3,3,2,16,256]{4,3,2,1,0:T(8,128)S(1)}, f32[3,3,2,16,256]{4,3,2,1,0:T(8,128)S(1)}, u32[]{:S(2)}, u32[]{:S(2)}) %collective-permute-start.3) | collective-permute-done | bytes 294944 | tf_op jit(solution)/shard_map/ppermute | solution.py:241
  54.8 1.0 concatenate.21.src_ref
  55.8 1.9 %shard_map.68 = f32[2,16,256]{2,1,0:T(8,128)} custom-call(s32[54]{0:T(128)} %reshape.67.tab_ref, f32[3,19,16,256]{3,2,1,0:T(8,128)} %concatenate.21.src_ref), custom_call_target="tpu_custom_call" | custom-call | flops 163840 | bytes 966872 | tf_op jit(solution)/shard_map/pallas_call | solution.py:229
  57.8 5.1 %collective-permute-start.4 = (f32[2,16,256]{2,1,0:T(8,128)}, f32[2,16,256]{2,1,0:T(8,128)S(1)}, u32[]{:S(2)}, u32[]{:S(2)}) collective-permute-start(f32[2,16,256]{2,1,0:T(8,128)} %shard_map.68), channel_id=1, source_target_pairs={{0,8},{8,16},{16,24},{24,32},{32,40},{40,48},{48,56},{56,64},{64,7... | collective-permute-start | bytes 98312 | tf_op jit(solution)/shard_map/ppermute | solution.py:241
  62.9 1.9 %collective-permute-start.5 = (f32[2,16,256]{2,1,0:T(8,128)}, f32[2,16,256]{2,1,0:T(8,128)S(1)}, u32[]{:S(2)}, u32[]{:S(2)}) collective-permute-start(f32[2,16,256]{2,1,0:T(8,128)} %shard_map.68), channel_id=1, source_target_pairs={{8,0},{16,8},{24,16},{32,24},{40,32},{48,40},{56,48},{64,56},{72,6... | collective-permute-start | bytes 98312 | tf_op jit(solution)/shard_map/ppermute | solution.py:241
  64.8 3.5 %collective-permute-done.5 = f32[2,16,256]{2,1,0:T(8,128)S(1)} collective-permute-done((f32[2,16,256]{2,1,0:T(8,128)}, f32[2,16,256]{2,1,0:T(8,128)S(1)}, u32[]{:S(2)}, u32[]{:S(2)}) %collective-permute-start.5) | collective-permute-done | bytes 32800 | tf_op jit(solution)/shard_map/ppermute | solution.py:241
  68.3 0.8 fusion.29
  69.1 4.0 %collective-permute-start.6 = (f32[3,2,16,256]{3,2,1,0:T(8,128)S(1)}, f32[3,2,16,256]{3,2,1,0:T(8,128)S(1)}, u32[]{:S(2)}, u32[]{:S(2)}) collective-permute-start(f32[3,2,16,256]{3,2,1,0:T(8,128)S(1)} %get-tuple-element.13), channel_id=1, source_target_pairs={{0,1},{1,2},{2,3},{3,4},{4,5},{5,6},{6,7},{8,9},{9,10},{10,11},{11... | collective-permute-start | bytes 294920 | tf_op jit(solution)/shard_map/ppermute | solution.py:241
  73.1 1.3 collective-permute-start.7
  74.4 0.6 fusion.20
  75.0 5.3 %collective-permute-done.7 = f32[3,2,16,256]{3,2,1,0:T(8,128)S(1)} collective-permute-done((f32[3,2,16,256]{3,2,1,0:T(8,128)S(1)}, f32[3,2,16,256]{3,2,1,0:T(8,128)S(1)}, u32[]{:S(2)}, u32[]{:S(2)}) %collective-permute-start.7) | collective-permute-done | bytes 98336 | tf_op jit(solution)/shard_map/ppermute | solution.py:241
  80.4 0.7 concatenate.22.src_ref
  81.1 2.3 %shard_map.69 = f32[2,16,256]{2,1,0:T(8,128)} custom-call(s32[54]{0:T(128)} %reshape.67.tab_ref, f32[19,16,256]{2,1,0:T(8,128)} %concatenate.22.src_ref, f32[2,16,256]{2,1,0:T(8,128)} %bitcast.71), custom_call_target="tpu_custom_call" | custom-call | flops 491520 | bytes 377048 | tf_op jit(solution)/shard_map/pallas_call | solution.py:229
  83.4 3.6 %collective-permute-start.8 = (f32[2,16,256]{2,1,0:T(8,128)}, f32[2,16,256]{2,1,0:T(8,128)S(1)}, u32[]{:S(2)}, u32[]{:S(2)}) collective-permute-start(f32[2,16,256]{2,1,0:T(8,128)} %shard_map.69), channel_id=1, source_target_pairs={{0,8},{8,16},{16,24},{24,32},{32,40},{40,48},{48,56},{56,64},{64,7... | collective-permute-start | bytes 98312 | tf_op jit(solution)/shard_map/ppermute | solution.py:241
  87.0 1.9 %collective-permute-start.9 = (f32[2,16,256]{2,1,0:T(8,128)}, f32[2,16,256]{2,1,0:T(8,128)S(1)}, u32[]{:S(2)}, u32[]{:S(2)}) collective-permute-start(f32[2,16,256]{2,1,0:T(8,128)} %shard_map.69), channel_id=1, source_target_pairs={{8,0},{16,8},{24,16},{32,24},{40,32},{48,40},{56,48},{64,56},{72,6... | collective-permute-start | bytes 98312 | tf_op jit(solution)/shard_map/ppermute | solution.py:241
  89.0 3.5 %collective-permute-done.9 = f32[2,16,256]{2,1,0:T(8,128)S(1)} collective-permute-done((f32[2,16,256]{2,1,0:T(8,128)}, f32[2,16,256]{2,1,0:T(8,128)S(1)}, u32[]{:S(2)}, u32[]{:S(2)}) %collective-permute-start.9) | collective-permute-done | bytes 32800 | tf_op jit(solution)/shard_map/ppermute | solution.py:241
  92.5 0.8 fusion.28
  93.2 5.1 %collective-permute-start.10 = (f32[3,2,16,256]{3,2,1,0:T(8,128)S(1)}, f32[3,2,16,256]{3,2,1,0:T(8,128)S(1)}, u32[]{:S(2)}, u32[]{:S(2)}) collective-permute-start(f32[3,2,16,256]{3,2,1,0:T(8,128)S(1)} %get-tuple-element.11), channel_id=1, source_target_pairs={{0,1},{1,2},{2,3},{3,4},{4,5},{5,6},{6,7},{8,9},{9,10},{10,11},{11... | collective-permute-start | bytes 294920 | tf_op jit(solution)/shard_map/ppermute | solution.py:241
  98.3 1.3 collective-permute-start.11
  99.6 0.3 collective-permute-done.10
  99.9 3.7 %collective-permute-done.11 = f32[3,2,16,256]{3,2,1,0:T(8,128)S(1)} collective-permute-done((f32[3,2,16,256]{3,2,1,0:T(8,128)S(1)}, f32[3,2,16,256]{3,2,1,0:T(8,128)S(1)}, u32[]{:S(2)}, u32[]{:S(2)}) %collective-permute-start.11) | collective-permute-done | bytes 98336 | tf_op jit(solution)/shard_map/ppermute | solution.py:241
  103.7 0.7 concatenate.23.src_ref
  104.5 2.3 %shard_map.70 = f32[2,16,256]{2,1,0:T(8,128)} custom-call(s32[54]{0:T(128)} %reshape.67.tab_ref, f32[19,16,256]{2,1,0:T(8,128)} %concatenate.23.src_ref, f32[2,16,256]{2,1,0:T(8,128)} %bitcast.72), custom_call_target="tpu_custom_call" | custom-call | flops 491520 | bytes 377048 | tf_op jit(solution)/shard_map/pallas_call | solution.py:229
  106.8 0.8 multiply_subtract_fusion.1
  107.6 3.4 %collective-permute-start.12 = (f32[2,16,256]{2,1,0:T(8,128)S(1)}, f32[2,16,256]{2,1,0:T(8,128)S(1)}, u32[]{:S(2)}, u32[]{:S(2)}) collective-permute-start(f32[2,16,256]{2,1,0:T(8,128)S(1)} %multiply_subtract_fusion.1), channel_id=1, source_target_pairs={{0,8},{8,16},{16,24},{24,32},{32,40},{40,48},{48,56},{56,64},{64,7... | collective-permute-start | bytes 98312 | tf_op jit(solution)/shard_map/ppermute | solution.py:241
  111.0 1.9 %collective-permute-start.13 = (f32[2,16,256]{2,1,0:T(8,128)S(1)}, f32[2,16,256]{2,1,0:T(8,128)S(1)}, u32[]{:S(2)}, u32[]{:S(2)}) collective-permute-start(f32[2,16,256]{2,1,0:T(8,128)S(1)} %multiply_subtract_fusion.1), channel_id=1, source_target_pairs={{8,0},{16,8},{24,16},{32,24},{40,32},{48,40},{56,48},{64,56},{72,6... | collective-permute-start | bytes 98312 | tf_op jit(solution)/shard_map/ppermute | solution.py:241
  113.0 3.3 %collective-permute-done.13 = f32[2,16,256]{2,1,0:T(8,128)S(1)} collective-permute-done((f32[2,16,256]{2,1,0:T(8,128)S(1)}, f32[2,16,256]{2,1,0:T(8,128)S(1)}, u32[]{:S(2)}, u32[]{:S(2)}) %collective-permute-start.13) | collective-permute-done | bytes 32800 | tf_op jit(solution)/shard_map/ppermute | solution.py:241
  116.3 3.4 %collective-permute-start.14 = (f32[3,2,16,256]{3,2,1,0:T(8,128)S(1)}, f32[3,2,16,256]{3,2,1,0:T(8,128)S(1)}, u32[]{:S(2)}, u32[]{:S(2)}) collective-permute-start(f32[3,2,16,256]{3,2,1,0:T(8,128)S(1)} %get-tuple-element.9), channel_id=1, source_target_pairs={{0,1},{1,2},{2,3},{3,4},{4,5},{5,6},{6,7},{8,9},{9,10},{10,11},{11... | collective-permute-start | bytes 294920 | tf_op jit(solution)/shard_map/ppermute | solution.py:241
  119.6 1.5 collective-permute-start.15
  121.1 0.1 collective-permute-done.14
  121.3 3.7 %collective-permute-done.15 = f32[3,2,16,256]{3,2,1,0:T(8,128)S(1)} collective-permute-done((f32[3,2,16,256]{3,2,1,0:T(8,128)S(1)}, f32[3,2,16,256]{3,2,1,0:T(8,128)S(1)}, u32[]{:S(2)}, u32[]{:S(2)}) %collective-permute-start.15) | collective-permute-done | bytes 98336 | tf_op jit(solution)/shard_map/ppermute | solution.py:241
  125.0 0.7 concatenate.24.src_ref
  125.8 2.4 %shard_map.71 = f32[2,16,256]{2,1,0:T(8,128)} custom-call(s32[54]{0:T(128)} %reshape.67.tab_ref, f32[19,16,256]{2,1,0:T(8,128)} %concatenate.24.src_ref, f32[2,16,256]{2,1,0:T(8,128)} %bitcast.73), custom_call_target="tpu_custom_call" | custom-call | flops 491520 | bytes 377048 | tf_op jit(solution)/shard_map/pallas_call | solution.py:229
  128.1 0.8 multiply_subtract_fusion
  128.9 0.6 pad_maximum_fusion.5.basis_ref
  129.6 2.2 %shard_map.72 = f32[8,128]{1,0:T(8,128)} custom-call(f32[4,32,256]{2,1,0:T(8,128)} %pad_maximum_fusion.5.basis_ref), custom_call_target="tpu_custom_call" | custom-call | tf_op jit(solution)/shard_map/pallas_call | solution.py:302
  131.8 0.7 slice.32
  132.5 0.1 broadcast_in_dim.12
  132.6 0.1 broadcast_in_dim.13
  132.7 36.9 %all_to_all.15 = f32[512,1,32]{2,1,0:T(1,128)S(1)} all-to-all(f32[512,1,32]{2,1,0:T(1,128)S(1)} %broadcast_in_dim.13), channel_id=1, replica_groups=mesh['wide'=64,'narrow'=8] {'wide','narrow'}, dimensions={0} | all-to-all | bytes 131072 | tf_op jit(solution)/shard_map/all_to_all | solution.py:306
  169.7 0.7 copy.30
  170.4 2.2 %shard_map.73 = (f32[32,256]{1,0:T(8,128)}, f32[32,256]{1,0:T(8,128)}) custom-call(f32[32,512]{1,0:T(8,128)} %bitcast.87, f32[4,32,256]{2,1,0:T(8,128)} %pad_maximum_fusion.5.basis_ref), custom_call_target="tpu_custom_call" | custom-call | tf_op jit(solution)/shard_map/pallas_call | solution.py:308
  172.6 1.4 reshape.74
  174.0 1.4 reshape.75
  (32 shorter events, 0.4 us)
Async XLA Ops:
  0.6 1.4 copy-start.2
  0.6 2.1 %copy-start.3 = (s32[1024]{0:T(1024)S(1)}, s32[1024]{0:T(1024)}, u32[]{:S(2)}) copy-start(s32[1024]{0:T(1024)} %param.6) | copy-start | bytes 12292
  0.6 2.1 %copy-start.4 = (f32[3,1024]{1,0:T(4,128)S(1)}, f32[3,1024]{1,0:T(4,128)}, u32[]{:S(2)}) copy-start(f32[3,1024]{1,0:T(4,128)} %param.7) | copy-start | bytes 36868
  32.9 14.1 %copy-start.5 = (s32[1,1,2,27]{3,2,1,0:T(2,128)S(1)}, s32[1,1,2,27]{3,2,1,0:T(2,128)}, u32[]{:S(2)}) copy-start(s32[1,1,2,27]{3,2,1,0:T(2,128)} %param.9) | copy-start | bytes 652
  33.0 4.7 %collective-permute-start = (f32[3,2,16,256]{3,2,1,0:T(8,128)S(1)}, f32[3,2,16,256]{3,2,1,0:T(8,128)S(1)}, u32[]{:S(2)}, u32[]{:S(2)}) collective-permute-start(f32[3,2,16,256]{3,2,1,0:T(8,128)S(1)} %bitcast.80), channel_id=1, source_target_pairs={{0,8},{8,16},{16,24},{24,32},{32,40},{40,48},{48,56},{56,64},{64,7... | collective-permute-start | bytes 294920 | tf_op jit(solution)/shard_map/ppermute | solution.py:241
  35.7 5.9 %collective-permute-start.1 = (f32[3,2,16,256]{3,2,1,0:T(8,128)S(1)}, f32[3,2,16,256]{3,2,1,0:T(8,128)S(1)}, u32[]{:S(2)}, u32[]{:S(2)}) collective-permute-start(f32[3,2,16,256]{3,2,1,0:T(8,128)S(1)} %bitcast.81), channel_id=1, source_target_pairs={{8,0},{16,8},{24,16},{32,24},{40,32},{48,40},{56,48},{64,56},{72,6... | collective-permute-start | bytes 294920 | tf_op jit(solution)/shard_map/ppermute | solution.py:241
  41.7 8.5 %collective-permute-start.2 = (f32[3,3,2,16,256]{4,3,2,1,0:T(8,128)S(1)}, f32[3,3,2,16,256]{4,3,2,1,0:T(8,128)S(1)}, u32[]{:S(2)}, u32[]{:S(2)}) collective-permute-start(f32[3,3,2,16,256]{4,3,2,1,0:T(8,128)S(1)} %get-tuple-element.7), channel_id=1, source_target_pairs={{0,1},{1,2},{2,3},{3,4},{4,5},{5,6},{6,7},{8,9},{9,10},{10,11},{11... | collective-permute-start | bytes 884744 | tf_op jit(solution)/shard_map/ppermute | solution.py:241
  45.7 9.0 %collective-permute-start.3 = (f32[3,3,2,16,256]{4,3,2,1,0:T(8,128)S(1)}, f32[3,3,2,16,256]{4,3,2,1,0:T(8,128)S(1)}, u32[]{:S(2)}, u32[]{:S(2)}) collective-permute-start(f32[3,3,2,16,256]{4,3,2,1,0:T(8,128)S(1)} %get-tuple-element.7), channel_id=1, source_target_pairs={{1,0},{2,1},{3,2},{4,3},{5,4},{6,5},{7,6},{9,8},{10,9},{11,10},{12... | collective-permute-start | bytes 884744 | tf_op jit(solution)/shard_map/ppermute | solution.py:241
  57.8 7.0 %collective-permute-start.4 = (f32[2,16,256]{2,1,0:T(8,128)}, f32[2,16,256]{2,1,0:T(8,128)S(1)}, u32[]{:S(2)}, u32[]{:S(2)}) collective-permute-start(f32[2,16,256]{2,1,0:T(8,128)} %shard_map.68), channel_id=1, source_target_pairs={{0,8},{8,16},{16,24},{24,32},{32,40},{40,48},{48,56},{56,64},{64,7... | collective-permute-start | bytes 98312 | tf_op jit(solution)/shard_map/ppermute | solution.py:241
  62.9 5.4 %collective-permute-start.5 = (f32[2,16,256]{2,1,0:T(8,128)}, f32[2,16,256]{2,1,0:T(8,128)S(1)}, u32[]{:S(2)}, u32[]{:S(2)}) collective-permute-start(f32[2,16,256]{2,1,0:T(8,128)} %shard_map.68), channel_id=1, source_target_pairs={{8,0},{16,8},{24,16},{32,24},{40,32},{48,40},{56,48},{64,56},{72,6... | collective-permute-start | bytes 98312 | tf_op jit(solution)/shard_map/ppermute | solution.py:241
  69.1 5.9 %collective-permute-start.6 = (f32[3,2,16,256]{3,2,1,0:T(8,128)S(1)}, f32[3,2,16,256]{3,2,1,0:T(8,128)S(1)}, u32[]{:S(2)}, u32[]{:S(2)}) collective-permute-start(f32[3,2,16,256]{3,2,1,0:T(8,128)S(1)} %get-tuple-element.13), channel_id=1, source_target_pairs={{0,1},{1,2},{2,3},{3,4},{4,5},{5,6},{6,7},{8,9},{9,10},{10,11},{11... | collective-permute-start | bytes 294920 | tf_op jit(solution)/shard_map/ppermute | solution.py:241
  73.1 7.2 %collective-permute-start.7 = (f32[3,2,16,256]{3,2,1,0:T(8,128)S(1)}, f32[3,2,16,256]{3,2,1,0:T(8,128)S(1)}, u32[]{:S(2)}, u32[]{:S(2)}) collective-permute-start(f32[3,2,16,256]{3,2,1,0:T(8,128)S(1)} %get-tuple-element.13), channel_id=1, source_target_pairs={{1,0},{2,1},{3,2},{4,3},{5,4},{6,5},{7,6},{9,8},{10,9},{11,10},{12... | collective-permute-start | bytes 294920 | tf_op jit(solution)/shard_map/ppermute | solution.py:241
  83.4 5.5 %collective-permute-start.8 = (f32[2,16,256]{2,1,0:T(8,128)}, f32[2,16,256]{2,1,0:T(8,128)S(1)}, u32[]{:S(2)}, u32[]{:S(2)}) collective-permute-start(f32[2,16,256]{2,1,0:T(8,128)} %shard_map.69), channel_id=1, source_target_pairs={{0,8},{8,16},{16,24},{24,32},{32,40},{40,48},{48,56},{56,64},{64,7... | collective-permute-start | bytes 98312 | tf_op jit(solution)/shard_map/ppermute | solution.py:241
  87.0 5.4 %collective-permute-start.9 = (f32[2,16,256]{2,1,0:T(8,128)}, f32[2,16,256]{2,1,0:T(8,128)S(1)}, u32[]{:S(2)}, u32[]{:S(2)}) collective-permute-start(f32[2,16,256]{2,1,0:T(8,128)} %shard_map.69), channel_id=1, source_target_pairs={{8,0},{16,8},{24,16},{32,24},{40,32},{48,40},{56,48},{64,56},{72,6... | collective-permute-start | bytes 98312 | tf_op jit(solution)/shard_map/ppermute | solution.py:241
  93.2 6.7 %collective-permute-start.10 = (f32[3,2,16,256]{3,2,1,0:T(8,128)S(1)}, f32[3,2,16,256]{3,2,1,0:T(8,128)S(1)}, u32[]{:S(2)}, u32[]{:S(2)}) collective-permute-start(f32[3,2,16,256]{3,2,1,0:T(8,128)S(1)} %get-tuple-element.11), channel_id=1, source_target_pairs={{0,1},{1,2},{2,3},{3,4},{4,5},{5,6},{6,7},{8,9},{9,10},{10,11},{11... | collective-permute-start | bytes 294920 | tf_op jit(solution)/shard_map/ppermute | solution.py:241
  98.3 5.4 %collective-permute-start.11 = (f32[3,2,16,256]{3,2,1,0:T(8,128)S(1)}, f32[3,2,16,256]{3,2,1,0:T(8,128)S(1)}, u32[]{:S(2)}, u32[]{:S(2)}) collective-permute-start(f32[3,2,16,256]{3,2,1,0:T(8,128)S(1)} %get-tuple-element.11), channel_id=1, source_target_pairs={{1,0},{2,1},{3,2},{4,3},{5,4},{6,5},{7,6},{9,8},{10,9},{11,10},{12... | collective-permute-start | bytes 294920 | tf_op jit(solution)/shard_map/ppermute | solution.py:241
  103.7 3.1 %copy-start = (f32[2,16,256]{2,1,0:T(8,128)S(1)}, f32[2,16,256]{2,1,0:T(8,128)}, u32[]{:S(2)}) copy-start(f32[2,16,256]{2,1,0:T(8,128)} %shard_map.68) | copy-start | bytes 98308
  107.6 5.4 %collective-permute-start.12 = (f32[2,16,256]{2,1,0:T(8,128)S(1)}, f32[2,16,256]{2,1,0:T(8,128)S(1)}, u32[]{:S(2)}, u32[]{:S(2)}) collective-permute-start(f32[2,16,256]{2,1,0:T(8,128)S(1)} %multiply_subtract_fusion.1), channel_id=1, source_target_pairs={{0,8},{8,16},{16,24},{24,32},{32,40},{40,48},{48,56},{56,64},{64,7... | collective-permute-start | bytes 98312 | tf_op jit(solution)/shard_map/ppermute | solution.py:241
  111.0 5.2 %collective-permute-start.13 = (f32[2,16,256]{2,1,0:T(8,128)S(1)}, f32[2,16,256]{2,1,0:T(8,128)S(1)}, u32[]{:S(2)}, u32[]{:S(2)}) collective-permute-start(f32[2,16,256]{2,1,0:T(8,128)S(1)} %multiply_subtract_fusion.1), channel_id=1, source_target_pairs={{8,0},{16,8},{24,16},{32,24},{40,32},{48,40},{56,48},{64,56},{72,6... | collective-permute-start | bytes 98312 | tf_op jit(solution)/shard_map/ppermute | solution.py:241
  116.3 5.0 %collective-permute-start.14 = (f32[3,2,16,256]{3,2,1,0:T(8,128)S(1)}, f32[3,2,16,256]{3,2,1,0:T(8,128)S(1)}, u32[]{:S(2)}, u32[]{:S(2)}) collective-permute-start(f32[3,2,16,256]{3,2,1,0:T(8,128)S(1)} %get-tuple-element.9), channel_id=1, source_target_pairs={{0,1},{1,2},{2,3},{3,4},{4,5},{5,6},{6,7},{8,9},{9,10},{10,11},{11... | collective-permute-start | bytes 294920 | tf_op jit(solution)/shard_map/ppermute | solution.py:241
  119.6 5.4 %collective-permute-start.15 = (f32[3,2,16,256]{3,2,1,0:T(8,128)S(1)}, f32[3,2,16,256]{3,2,1,0:T(8,128)S(1)}, u32[]{:S(2)}, u32[]{:S(2)}) collective-permute-start(f32[3,2,16,256]{3,2,1,0:T(8,128)S(1)} %get-tuple-element.9), channel_id=1, source_target_pairs={{1,0},{2,1},{3,2},{4,3},{5,4},{6,5},{7,6},{9,8},{10,9},{11,10},{12... | collective-permute-start | bytes 294920 | tf_op jit(solution)/shard_map/ppermute | solution.py:241
  125.0 3.2 %copy-start.1 = (f32[2,16,256]{2,1,0:T(8,128)S(1)}, f32[2,16,256]{2,1,0:T(8,128)}, u32[]{:S(2)}) copy-start(f32[2,16,256]{2,1,0:T(8,128)} %shard_map.69) | copy-start | bytes 98308

commit v7 on v6

--- a/solution.py
+++ b/solution.py
@@ -243,8 +243,8 @@
 
 def halo(field):
     lead, bricks = field.shape[:-3], field.shape[-3]
-    column = jnp.stack([_shift(field, "wide", -1), field, _shift(field, "wide", 1)], axis=-4)
-    block = jnp.stack([_shift(column, "narrow", -1), column, _shift(column, "narrow", 1)], axis=-4)
+    column = jnp.stack([_shift(field, "narrow", -1), field, _shift(field, "narrow", 1)], axis=-4)
+    block = jnp.stack([_shift(column, "wide", -1), column, _shift(column, "wide", 1)], axis=-5)
     block = block.reshape(lead + (9 * bricks,) + field.shape[-2:])
     zero = jnp.zeros(lead + (1,) + field.shape[-2:], field.dtype)
     return jnp.concatenate([block, zero], axis=-3)

time: 177 us -> 177 us (level)
  blocking collectives: 57.7 us -> 61.1 us
    all_to_all x1, blocking collectives: 36.9 us -> 40.3 us  [shards(): lax.all_to_all(jnp.broadcast_to(payload, (devices, 32)), ('wide', 'narrow...]
  transfers between devices with their start and end apart: 16 -> 16, of which waited for: 11 -> 10; matrix products, arithmetic and copies ran while one was open for 1% -> 1% of each run, Pallas kernels for 0% -> 0%
where the time goes in v7:
time: 177 us; the launch traced here: 176 us
  blocking collectives  61.1 us (35%)
  starting transfers between devices  42.8 us (24%)
  waiting for transfers between devices  33.7 us (19%)
  Pallas kernels  13.4 us (8%)
  local copies, waits for them, and re-layouts  9.5 us (5%)
  matrix products  7.35 us (4%)
  other arithmetic  6.77 us (4%)
    ppermute x16, starting transfers between devices, _shift(): return lax.ppermute(field, axis, pairs)  42.8 us
    all_to_all x1, blocking collectives, shards(): lax.all_to_all(jnp.broadcast_to(payload, (devices, 32)), ('wide', 'narrow...  40.3 us
    ppermute x16, waiting for transfers between devices, _shift(): return lax.ppermute(field, axis, pairs)  33.7 us
    all_to_all x1, blocking collectives, shards(): lax.all_to_all(send.reshape(owners, CAP, 4), 'wide', 0, 0, tiled=True)  20.8 us
    pallas_call x4, Pallas kernels, _local_call(): pl.pallas_call(kernel, out_shape=jax.ShapeDtypeStruct(out_shape, jnp.floa...  9 us
    dot_general x1, matrix products, shards(): jnp.dot(place_hot, payload, precision=HIGHEST, preferred_element_type=jnp...  3.74 us
  transfers between devices with their start and end apart: 16, of which 10 were waited for; matrix products, arithmetic and copies ran while one was open for 1% of the time, Pallas kernels for 0%

profile of v7, /device:TPU:1, one launch (start us, length us, event | category | flops | bytes accessed | tf_op | source)
XLA Modules:
  0.0 176.3 jit_solution(10346601857923631759)
XLA Ops:
  0.7 1.4 fusion.5
  2.7 3.7 %fusion = f32[2048,4]{0,1:T(4,128)S(1)} fusion(s32[1024]{0:T(1024)S(1)} %convert_add_fusion, f32[1024,3]{0,1:T(4,128)S(1)} %bitcast.112, f32[1024,1]{0,1:T(1,128)S(1)} %bitcast.111), kind=kOutput, calls=%fused_computation.1 | convolution fusion | flops 102764544 | bytes 53248 | tf_op jit(solution)/shard_map/dot_general | solution.py:271
  6.5 0.1 reshape.68
  6.6 0.1 copy.23
  6.7 0.1 reshape.76
  6.8 20.8 %all_to_all.14 = f32[64,1,128]{2,1,0:T(1,128)S(1)} all-to-all(f32[64,1,128]{2,1,0:T(1,128)S(1)} %reshape.76), channel_id=1, replica_groups=mesh['wide'=64,'narrow'=8] {'wide'}, dimensions={0} | all-to-all | bytes 65536 | tf_op jit(solution)/shard_map/all_to_all | solution.py:272
  27.6 0.5 broadcast.52
  28.1 0.7 reduce
  28.9 0.1 reshape.77
  29.0 0.1 reshape.69
  29.2 0.3 fusion.14
  29.5 1.1 fusion.17
  30.7 2.2 %fusion.3 = f32[128,256]{1,0:T(8,128)S(1)} fusion(f32[2048,32]{1,0:T(8,128)S(1)} %fusion.14, f32[2048,32]{1,0:T(8,128)S(1)} %get-tuple-element.20, f32[2048,32]{1,0:T(8,128)S(1)} %get-tuple-element.21, f32[2048,32]{1,0:T(8,128)S(1)} %get-tuple-element.19, s32[2048]{0:T(1024)S(1)} %bitcast.99), kind=kOutput, calls=%fused_computation.6 | convolution fusion | flops 806617088 | bytes 1187840 | tf_op jit(solution)/shard_map/pa,pb->ab/dot_general | solution.py:280
  33.0 4.0 %collective-permute-start = (f32[3,2,16,256]{3,2,1,0:T(8,128)S(1)}, f32[3,2,16,256]{3,2,1,0:T(8,128)S(1)}, u32[]{:S(2)}, u32[]{:S(2)}) collective-permute-start(f32[3,2,16,256]{3,2,1,0:T(8,128)S(1)} %bitcast.80), channel_id=1, source_target_pairs={{0,1},{1,2},{2,3},{3,4},{4,5},{5,6},{6,7},{8,9},{9,10},{10,11},{11... | collective-permute-start | bytes 294920 | tf_op jit(solution)/shard_map/ppermute | solution.py:241
  37.0 1.3 collective-permute-start.1
  38.3 0.3 collective-permute-done
  38.6 4.4 %collective-permute-done.1 = f32[3,2,16,256]{3,2,1,0:T(8,128)S(1)} collective-permute-done((f32[3,2,16,256]{3,2,1,0:T(8,128)S(1)}, f32[3,2,16,256]{3,2,1,0:T(8,128)S(1)}, u32[]{:S(2)}, u32[]{:S(2)}) %collective-permute-start.1) | collective-permute-done | bytes 98336 | tf_op jit(solution)/shard_map/ppermute | solution.py:241
  43.0 3.9 %collective-permute-start.2 = (f32[3,3,2,16,256]{4,3,2,1,0:T(8,128)S(1)}, f32[3,3,2,16,256]{4,3,2,1,0:T(8,128)S(1)}, u32[]{:S(2)}, u32[]{:S(2)}) collective-permute-start(f32[3,3,2,16,256]{4,3,2,1,0:T(8,128)S(1)} %get-tuple-element.7), channel_id=1, source_target_pairs={{0,8},{8,16},{16,24},{24,32},{32,40},{40,48},{48,56},{56,64},{64,7... | collective-permute-start | bytes 884744 | tf_op jit(solution)/shard_map/ppermute | solution.py:241
  46.9 1.9 %collective-permute-start.3 = (f32[3,3,2,16,256]{4,3,2,1,0:T(8,128)S(1)}, f32[3,3,2,16,256]{4,3,2,1,0:T(8,128)S(1)}, u32[]{:S(2)}, u32[]{:S(2)}) collective-permute-start(f32[3,3,2,16,256]{4,3,2,1,0:T(8,128)S(1)} %get-tuple-element.7), channel_id=1, source_target_pairs={{8,0},{16,8},{24,16},{32,24},{40,32},{48,40},{56,48},{64,56},{72,6... | collective-permute-start | bytes 884744 | tf_op jit(solution)/shard_map/ppermute | solution.py:241
  48.9 0.7 reshape.67.tab_ref
  49.5 1.1 collective-permute-done.2
  50.6 4.4 %collective-permute-done.3 = f32[3,3,2,16,256]{4,3,2,1,0:T(8,128)S(1)} collective-permute-done((f32[3,3,2,16,256]{4,3,2,1,0:T(8,128)S(1)}, f32[3,3,2,16,256]{4,3,2,1,0:T(8,128)S(1)}, u32[]{:S(2)}, u32[]{:S(2)}) %collective-permute-start.3) | collective-permute-done | bytes 294944 | tf_op jit(solution)/shard_map/ppermute | solution.py:241
  55.0 0.1 pad_maximum_fusion
  55.1 1.0 concatenate.21.src_ref
  56.1 1.9 %shard_map.68 = f32[2,16,256]{2,1,0:T(8,128)} custom-call(s32[54]{0:T(128)} %reshape.67.tab_ref, f32[3,19,16,256]{3,2,1,0:T(8,128)} %concatenate.21.src_ref), custom_call_target="tpu_custom_call" | custom-call | flops 163840 | bytes 966872 | tf_op jit(solution)/shard_map/pallas_call | solution.py:229
  58.0 4.0 %collective-permute-start.4 = (f32[2,16,256]{2,1,0:T(8,128)}, f32[2,16,256]{2,1,0:T(8,128)S(1)}, u32[]{:S(2)}, u32[]{:S(2)}) collective-permute-start(f32[2,16,256]{2,1,0:T(8,128)} %shard_map.68), channel_id=1, source_target_pairs={{0,1},{1,2},{2,3},{3,4},{4,5},{5,6},{6,7},{8,9},{9,10},{10,11},{11... | collective-permute-start | bytes 98312 | tf_op jit(solution)/shard_map/ppermute | solution.py:241
  62.0 1.3 collective-permute-start.5
  63.4 5.4 %collective-permute-done.5 = f32[2,16,256]{2,1,0:T(8,128)S(1)} collective-permute-done((f32[2,16,256]{2,1,0:T(8,128)}, f32[2,16,256]{2,1,0:T(8,128)S(1)}, u32[]{:S(2)}, u32[]{:S(2)}) %collective-permute-start.5) | collective-permute-done | bytes 32800 | tf_op jit(solution)/shard_map/ppermute | solution.py:241
  68.8 0.8 fusion.29
  69.5 3.2 %collective-permute-start.6 = (f32[3,2,16,256]{3,2,1,0:T(8,128)S(1)}, f32[3,2,16,256]{3,2,1,0:T(8,128)S(1)}, u32[]{:S(2)}, u32[]{:S(2)}) collective-permute-start(f32[3,2,16,256]{3,2,1,0:T(8,128)S(1)} %get-tuple-element.13), channel_id=1, source_target_pairs={{0,8},{8,16},{16,24},{24,32},{32,40},{40,48},{48,56},{56,64},{64,7... | collective-permute-start | bytes 294920 | tf_op jit(solution)/shard_map/ppermute | solution.py:241
  72.7 1.9 %collective-permute-start.7 = (f32[3,2,16,256]{3,2,1,0:T(8,128)S(1)}, f32[3,2,16,256]{3,2,1,0:T(8,128)S(1)}, u32[]{:S(2)}, u32[]{:S(2)}) collective-permute-start(f32[3,2,16,256]{3,2,1,0:T(8,128)S(1)} %get-tuple-element.13), channel_id=1, source_target_pairs={{8,0},{16,8},{24,16},{32,24},{40,32},{48,40},{56,48},{64,56},{72,6... | collective-permute-start | bytes 294920 | tf_op jit(solution)/shard_map/ppermute | solution.py:241
  74.6 0.6 fusion.20
  75.3 3.4 %collective-permute-done.7 = f32[3,2,16,256]{3,2,1,0:T(8,128)S(1)} collective-permute-done((f32[3,2,16,256]{3,2,1,0:T(8,128)S(1)}, f32[3,2,16,256]{3,2,1,0:T(8,128)S(1)}, u32[]{:S(2)}, u32[]{:S(2)}) %collective-permute-start.7) | collective-permute-done | bytes 98336 | tf_op jit(solution)/shard_map/ppermute | solution.py:241
  78.7 0.7 concatenate.22.src_ref
  79.4 2.4 %shard_map.69 = f32[2,16,256]{2,1,0:T(8,128)} custom-call(s32[54]{0:T(128)} %reshape.67.tab_ref, f32[19,16,256]{2,1,0:T(8,128)} %concatenate.22.src_ref, f32[2,16,256]{2,1,0:T(8,128)} %bitcast.71), custom_call_target="tpu_custom_call" | custom-call | flops 491520 | bytes 377048 | tf_op jit(solution)/shard_map/pallas_call | solution.py:229
  81.8 4.8 %collective-permute-start.8 = (f32[2,16,256]{2,1,0:T(8,128)}, f32[2,16,256]{2,1,0:T(8,128)S(1)}, u32[]{:S(2)}, u32[]{:S(2)}) collective-permute-start(f32[2,16,256]{2,1,0:T(8,128)} %shard_map.69), channel_id=1, source_target_pairs={{0,1},{1,2},{2,3},{3,4},{4,5},{5,6},{6,7},{8,9},{9,10},{10,11},{11... | collective-permute-start | bytes 98312 | tf_op jit(solution)/shard_map/ppermute | solution.py:241
  86.6 1.3 collective-permute-start.9
  87.9 3.6 %collective-permute-done.9 = f32[2,16,256]{2,1,0:T(8,128)S(1)} collective-permute-done((f32[2,16,256]{2,1,0:T(8,128)}, f32[2,16,256]{2,1,0:T(8,128)S(1)}, u32[]{:S(2)}, u32[]{:S(2)}) %collective-permute-start.9) | collective-permute-done | bytes 32800 | tf_op jit(solution)/shard_map/ppermute | solution.py:241
  91.5 0.8 fusion.28
  92.3 3.2 %collective-permute-start.10 = (f32[3,2,16,256]{3,2,1,0:T(8,128)S(1)}, f32[3,2,16,256]{3,2,1,0:T(8,128)S(1)}, u32[]{:S(2)}, u32[]{:S(2)}) collective-permute-start(f32[3,2,16,256]{3,2,1,0:T(8,128)S(1)} %get-tuple-element.11), channel_id=1, source_target_pairs={{0,8},{8,16},{16,24},{24,32},{32,40},{40,48},{48,56},{56,64},{64,7... | collective-permute-start | bytes 294920 | tf_op jit(solution)/shard_map/ppermute | solution.py:241
  95.5 1.9 %collective-permute-start.11 = (f32[3,2,16,256]{3,2,1,0:T(8,128)S(1)}, f32[3,2,16,256]{3,2,1,0:T(8,128)S(1)}, u32[]{:S(2)}, u32[]{:S(2)}) collective-permute-start(f32[3,2,16,256]{3,2,1,0:T(8,128)S(1)} %get-tuple-element.11), channel_id=1, source_target_pairs={{8,0},{16,8},{24,16},{32,24},{40,32},{48,40},{56,48},{64,56},{72,6... | collective-permute-start | bytes 294920 | tf_op jit(solution)/shard_map/ppermute | solution.py:241
  97.5 4.0 %collective-permute-done.11 = f32[3,2,16,256]{3,2,1,0:T(8,128)S(1)} collective-permute-done((f32[3,2,16,256]{3,2,1,0:T(8,128)S(1)}, f32[3,2,16,256]{3,2,1,0:T(8,128)S(1)}, u32[]{:S(2)}, u32[]{:S(2)}) %collective-permute-start.11) | collective-permute-done | bytes 98336 | tf_op jit(solution)/shard_map/ppermute | solution.py:241
  101.5 0.7 concatenate.23.src_ref
  102.2 2.3 %shard_map.70 = f32[2,16,256]{2,1,0:T(8,128)} custom-call(s32[54]{0:T(128)} %reshape.67.tab_ref, f32[19,16,256]{2,1,0:T(8,128)} %concatenate.23.src_ref, f32[2,16,256]{2,1,0:T(8,128)} %bitcast.72), custom_call_target="tpu_custom_call" | custom-call | flops 491520 | bytes 377048 | tf_op jit(solution)/shard_map/pallas_call | solution.py:229
  104.6 0.8 multiply_subtract_fusion.1
  105.3 3.4 %collective-permute-start.12 = (f32[2,16,256]{2,1,0:T(8,128)S(1)}, f32[2,16,256]{2,1,0:T(8,128)S(1)}, u32[]{:S(2)}, u32[]{:S(2)}) collective-permute-start(f32[2,16,256]{2,1,0:T(8,128)S(1)} %multiply_subtract_fusion.1), channel_id=1, source_target_pairs={{0,1},{1,2},{2,3},{3,4},{4,5},{5,6},{6,7},{8,9},{9,10},{10,11},{11... | collective-permute-start | bytes 98312 | tf_op jit(solution)/shard_map/ppermute | solution.py:241
  108.7 1.3 collective-permute-start.13
  110.0 3.3 %collective-permute-done.13 = f32[2,16,256]{2,1,0:T(8,128)S(1)} collective-permute-done((f32[2,16,256]{2,1,0:T(8,128)S(1)}, f32[2,16,256]{2,1,0:T(8,128)S(1)}, u32[]{:S(2)}, u32[]{:S(2)}) %collective-permute-start.13) | collective-permute-done | bytes 32800 | tf_op jit(solution)/shard_map/ppermute | solution.py:241
  113.4 3.3 %collective-permute-start.14 = (f32[3,2,16,256]{3,2,1,0:T(8,128)S(1)}, f32[3,2,16,256]{3,2,1,0:T(8,128)S(1)}, u32[]{:S(2)}, u32[]{:S(2)}) collective-permute-start(f32[3,2,16,256]{3,2,1,0:T(8,128)S(1)} %get-tuple-element.9), channel_id=1, source_target_pairs={{0,8},{8,16},{16,24},{24,32},{32,40},{40,48},{48,56},{56,64},{64,7... | collective-permute-start | bytes 294920 | tf_op jit(solution)/shard_map/ppermute | solution.py:241
  116.6 2.1 %collective-permute-start.15 = (f32[3,2,16,256]{3,2,1,0:T(8,128)S(1)}, f32[3,2,16,256]{3,2,1,0:T(8,128)S(1)}, u32[]{:S(2)}, u32[]{:S(2)}) collective-permute-start(f32[3,2,16,256]{3,2,1,0:T(8,128)S(1)} %get-tuple-element.9), channel_id=1, source_target_pairs={{8,0},{16,8},{24,16},{32,24},{40,32},{48,40},{56,48},{64,56},{72,6... | collective-permute-start | bytes 294920 | tf_op jit(solution)/shard_map/ppermute | solution.py:241
  118.8 3.8 %collective-permute-done.15 = f32[3,2,16,256]{3,2,1,0:T(8,128)S(1)} collective-permute-done((f32[3,2,16,256]{3,2,1,0:T(8,128)S(1)}, f32[3,2,16,256]{3,2,1,0:T(8,128)S(1)}, u32[]{:S(2)}, u32[]{:S(2)}) %collective-permute-start.15) | collective-permute-done | bytes 98336 | tf_op jit(solution)/shard_map/ppermute | solution.py:241
  122.6 0.7 concatenate.24.src_ref
  123.3 2.4 %shard_map.71 = f32[2,16,256]{2,1,0:T(8,128)} custom-call(s32[54]{0:T(128)} %reshape.67.tab_ref, f32[19,16,256]{2,1,0:T(8,128)} %concatenate.24.src_ref, f32[2,16,256]{2,1,0:T(8,128)} %bitcast.73), custom_call_target="tpu_custom_call" | custom-call | flops 491520 | bytes 377048 | tf_op jit(solution)/shard_map/pallas_call | solution.py:229
  125.7 0.8 multiply_subtract_fusion
  126.5 0.6 pad_maximum_fusion.5.basis_ref
  127.1 2.2 %shard_map.72 = f32[8,128]{1,0:T(8,128)} custom-call(f32[4,32,256]{2,1,0:T(8,128)} %pad_maximum_fusion.5.basis_ref), custom_call_target="tpu_custom_call" | custom-call | tf_op jit(solution)/shard_map/pallas_call | solution.py:302
  129.4 0.7 slice.32
  130.0 0.1 broadcast_in_dim.12
  130.1 0.1 broadcast_in_dim.13
  130.3 40.3 %all_to_all.15 = f32[512,1,32]{2,1,0:T(1,128)S(1)} all-to-all(f32[512,1,32]{2,1,0:T(1,128)S(1)} %broadcast_in_dim.13), channel_id=1, replica_groups=mesh['wide'=64,'narrow'=8] {'wide','narrow'}, dimensions={0} | all-to-all | bytes 131072 | tf_op jit(solution)/shard_map/all_to_all | solution.py:306
  170.5 0.7 copy.21
  171.3 2.2 %shard_map.73 = (f32[32,256]{1,0:T(8,128)}, f32[32,256]{1,0:T(8,128)}) custom-call(f32[32,512]{1,0:T(8,128)} %bitcast.87, f32[4,32,256]{2,1,0:T(8,128)} %pad_maximum_fusion.5.basis_ref), custom_call_target="tpu_custom_call" | custom-call | tf_op jit(solution)/shard_map/pallas_call | solution.py:308
  173.5 1.4 reshape.74
  174.9 1.4 reshape.75
  (29 shorter events, 0.3 us)
Async XLA Ops:
  0.6 1.4 copy-start.2
  0.6 2.1 %copy-start.3 = (s32[1024]{0:T(1024)S(1)}, s32[1024]{0:T(1024)}, u32[]{:S(2)}) copy-start(s32[1024]{0:T(1024)} %param.6) | copy-start | bytes 12292
  0.6 2.1 %copy-start.4 = (f32[3,1024]{1,0:T(4,128)S(1)}, f32[3,1024]{1,0:T(4,128)}, u32[]{:S(2)}) copy-start(f32[3,1024]{1,0:T(4,128)} %param.7) | copy-start | bytes 36868
  32.9 16.0 %copy-start.5 = (s32[1,1,2,27]{3,2,1,0:T(2,128)S(1)}, s32[1,1,2,27]{3,2,1,0:T(2,128)}, u32[]{:S(2)}) copy-start(s32[1,1,2,27]{3,2,1,0:T(2,128)} %param.9) | copy-start | bytes 652
  33.0 5.6 %collective-permute-start = (f32[3,2,16,256]{3,2,1,0:T(8,128)S(1)}, f32[3,2,16,256]{3,2,1,0:T(8,128)S(1)}, u32[]{:S(2)}, u32[]{:S(2)}) collective-permute-start(f32[3,2,16,256]{3,2,1,0:T(8,128)S(1)} %bitcast.80), channel_id=1, source_target_pairs={{0,1},{1,2},{2,3},{3,4},{4,5},{5,6},{6,7},{8,9},{9,10},{10,11},{11... | collective-permute-start | bytes 294920 | tf_op jit(solution)/shard_map/ppermute | solution.py:241
  37.0 6.0 %collective-permute-start.1 = (f32[3,2,16,256]{3,2,1,0:T(8,128)S(1)}, f32[3,2,16,256]{3,2,1,0:T(8,128)S(1)}, u32[]{:S(2)}, u32[]{:S(2)}) collective-permute-start(f32[3,2,16,256]{3,2,1,0:T(8,128)S(1)} %bitcast.81), channel_id=1, source_target_pairs={{1,0},{2,1},{3,2},{4,3},{5,4},{6,5},{7,6},{9,8},{10,9},{11,10},{12... | collective-permute-start | bytes 294920 | tf_op jit(solution)/shard_map/ppermute | solution.py:241
  43.0 7.6 %collective-permute-start.2 = (f32[3,3,2,16,256]{4,3,2,1,0:T(8,128)S(1)}, f32[3,3,2,16,256]{4,3,2,1,0:T(8,128)S(1)}, u32[]{:S(2)}, u32[]{:S(2)}) collective-permute-start(f32[3,3,2,16,256]{4,3,2,1,0:T(8,128)S(1)} %get-tuple-element.7), channel_id=1, source_target_pairs={{0,8},{8,16},{16,24},{24,32},{32,40},{40,48},{48,56},{56,64},{64,7... | collective-permute-start | bytes 884744 | tf_op jit(solution)/shard_map/ppermute | solution.py:241
  46.9 8.0 %collective-permute-start.3 = (f32[3,3,2,16,256]{4,3,2,1,0:T(8,128)S(1)}, f32[3,3,2,16,256]{4,3,2,1,0:T(8,128)S(1)}, u32[]{:S(2)}, u32[]{:S(2)}) collective-permute-start(f32[3,3,2,16,256]{4,3,2,1,0:T(8,128)S(1)} %get-tuple-element.7), channel_id=1, source_target_pairs={{8,0},{16,8},{24,16},{32,24},{40,32},{48,40},{56,48},{64,56},{72,6... | collective-permute-start | bytes 884744 | tf_op jit(solution)/shard_map/ppermute | solution.py:241
  58.0 5.3 %collective-permute-start.4 = (f32[2,16,256]{2,1,0:T(8,128)}, f32[2,16,256]{2,1,0:T(8,128)S(1)}, u32[]{:S(2)}, u32[]{:S(2)}) collective-permute-start(f32[2,16,256]{2,1,0:T(8,128)} %shard_map.68), channel_id=1, source_target_pairs={{0,1},{1,2},{2,3},{3,4},{4,5},{5,6},{6,7},{8,9},{9,10},{10,11},{11... | collective-permute-start | bytes 98312 | tf_op jit(solution)/shard_map/ppermute | solution.py:241
  62.0 6.7 %collective-permute-start.5 = (f32[2,16,256]{2,1,0:T(8,128)}, f32[2,16,256]{2,1,0:T(8,128)S(1)}, u32[]{:S(2)}, u32[]{:S(2)}) collective-permute-start(f32[2,16,256]{2,1,0:T(8,128)} %shard_map.68), channel_id=1, source_target_pairs={{1,0},{2,1},{3,2},{4,3},{5,4},{6,5},{7,6},{9,8},{10,9},{11,10},{12... | collective-permute-start | bytes 98312 | tf_op jit(solution)/shard_map/ppermute | solution.py:241
  69.5 5.7 %collective-permute-start.6 = (f32[3,2,16,256]{3,2,1,0:T(8,128)S(1)}, f32[3,2,16,256]{3,2,1,0:T(8,128)S(1)}, u32[]{:S(2)}, u32[]{:S(2)}) collective-permute-start(f32[3,2,16,256]{3,2,1,0:T(8,128)S(1)} %get-tuple-element.13), channel_id=1, source_target_pairs={{0,8},{8,16},{16,24},{24,32},{32,40},{40,48},{48,56},{56,64},{64,7... | collective-permute-start | bytes 294920 | tf_op jit(solution)/shard_map/ppermute | solution.py:241
  72.7 5.9 %collective-permute-start.7 = (f32[3,2,16,256]{3,2,1,0:T(8,128)S(1)}, f32[3,2,16,256]{3,2,1,0:T(8,128)S(1)}, u32[]{:S(2)}, u32[]{:S(2)}) collective-permute-start(f32[3,2,16,256]{3,2,1,0:T(8,128)S(1)} %get-tuple-element.13), channel_id=1, source_target_pairs={{8,0},{16,8},{24,16},{32,24},{40,32},{48,40},{56,48},{64,56},{72,6... | collective-permute-start | bytes 294920 | tf_op jit(solution)/shard_map/ppermute | solution.py:241
  79.4 25.2 %copy-start = (f32[2,16,256]{2,1,0:T(8,128)S(1)}, f32[2,16,256]{2,1,0:T(8,128)}, u32[]{:S(2)}) copy-start(f32[2,16,256]{2,1,0:T(8,128)} %shard_map.68) | copy-start | bytes 98308
  81.8 6.2 %collective-permute-start.8 = (f32[2,16,256]{2,1,0:T(8,128)}, f32[2,16,256]{2,1,0:T(8,128)S(1)}, u32[]{:S(2)}, u32[]{:S(2)}) collective-permute-start(f32[2,16,256]{2,1,0:T(8,128)} %shard_map.69), channel_id=1, source_target_pairs={{0,1},{1,2},{2,3},{3,4},{4,5},{5,6},{6,7},{8,9},{9,10},{10,11},{11... | collective-permute-start | bytes 98312 | tf_op jit(solution)/shard_map/ppermute | solution.py:241
  86.6 4.9 %collective-permute-start.9 = (f32[2,16,256]{2,1,0:T(8,128)}, f32[2,16,256]{2,1,0:T(8,128)S(1)}, u32[]{:S(2)}, u32[]{:S(2)}) collective-permute-start(f32[2,16,256]{2,1,0:T(8,128)} %shard_map.69), channel_id=1, source_target_pairs={{1,0},{2,1},{3,2},{4,3},{5,4},{6,5},{7,6},{9,8},{10,9},{11,10},{12... | collective-permute-start | bytes 98312 | tf_op jit(solution)/shard_map/ppermute | solution.py:241
  92.3 5.2 %collective-permute-start.10 = (f32[3,2,16,256]{3,2,1,0:T(8,128)S(1)}, f32[3,2,16,256]{3,2,1,0:T(8,128)S(1)}, u32[]{:S(2)}, u32[]{:S(2)}) collective-permute-start(f32[3,2,16,256]{3,2,1,0:T(8,128)S(1)} %get-tuple-element.11), channel_id=1, source_target_pairs={{0,8},{8,16},{16,24},{24,32},{32,40},{40,48},{48,56},{56,64},{64,7... | collective-permute-start | bytes 294920 | tf_op jit(solution)/shard_map/ppermute | solution.py:241
  95.5 5.9 %collective-permute-start.11 = (f32[3,2,16,256]{3,2,1,0:T(8,128)S(1)}, f32[3,2,16,256]{3,2,1,0:T(8,128)S(1)}, u32[]{:S(2)}, u32[]{:S(2)}) collective-permute-start(f32[3,2,16,256]{3,2,1,0:T(8,128)S(1)} %get-tuple-element.11), channel_id=1, source_target_pairs={{8,0},{16,8},{24,16},{32,24},{40,32},{48,40},{56,48},{64,56},{72,6... | collective-permute-start | bytes 294920 | tf_op jit(solution)/shard_map/ppermute | solution.py:241
  104.6 21.1 %copy-start.1 = (f32[2,16,256]{2,1,0:T(8,128)S(1)}, f32[2,16,256]{2,1,0:T(8,128)}, u32[]{:S(2)}) copy-start(f32[2,16,256]{2,1,0:T(8,128)} %shard_map.69) | copy-start | bytes 98308
  105.3 4.7 %collective-permute-start.12 = (f32[2,16,256]{2,1,0:T(8,128)S(1)}, f32[2,16,256]{2,1,0:T(8,128)S(1)}, u32[]{:S(2)}, u32[]{:S(2)}) collective-permute-start(f32[2,16,256]{2,1,0:T(8,128)S(1)} %multiply_subtract_fusion.1), channel_id=1, source_target_pairs={{0,1},{1,2},{2,3},{3,4},{4,5},{5,6},{6,7},{8,9},{9,10},{10,11},{11... | collective-permute-start | bytes 98312 | tf_op jit(solution)/shard_map/ppermute | solution.py:241
  108.7 4.7 %collective-permute-start.13 = (f32[2,16,256]{2,1,0:T(8,128)S(1)}, f32[2,16,256]{2,1,0:T(8,128)S(1)}, u32[]{:S(2)}, u32[]{:S(2)}) collective-permute-start(f32[2,16,256]{2,1,0:T(8,128)S(1)} %multiply_subtract_fusion.1), channel_id=1, source_target_pairs={{1,0},{2,1},{3,2},{4,3},{5,4},{6,5},{7,6},{9,8},{10,9},{11,10},{12... | collective-permute-start | bytes 98312 | tf_op jit(solution)/shard_map/ppermute | solution.py:241
  113.4 5.4 %collective-permute-start.14 = (f32[3,2,16,256]{3,2,1,0:T(8,128)S(1)}, f32[3,2,16,256]{3,2,1,0:T(8,128)S(1)}, u32[]{:S(2)}, u32[]{:S(2)}) collective-permute-start(f32[3,2,16,256]{3,2,1,0:T(8,128)S(1)} %get-tuple-element.9), channel_id=1, source_target_pairs={{0,8},{8,16},{16,24},{24,32},{32,40},{40,48},{48,56},{56,64},{64,7... | collective-permute-start | bytes 294920 | tf_op jit(solution)/shard_map/ppermute | solution.py:241
  116.6 5.9 %collective-permute-start.15 = (f32[3,2,16,256]{3,2,1,0:T(8,128)S(1)}, f32[3,2,16,256]{3,2,1,0:T(8,128)S(1)}, u32[]{:S(2)}, u32[]{:S(2)}) collective-permute-start(f32[3,2,16,256]{3,2,1,0:T(8,128)S(1)} %get-tuple-element.9), channel_id=1, source_target_pairs={{8,0},{16,8},{24,16},{32,24},{40,32},{48,40},{56,48},{64,56},{72,6... | collective-permute-start | bytes 294920 | tf_op jit(solution)/shard_map/ppermute | solution.py:241

commit v8 on v6

--- a/solution.py
+++ b/solution.py
@@ -74,15 +74,20 @@
     return _two_sum(s, e + (x[1] + y[1]))
 
 
-def _gram_kernel(basis_ref, out_ref):
+def _rows(ref):
+    return jnp.concatenate([ref[b] for b in range(ref.shape[0])], axis=0)
+
+
+def _gram_kernel(*refs):
+    basis_ref, out_ref = refs[:-1], refs[-1]
     row = lax.broadcasted_iota(jnp.int32, out_ref.shape, 0)
     lane = lax.broadcasted_iota(jnp.int32, out_ref.shape, 1)
-    count = basis_ref.shape[0]
+    count = len(basis_ref)
     acc = jnp.zeros(out_ref.shape, jnp.float32)
     k = 0
     for i in range(count):
         for j in range(i, count):
-            s, e = _two_prod(basis_ref[i], basis_ref[j])
+            s, e = _two_prod(_rows(basis_ref[i]), _rows(basis_ref[j]))
             s, e = _halve(s, e, 0, 8)
             s, e = _halve(s, e, 1, 128)
             s, e = _spread(s, e, 0)
@@ -94,7 +99,8 @@
     out_ref[...] = acc
 
 
-def _galerkin_kernel(parts_ref, basis_ref, solution_ref, residual_ref, lift=None):
+def _galerkin_kernel(parts_ref, *refs, lift=None):
+    basis_ref, (solution_ref, residual_ref) = refs[:-2], refs[-2:]
     half = parts_ref.shape[0] // 2
     s, e = _halve(parts_ref[0:half, :], parts_ref[half:, :], 1, 128)
     s, e = _spread(s, e, 1)
@@ -134,20 +140,26 @@
     for k in range(size):
         terms = [lift[k][j] * coeff[j] for j in range(n) if lift[k][j] != 0.0]
         weights.append((1.0 if k == 0 else 0.0) - sum(terms[1:], terms[0]))
-    shape = solution_ref.shape
+    blocks = [_rows(r) for r in basis_ref]
+    shape = blocks[0].shape
 
     def wide(v):
         v = jnp.broadcast_to(v, (shape[0], v.shape[1]))
         return jnp.concatenate([v] * (shape[1] // v.shape[1]), axis=1)
 
-    total = wide(coeff[0]) * basis_ref[0]
+    def store(out_ref, total):
+        for r in range(shape[0]):
+            b, x = divmod(r, ROWS)
+            out_ref[pl.ds(b, 1), pl.ds(x * LANES, LANES)] = total[r : r + 1, :]
+
+    total = wide(coeff[0]) * blocks[0]
     for j in range(1, n):
-        total = total + wide(coeff[j]) * basis_ref[j]
-    solution_ref[...] = total
-    total = wide(weights[0]) * basis_ref[0]
+        total = total + wide(coeff[j]) * blocks[j]
+    store(solution_ref, total)
+    total = wide(weights[0]) * blocks[0]
     for k in range(1, size):
-        total = total + wide(weights[k]) * basis_ref[k]
-    residual_ref[...] = total
+        total = total + wide(weights[k]) * blocks[k]
+    store(residual_ref, total)
 
 
 def _masks():
@@ -298,19 +310,18 @@
         else:
             lift[k - 1][k] = lift[k + 1][k] = 0.5 * SPAN
     vmem = pl.BlockSpec(memory_space=pltpu.VMEM)
-    stacked = jnp.stack(basis).reshape(ITERS + 1, bricks * ROWS, LANES)
     partial_sums = pl.pallas_call(
-        _gram_kernel, out_shape=jax.ShapeDtypeStruct((8, 128), jnp.float32), in_specs=[vmem], out_specs=vmem
-    )(stacked)
+        _gram_kernel, out_shape=jax.ShapeDtypeStruct((8, 128), jnp.float32), in_specs=[vmem] * len(basis), out_specs=vmem
+    )(*basis)
     payload = partial_sums[0:2, 0:16].reshape(1, 32)
     gathered = lax.all_to_all(jnp.broadcast_to(payload, (devices, 32)), ("wide", "narrow"), 0, 0, tiled=True)
-    flat = jax.ShapeDtypeStruct((bricks * ROWS, LANES), jnp.float32)
+    flat = jax.ShapeDtypeStruct((bricks, ROWS * LANES), jnp.float32)
     solution, residual = pl.pallas_call(
         functools.partial(_galerkin_kernel, lift=lift),
         out_shape=(flat, flat),
-        in_specs=[vmem, vmem],
+        in_specs=[vmem] * (1 + len(basis)),
         out_specs=(vmem, vmem),
-    )(jnp.pad(gathered.T, ((0, 0), (0, max(0, 128 - devices)))), stacked)
+    )(jnp.pad(gathered.T, ((0, 0), (0, max(0, 128 - devices)))), *basis)
     out = (1, 1, bricks, ROWS * LANES)
     return solution.reshape(out), residual.reshape(out)
 

time: 177 us -> 174 us (0.983)
  local copies, waits for them, and re-layouts: 9.57 us -> 6.77 us
    reshape x2 -> x0, local copies, waits for them, and re-layouts: 2.79 us -> none  [shards(): return (solution.reshape(out), residual.reshape(out))]
where the time goes in v8:
time: 174 us; the launch traced here: 172 us
  blocking collectives  57.7 us (33%)
  starting transfers between devices  44.3 us (25%)
  waiting for transfers between devices  34.6 us (20%)
  Pallas kernels  13.3 us (8%)
  matrix products  7.35 us (4%)
  local copies, waits for them, and re-layouts  6.77 us (4%)
  other arithmetic  6.71 us (4%)
    ppermute x16, starting transfers between devices, _shift(): return lax.ppermute(field, axis, pairs)  44.3 us
    all_to_all x1, blocking collectives, shards(): lax.all_to_all(jnp.broadcast_to(payload, (devices, 32)), ('wide', 'narrow...  36.9 us
    ppermute x16, waiting for transfers between devices, _shift(): return lax.ppermute(field, axis, pairs)  34.6 us
    all_to_all x1, blocking collectives, shards(): lax.all_to_all(send.reshape(owners, CAP, 4), 'wide', 0, 0, tiled=True)  20.8 us
    pallas_call x4, Pallas kernels, _local_call(): pl.pallas_call(kernel, out_shape=jax.ShapeDtypeStruct(out_shape, jnp.floa...  9.02 us
    dot_general x1, matrix products, shards(): jnp.dot(place_hot, payload, precision=HIGHEST, preferred_element_type=jnp...  3.74 us
  transfers between devices with their start and end apart: 16, of which 11 were waited for; matrix products, arithmetic and copies ran while one was open for 1% of the time, Pallas kernels for 0%

profile of v8, /device:TPU:1, one launch (start us, length us, event | category | flops | bytes accessed | tf_op | source)
XLA Modules:
  0.0 172.4 jit_solution(18029199915135687534)
XLA Ops:
  0.7 1.4 fusion.5
  2.7 3.7 %fusion = f32[2048,4]{0,1:T(4,128)S(1)} fusion(s32[1024]{0:T(1024)S(1)} %convert_add_fusion, f32[1024,3]{0,1:T(4,128)S(1)} %bitcast.108, f32[1024,1]{0,1:T(1,128)S(1)} %bitcast.105), kind=kOutput, calls=%fused_computation.1 | convolution fusion | flops 102764544 | bytes 53248 | tf_op jit(solution)/shard_map/dot_general | solution.py:283
  6.5 0.1 reshape.59
  6.6 0.1 copy.31
  6.7 0.1 reshape.67
  6.8 20.8 %all_to_all.14 = f32[64,1,128]{2,1,0:T(1,128)S(1)} all-to-all(f32[64,1,128]{2,1,0:T(1,128)S(1)} %reshape.67), channel_id=1, replica_groups=mesh['wide'=64,'narrow'=8] {'wide'}, dimensions={0} | all-to-all | bytes 65536 | tf_op jit(solution)/shard_map/all_to_all | solution.py:284
  27.6 0.5 broadcast.52
  28.1 0.7 reduce
  28.9 0.1 reshape.68
  29.0 0.1 reshape.60
  29.2 0.3 fusion.14
  29.5 1.1 fusion.17
  30.7 2.2 %fusion.3 = f32[128,256]{1,0:T(8,128)S(1)} fusion(f32[2048,32]{1,0:T(8,128)S(1)} %fusion.14, f32[2048,32]{1,0:T(8,128)S(1)} %get-tuple-element.20, f32[2048,32]{1,0:T(8,128)S(1)} %get-tuple-element.21, f32[2048,32]{1,0:T(8,128)S(1)} %get-tuple-element.19, s32[2048]{0:T(1024)S(1)} %bitcast.93), kind=kOutput, calls=%fused_computation.6 | convolution fusion | flops 806617088 | bytes 1187840 | tf_op jit(solution)/shard_map/pa,pb->ab/dot_general | solution.py:292
  32.9 0.0 copy-start.6
  33.0 2.8 %collective-permute-start = (f32[3,2,16,256]{3,2,1,0:T(8,128)S(1)}, f32[3,2,16,256]{3,2,1,0:T(8,128)S(1)}, u32[]{:S(2)}, u32[]{:S(2)}) collective-permute-start(f32[3,2,16,256]{3,2,1,0:T(8,128)S(1)} %bitcast.77), channel_id=1, source_target_pairs={{0,8},{8,16},{16,24},{24,32},{32,40},{40,48},{48,56},{56,64},{64,7... | collective-permute-start | bytes 294920 | tf_op jit(solution)/shard_map/ppermute | solution.py:253
  35.7 1.9 %collective-permute-start.1 = (f32[3,2,16,256]{3,2,1,0:T(8,128)S(1)}, f32[3,2,16,256]{3,2,1,0:T(8,128)S(1)}, u32[]{:S(2)}, u32[]{:S(2)}) collective-permute-start(f32[3,2,16,256]{3,2,1,0:T(8,128)S(1)} %bitcast.78), channel_id=1, source_target_pairs={{8,0},{16,8},{24,16},{32,24},{40,32},{48,40},{56,48},{64,56},{72,6... | collective-permute-start | bytes 294920 | tf_op jit(solution)/shard_map/ppermute | solution.py:253
  37.7 4.0 %collective-permute-done.1 = f32[3,2,16,256]{3,2,1,0:T(8,128)S(1)} collective-permute-done((f32[3,2,16,256]{3,2,1,0:T(8,128)S(1)}, f32[3,2,16,256]{3,2,1,0:T(8,128)S(1)}, u32[]{:S(2)}, u32[]{:S(2)}) %collective-permute-start.1) | collective-permute-done | bytes 98336 | tf_op jit(solution)/shard_map/ppermute | solution.py:253
  41.7 0.1 fusion.30
  41.7 4.0 %collective-permute-start.2 = (f32[3,3,2,16,256]{4,3,2,1,0:T(8,128)S(1)}, f32[3,3,2,16,256]{4,3,2,1,0:T(8,128)S(1)}, u32[]{:S(2)}, u32[]{:S(2)}) collective-permute-start(f32[3,3,2,16,256]{4,3,2,1,0:T(8,128)S(1)} %get-tuple-element.7), channel_id=1, source_target_pairs={{0,1},{1,2},{2,3},{3,4},{4,5},{5,6},{6,7},{8,9},{9,10},{10,11},{11... | collective-permute-start | bytes 884744 | tf_op jit(solution)/shard_map/ppermute | solution.py:253
  45.7 1.3 collective-permute-start.3
  47.1 0.7 reshape.58.tab_ref
  47.7 2.6 %collective-permute-done.2 = f32[3,3,2,16,256]{4,3,2,1,0:T(8,128)S(1)} collective-permute-done((f32[3,3,2,16,256]{4,3,2,1,0:T(8,128)S(1)}, f32[3,3,2,16,256]{4,3,2,1,0:T(8,128)S(1)}, u32[]{:S(2)}, u32[]{:S(2)}) %collective-permute-start.2) | collective-permute-done | bytes 294944 | tf_op jit(solution)/shard_map/ppermute | solution.py:253
  50.3 4.5 %collective-permute-done.3 = f32[3,3,2,16,256]{4,3,2,1,0:T(8,128)S(1)} collective-permute-done((f32[3,3,2,16,256]{4,3,2,1,0:T(8,128)S(1)}, f32[3,3,2,16,256]{4,3,2,1,0:T(8,128)S(1)}, u32[]{:S(2)}, u32[]{:S(2)}) %collective-permute-start.3) | collective-permute-done | bytes 294944 | tf_op jit(solution)/shard_map/ppermute | solution.py:253
  54.7 0.1 pad_maximum_fusion
  54.8 1.0 concatenate.20.src_ref
  55.8 1.9 %shard_map.68.refs_0_ = f32[2,16,256]{2,1,0:T(8,128)} custom-call(s32[54]{0:T(128)} %reshape.58.tab_ref, f32[3,19,16,256]{3,2,1,0:T(8,128)} %concatenate.20.src_ref), custom_call_target="tpu_custom_call" | custom-call | flops 163840 | bytes 966872 | tf_op jit(solution)/shard_map/pallas_call | solution.py:241
  57.8 5.1 %collective-permute-start.4 = (f32[2,16,256]{2,1,0:T(8,128)}, f32[2,16,256]{2,1,0:T(8,128)S(1)}, u32[]{:S(2)}, u32[]{:S(2)}) collective-permute-start(f32[2,16,256]{2,1,0:T(8,128)} %shard_map.68.refs_0_), channel_id=1, source_target_pairs={{0,8},{8,16},{16,24},{24,32},{32,40},{40,48},{48,56},{56,64},{64,7... | collective-permute-start | bytes 98312 | tf_op jit(solution)/shard_map/ppermute | solution.py:253
  62.9 1.9 %collective-permute-start.5 = (f32[2,16,256]{2,1,0:T(8,128)}, f32[2,16,256]{2,1,0:T(8,128)S(1)}, u32[]{:S(2)}, u32[]{:S(2)}) collective-permute-start(f32[2,16,256]{2,1,0:T(8,128)} %shard_map.68.refs_0_), channel_id=1, source_target_pairs={{8,0},{16,8},{24,16},{32,24},{40,32},{48,40},{56,48},{64,56},{72,6... | collective-permute-start | bytes 98312 | tf_op jit(solution)/shard_map/ppermute | solution.py:253
  64.8 3.5 %collective-permute-done.5 = f32[2,16,256]{2,1,0:T(8,128)S(1)} collective-permute-done((f32[2,16,256]{2,1,0:T(8,128)}, f32[2,16,256]{2,1,0:T(8,128)S(1)}, u32[]{:S(2)}, u32[]{:S(2)}) %collective-permute-start.5) | collective-permute-done | bytes 32800 | tf_op jit(solution)/shard_map/ppermute | solution.py:253
  68.3 0.8 fusion.29
  69.1 4.0 %collective-permute-start.6 = (f32[3,2,16,256]{3,2,1,0:T(8,128)S(1)}, f32[3,2,16,256]{3,2,1,0:T(8,128)S(1)}, u32[]{:S(2)}, u32[]{:S(2)}) collective-permute-start(f32[3,2,16,256]{3,2,1,0:T(8,128)S(1)} %get-tuple-element.13), channel_id=1, source_target_pairs={{0,1},{1,2},{2,3},{3,4},{4,5},{5,6},{6,7},{8,9},{9,10},{10,11},{11... | collective-permute-start | bytes 294920 | tf_op jit(solution)/shard_map/ppermute | solution.py:253
  73.1 1.3 collective-permute-start.7
  74.4 0.6 fusion.20
  75.0 5.3 %collective-permute-done.7 = f32[3,2,16,256]{3,2,1,0:T(8,128)S(1)} collective-permute-done((f32[3,2,16,256]{3,2,1,0:T(8,128)S(1)}, f32[3,2,16,256]{3,2,1,0:T(8,128)S(1)}, u32[]{:S(2)}, u32[]{:S(2)}) %collective-permute-start.7) | collective-permute-done | bytes 98336 | tf_op jit(solution)/shard_map/ppermute | solution.py:253
  80.4 0.7 concatenate.21.src_ref
  81.1 2.4 %shard_map.69.refs_1_ = f32[2,16,256]{2,1,0:T(8,128)} custom-call(s32[54]{0:T(128)} %reshape.58.tab_ref, f32[19,16,256]{2,1,0:T(8,128)} %concatenate.21.src_ref, f32[2,16,256]{2,1,0:T(8,128)} %bitcast.71), custom_call_target="tpu_custom_call" | custom-call | flops 491520 | bytes 377048 | tf_op jit(solution)/shard_map/pallas_call | solution.py:241
  83.5 3.6 %collective-permute-start.8 = (f32[2,16,256]{2,1,0:T(8,128)}, f32[2,16,256]{2,1,0:T(8,128)S(1)}, u32[]{:S(2)}, u32[]{:S(2)}) collective-permute-start(f32[2,16,256]{2,1,0:T(8,128)} %shard_map.69.refs_1_), channel_id=1, source_target_pairs={{0,8},{8,16},{16,24},{24,32},{32,40},{40,48},{48,56},{56,64},{64,7... | collective-permute-start | bytes 98312 | tf_op jit(solution)/shard_map/ppermute | solution.py:253
  87.0 1.9 %collective-permute-start.9 = (f32[2,16,256]{2,1,0:T(8,128)}, f32[2,16,256]{2,1,0:T(8,128)S(1)}, u32[]{:S(2)}, u32[]{:S(2)}) collective-permute-start(f32[2,16,256]{2,1,0:T(8,128)} %shard_map.69.refs_1_), channel_id=1, source_target_pairs={{8,0},{16,8},{24,16},{32,24},{40,32},{48,40},{56,48},{64,56},{72,6... | collective-permute-start | bytes 98312 | tf_op jit(solution)/shard_map/ppermute | solution.py:253
  89.0 3.5 %collective-permute-done.9 = f32[2,16,256]{2,1,0:T(8,128)S(1)} collective-permute-done((f32[2,16,256]{2,1,0:T(8,128)}, f32[2,16,256]{2,1,0:T(8,128)S(1)}, u32[]{:S(2)}, u32[]{:S(2)}) %collective-permute-start.9) | collective-permute-done | bytes 32800 | tf_op jit(solution)/shard_map/ppermute | solution.py:253
  92.5 0.8 fusion.28
  93.2 5.1 %collective-permute-start.10 = (f32[3,2,16,256]{3,2,1,0:T(8,128)S(1)}, f32[3,2,16,256]{3,2,1,0:T(8,128)S(1)}, u32[]{:S(2)}, u32[]{:S(2)}) collective-permute-start(f32[3,2,16,256]{3,2,1,0:T(8,128)S(1)} %get-tuple-element.11), channel_id=1, source_target_pairs={{0,1},{1,2},{2,3},{3,4},{4,5},{5,6},{6,7},{8,9},{9,10},{10,11},{11... | collective-permute-start | bytes 294920 | tf_op jit(solution)/shard_map/ppermute | solution.py:253
  98.3 1.3 collective-permute-start.11
  99.6 0.3 collective-permute-done.10
  99.9 3.7 %collective-permute-done.11 = f32[3,2,16,256]{3,2,1,0:T(8,128)S(1)} collective-permute-done((f32[3,2,16,256]{3,2,1,0:T(8,128)S(1)}, f32[3,2,16,256]{3,2,1,0:T(8,128)S(1)}, u32[]{:S(2)}, u32[]{:S(2)}) %collective-permute-start.11) | collective-permute-done | bytes 98336 | tf_op jit(solution)/shard_map/ppermute | solution.py:253
  103.7 0.7 concatenate.22.src_ref
  104.5 2.4 %shard_map.70 = f32[2,16,256]{2,1,0:T(8,128)} custom-call(s32[54]{0:T(128)} %reshape.58.tab_ref, f32[19,16,256]{2,1,0:T(8,128)} %concatenate.22.src_ref, f32[2,16,256]{2,1,0:T(8,128)} %bitcast.72), custom_call_target="tpu_custom_call" | custom-call | flops 491520 | bytes 377048 | tf_op jit(solution)/shard_map/pallas_call | solution.py:241
  106.8 0.8 multiply_subtract_fusion.1.refs_2_
  107.6 3.4 %collective-permute-start.12 = (f32[2,16,256]{2,1,0:T(8,128)S(1)}, f32[2,16,256]{2,1,0:T(8,128)S(1)}, u32[]{:S(2)}, u32[]{:S(2)}) collective-permute-start(f32[2,16,256]{2,1,0:T(8,128)S(1)} %multiply_subtract_fusion.1.refs_2_), channel_id=1, source_target_pairs={{0,8},{8,16},{16,24},{24,32},{32,40},{40,48},{48,56},{56,64},{64,7... | collective-permute-start | bytes 98312 | tf_op jit(solution)/shard_map/ppermute | solution.py:253
  111.0 1.9 %collective-permute-start.13 = (f32[2,16,256]{2,1,0:T(8,128)S(1)}, f32[2,16,256]{2,1,0:T(8,128)S(1)}, u32[]{:S(2)}, u32[]{:S(2)}) collective-permute-start(f32[2,16,256]{2,1,0:T(8,128)S(1)} %multiply_subtract_fusion.1.refs_2_), channel_id=1, source_target_pairs={{8,0},{16,8},{24,16},{32,24},{40,32},{48,40},{56,48},{64,56},{72,6... | collective-permute-start | bytes 98312 | tf_op jit(solution)/shard_map/ppermute | solution.py:253
  113.0 3.3 %collective-permute-done.13 = f32[2,16,256]{2,1,0:T(8,128)S(1)} collective-permute-done((f32[2,16,256]{2,1,0:T(8,128)S(1)}, f32[2,16,256]{2,1,0:T(8,128)S(1)}, u32[]{:S(2)}, u32[]{:S(2)}) %collective-permute-start.13) | collective-permute-done | bytes 32800 | tf_op jit(solution)/shard_map/ppermute | solution.py:253
  116.3 3.4 %collective-permute-start.14 = (f32[3,2,16,256]{3,2,1,0:T(8,128)S(1)}, f32[3,2,16,256]{3,2,1,0:T(8,128)S(1)}, u32[]{:S(2)}, u32[]{:S(2)}) collective-permute-start(f32[3,2,16,256]{3,2,1,0:T(8,128)S(1)} %get-tuple-element.9), channel_id=1, source_target_pairs={{0,1},{1,2},{2,3},{3,4},{4,5},{5,6},{6,7},{8,9},{9,10},{10,11},{11... | collective-permute-start | bytes 294920 | tf_op jit(solution)/shard_map/ppermute | solution.py:253
  119.7 1.5 collective-permute-start.15
  121.2 0.1 collective-permute-done.14
  121.3 3.7 %collective-permute-done.15 = f32[3,2,16,256]{3,2,1,0:T(8,128)S(1)} collective-permute-done((f32[3,2,16,256]{3,2,1,0:T(8,128)S(1)}, f32[3,2,16,256]{3,2,1,0:T(8,128)S(1)}, u32[]{:S(2)}, u32[]{:S(2)}) %collective-permute-start.15) | collective-permute-done | bytes 98336 | tf_op jit(solution)/shard_map/ppermute | solution.py:253
  125.1 0.7 concatenate.23.src_ref
  125.8 2.4 %shard_map.71 = f32[2,16,256]{2,1,0:T(8,128)} custom-call(s32[54]{0:T(128)} %reshape.58.tab_ref, f32[19,16,256]{2,1,0:T(8,128)} %concatenate.23.src_ref, f32[2,16,256]{2,1,0:T(8,128)} %bitcast.73), custom_call_target="tpu_custom_call" | custom-call | flops 491520 | bytes 377048 | tf_op jit(solution)/shard_map/pallas_call | solution.py:241
  128.2 1.4 multiply_subtract_fusion.refs_3_
  129.6 2.1 %shard_map.72 = f32[8,128]{1,0:T(8,128)} custom-call(f32[2,16,256]{2,1,0:T(8,128)} %shard_map.68.refs_0_, f32[2,16,256]{2,1,0:T(8,128)} %shard_map.69.refs_1_, f32[2,16,256]{2,1,0:T(8,128)} %copy-done.2, f32[2,16,256]{2,1,0:T(8,128)} %multiply_subtract_fusion.refs_3_), custom_call_target="tpu_custom_call" | custom-call | tf_op jit(solution)/shard_map/pallas_call | solution.py:313
  131.7 0.7 slice.32
  132.4 0.1 broadcast_in_dim.12
  132.5 0.1 broadcast_in_dim.13
  132.6 36.9 %all_to_all.15 = f32[512,1,32]{2,1,0:T(1,128)S(1)} all-to-all(f32[512,1,32]{2,1,0:T(1,128)S(1)} %broadcast_in_dim.13), channel_id=1, replica_groups=mesh['wide'=64,'narrow'=8] {'wide','narrow'}, dimensions={0} | all-to-all | bytes 131072 | tf_op jit(solution)/shard_map/all_to_all | solution.py:317
  169.6 0.7 copy.29
  170.3 2.1 %shard_map.73 = (f32[2,4096]{1,0:T(2,128)}, f32[2,4096]{1,0:T(2,128)}) custom-call(f32[32,512]{1,0:T(8,128)} %bitcast.82, f32[2,16,256]{2,1,0:T(8,128)} %shard_map.68.refs_0_, f32[2,16,256]{2,1,0:T(8,128)} %shard_map.69.refs_1_, f32[2,16,256]{2,1,0:T(8,128)} %copy-done.2, f32[2,16,256]{2,1,0:T(8,128)} %multiply_subtract_fusion.refs_3_), custom_call_target="tpu_custom_call" | custom-call | tf_op jit(solution)/shard_map/pallas_call | solution.py:319
  (31 shorter events, 0.2 us)
Async XLA Ops:
  0.6 1.4 copy-start.3
  0.6 2.1 %copy-start.4 = (s32[1024]{0:T(1024)S(1)}, s32[1024]{0:T(1024)}, u32[]{:S(2)}) copy-start(s32[1024]{0:T(1024)} %param.6) | copy-start | bytes 12292
  0.6 2.1 %copy-start.5 = (f32[3,1024]{1,0:T(4,128)S(1)}, f32[3,1024]{1,0:T(4,128)}, u32[]{:S(2)}) copy-start(f32[3,1024]{1,0:T(4,128)} %param.7) | copy-start | bytes 36868
  32.9 14.1 %copy-start.6 = (s32[1,1,2,27]{3,2,1,0:T(2,128)S(1)}, s32[1,1,2,27]{3,2,1,0:T(2,128)}, u32[]{:S(2)}) copy-start(s32[1,1,2,27]{3,2,1,0:T(2,128)} %param.9) | copy-start | bytes 652
  33.0 4.7 %collective-permute-start = (f32[3,2,16,256]{3,2,1,0:T(8,128)S(1)}, f32[3,2,16,256]{3,2,1,0:T(8,128)S(1)}, u32[]{:S(2)}, u32[]{:S(2)}) collective-permute-start(f32[3,2,16,256]{3,2,1,0:T(8,128)S(1)} %bitcast.77), channel_id=1, source_target_pairs={{0,8},{8,16},{16,24},{24,32},{32,40},{40,48},{48,56},{56,64},{64,7... | collective-permute-start | bytes 294920 | tf_op jit(solution)/shard_map/ppermute | solution.py:253
  35.7 5.9 %collective-permute-start.1 = (f32[3,2,16,256]{3,2,1,0:T(8,128)S(1)}, f32[3,2,16,256]{3,2,1,0:T(8,128)S(1)}, u32[]{:S(2)}, u32[]{:S(2)}) collective-permute-start(f32[3,2,16,256]{3,2,1,0:T(8,128)S(1)} %bitcast.78), channel_id=1, source_target_pairs={{8,0},{16,8},{24,16},{32,24},{40,32},{48,40},{56,48},{64,56},{72,6... | collective-permute-start | bytes 294920 | tf_op jit(solution)/shard_map/ppermute | solution.py:253
  41.7 8.5 %collective-permute-start.2 = (f32[3,3,2,16,256]{4,3,2,1,0:T(8,128)S(1)}, f32[3,3,2,16,256]{4,3,2,1,0:T(8,128)S(1)}, u32[]{:S(2)}, u32[]{:S(2)}) collective-permute-start(f32[3,3,2,16,256]{4,3,2,1,0:T(8,128)S(1)} %get-tuple-element.7), channel_id=1, source_target_pairs={{0,1},{1,2},{2,3},{3,4},{4,5},{5,6},{6,7},{8,9},{9,10},{10,11},{11... | collective-permute-start | bytes 884744 | tf_op jit(solution)/shard_map/ppermute | solution.py:253
  45.7 9.0 %collective-permute-start.3 = (f32[3,3,2,16,256]{4,3,2,1,0:T(8,128)S(1)}, f32[3,3,2,16,256]{4,3,2,1,0:T(8,128)S(1)}, u32[]{:S(2)}, u32[]{:S(2)}) collective-permute-start(f32[3,3,2,16,256]{4,3,2,1,0:T(8,128)S(1)} %get-tuple-element.7), channel_id=1, source_target_pairs={{1,0},{2,1},{3,2},{4,3},{5,4},{6,5},{7,6},{9,8},{10,9},{11,10},{12... | collective-permute-start | bytes 884744 | tf_op jit(solution)/shard_map/ppermute | solution.py:253
  57.8 7.0 %collective-permute-start.4 = (f32[2,16,256]{2,1,0:T(8,128)}, f32[2,16,256]{2,1,0:T(8,128)S(1)}, u32[]{:S(2)}, u32[]{:S(2)}) collective-permute-start(f32[2,16,256]{2,1,0:T(8,128)} %shard_map.68.refs_0_), channel_id=1, source_target_pairs={{0,8},{8,16},{16,24},{24,32},{32,40},{40,48},{48,56},{56,64},{64,7... | collective-permute-start | bytes 98312 | tf_op jit(solution)/shard_map/ppermute | solution.py:253
  62.9 5.4 %collective-permute-start.5 = (f32[2,16,256]{2,1,0:T(8,128)}, f32[2,16,256]{2,1,0:T(8,128)S(1)}, u32[]{:S(2)}, u32[]{:S(2)}) collective-permute-start(f32[2,16,256]{2,1,0:T(8,128)} %shard_map.68.refs_0_), channel_id=1, source_target_pairs={{8,0},{16,8},{24,16},{32,24},{40,32},{48,40},{56,48},{64,56},{72,6... | collective-permute-start | bytes 98312 | tf_op jit(solution)/shard_map/ppermute | solution.py:253
  69.1 5.9 %collective-permute-start.6 = (f32[3,2,16,256]{3,2,1,0:T(8,128)S(1)}, f32[3,2,16,256]{3,2,1,0:T(8,128)S(1)}, u32[]{:S(2)}, u32[]{:S(2)}) collective-permute-start(f32[3,2,16,256]{3,2,1,0:T(8,128)S(1)} %get-tuple-element.13), channel_id=1, source_target_pairs={{0,1},{1,2},{2,3},{3,4},{4,5},{5,6},{6,7},{8,9},{9,10},{10,11},{11... | collective-permute-start | bytes 294920 | tf_op jit(solution)/shard_map/ppermute | solution.py:253
  73.1 7.2 %collective-permute-start.7 = (f32[3,2,16,256]{3,2,1,0:T(8,128)S(1)}, f32[3,2,16,256]{3,2,1,0:T(8,128)S(1)}, u32[]{:S(2)}, u32[]{:S(2)}) collective-permute-start(f32[3,2,16,256]{3,2,1,0:T(8,128)S(1)} %get-tuple-element.13), channel_id=1, source_target_pairs={{1,0},{2,1},{3,2},{4,3},{5,4},{6,5},{7,6},{9,8},{10,9},{11,10},{12... | collective-permute-start | bytes 294920 | tf_op jit(solution)/shard_map/ppermute | solution.py:253
  83.5 5.5 %collective-permute-start.8 = (f32[2,16,256]{2,1,0:T(8,128)}, f32[2,16,256]{2,1,0:T(8,128)S(1)}, u32[]{:S(2)}, u32[]{:S(2)}) collective-permute-start(f32[2,16,256]{2,1,0:T(8,128)} %shard_map.69.refs_1_), channel_id=1, source_target_pairs={{0,8},{8,16},{16,24},{24,32},{32,40},{40,48},{48,56},{56,64},{64,7... | collective-permute-start | bytes 98312 | tf_op jit(solution)/shard_map/ppermute | solution.py:253
  87.0 5.4 %collective-permute-start.9 = (f32[2,16,256]{2,1,0:T(8,128)}, f32[2,16,256]{2,1,0:T(8,128)S(1)}, u32[]{:S(2)}, u32[]{:S(2)}) collective-permute-start(f32[2,16,256]{2,1,0:T(8,128)} %shard_map.69.refs_1_), channel_id=1, source_target_pairs={{8,0},{16,8},{24,16},{32,24},{40,32},{48,40},{56,48},{64,56},{72,6... | collective-permute-start | bytes 98312 | tf_op jit(solution)/shard_map/ppermute | solution.py:253
  93.2 6.7 %collective-permute-start.10 = (f32[3,2,16,256]{3,2,1,0:T(8,128)S(1)}, f32[3,2,16,256]{3,2,1,0:T(8,128)S(1)}, u32[]{:S(2)}, u32[]{:S(2)}) collective-permute-start(f32[3,2,16,256]{3,2,1,0:T(8,128)S(1)} %get-tuple-element.11), channel_id=1, source_target_pairs={{0,1},{1,2},{2,3},{3,4},{4,5},{5,6},{6,7},{8,9},{9,10},{10,11},{11... | collective-permute-start | bytes 294920 | tf_op jit(solution)/shard_map/ppermute | solution.py:253
  98.3 5.4 %collective-permute-start.11 = (f32[3,2,16,256]{3,2,1,0:T(8,128)S(1)}, f32[3,2,16,256]{3,2,1,0:T(8,128)S(1)}, u32[]{:S(2)}, u32[]{:S(2)}) collective-permute-start(f32[3,2,16,256]{3,2,1,0:T(8,128)S(1)} %get-tuple-element.11), channel_id=1, source_target_pairs={{1,0},{2,1},{3,2},{4,3},{5,4},{6,5},{7,6},{9,8},{10,9},{11,10},{12... | collective-permute-start | bytes 294920 | tf_op jit(solution)/shard_map/ppermute | solution.py:253
  103.7 3.2 %copy-start = (f32[2,16,256]{2,1,0:T(8,128)S(1)}, f32[2,16,256]{2,1,0:T(8,128)}, u32[]{:S(2)}) copy-start(f32[2,16,256]{2,1,0:T(8,128)} %shard_map.68.refs_0_) | copy-start | bytes 98308
  107.6 20.6 %copy-start.2 = (f32[2,16,256]{2,1,0:T(8,128)}, f32[2,16,256]{2,1,0:T(8,128)S(1)}, u32[]{:S(2)}) copy-start(f32[2,16,256]{2,1,0:T(8,128)S(1)} %multiply_subtract_fusion.1.refs_2_) | copy-start | bytes 98308
  107.6 5.4 %collective-permute-start.12 = (f32[2,16,256]{2,1,0:T(8,128)S(1)}, f32[2,16,256]{2,1,0:T(8,128)S(1)}, u32[]{:S(2)}, u32[]{:S(2)}) collective-permute-start(f32[2,16,256]{2,1,0:T(8,128)S(1)} %multiply_subtract_fusion.1.refs_2_), channel_id=1, source_target_pairs={{0,8},{8,16},{16,24},{24,32},{32,40},{40,48},{48,56},{56,64},{64,7... | collective-permute-start | bytes 98312 | tf_op jit(solution)/shard_map/ppermute | solution.py:253
  111.0 5.2 %collective-permute-start.13 = (f32[2,16,256]{2,1,0:T(8,128)S(1)}, f32[2,16,256]{2,1,0:T(8,128)S(1)}, u32[]{:S(2)}, u32[]{:S(2)}) collective-permute-start(f32[2,16,256]{2,1,0:T(8,128)S(1)} %multiply_subtract_fusion.1.refs_2_), channel_id=1, source_target_pairs={{8,0},{16,8},{24,16},{32,24},{40,32},{48,40},{56,48},{64,56},{72,6... | collective-permute-start | bytes 98312 | tf_op jit(solution)/shard_map/ppermute | solution.py:253
  116.3 5.0 %collective-permute-start.14 = (f32[3,2,16,256]{3,2,1,0:T(8,128)S(1)}, f32[3,2,16,256]{3,2,1,0:T(8,128)S(1)}, u32[]{:S(2)}, u32[]{:S(2)}) collective-permute-start(f32[3,2,16,256]{3,2,1,0:T(8,128)S(1)} %get-tuple-element.9), channel_id=1, source_target_pairs={{0,1},{1,2},{2,3},{3,4},{4,5},{5,6},{6,7},{8,9},{9,10},{10,11},{11... | collective-permute-start | bytes 294920 | tf_op jit(solution)/shard_map/ppermute | solution.py:253
  119.7 5.4 %collective-permute-start.15 = (f32[3,2,16,256]{3,2,1,0:T(8,128)S(1)}, f32[3,2,16,256]{3,2,1,0:T(8,128)S(1)}, u32[]{:S(2)}, u32[]{:S(2)}) collective-permute-start(f32[3,2,16,256]{3,2,1,0:T(8,128)S(1)} %get-tuple-element.9), channel_id=1, source_target_pairs={{1,0},{2,1},{3,2},{4,3},{5,4},{6,5},{7,6},{9,8},{10,9},{11,10},{12... | collective-permute-start | bytes 294920 | tf_op jit(solution)/shard_map/ppermute | solution.py:253
  125.0 3.2 %copy-start.1 = (f32[2,16,256]{2,1,0:T(8,128)S(1)}, f32[2,16,256]{2,1,0:T(8,128)}, u32[]{:S(2)}) copy-start(f32[2,16,256]{2,1,0:T(8,128)} %shard_map.69.refs_1_) | copy-start | bytes 98308

commit v9 on v8

--- a/solution.py
+++ b/solution.py
@@ -80,10 +80,9 @@
 
 def _gram_kernel(*refs):
     basis_ref, out_ref = refs[:-1], refs[-1]
-    row = lax.broadcasted_iota(jnp.int32, out_ref.shape, 0)
-    lane = lax.broadcasted_iota(jnp.int32, out_ref.shape, 1)
+    lane = lax.broadcasted_iota(jnp.int32, (1, 128), 1)
     count = len(basis_ref)
-    acc = jnp.zeros(out_ref.shape, jnp.float32)
+    acc = jnp.zeros((1, 128), jnp.float32)
     k = 0
     for i in range(count):
         for j in range(i, count):
@@ -93,10 +92,10 @@
             s, e = _spread(s, e, 0)
             s, e = _spread(s, e, 1)
             high, low = _two_sum(s, e)
-            acc = jnp.where((row == 0) & (lane == k), high, acc)
-            acc = jnp.where((row == 1) & (lane == k), low, acc)
+            acc = jnp.where(lane == k, high[0:1, :], acc)
+            acc = jnp.where(lane == 16 + k, low[0:1, :], acc)
             k += 1
-    out_ref[...] = acc
+    out_ref[...] = acc[:, 0 : out_ref.shape[1]]
 
 
 def _galerkin_kernel(parts_ref, *refs, lift=None):
@@ -191,7 +190,8 @@
     return (ex + 1) * 9 + (ey + 1) * 3 + (ez + 1)
 
 
-def _stencil_kernel(tab_ref, src_ref, diag_ref, out_ref, shift=0.0, scale=1.0):
+def _stencil_kernel(tab_ref, src_ref, diag_ref, *rest, shift=0.0, scale=1.0):
+    previous, out_ref = rest[:-1], rest[-1]
     row, y, z = _masks()
     bricks = out_ref.shape[0]
     for b in range(bricks):
@@ -213,7 +213,8 @@
             planes[ex] = lines[0] + 0.5 * (lo + hi)
         lo, hi = _neighbour_x(planes[0], planes[-1], planes[1], row)
         smoothed = planes[0] + 0.5 * (lo + hi)
-        out_ref[b] = ((diag_ref[b] + (2.0 - shift)) * own - 2.0 * smoothed) * scale
+        image = ((diag_ref[b] + (2.0 - shift)) * own - 2.0 * smoothed) * scale
+        out_ref[b] = 2.0 * image - previous[0][b] if previous else image
 
 
 def _divergence_kernel(tab_ref, src_ref, out_ref):
@@ -300,8 +301,8 @@
     basis = [right_side]
     kernel = functools.partial(_stencil_kernel, shift=SHIFT, scale=1.0 / SPAN)
     for k in range(ITERS):
-        image = _local_call(kernel, shape, [table, halo(basis[-1]), diagonal], 60 * bricks * 4096)
-        basis.append(image if k == 0 else 2.0 * image - basis[-2])
+        operands = [table, halo(basis[-1]), diagonal] + ([basis[-2]] if k > 0 else [])
+        basis.append(_local_call(kernel, shape, operands, 60 * bricks * 4096))
     lift = [[0.0] * ITERS for _ in range(ITERS + 1)]
     for k in range(ITERS):
         lift[k][k] = SHIFT
@@ -310,10 +311,9 @@
         else:
             lift[k - 1][k] = lift[k + 1][k] = 0.5 * SPAN
     vmem = pl.BlockSpec(memory_space=pltpu.VMEM)
-    partial_sums = pl.pallas_call(
-        _gram_kernel, out_shape=jax.ShapeDtypeStruct((8, 128), jnp.float32), in_specs=[vmem] * len(basis), out_specs=vmem
+    payload = pl.pallas_call(
+        _gram_kernel, out_shape=jax.ShapeDtypeStruct((1, 32), jnp.float32), in_specs=[vmem] * len(basis), out_specs=vmem
     )(*basis)
-    payload = partial_sums[0:2, 0:16].reshape(1, 32)
     gathered = lax.all_to_all(jnp.broadcast_to(payload, (devices, 32)), ("wide", "narrow"), 0, 0, tiled=True)
     flat = jax.ShapeDtypeStruct((bricks, ROWS * LANES), jnp.float32)
     solution, residual = pl.pallas_call(

time: 174 us -> 172 us (0.989)
    sub x2 -> x0, other arithmetic: 2.13 us -> none  [shards(): basis.append(image if k == 0 else 2.0 * image - basis[-2])]
where the time goes in v9:
time: 172 us; the launch traced here: 171 us
  blocking collectives  57.7 us (34%)
  starting transfers between devices  44.3 us (26%)
  waiting for transfers between devices  34.8 us (20%)
  Pallas kernels  13.2 us (8%)
  matrix products  7.35 us (4%)
  local copies, waits for them, and re-layouts  6.58 us (4%)
  other arithmetic  5.34 us (3%)
    ppermute x16, starting transfers between devices, _shift(): return lax.ppermute(field, axis, pairs)  44.3 us
    all_to_all x1, blocking collectives, shards(): lax.all_to_all(jnp.broadcast_to(payload, (devices, 32)), ('wide', 'narrow...  36.9 us
    ppermute x16, waiting for transfers between devices, _shift(): return lax.ppermute(field, axis, pairs)  34.8 us
    all_to_all x1, blocking collectives, shards(): lax.all_to_all(send.reshape(owners, CAP, 4), 'wide', 0, 0, tiled=True)  20.8 us
    pallas_call x4, Pallas kernels, _local_call(): pl.pallas_call(kernel, out_shape=jax.ShapeDtypeStruct(out_shape, jnp.floa...  9.01 us
    dot_general x1, matrix products, shards(): jnp.dot(place_hot, payload, precision=HIGHEST, preferred_element_type=jnp...  3.74 us
  transfers between devices with their start and end apart: 16, of which 11 were waited for; matrix products, arithmetic and copies ran while one was open for 1% of the time, Pallas kernels for 0%

profile of v9, /device:TPU:1, one launch (start us, length us, event | category | flops | bytes accessed | tf_op | source)
XLA Modules:
  0.0 171.1 jit_solution(8095138081228470353)
XLA Ops:
  0.7 1.4 fusion.5
  2.7 3.7 %fusion = f32[2048,4]{0,1:T(4,128)S(1)} fusion(s32[1024]{0:T(1024)S(1)} %convert_add_fusion, f32[1024,3]{0,1:T(4,128)S(1)} %bitcast.110, f32[1024,1]{0,1:T(1,128)S(1)} %bitcast.106), kind=kOutput, calls=%fused_computation.1 | convolution fusion | flops 102764544 | bytes 53248 | tf_op jit(solution)/shard_map/dot_general | solution.py:284
  6.5 0.1 reshape.56
  6.6 0.1 copy.32
  6.7 0.1 reshape.64
  6.8 20.8 %all_to_all.14 = f32[64,1,128]{2,1,0:T(1,128)S(1)} all-to-all(f32[64,1,128]{2,1,0:T(1,128)S(1)} %reshape.64), channel_id=1, replica_groups=mesh['wide'=64,'narrow'=8] {'wide'}, dimensions={0} | all-to-all | bytes 65536 | tf_op jit(solution)/shard_map/all_to_all | solution.py:285
  27.6 0.5 broadcast.43
  28.1 0.7 reduce
  28.9 0.1 reshape.65
  29.0 0.1 reshape.57
  29.2 0.3 fusion.14
  29.5 1.1 fusion.17
  30.7 2.2 %fusion.3 = f32[128,256]{1,0:T(8,128)S(1)} fusion(f32[2048,32]{1,0:T(8,128)S(1)} %fusion.14, f32[2048,32]{1,0:T(8,128)S(1)} %get-tuple-element.20, f32[2048,32]{1,0:T(8,128)S(1)} %get-tuple-element.21, f32[2048,32]{1,0:T(8,128)S(1)} %get-tuple-element.19, s32[2048]{0:T(1024)S(1)} %bitcast.94), kind=kOutput, calls=%fused_computation.6 | convolution fusion | flops 806617088 | bytes 1187840 | tf_op jit(solution)/shard_map/pa,pb->ab/dot_general | solution.py:293
  32.9 0.0 copy-start.3
  33.0 2.8 %collective-permute-start = (f32[3,2,16,256]{3,2,1,0:T(8,128)S(1)}, f32[3,2,16,256]{3,2,1,0:T(8,128)S(1)}, u32[]{:S(2)}, u32[]{:S(2)}) collective-permute-start(f32[3,2,16,256]{3,2,1,0:T(8,128)S(1)} %bitcast.78), channel_id=1, source_target_pairs={{0,8},{8,16},{16,24},{24,32},{32,40},{40,48},{48,56},{56,64},{64,7... | collective-permute-start | bytes 294920 | tf_op jit(solution)/shard_map/ppermute | solution.py:254
  35.7 1.9 %collective-permute-start.1 = (f32[3,2,16,256]{3,2,1,0:T(8,128)S(1)}, f32[3,2,16,256]{3,2,1,0:T(8,128)S(1)}, u32[]{:S(2)}, u32[]{:S(2)}) collective-permute-start(f32[3,2,16,256]{3,2,1,0:T(8,128)S(1)} %bitcast.79), channel_id=1, source_target_pairs={{8,0},{16,8},{24,16},{32,24},{40,32},{48,40},{56,48},{64,56},{72,6... | collective-permute-start | bytes 294920 | tf_op jit(solution)/shard_map/ppermute | solution.py:254
  37.7 0.0 collective-permute-done
  37.7 4.0 %collective-permute-done.1 = f32[3,2,16,256]{3,2,1,0:T(8,128)S(1)} collective-permute-done((f32[3,2,16,256]{3,2,1,0:T(8,128)S(1)}, f32[3,2,16,256]{3,2,1,0:T(8,128)S(1)}, u32[]{:S(2)}, u32[]{:S(2)}) %collective-permute-start.1) | collective-permute-done | bytes 98336 | tf_op jit(solution)/shard_map/ppermute | solution.py:254
  41.7 0.1 fusion.30
  41.7 4.0 %collective-permute-start.2 = (f32[3,3,2,16,256]{4,3,2,1,0:T(8,128)S(1)}, f32[3,3,2,16,256]{4,3,2,1,0:T(8,128)S(1)}, u32[]{:S(2)}, u32[]{:S(2)}) collective-permute-start(f32[3,3,2,16,256]{4,3,2,1,0:T(8,128)S(1)} %get-tuple-element.7), channel_id=1, source_target_pairs={{0,1},{1,2},{2,3},{3,4},{4,5},{5,6},{6,7},{8,9},{9,10},{10,11},{11... | collective-permute-start | bytes 884744 | tf_op jit(solution)/shard_map/ppermute | solution.py:254
  45.7 1.3 collective-permute-start.3
  47.1 0.6 reshape.55.tab_ref
  47.7 2.6 %collective-permute-done.2 = f32[3,3,2,16,256]{4,3,2,1,0:T(8,128)S(1)} collective-permute-done((f32[3,3,2,16,256]{4,3,2,1,0:T(8,128)S(1)}, f32[3,3,2,16,256]{4,3,2,1,0:T(8,128)S(1)}, u32[]{:S(2)}, u32[]{:S(2)}) %collective-permute-start.2) | collective-permute-done | bytes 294944 | tf_op jit(solution)/shard_map/ppermute | solution.py:254
  50.3 4.5 %collective-permute-done.3 = f32[3,3,2,16,256]{4,3,2,1,0:T(8,128)S(1)} collective-permute-done((f32[3,3,2,16,256]{4,3,2,1,0:T(8,128)S(1)}, f32[3,3,2,16,256]{4,3,2,1,0:T(8,128)S(1)}, u32[]{:S(2)}, u32[]{:S(2)}) %collective-permute-start.3) | collective-permute-done | bytes 294944 | tf_op jit(solution)/shard_map/ppermute | solution.py:254
  54.7 0.1 pad_maximum_fusion
  54.8 1.0 concatenate.20.src_ref
  55.8 1.9 %shard_map.68.rest_0_.refs_0_ = f32[2,16,256]{2,1,0:T(8,128)} custom-call(s32[54]{0:T(128)} %reshape.55.tab_ref, f32[3,19,16,256]{3,2,1,0:T(8,128)} %concatenate.20.src_ref), custom_call_target="tpu_custom_call" | custom-call | flops 163840 | bytes 966872 | tf_op jit(solution)/shard_map/pallas_call | solution.py:242
  57.8 5.1 %collective-permute-start.4 = (f32[2,16,256]{2,1,0:T(8,128)}, f32[2,16,256]{2,1,0:T(8,128)S(1)}, u32[]{:S(2)}, u32[]{:S(2)}) collective-permute-start(f32[2,16,256]{2,1,0:T(8,128)} %shard_map.68.rest_0_.refs_0_), channel_id=1, source_target_pairs={{0,8},{8,16},{16,24},{24,32},{32,40},{40,48},{48,56},{56,64},{64,7... | collective-permute-start | bytes 98312 | tf_op jit(solution)/shard_map/ppermute | solution.py:254
  62.9 1.9 %collective-permute-start.5 = (f32[2,16,256]{2,1,0:T(8,128)}, f32[2,16,256]{2,1,0:T(8,128)S(1)}, u32[]{:S(2)}, u32[]{:S(2)}) collective-permute-start(f32[2,16,256]{2,1,0:T(8,128)} %shard_map.68.rest_0_.refs_0_), channel_id=1, source_target_pairs={{8,0},{16,8},{24,16},{32,24},{40,32},{48,40},{56,48},{64,56},{72,6... | collective-permute-start | bytes 98312 | tf_op jit(solution)/shard_map/ppermute | solution.py:254
  64.8 0.0 collective-permute-done.4
  64.8 3.5 %collective-permute-done.5 = f32[2,16,256]{2,1,0:T(8,128)S(1)} collective-permute-done((f32[2,16,256]{2,1,0:T(8,128)}, f32[2,16,256]{2,1,0:T(8,128)S(1)}, u32[]{:S(2)}, u32[]{:S(2)}) %collective-permute-start.5) | collective-permute-done | bytes 32800 | tf_op jit(solution)/shard_map/ppermute | solution.py:254
  68.3 0.8 fusion.29
  69.1 4.0 %collective-permute-start.6 = (f32[3,2,16,256]{3,2,1,0:T(8,128)S(1)}, f32[3,2,16,256]{3,2,1,0:T(8,128)S(1)}, u32[]{:S(2)}, u32[]{:S(2)}) collective-permute-start(f32[3,2,16,256]{3,2,1,0:T(8,128)S(1)} %get-tuple-element.13), channel_id=1, source_target_pairs={{0,1},{1,2},{2,3},{3,4},{4,5},{5,6},{6,7},{8,9},{9,10},{10,11},{11... | collective-permute-start | bytes 294920 | tf_op jit(solution)/shard_map/ppermute | solution.py:254
  73.1 1.3 collective-permute-start.7
  74.4 0.6 fusion.20
  75.0 5.3 %collective-permute-done.7 = f32[3,2,16,256]{3,2,1,0:T(8,128)S(1)} collective-permute-done((f32[3,2,16,256]{3,2,1,0:T(8,128)S(1)}, f32[3,2,16,256]{3,2,1,0:T(8,128)S(1)}, u32[]{:S(2)}, u32[]{:S(2)}) %collective-permute-start.7) | collective-permute-done | bytes 98336 | tf_op jit(solution)/shard_map/ppermute | solution.py:254
  80.3 0.7 concatenate.21.src_ref
  81.1 2.4 %shard_map.69.rest_0_.refs_1_ = f32[2,16,256]{2,1,0:T(8,128)} custom-call(s32[54]{0:T(128)} %reshape.55.tab_ref, f32[19,16,256]{2,1,0:T(8,128)} %concatenate.21.src_ref, f32[2,16,256]{2,1,0:T(8,128)} %bitcast.72), custom_call_target="tpu_custom_call" | custom-call | flops 491520 | bytes 377048 | tf_op jit(solution)/shard_map/pallas_call | solution.py:242
  83.4 3.6 %collective-permute-start.8 = (f32[2,16,256]{2,1,0:T(8,128)}, f32[2,16,256]{2,1,0:T(8,128)S(1)}, u32[]{:S(2)}, u32[]{:S(2)}) collective-permute-start(f32[2,16,256]{2,1,0:T(8,128)} %shard_map.69.rest_0_.refs_1_), channel_id=1, source_target_pairs={{0,8},{8,16},{16,24},{24,32},{32,40},{40,48},{48,56},{56,64},{64,7... | collective-permute-start | bytes 98312 | tf_op jit(solution)/shard_map/ppermute | solution.py:254
  87.0 1.9 %collective-permute-start.9 = (f32[2,16,256]{2,1,0:T(8,128)}, f32[2,16,256]{2,1,0:T(8,128)S(1)}, u32[]{:S(2)}, u32[]{:S(2)}) collective-permute-start(f32[2,16,256]{2,1,0:T(8,128)} %shard_map.69.rest_0_.refs_1_), channel_id=1, source_target_pairs={{8,0},{16,8},{24,16},{32,24},{40,32},{48,40},{56,48},{64,56},{72,6... | collective-permute-start | bytes 98312 | tf_op jit(solution)/shard_map/ppermute | solution.py:254
  88.9 0.0 collective-permute-done.8
  88.9 3.5 %collective-permute-done.9 = f32[2,16,256]{2,1,0:T(8,128)S(1)} collective-permute-done((f32[2,16,256]{2,1,0:T(8,128)}, f32[2,16,256]{2,1,0:T(8,128)S(1)}, u32[]{:S(2)}, u32[]{:S(2)}) %collective-permute-start.9) | collective-permute-done | bytes 32800 | tf_op jit(solution)/shard_map/ppermute | solution.py:254
  92.5 0.8 fusion.28
  93.2 5.1 %collective-permute-start.10 = (f32[3,2,16,256]{3,2,1,0:T(8,128)S(1)}, f32[3,2,16,256]{3,2,1,0:T(8,128)S(1)}, u32[]{:S(2)}, u32[]{:S(2)}) collective-permute-start(f32[3,2,16,256]{3,2,1,0:T(8,128)S(1)} %get-tuple-element.11), channel_id=1, source_target_pairs={{0,1},{1,2},{2,3},{3,4},{4,5},{5,6},{6,7},{8,9},{9,10},{10,11},{11... | collective-permute-start | bytes 294920 | tf_op jit(solution)/shard_map/ppermute | solution.py:254
  98.3 1.3 collective-permute-start.11
  99.6 0.3 collective-permute-done.10
  99.9 3.7 %collective-permute-done.11 = f32[3,2,16,256]{3,2,1,0:T(8,128)S(1)} collective-permute-done((f32[3,2,16,256]{3,2,1,0:T(8,128)S(1)}, f32[3,2,16,256]{3,2,1,0:T(8,128)S(1)}, u32[]{:S(2)}, u32[]{:S(2)}) %collective-permute-start.11) | collective-permute-done | bytes 98336 | tf_op jit(solution)/shard_map/ppermute | solution.py:254
  103.7 0.7 concatenate.22.src_ref
  104.5 2.4 %shard_map.70.refs_2_ = f32[2,16,256]{2,1,0:T(8,128)} custom-call(s32[54]{0:T(128)} %reshape.55.tab_ref, f32[19,16,256]{2,1,0:T(8,128)} %concatenate.22.src_ref, f32[2,16,256]{2,1,0:T(8,128)} %bitcast.73, f32[2,16,256]{2,1,0:T(8,128)} %shard_map.68.rest_0_.refs_0_), custom_call_target="tpu_custom_call" | custom-call | flops 491520 | bytes 409816 | tf_op jit(solution)/shard_map/pallas_call | solution.py:242
  106.8 3.4 %collective-permute-start.12 = (f32[2,16,256]{2,1,0:T(8,128)}, f32[2,16,256]{2,1,0:T(8,128)S(1)}, u32[]{:S(2)}, u32[]{:S(2)}) collective-permute-start(f32[2,16,256]{2,1,0:T(8,128)} %shard_map.70.refs_2_), channel_id=1, source_target_pairs={{0,8},{8,16},{16,24},{24,32},{32,40},{40,48},{48,56},{56,64},{64,7... | collective-permute-start | bytes 98312 | tf_op jit(solution)/shard_map/ppermute | solution.py:254
  110.3 1.9 %collective-permute-start.13 = (f32[2,16,256]{2,1,0:T(8,128)}, f32[2,16,256]{2,1,0:T(8,128)S(1)}, u32[]{:S(2)}, u32[]{:S(2)}) collective-permute-start(f32[2,16,256]{2,1,0:T(8,128)} %shard_map.70.refs_2_), channel_id=1, source_target_pairs={{8,0},{16,8},{24,16},{32,24},{40,32},{48,40},{56,48},{64,56},{72,6... | collective-permute-start | bytes 98312 | tf_op jit(solution)/shard_map/ppermute | solution.py:254
  112.2 3.5 %collective-permute-done.13 = f32[2,16,256]{2,1,0:T(8,128)S(1)} collective-permute-done((f32[2,16,256]{2,1,0:T(8,128)}, f32[2,16,256]{2,1,0:T(8,128)S(1)}, u32[]{:S(2)}, u32[]{:S(2)}) %collective-permute-start.13) | collective-permute-done | bytes 32800 | tf_op jit(solution)/shard_map/ppermute | solution.py:254
  115.7 0.8 fusion.27
  116.5 3.4 %collective-permute-start.14 = (f32[3,2,16,256]{3,2,1,0:T(8,128)S(1)}, f32[3,2,16,256]{3,2,1,0:T(8,128)S(1)}, u32[]{:S(2)}, u32[]{:S(2)}) collective-permute-start(f32[3,2,16,256]{3,2,1,0:T(8,128)S(1)} %get-tuple-element.9), channel_id=1, source_target_pairs={{0,1},{1,2},{2,3},{3,4},{4,5},{5,6},{6,7},{8,9},{9,10},{10,11},{11... | collective-permute-start | bytes 294920 | tf_op jit(solution)/shard_map/ppermute | solution.py:254
  119.9 1.5 collective-permute-start.15
  121.3 0.1 collective-permute-done.14
  121.5 3.7 %collective-permute-done.15 = f32[3,2,16,256]{3,2,1,0:T(8,128)S(1)} collective-permute-done((f32[3,2,16,256]{3,2,1,0:T(8,128)S(1)}, f32[3,2,16,256]{3,2,1,0:T(8,128)S(1)}, u32[]{:S(2)}, u32[]{:S(2)}) %collective-permute-start.15) | collective-permute-done | bytes 98336 | tf_op jit(solution)/shard_map/ppermute | solution.py:254
  125.3 0.7 concatenate.23.src_ref
  126.0 2.4 %shard_map.71.refs_3_ = f32[2,16,256]{2,1,0:T(8,128)} custom-call(s32[54]{0:T(128)} %reshape.55.tab_ref, f32[19,16,256]{2,1,0:T(8,128)} %concatenate.23.src_ref, f32[2,16,256]{2,1,0:T(8,128)} %bitcast.74, f32[2,16,256]{2,1,0:T(8,128)} %shard_map.69.rest_0_.refs_1_), custom_call_target="tpu_custom_call" | custom-call | flops 491520 | bytes 409816 | tf_op jit(solution)/shard_map/pallas_call | solution.py:242
  128.4 2.1 %shard_map.72 = f32[1,32]{1,0:T(1,128)} custom-call(f32[2,16,256]{2,1,0:T(8,128)} %shard_map.68.rest_0_.refs_0_, f32[2,16,256]{2,1,0:T(8,128)} %shard_map.69.rest_0_.refs_1_, f32[2,16,256]{2,1,0:T(8,128)} %shard_map.70.refs_2_, f32[2,16,256]{2,1,0:T(8,128)} %shard_map.71.refs_3_), custom_call_target="tpu_custom_call" | custom-call | tf_op jit(solution)/shard_map/pallas_call | solution.py:314
  130.4 0.8 broadcast_in_dim.10
  131.2 36.9 %all_to_all.15 = f32[512,1,32]{2,1,0:T(1,128)S(1)} all-to-all(f32[512,1,32]{2,1,0:T(1,128)S(1)} %broadcast_in_dim.10), channel_id=1, replica_groups=mesh['wide'=64,'narrow'=8] {'wide','narrow'}, dimensions={0} | all-to-all | bytes 131072 | tf_op jit(solution)/shard_map/all_to_all | solution.py:317
  168.2 0.7 copy.30
  168.9 2.1 %shard_map.73 = (f32[2,4096]{1,0:T(2,128)}, f32[2,4096]{1,0:T(2,128)}) custom-call(f32[32,512]{1,0:T(8,128)} %bitcast.83, f32[2,16,256]{2,1,0:T(8,128)} %shard_map.68.rest_0_.refs_0_, f32[2,16,256]{2,1,0:T(8,128)} %shard_map.69.rest_0_.refs_1_, f32[2,16,256]{2,1,0:T(8,128)} %shard_map.70.refs_2_, f32[2,16,256]{2,1,0:T(8,128)} %shard_map.71.refs_3_), custom_call_target="tpu_custom_call" | custom-call | tf_op jit(solution)/shard_map/pallas_call | solution.py:319
  (21 shorter events, 0.2 us)
Async XLA Ops:
  0.6 1.4 copy-start
  0.6 2.1 %copy-start.1 = (s32[1024]{0:T(1024)S(1)}, s32[1024]{0:T(1024)}, u32[]{:S(2)}) copy-start(s32[1024]{0:T(1024)} %param.6) | copy-start | bytes 12292
  0.6 2.1 %copy-start.2 = (f32[3,1024]{1,0:T(4,128)S(1)}, f32[3,1024]{1,0:T(4,128)}, u32[]{:S(2)}) copy-start(f32[3,1024]{1,0:T(4,128)} %param.7) | copy-start | bytes 36868
  32.9 14.1 %copy-start.3 = (s32[1,1,2,27]{3,2,1,0:T(2,128)S(1)}, s32[1,1,2,27]{3,2,1,0:T(2,128)}, u32[]{:S(2)}) copy-start(s32[1,1,2,27]{3,2,1,0:T(2,128)} %param.9) | copy-start | bytes 652
  33.0 4.7 %collective-permute-start = (f32[3,2,16,256]{3,2,1,0:T(8,128)S(1)}, f32[3,2,16,256]{3,2,1,0:T(8,128)S(1)}, u32[]{:S(2)}, u32[]{:S(2)}) collective-permute-start(f32[3,2,16,256]{3,2,1,0:T(8,128)S(1)} %bitcast.78), channel_id=1, source_target_pairs={{0,8},{8,16},{16,24},{24,32},{32,40},{40,48},{48,56},{56,64},{64,7... | collective-permute-start | bytes 294920 | tf_op jit(solution)/shard_map/ppermute | solution.py:254
  35.7 5.9 %collective-permute-start.1 = (f32[3,2,16,256]{3,2,1,0:T(8,128)S(1)}, f32[3,2,16,256]{3,2,1,0:T(8,128)S(1)}, u32[]{:S(2)}, u32[]{:S(2)}) collective-permute-start(f32[3,2,16,256]{3,2,1,0:T(8,128)S(1)} %bitcast.79), channel_id=1, source_target_pairs={{8,0},{16,8},{24,16},{32,24},{40,32},{48,40},{56,48},{64,56},{72,6... | collective-permute-start | bytes 294920 | tf_op jit(solution)/shard_map/ppermute | solution.py:254
  41.7 8.5 %collective-permute-start.2 = (f32[3,3,2,16,256]{4,3,2,1,0:T(8,128)S(1)}, f32[3,3,2,16,256]{4,3,2,1,0:T(8,128)S(1)}, u32[]{:S(2)}, u32[]{:S(2)}) collective-permute-start(f32[3,3,2,16,256]{4,3,2,1,0:T(8,128)S(1)} %get-tuple-element.7), channel_id=1, source_target_pairs={{0,1},{1,2},{2,3},{3,4},{4,5},{5,6},{6,7},{8,9},{9,10},{10,11},{11... | collective-permute-start | bytes 884744 | tf_op jit(solution)/shard_map/ppermute | solution.py:254
  45.7 9.0 %collective-permute-start.3 = (f32[3,3,2,16,256]{4,3,2,1,0:T(8,128)S(1)}, f32[3,3,2,16,256]{4,3,2,1,0:T(8,128)S(1)}, u32[]{:S(2)}, u32[]{:S(2)}) collective-permute-start(f32[3,3,2,16,256]{4,3,2,1,0:T(8,128)S(1)} %get-tuple-element.7), channel_id=1, source_target_pairs={{1,0},{2,1},{3,2},{4,3},{5,4},{6,5},{7,6},{9,8},{10,9},{11,10},{12... | collective-permute-start | bytes 884744 | tf_op jit(solution)/shard_map/ppermute | solution.py:254
  57.8 7.0 %collective-permute-start.4 = (f32[2,16,256]{2,1,0:T(8,128)}, f32[2,16,256]{2,1,0:T(8,128)S(1)}, u32[]{:S(2)}, u32[]{:S(2)}) collective-permute-start(f32[2,16,256]{2,1,0:T(8,128)} %shard_map.68.rest_0_.refs_0_), channel_id=1, source_target_pairs={{0,8},{8,16},{16,24},{24,32},{32,40},{40,48},{48,56},{56,64},{64,7... | collective-permute-start | bytes 98312 | tf_op jit(solution)/shard_map/ppermute | solution.py:254
  62.9 5.4 %collective-permute-start.5 = (f32[2,16,256]{2,1,0:T(8,128)}, f32[2,16,256]{2,1,0:T(8,128)S(1)}, u32[]{:S(2)}, u32[]{:S(2)}) collective-permute-start(f32[2,16,256]{2,1,0:T(8,128)} %shard_map.68.rest_0_.refs_0_), channel_id=1, source_target_pairs={{8,0},{16,8},{24,16},{32,24},{40,32},{48,40},{56,48},{64,56},{72,6... | collective-permute-start | bytes 98312 | tf_op jit(solution)/shard_map/ppermute | solution.py:254
  69.1 5.9 %collective-permute-start.6 = (f32[3,2,16,256]{3,2,1,0:T(8,128)S(1)}, f32[3,2,16,256]{3,2,1,0:T(8,128)S(1)}, u32[]{:S(2)}, u32[]{:S(2)}) collective-permute-start(f32[3,2,16,256]{3,2,1,0:T(8,128)S(1)} %get-tuple-element.13), channel_id=1, source_target_pairs={{0,1},{1,2},{2,3},{3,4},{4,5},{5,6},{6,7},{8,9},{9,10},{10,11},{11... | collective-permute-start | bytes 294920 | tf_op jit(solution)/shard_map/ppermute | solution.py:254
  73.1 7.2 %collective-permute-start.7 = (f32[3,2,16,256]{3,2,1,0:T(8,128)S(1)}, f32[3,2,16,256]{3,2,1,0:T(8,128)S(1)}, u32[]{:S(2)}, u32[]{:S(2)}) collective-permute-start(f32[3,2,16,256]{3,2,1,0:T(8,128)S(1)} %get-tuple-element.13), channel_id=1, source_target_pairs={{1,0},{2,1},{3,2},{4,3},{5,4},{6,5},{7,6},{9,8},{10,9},{11,10},{12... | collective-permute-start | bytes 294920 | tf_op jit(solution)/shard_map/ppermute | solution.py:254
  83.4 5.5 %collective-permute-start.8 = (f32[2,16,256]{2,1,0:T(8,128)}, f32[2,16,256]{2,1,0:T(8,128)S(1)}, u32[]{:S(2)}, u32[]{:S(2)}) collective-permute-start(f32[2,16,256]{2,1,0:T(8,128)} %shard_map.69.rest_0_.refs_1_), channel_id=1, source_target_pairs={{0,8},{8,16},{16,24},{24,32},{32,40},{40,48},{48,56},{56,64},{64,7... | collective-permute-start | bytes 98312 | tf_op jit(solution)/shard_map/ppermute | solution.py:254
  87.0 5.4 %collective-permute-start.9 = (f32[2,16,256]{2,1,0:T(8,128)}, f32[2,16,256]{2,1,0:T(8,128)S(1)}, u32[]{:S(2)}, u32[]{:S(2)}) collective-permute-start(f32[2,16,256]{2,1,0:T(8,128)} %shard_map.69.rest_0_.refs_1_), channel_id=1, source_target_pairs={{8,0},{16,8},{24,16},{32,24},{40,32},{48,40},{56,48},{64,56},{72,6... | collective-permute-start | bytes 98312 | tf_op jit(solution)/shard_map/ppermute | solution.py:254
  93.2 6.7 %collective-permute-start.10 = (f32[3,2,16,256]{3,2,1,0:T(8,128)S(1)}, f32[3,2,16,256]{3,2,1,0:T(8,128)S(1)}, u32[]{:S(2)}, u32[]{:S(2)}) collective-permute-start(f32[3,2,16,256]{3,2,1,0:T(8,128)S(1)} %get-tuple-element.11), channel_id=1, source_target_pairs={{0,1},{1,2},{2,3},{3,4},{4,5},{5,6},{6,7},{8,9},{9,10},{10,11},{11... | collective-permute-start | bytes 294920 | tf_op jit(solution)/shard_map/ppermute | solution.py:254
  98.3 5.4 %collective-permute-start.11 = (f32[3,2,16,256]{3,2,1,0:T(8,128)S(1)}, f32[3,2,16,256]{3,2,1,0:T(8,128)S(1)}, u32[]{:S(2)}, u32[]{:S(2)}) collective-permute-start(f32[3,2,16,256]{3,2,1,0:T(8,128)S(1)} %get-tuple-element.11), channel_id=1, source_target_pairs={{1,0},{2,1},{3,2},{4,3},{5,4},{6,5},{7,6},{9,8},{10,9},{11,10},{12... | collective-permute-start | bytes 294920 | tf_op jit(solution)/shard_map/ppermute | solution.py:254
  106.8 5.4 %collective-permute-start.12 = (f32[2,16,256]{2,1,0:T(8,128)}, f32[2,16,256]{2,1,0:T(8,128)S(1)}, u32[]{:S(2)}, u32[]{:S(2)}) collective-permute-start(f32[2,16,256]{2,1,0:T(8,128)} %shard_map.70.refs_2_), channel_id=1, source_target_pairs={{0,8},{8,16},{16,24},{24,32},{32,40},{40,48},{48,56},{56,64},{64,7... | collective-permute-start | bytes 98312 | tf_op jit(solution)/shard_map/ppermute | solution.py:254
  110.3 5.4 %collective-permute-start.13 = (f32[2,16,256]{2,1,0:T(8,128)}, f32[2,16,256]{2,1,0:T(8,128)S(1)}, u32[]{:S(2)}, u32[]{:S(2)}) collective-permute-start(f32[2,16,256]{2,1,0:T(8,128)} %shard_map.70.refs_2_), channel_id=1, source_target_pairs={{8,0},{16,8},{24,16},{32,24},{40,32},{48,40},{56,48},{64,56},{72,6... | collective-permute-start | bytes 98312 | tf_op jit(solution)/shard_map/ppermute | solution.py:254
  116.5 5.0 %collective-permute-start.14 = (f32[3,2,16,256]{3,2,1,0:T(8,128)S(1)}, f32[3,2,16,256]{3,2,1,0:T(8,128)S(1)}, u32[]{:S(2)}, u32[]{:S(2)}) collective-permute-start(f32[3,2,16,256]{3,2,1,0:T(8,128)S(1)} %get-tuple-element.9), channel_id=1, source_target_pairs={{0,1},{1,2},{2,3},{3,4},{4,5},{5,6},{6,7},{8,9},{9,10},{10,11},{11... | collective-permute-start | bytes 294920 | tf_op jit(solution)/shard_map/ppermute | solution.py:254
  119.9 5.4 %collective-permute-start.15 = (f32[3,2,16,256]{3,2,1,0:T(8,128)S(1)}, f32[3,2,16,256]{3,2,1,0:T(8,128)S(1)}, u32[]{:S(2)}, u32[]{:S(2)}) collective-permute-start(f32[3,2,16,256]{3,2,1,0:T(8,128)S(1)} %get-tuple-element.9), channel_id=1, source_target_pairs={{1,0},{2,1},{3,2},{4,3},{5,4},{6,5},{7,6},{9,8},{10,9},{11,10},{12... | collective-permute-start | bytes 294920 | tf_op jit(solution)/shard_map/ppermute | solution.py:254

commit v10 on v9

--- a/solution.py
+++ b/solution.py
@@ -190,17 +190,18 @@
     return (ex + 1) * 9 + (ey + 1) * 3 + (ez + 1)
 
 
-def _stencil_kernel(tab_ref, src_ref, diag_ref, *rest, shift=0.0, scale=1.0):
+def _stencil_kernel(tab_ref, low_ref, mid_ref, high_ref, diag_ref, *rest, shift=0.0, scale=1.0):
     previous, out_ref = rest[:-1], rest[-1]
     row, y, z = _masks()
     bricks = out_ref.shape[0]
+    pieces = (low_ref, mid_ref, high_ref)
     for b in range(bricks):
-        own = src_ref[4 * bricks + b]
+        own = mid_ref[bricks + b]
 
         def brick(ex, ey, ez):
             if ex == 0 and ey == 0 and ez == 0:
                 return own
-            return src_ref[tab_ref[b * 27 + _column(ex, ey, ez)]]
+            return _lookup(pieces, tab_ref[b * 27 + _column(ex, ey, ez)], bricks)
 
         planes = {}
         for ex in (-1, 0, 1):
@@ -217,15 +218,16 @@
         out_ref[b] = 2.0 * image - previous[0][b] if previous else image
 
 
-def _divergence_kernel(tab_ref, src_ref, out_ref):
+def _divergence_kernel(tab_ref, low_ref, mid_ref, high_ref, out_ref):
     row, y, z = _masks()
     bricks = out_ref.shape[0]
+    pieces = (low_ref, mid_ref, high_ref)
     for b in range(bricks):
 
         def brick(k, ex, ey, ez):
             if ex == 0 and ey == 0 and ez == 0:
-                return src_ref[k, 4 * bricks + b]
-            return src_ref[k, tab_ref[b * 27 + _column(ex, ey, ez)]]
+                return mid_ref[k, bricks + b]
+            return _lookup(pieces, tab_ref[b * 27 + _column(ex, ey, ez)], bricks, (k,))
 
         lo, hi = _neighbour_x(brick(0, 0, 0, 0), brick(0, -1, 0, 0), brick(0, 1, 0, 0), row)
         change_x = hi - lo
@@ -257,10 +259,16 @@
 def halo(field):
     lead, bricks = field.shape[:-3], field.shape[-3]
     column = jnp.stack([_shift(field, "wide", -1), field, _shift(field, "wide", 1)], axis=-4)
-    block = jnp.stack([_shift(column, "narrow", -1), column, _shift(column, "narrow", 1)], axis=-4)
-    block = block.reshape(lead + (9 * bricks,) + field.shape[-2:])
-    zero = jnp.zeros(lead + (1,) + field.shape[-2:], field.dtype)
-    return jnp.concatenate([block, zero], axis=-3)
+    pieces = [_shift(column, "narrow", -1), column, _shift(column, "narrow", 1)]
+    return [p.reshape(lead + (3 * bricks,) + field.shape[-2:]) for p in pieces]
+
+
+def _lookup(pieces, k, bricks, lead=()):
+    q = k // bricks
+    j = jnp.minimum((q // 3) * bricks + (k - q * bricks), 3 * bricks - 1)
+    piece = q % 3
+    value = jnp.where(piece == 0, pieces[0][lead + (j,)], jnp.where(piece == 1, pieces[1][lead + (j,)], pieces[2][lead + (j,)]))
+    return jnp.where(k >= 9 * bricks, 0.0, value)
 
 
 def shards(point_owner, point_cell, normals, strip_count, neighbours):
@@ -296,12 +304,12 @@
     diagonal = 14.5 + 2.0 * splatted[3]
 
     shape = (bricks, ROWS, LANES)
-    right_side = _local_call(_divergence_kernel, shape, [table, halo(vector_field)], 20 * bricks * 4096)
+    right_side = _local_call(_divergence_kernel, shape, [table, *halo(vector_field)], 20 * bricks * 4096)
 
     basis = [right_side]
     kernel = functools.partial(_stencil_kernel, shift=SHIFT, scale=1.0 / SPAN)
     for k in range(ITERS):
-        operands = [table, halo(basis[-1]), diagonal] + ([basis[-2]] if k > 0 else [])
+        operands = [table, *halo(basis[-1]), diagonal] + ([basis[-2]] if k > 0 else [])
         basis.append(_local_call(kernel, shape, operands, 60 * bricks * 4096))
     lift = [[0.0] * ITERS for _ in range(ITERS + 1)]
     for k in range(ITERS):

time: 172 us -> 172 us (level)
    concatenate x4 -> x0, local copies, waits for them, and re-layouts: 3.27 us -> none  [halo(): return jnp.concatenate([block, zero], axis=-3)]
    unnamed x10 -> x34, local copies, waits for them, and re-layouts: 0.27 us -> 2.91 us
where the time goes in v10:
time: 172 us; the launch traced here: 171 us
  blocking collectives  57.8 us (34%)
  starting transfers between devices  44.3 us (26%)
  waiting for transfers between devices  34.8 us (20%)
  Pallas kernels  14.1 us (8%)
  matrix products  7.35 us (4%)
  local copies, waits for them, and re-layouts  5.89 us (3%)
  other arithmetic  5.16 us (3%)
    ppermute x16, starting transfers between devices, _shift(): return lax.ppermute(field, axis, pairs)  44.3 us
    all_to_all x1, blocking collectives, shards(): lax.all_to_all(jnp.broadcast_to(payload, (devices, 32)), ('wide', 'narrow...  37 us
    ppermute x16, waiting for transfers between devices, _shift(): return lax.ppermute(field, axis, pairs)  34.8 us
    all_to_all x1, blocking collectives, shards(): lax.all_to_all(send.reshape(owners, CAP, 4), 'wide', 0, 0, tiled=True)  20.8 us
    pallas_call x4, Pallas kernels, _local_call(): pl.pallas_call(kernel, out_shape=jax.ShapeDtypeStruct(out_shape, jnp.floa...  9.87 us
    dot_general x1, matrix products, shards(): jnp.dot(place_hot, payload, precision=HIGHEST, preferred_element_type=jnp...  3.74 us
  transfers between devices with their start and end apart: 16, of which 11 were waited for; matrix products, arithmetic and copies ran while one was open for 1% of the time, Pallas kernels for 0%

profile of v10, /device:TPU:1, one launch (start us, length us, event | category | flops | bytes accessed | tf_op | source)
XLA Modules:
  0.0 171.0 jit_solution(11856671638363924790)
XLA Ops:
  0.7 1.4 fusion.5
  2.7 3.7 %fusion = f32[2048,4]{0,1:T(4,128)S(1)} fusion(s32[1024]{0:T(1024)S(1)} %convert_add_fusion, f32[1024,3]{0,1:T(4,128)S(1)} %bitcast.98, f32[1024,1]{0,1:T(1,128)S(1)} %bitcast.94), kind=kOutput, calls=%fused_computation.1 | convolution fusion | flops 102764544 | bytes 53248 | tf_op jit(solution)/shard_map/dot_general | solution.py:292
  6.5 0.1 reshape.80
  6.6 0.1 copy.17
  6.7 0.1 reshape.96
  6.8 20.8 %all_to_all.14 = f32[64,1,128]{2,1,0:T(1,128)S(1)} all-to-all(f32[64,1,128]{2,1,0:T(1,128)S(1)} %reshape.96), channel_id=1, replica_groups=mesh['wide'=64,'narrow'=8] {'wide'}, dimensions={0} | all-to-all | bytes 65536 | tf_op jit(solution)/shard_map/all_to_all | solution.py:293
  27.6 0.5 broadcast.34
  28.1 0.7 reduce
  28.9 0.1 reshape.97
  29.0 0.1 reshape.81
  29.2 0.3 fusion.14
  29.5 1.1 fusion.17
  30.7 0.0 copy-start.15
  30.7 2.2 %fusion.3 = f32[128,256]{1,0:T(8,128)S(1)} fusion(f32[2048,32]{1,0:T(8,128)S(1)} %fusion.14, f32[2048,32]{1,0:T(8,128)S(1)} %get-tuple-element.12, f32[2048,32]{1,0:T(8,128)S(1)} %get-tuple-element.13, f32[2048,32]{1,0:T(8,128)S(1)} %get-tuple-element.11, s32[2048]{0:T(1024)S(1)} %bitcast.82), kind=kOutput, calls=%fused_computation.6 | convolution fusion | flops 806617088 | bytes 1187840 | tf_op jit(solution)/shard_map/pa,pb->ab/dot_general | solution.py:301
  33.0 2.8 %collective-permute-start = (f32[3,2,16,256]{3,2,1,0:T(8,128)S(1)}, f32[3,2,16,256]{3,2,1,0:T(8,128)S(1)}, u32[]{:S(2)}, u32[]{:S(2)}) collective-permute-start(f32[3,2,16,256]{3,2,1,0:T(8,128)S(1)} %bitcast.63), channel_id=1, source_target_pairs={{0,8},{8,16},{16,24},{24,32},{32,40},{40,48},{48,56},{56,64},{64,7... | collective-permute-start | bytes 294920 | tf_op jit(solution)/shard_map/ppermute | solution.py:256
  35.7 1.9 %collective-permute-start.1 = (f32[3,2,16,256]{3,2,1,0:T(8,128)S(1)}, f32[3,2,16,256]{3,2,1,0:T(8,128)S(1)}, u32[]{:S(2)}, u32[]{:S(2)}) collective-permute-start(f32[3,2,16,256]{3,2,1,0:T(8,128)S(1)} %bitcast.64), channel_id=1, source_target_pairs={{8,0},{16,8},{24,16},{32,24},{40,32},{48,40},{56,48},{64,56},{72,6... | collective-permute-start | bytes 294920 | tf_op jit(solution)/shard_map/ppermute | solution.py:256
  37.7 0.0 collective-permute-done
  37.7 4.0 %collective-permute-done.1 = f32[3,2,16,256]{3,2,1,0:T(8,128)S(1)} collective-permute-done((f32[3,2,16,256]{3,2,1,0:T(8,128)S(1)}, f32[3,2,16,256]{3,2,1,0:T(8,128)S(1)}, u32[]{:S(2)}, u32[]{:S(2)}) %collective-permute-start.1) | collective-permute-done | bytes 98336 | tf_op jit(solution)/shard_map/ppermute | solution.py:256
  41.7 4.0 %collective-permute-start.2 = (f32[3,3,2,16,256]{4,3,2,1,0:T(8,128)S(1)}, f32[3,3,2,16,256]{4,3,2,1,0:T(8,128)S(1)}, u32[]{:S(2)}, u32[]{:S(2)}) collective-permute-start(f32[3,3,2,16,256]{4,3,2,1,0:T(8,128)S(1)} %pad_maximum_fusion), channel_id=1, source_target_pairs={{0,1},{1,2},{2,3},{3,4},{4,5},{5,6},{6,7},{8,9},{9,10},{10,11},{11... | collective-permute-start | bytes 884744 | tf_op jit(solution)/shard_map/ppermute | solution.py:256
  45.7 1.3 collective-permute-start.3
  47.0 0.6 reshape.79.tab_ref
  47.6 2.6 %collective-permute-done.2 = f32[3,3,2,16,256]{4,3,2,1,0:T(8,128)S(1)} collective-permute-done((f32[3,3,2,16,256]{4,3,2,1,0:T(8,128)S(1)}, f32[3,3,2,16,256]{4,3,2,1,0:T(8,128)S(1)}, u32[]{:S(2)}, u32[]{:S(2)}) %collective-permute-start.2) | collective-permute-done | bytes 294944 | tf_op jit(solution)/shard_map/ppermute | solution.py:256
  50.2 4.5 %collective-permute-done.3 = f32[3,3,2,16,256]{4,3,2,1,0:T(8,128)S(1)} collective-permute-done((f32[3,3,2,16,256]{4,3,2,1,0:T(8,128)S(1)}, f32[3,3,2,16,256]{4,3,2,1,0:T(8,128)S(1)}, u32[]{:S(2)}, u32[]{:S(2)}) %collective-permute-start.3) | collective-permute-done | bytes 294944 | tf_op jit(solution)/shard_map/ppermute | solution.py:256
  54.7 0.7 copy-done.5
  55.4 2.0 %shard_map.68.rest_0_.refs_0_ = f32[2,16,256]{2,1,0:T(8,128)} custom-call(s32[54]{0:T(128)} %reshape.79.tab_ref, f32[3,6,16,256]{3,2,1,0:T(8,128)} %bitcast.69, f32[3,6,16,256]{3,2,1,0:T(8,128)} %bitcast.54, f32[3,6,16,256]{3,2,1,0:T(8,128)} %bitcast.70), custom_call_target="tpu_custom_call" | custom-call | flops 163840 | bytes 917720 | tf_op jit(solution)/shard_map/pallas_call | solution.py:244
  57.4 5.1 %collective-permute-start.4 = (f32[2,16,256]{2,1,0:T(8,128)}, f32[2,16,256]{2,1,0:T(8,128)S(1)}, u32[]{:S(2)}, u32[]{:S(2)}) collective-permute-start(f32[2,16,256]{2,1,0:T(8,128)} %shard_map.68.rest_0_.refs_0_), channel_id=1, source_target_pairs={{0,8},{8,16},{16,24},{24,32},{32,40},{40,48},{48,56},{56,64},{64,7... | collective-permute-start | bytes 98312 | tf_op jit(solution)/shard_map/ppermute | solution.py:256
  62.5 1.9 %collective-permute-start.5 = (f32[2,16,256]{2,1,0:T(8,128)}, f32[2,16,256]{2,1,0:T(8,128)S(1)}, u32[]{:S(2)}, u32[]{:S(2)}) collective-permute-start(f32[2,16,256]{2,1,0:T(8,128)} %shard_map.68.rest_0_.refs_0_), channel_id=1, source_target_pairs={{8,0},{16,8},{24,16},{32,24},{40,32},{48,40},{56,48},{64,56},{72,6... | collective-permute-start | bytes 98312 | tf_op jit(solution)/shard_map/ppermute | solution.py:256
  64.4 0.0 collective-permute-done.4
  64.4 3.5 %collective-permute-done.5 = f32[2,16,256]{2,1,0:T(8,128)S(1)} collective-permute-done((f32[2,16,256]{2,1,0:T(8,128)}, f32[2,16,256]{2,1,0:T(8,128)S(1)}, u32[]{:S(2)}, u32[]{:S(2)}) %collective-permute-start.5) | collective-permute-done | bytes 32800 | tf_op jit(solution)/shard_map/ppermute | solution.py:256
  67.9 0.8 pad_maximum_fusion.1
  68.7 4.0 %collective-permute-start.6 = (f32[3,2,16,256]{3,2,1,0:T(8,128)S(1)}, f32[3,2,16,256]{3,2,1,0:T(8,128)S(1)}, u32[]{:S(2)}, u32[]{:S(2)}) collective-permute-start(f32[3,2,16,256]{3,2,1,0:T(8,128)S(1)} %pad_maximum_fusion.1), channel_id=1, source_target_pairs={{0,1},{1,2},{2,3},{3,4},{4,5},{5,6},{6,7},{8,9},{9,10},{10,11},{11... | collective-permute-start | bytes 294920 | tf_op jit(solution)/shard_map/ppermute | solution.py:256
  72.7 1.3 collective-permute-start.7
  74.0 0.6 fusion.20
  74.6 0.0 collective-permute-done.6
  74.6 5.3 %collective-permute-done.7 = f32[3,2,16,256]{3,2,1,0:T(8,128)S(1)} collective-permute-done((f32[3,2,16,256]{3,2,1,0:T(8,128)S(1)}, f32[3,2,16,256]{3,2,1,0:T(8,128)S(1)}, u32[]{:S(2)}, u32[]{:S(2)}) %collective-permute-start.7) | collective-permute-done | bytes 98336 | tf_op jit(solution)/shard_map/ppermute | solution.py:256
  79.9 0.6 copy-done.9
  80.5 2.6 %shard_map.69.rest_0_.refs_1_ = f32[2,16,256]{2,1,0:T(8,128)} custom-call(s32[54]{0:T(128)} %reshape.79.tab_ref, f32[6,16,256]{2,1,0:T(8,128)} %bitcast.74, f32[6,16,256]{2,1,0:T(8,128)} %bitcast.66, f32[6,16,256]{2,1,0:T(8,128)} %bitcast.77, f32[2,16,256]{2,1,0:T(8,128)} %bitcast.59), custom_call_target="tpu_custom_call" | custom-call | flops 491520 | bytes 360664 | tf_op jit(solution)/shard_map/pallas_call | solution.py:244
  83.2 3.6 %collective-permute-start.8 = (f32[2,16,256]{2,1,0:T(8,128)}, f32[2,16,256]{2,1,0:T(8,128)S(1)}, u32[]{:S(2)}, u32[]{:S(2)}) collective-permute-start(f32[2,16,256]{2,1,0:T(8,128)} %shard_map.69.rest_0_.refs_1_), channel_id=1, source_target_pairs={{0,8},{8,16},{16,24},{24,32},{32,40},{40,48},{48,56},{56,64},{64,7... | collective-permute-start | bytes 98312 | tf_op jit(solution)/shard_map/ppermute | solution.py:256
  86.7 1.9 %collective-permute-start.9 = (f32[2,16,256]{2,1,0:T(8,128)}, f32[2,16,256]{2,1,0:T(8,128)S(1)}, u32[]{:S(2)}, u32[]{:S(2)}) collective-permute-start(f32[2,16,256]{2,1,0:T(8,128)} %shard_map.69.rest_0_.refs_1_), channel_id=1, source_target_pairs={{8,0},{16,8},{24,16},{32,24},{40,32},{48,40},{56,48},{64,56},{72,6... | collective-permute-start | bytes 98312 | tf_op jit(solution)/shard_map/ppermute | solution.py:256
  88.6 0.0 collective-permute-done.8
  88.7 3.5 %collective-permute-done.9 = f32[2,16,256]{2,1,0:T(8,128)S(1)} collective-permute-done((f32[2,16,256]{2,1,0:T(8,128)}, f32[2,16,256]{2,1,0:T(8,128)S(1)}, u32[]{:S(2)}, u32[]{:S(2)}) %collective-permute-start.9) | collective-permute-done | bytes 32800 | tf_op jit(solution)/shard_map/ppermute | solution.py:256
  92.2 0.8 pad_maximum_fusion.2
  92.9 5.1 %collective-permute-start.10 = (f32[3,2,16,256]{3,2,1,0:T(8,128)S(1)}, f32[3,2,16,256]{3,2,1,0:T(8,128)S(1)}, u32[]{:S(2)}, u32[]{:S(2)}) collective-permute-start(f32[3,2,16,256]{3,2,1,0:T(8,128)S(1)} %pad_maximum_fusion.2), channel_id=1, source_target_pairs={{0,1},{1,2},{2,3},{3,4},{4,5},{5,6},{6,7},{8,9},{9,10},{10,11},{11... | collective-permute-start | bytes 294920 | tf_op jit(solution)/shard_map/ppermute | solution.py:256
  98.0 1.3 collective-permute-start.11
  99.3 0.3 collective-permute-done.10
  99.6 3.7 %collective-permute-done.11 = f32[3,2,16,256]{3,2,1,0:T(8,128)S(1)} collective-permute-done((f32[3,2,16,256]{3,2,1,0:T(8,128)S(1)}, f32[3,2,16,256]{3,2,1,0:T(8,128)S(1)}, u32[]{:S(2)}, u32[]{:S(2)}) %collective-permute-start.11) | collective-permute-done | bytes 98336 | tf_op jit(solution)/shard_map/ppermute | solution.py:256
  103.4 0.6 copy-done.11
  104.0 2.6 %shard_map.70.refs_2_ = f32[2,16,256]{2,1,0:T(8,128)} custom-call(s32[54]{0:T(128)} %reshape.79.tab_ref, f32[6,16,256]{2,1,0:T(8,128)} %bitcast.76, f32[6,16,256]{2,1,0:T(8,128)} %bitcast.68, f32[6,16,256]{2,1,0:T(8,128)} %bitcast.79, f32[2,16,256]{2,1,0:T(8,128)} %bitcast.60, f32[2,16,256]{2,1,0:T(8,128)} %shard_map.68.rest_0_.refs_0_), custom_call_target="tpu_custom_call" | custom-call | flops 491520 | bytes 393432 | tf_op jit(solution)/shard_map/pallas_call | solution.py:244
  106.7 3.4 %collective-permute-start.12 = (f32[2,16,256]{2,1,0:T(8,128)}, f32[2,16,256]{2,1,0:T(8,128)S(1)}, u32[]{:S(2)}, u32[]{:S(2)}) collective-permute-start(f32[2,16,256]{2,1,0:T(8,128)} %shard_map.70.refs_2_), channel_id=1, source_target_pairs={{0,8},{8,16},{16,24},{24,32},{32,40},{40,48},{48,56},{56,64},{64,7... | collective-permute-start | bytes 98312 | tf_op jit(solution)/shard_map/ppermute | solution.py:256
  110.1 1.9 %collective-permute-start.13 = (f32[2,16,256]{2,1,0:T(8,128)}, f32[2,16,256]{2,1,0:T(8,128)S(1)}, u32[]{:S(2)}, u32[]{:S(2)}) collective-permute-start(f32[2,16,256]{2,1,0:T(8,128)} %shard_map.70.refs_2_), channel_id=1, source_target_pairs={{8,0},{16,8},{24,16},{32,24},{40,32},{48,40},{56,48},{64,56},{72,6... | collective-permute-start | bytes 98312 | tf_op jit(solution)/shard_map/ppermute | solution.py:256
  112.0 0.0 collective-permute-done.12
  112.0 3.5 %collective-permute-done.13 = f32[2,16,256]{2,1,0:T(8,128)S(1)} collective-permute-done((f32[2,16,256]{2,1,0:T(8,128)}, f32[2,16,256]{2,1,0:T(8,128)S(1)}, u32[]{:S(2)}, u32[]{:S(2)}) %collective-permute-start.13) | collective-permute-done | bytes 32800 | tf_op jit(solution)/shard_map/ppermute | solution.py:256
  115.5 0.8 pad_maximum_fusion.3
  116.3 3.4 %collective-permute-start.14 = (f32[3,2,16,256]{3,2,1,0:T(8,128)S(1)}, f32[3,2,16,256]{3,2,1,0:T(8,128)S(1)}, u32[]{:S(2)}, u32[]{:S(2)}) collective-permute-start(f32[3,2,16,256]{3,2,1,0:T(8,128)S(1)} %pad_maximum_fusion.3), channel_id=1, source_target_pairs={{0,1},{1,2},{2,3},{3,4},{4,5},{5,6},{6,7},{8,9},{9,10},{10,11},{11... | collective-permute-start | bytes 294920 | tf_op jit(solution)/shard_map/ppermute | solution.py:256
  119.7 1.5 collective-permute-start.15
  121.2 0.1 collective-permute-done.14
  121.3 3.7 %collective-permute-done.15 = f32[3,2,16,256]{3,2,1,0:T(8,128)S(1)} collective-permute-done((f32[3,2,16,256]{3,2,1,0:T(8,128)S(1)}, f32[3,2,16,256]{3,2,1,0:T(8,128)S(1)}, u32[]{:S(2)}, u32[]{:S(2)}) %collective-permute-start.15) | collective-permute-done | bytes 98336 | tf_op jit(solution)/shard_map/ppermute | solution.py:256
  125.0 0.6 copy-done.10
  125.7 2.6 %shard_map.71.refs_3_ = f32[2,16,256]{2,1,0:T(8,128)} custom-call(s32[54]{0:T(128)} %reshape.79.tab_ref, f32[6,16,256]{2,1,0:T(8,128)} %bitcast.75, f32[6,16,256]{2,1,0:T(8,128)} %bitcast.67, f32[6,16,256]{2,1,0:T(8,128)} %bitcast.78, f32[2,16,256]{2,1,0:T(8,128)} %bitcast.61, f32[2,16,256]{2,1,0:T(8,128)} %shard_map.69.rest_0_.refs_1_), custom_call_target="tpu_custom_call" | custom-call | flops 491520 | bytes 393432 | tf_op jit(solution)/shard_map/pallas_call | solution.py:244
  128.3 2.1 %shard_map.72 = f32[1,32]{1,0:T(1,128)} custom-call(f32[2,16,256]{2,1,0:T(8,128)} %shard_map.68.rest_0_.refs_0_, f32[2,16,256]{2,1,0:T(8,128)} %shard_map.69.rest_0_.refs_1_, f32[2,16,256]{2,1,0:T(8,128)} %shard_map.70.refs_2_, f32[2,16,256]{2,1,0:T(8,128)} %shard_map.71.refs_3_), custom_call_target="tpu_custom_call" | custom-call | tf_op jit(solution)/shard_map/pallas_call | solution.py:322
  130.4 0.8 broadcast_in_dim.10
  131.2 37.0 %all_to_all.15 = f32[512,1,32]{2,1,0:T(1,128)S(1)} all-to-all(f32[512,1,32]{2,1,0:T(1,128)S(1)} %broadcast_in_dim.10), channel_id=1, replica_groups=mesh['wide'=64,'narrow'=8] {'wide','narrow'}, dimensions={0} | all-to-all | bytes 131072 | tf_op jit(solution)/shard_map/all_to_all | solution.py:325
  168.1 0.7 copy.15
  168.9 2.1 %shard_map.73 = (f32[2,4096]{1,0:T(2,128)}, f32[2,4096]{1,0:T(2,128)}) custom-call(f32[32,512]{1,0:T(8,128)} %bitcast.71, f32[2,16,256]{2,1,0:T(8,128)} %shard_map.68.rest_0_.refs_0_, f32[2,16,256]{2,1,0:T(8,128)} %shard_map.69.rest_0_.refs_1_, f32[2,16,256]{2,1,0:T(8,128)} %shard_map.70.refs_2_, f32[2,16,256]{2,1,0:T(8,128)} %shard_map.71.refs_3_), custom_call_target="tpu_custom_call" | custom-call | tf_op jit(solution)/shard_map/pallas_call | solution.py:327
  (34 shorter events, 0.1 us)
Async XLA Ops:
  0.6 1.4 copy-start.12
  0.6 2.1 %copy-start.13 = (s32[1024]{0:T(1024)S(1)}, s32[1024]{0:T(1024)}, u32[]{:S(2)}) copy-start(s32[1024]{0:T(1024)} %param.6) | copy-start | bytes 12292
  0.6 2.1 %copy-start.14 = (f32[3,1024]{1,0:T(4,128)S(1)}, f32[3,1024]{1,0:T(4,128)}, u32[]{:S(2)}) copy-start(f32[3,1024]{1,0:T(4,128)} %param.7) | copy-start | bytes 36868
  30.7 16.3 %copy-start.15 = (s32[1,1,2,27]{3,2,1,0:T(2,128)S(1)}, s32[1,1,2,27]{3,2,1,0:T(2,128)}, u32[]{:S(2)}) copy-start(s32[1,1,2,27]{3,2,1,0:T(2,128)} %param.9) | copy-start | bytes 652
  33.0 4.7 %collective-permute-start = (f32[3,2,16,256]{3,2,1,0:T(8,128)S(1)}, f32[3,2,16,256]{3,2,1,0:T(8,128)S(1)}, u32[]{:S(2)}, u32[]{:S(2)}) collective-permute-start(f32[3,2,16,256]{3,2,1,0:T(8,128)S(1)} %bitcast.63), channel_id=1, source_target_pairs={{0,8},{8,16},{16,24},{24,32},{32,40},{40,48},{48,56},{56,64},{64,7... | collective-permute-start | bytes 294920 | tf_op jit(solution)/shard_map/ppermute | solution.py:256
  35.7 5.9 %collective-permute-start.1 = (f32[3,2,16,256]{3,2,1,0:T(8,128)S(1)}, f32[3,2,16,256]{3,2,1,0:T(8,128)S(1)}, u32[]{:S(2)}, u32[]{:S(2)}) collective-permute-start(f32[3,2,16,256]{3,2,1,0:T(8,128)S(1)} %bitcast.64), channel_id=1, source_target_pairs={{8,0},{16,8},{24,16},{32,24},{40,32},{48,40},{56,48},{64,56},{72,6... | collective-permute-start | bytes 294920 | tf_op jit(solution)/shard_map/ppermute | solution.py:256
  41.7 13.0 %copy-start = (f32[3,3,2,16,256]{4,3,2,1,0:T(8,128)}, f32[3,3,2,16,256]{4,3,2,1,0:T(8,128)S(1)}, u32[]{:S(2)}) copy-start(f32[3,3,2,16,256]{4,3,2,1,0:T(8,128)S(1)} %pad_maximum_fusion) | copy-start | bytes 884740
  41.7 8.5 %collective-permute-start.2 = (f32[3,3,2,16,256]{4,3,2,1,0:T(8,128)S(1)}, f32[3,3,2,16,256]{4,3,2,1,0:T(8,128)S(1)}, u32[]{:S(2)}, u32[]{:S(2)}) collective-permute-start(f32[3,3,2,16,256]{4,3,2,1,0:T(8,128)S(1)} %pad_maximum_fusion), channel_id=1, source_target_pairs={{0,1},{1,2},{2,3},{3,4},{4,5},{5,6},{6,7},{8,9},{9,10},{10,11},{11... | collective-permute-start | bytes 884744 | tf_op jit(solution)/shard_map/ppermute | solution.py:256
  45.7 9.0 %collective-permute-start.3 = (f32[3,3,2,16,256]{4,3,2,1,0:T(8,128)S(1)}, f32[3,3,2,16,256]{4,3,2,1,0:T(8,128)S(1)}, u32[]{:S(2)}, u32[]{:S(2)}) collective-permute-start(f32[3,3,2,16,256]{4,3,2,1,0:T(8,128)S(1)} %pad_maximum_fusion), channel_id=1, source_target_pairs={{1,0},{2,1},{3,2},{4,3},{5,4},{6,5},{7,6},{9,8},{10,9},{11,10},{12... | collective-permute-start | bytes 884744 | tf_op jit(solution)/shard_map/ppermute | solution.py:256
  50.2 4.5 %copy-start.4 = (f32[3,3,2,16,256]{4,3,2,1,0:T(8,128)}, f32[3,3,2,16,256]{4,3,2,1,0:T(8,128)S(1)}, u32[]{:S(2)}) copy-start(f32[3,3,2,16,256]{4,3,2,1,0:T(8,128)S(1)} %collective-permute-done.2) | copy-start | bytes 884740
  54.7 0.7 copy-start.5
  57.4 7.0 %collective-permute-start.4 = (f32[2,16,256]{2,1,0:T(8,128)}, f32[2,16,256]{2,1,0:T(8,128)S(1)}, u32[]{:S(2)}, u32[]{:S(2)}) collective-permute-start(f32[2,16,256]{2,1,0:T(8,128)} %shard_map.68.rest_0_.refs_0_), channel_id=1, source_target_pairs={{0,8},{8,16},{16,24},{24,32},{32,40},{40,48},{48,56},{56,64},{64,7... | collective-permute-start | bytes 98312 | tf_op jit(solution)/shard_map/ppermute | solution.py:256
  62.5 5.4 %collective-permute-start.5 = (f32[2,16,256]{2,1,0:T(8,128)}, f32[2,16,256]{2,1,0:T(8,128)S(1)}, u32[]{:S(2)}, u32[]{:S(2)}) collective-permute-start(f32[2,16,256]{2,1,0:T(8,128)} %shard_map.68.rest_0_.refs_0_), channel_id=1, source_target_pairs={{8,0},{16,8},{24,16},{32,24},{40,32},{48,40},{56,48},{64,56},{72,6... | collective-permute-start | bytes 98312 | tf_op jit(solution)/shard_map/ppermute | solution.py:256
  68.7 11.2 %copy-start.1 = (f32[3,2,16,256]{3,2,1,0:T(8,128)}, f32[3,2,16,256]{3,2,1,0:T(8,128)S(1)}, u32[]{:S(2)}) copy-start(f32[3,2,16,256]{3,2,1,0:T(8,128)S(1)} %pad_maximum_fusion.1) | copy-start | bytes 294916
  68.7 5.9 %collective-permute-start.6 = (f32[3,2,16,256]{3,2,1,0:T(8,128)S(1)}, f32[3,2,16,256]{3,2,1,0:T(8,128)S(1)}, u32[]{:S(2)}, u32[]{:S(2)}) collective-permute-start(f32[3,2,16,256]{3,2,1,0:T(8,128)S(1)} %pad_maximum_fusion.1), channel_id=1, source_target_pairs={{0,1},{1,2},{2,3},{3,4},{4,5},{5,6},{6,7},{8,9},{9,10},{10,11},{11... | collective-permute-start | bytes 294920 | tf_op jit(solution)/shard_map/ppermute | solution.py:256
  72.7 7.2 %collective-permute-start.7 = (f32[3,2,16,256]{3,2,1,0:T(8,128)S(1)}, f32[3,2,16,256]{3,2,1,0:T(8,128)S(1)}, u32[]{:S(2)}, u32[]{:S(2)}) collective-permute-start(f32[3,2,16,256]{3,2,1,0:T(8,128)S(1)} %pad_maximum_fusion.1), channel_id=1, source_target_pairs={{1,0},{2,1},{3,2},{4,3},{5,4},{6,5},{7,6},{9,8},{10,9},{11,10},{12... | collective-permute-start | bytes 294920 | tf_op jit(solution)/shard_map/ppermute | solution.py:256
  74.6 5.3 %copy-start.6 = (f32[3,2,16,256]{3,2,1,0:T(8,128)}, f32[3,2,16,256]{3,2,1,0:T(8,128)S(1)}, u32[]{:S(2)}) copy-start(f32[3,2,16,256]{3,2,1,0:T(8,128)S(1)} %collective-permute-done.6) | copy-start | bytes 294916
  79.9 0.6 copy-start.9
  83.2 5.5 %collective-permute-start.8 = (f32[2,16,256]{2,1,0:T(8,128)}, f32[2,16,256]{2,1,0:T(8,128)S(1)}, u32[]{:S(2)}, u32[]{:S(2)}) collective-permute-start(f32[2,16,256]{2,1,0:T(8,128)} %shard_map.69.rest_0_.refs_1_), channel_id=1, source_target_pairs={{0,8},{8,16},{16,24},{24,32},{32,40},{40,48},{48,56},{56,64},{64,7... | collective-permute-start | bytes 98312 | tf_op jit(solution)/shard_map/ppermute | solution.py:256
  86.7 5.4 %collective-permute-start.9 = (f32[2,16,256]{2,1,0:T(8,128)}, f32[2,16,256]{2,1,0:T(8,128)S(1)}, u32[]{:S(2)}, u32[]{:S(2)}) collective-permute-start(f32[2,16,256]{2,1,0:T(8,128)} %shard_map.69.rest_0_.refs_1_), channel_id=1, source_target_pairs={{8,0},{16,8},{24,16},{32,24},{40,32},{48,40},{56,48},{64,56},{72,6... | collective-permute-start | bytes 98312 | tf_op jit(solution)/shard_map/ppermute | solution.py:256
  92.9 10.4 %copy-start.3 = (f32[3,2,16,256]{3,2,1,0:T(8,128)}, f32[3,2,16,256]{3,2,1,0:T(8,128)S(1)}, u32[]{:S(2)}) copy-start(f32[3,2,16,256]{3,2,1,0:T(8,128)S(1)} %pad_maximum_fusion.2) | copy-start | bytes 294916
  92.9 6.7 %collective-permute-start.10 = (f32[3,2,16,256]{3,2,1,0:T(8,128)S(1)}, f32[3,2,16,256]{3,2,1,0:T(8,128)S(1)}, u32[]{:S(2)}, u32[]{:S(2)}) collective-permute-start(f32[3,2,16,256]{3,2,1,0:T(8,128)S(1)} %pad_maximum_fusion.2), channel_id=1, source_target_pairs={{0,1},{1,2},{2,3},{3,4},{4,5},{5,6},{6,7},{8,9},{9,10},{10,11},{11... | collective-permute-start | bytes 294920 | tf_op jit(solution)/shard_map/ppermute | solution.py:256
  98.0 5.4 %collective-permute-start.11 = (f32[3,2,16,256]{3,2,1,0:T(8,128)S(1)}, f32[3,2,16,256]{3,2,1,0:T(8,128)S(1)}, u32[]{:S(2)}, u32[]{:S(2)}) collective-permute-start(f32[3,2,16,256]{3,2,1,0:T(8,128)S(1)} %pad_maximum_fusion.2), channel_id=1, source_target_pairs={{1,0},{2,1},{3,2},{4,3},{5,4},{6,5},{7,6},{9,8},{10,9},{11,10},{12... | collective-permute-start | bytes 294920 | tf_op jit(solution)/shard_map/ppermute | solution.py:256
  99.6 3.8 %copy-start.8 = (f32[3,2,16,256]{3,2,1,0:T(8,128)}, f32[3,2,16,256]{3,2,1,0:T(8,128)S(1)}, u32[]{:S(2)}) copy-start(f32[3,2,16,256]{3,2,1,0:T(8,128)S(1)} %collective-permute-done.10) | copy-start | bytes 294916
  103.4 0.6 copy-start.11
  106.7 5.4 %collective-permute-start.12 = (f32[2,16,256]{2,1,0:T(8,128)}, f32[2,16,256]{2,1,0:T(8,128)S(1)}, u32[]{:S(2)}, u32[]{:S(2)}) collective-permute-start(f32[2,16,256]{2,1,0:T(8,128)} %shard_map.70.refs_2_), channel_id=1, source_target_pairs={{0,8},{8,16},{16,24},{24,32},{32,40},{40,48},{48,56},{56,64},{64,7... | collective-permute-start | bytes 98312 | tf_op jit(solution)/shard_map/ppermute | solution.py:256
  110.1 5.4 %collective-permute-start.13 = (f32[2,16,256]{2,1,0:T(8,128)}, f32[2,16,256]{2,1,0:T(8,128)S(1)}, u32[]{:S(2)}, u32[]{:S(2)}) collective-permute-start(f32[2,16,256]{2,1,0:T(8,128)} %shard_map.70.refs_2_), channel_id=1, source_target_pairs={{8,0},{16,8},{24,16},{32,24},{40,32},{48,40},{56,48},{64,56},{72,6... | collective-permute-start | bytes 98312 | tf_op jit(solution)/shard_map/ppermute | solution.py:256
  116.3 8.7 %copy-start.2 = (f32[3,2,16,256]{3,2,1,0:T(8,128)}, f32[3,2,16,256]{3,2,1,0:T(8,128)S(1)}, u32[]{:S(2)}) copy-start(f32[3,2,16,256]{3,2,1,0:T(8,128)S(1)} %pad_maximum_fusion.3) | copy-start | bytes 294916
  116.3 5.0 %collective-permute-start.14 = (f32[3,2,16,256]{3,2,1,0:T(8,128)S(1)}, f32[3,2,16,256]{3,2,1,0:T(8,128)S(1)}, u32[]{:S(2)}, u32[]{:S(2)}) collective-permute-start(f32[3,2,16,256]{3,2,1,0:T(8,128)S(1)} %pad_maximum_fusion.3), channel_id=1, source_target_pairs={{0,1},{1,2},{2,3},{3,4},{4,5},{5,6},{6,7},{8,9},{9,10},{10,11},{11... | collective-permute-start | bytes 294920 | tf_op jit(solution)/shard_map/ppermute | solution.py:256
  119.7 5.4 %collective-permute-start.15 = (f32[3,2,16,256]{3,2,1,0:T(8,128)S(1)}, f32[3,2,16,256]{3,2,1,0:T(8,128)S(1)}, u32[]{:S(2)}, u32[]{:S(2)}) collective-permute-start(f32[3,2,16,256]{3,2,1,0:T(8,128)S(1)} %pad_maximum_fusion.3), channel_id=1, source_target_pairs={{1,0},{2,1},{3,2},{4,3},{5,4},{6,5},{7,6},{9,8},{10,9},{11,10},{12... | collective-permute-start | bytes 294920 | tf_op jit(solution)/shard_map/ppermute | solution.py:256
  121.3 3.8 %copy-start.7 = (f32[3,2,16,256]{3,2,1,0:T(8,128)}, f32[3,2,16,256]{3,2,1,0:T(8,128)S(1)}, u32[]{:S(2)}) copy-start(f32[3,2,16,256]{3,2,1,0:T(8,128)S(1)} %collective-permute-done.14) | copy-start | bytes 294916
  125.0 0.6 copy-start.10

commit v11 on v9

--- a/solution.py
+++ b/solution.py
@@ -161,6 +161,22 @@
     store(residual_ref, total)
 
 
+def _bf16_parts(x):
+    high = lax.reduce_precision(x, exponent_bits=8, mantissa_bits=7)
+    rest = x - high
+    middle = lax.reduce_precision(rest, exponent_bits=8, mantissa_bits=7)
+    return [high, middle, rest - middle]
+
+
+def _exact_rows(hot, values):
+    parts = _bf16_parts(values)
+    width = values.shape[1]
+    stacked = jnp.concatenate(parts, axis=1).astype(jnp.bfloat16)
+    picked = jnp.dot(hot, stacked, preferred_element_type=jnp.float32)
+    high, middle, low = (picked[:, i * width : (i + 1) * width] for i in range(3))
+    return (high + middle) + low
+
+
 def _masks():
     shape = (ROWS, LANES)
     lane = lax.broadcasted_iota(jnp.int32, shape, 1)
@@ -280,8 +296,8 @@
     rank = jnp.sum(before * owner_hot.astype(jnp.float32), axis=1).astype(jnp.int32)
     dest = owner * CAP + rank
     payload = jnp.concatenate([code[:, None], normals.T], axis=1)
-    place_hot = (jnp.arange(owners * CAP, dtype=jnp.int32)[:, None] == dest[None, :]).astype(jnp.float32)
-    send = jnp.dot(place_hot, payload, precision=HIGHEST, preferred_element_type=jnp.float32)
+    place_hot = (jnp.arange(owners * CAP, dtype=jnp.int32)[:, None] == dest[None, :]).astype(jnp.bfloat16)
+    send = _exact_rows(place_hot, payload)
     got = lax.all_to_all(send.reshape(owners, CAP, 4), "wide", 0, 0, tiled=True).reshape(owners * CAP, 4)
 
     cell = got[:, 0].astype(jnp.int32) - 1

time: 172 us -> 170 us (0.988)
  matrix products: 7.35 us -> 5.08 us
    dot_general x1, matrix products: 3.74 us -> 1.48 us  [_exact_rows(): picked = jnp.dot(hot, stacked, preferred_element_type=jnp.float32)]
where the time goes in v11:
time: 170 us; the launch traced here: 169 us
  blocking collectives  57.7 us (34%)
  starting transfers between devices  44.1 us (26%)
  waiting for transfers between devices  35 us (21%)
  Pallas kernels  13.2 us (8%)
  local copies, waits for them, and re-layouts  6.55 us (4%)
  other arithmetic  5.38 us (3%)
  matrix products  5.08 us (3%)
  between operations  1.72 us (1%)
    ppermute x16, starting transfers between devices, _shift(): return lax.ppermute(field, axis, pairs)  44.1 us
    all_to_all x1, blocking collectives, shards(): lax.all_to_all(jnp.broadcast_to(payload, (devices, 32)), ('wide', 'narrow...  37 us
    ppermute x16, waiting for transfers between devices, _shift(): return lax.ppermute(field, axis, pairs)  35 us
    all_to_all x1, blocking collectives, shards(): lax.all_to_all(send.reshape(owners, CAP, 4), 'wide', 0, 0, tiled=True)  20.8 us
    pallas_call x4, Pallas kernels, _local_call(): pl.pallas_call(kernel, out_shape=jax.ShapeDtypeStruct(out_shape, jnp.floa...  9.03 us
  transfers between devices with their start and end apart: 16, of which 11 were waited for; matrix products, arithmetic and copies ran while one was open for 1% of the time, Pallas kernels for 0%

profile of v11, /device:TPU:1, one launch (start us, length us, event | category | flops | bytes accessed | tf_op | source)
XLA Modules:
  0.0 168.9 jit_solution(1828404353112403964)
XLA Ops:
  1.3 1.4 fusion.5
  2.8 1.5 fusion
  4.3 0.1 reshape.56
  4.4 0.1 copy.32
  4.5 0.1 reshape.64
  4.6 20.8 %all_to_all.14 = f32[64,1,128]{2,1,0:T(1,128)S(1)} all-to-all(f32[64,1,128]{2,1,0:T(1,128)S(1)} %reshape.64), channel_id=1, replica_groups=mesh['wide'=64,'narrow'=8] {'wide'}, dimensions={0} | all-to-all | bytes 65536 | tf_op jit(solution)/shard_map/all_to_all | solution.py:301
  25.4 0.5 broadcast.43
  25.9 0.7 reduce
  26.6 0.1 reshape.65
  26.8 0.1 reshape.57
  27.0 0.3 fusion.14
  27.3 1.1 fusion.17
  28.4 2.2 %fusion.3 = f32[128,256]{1,0:T(8,128)S(1)} fusion(f32[2048,32]{1,0:T(8,128)S(1)} %fusion.14, f32[2048,32]{1,0:T(8,128)S(1)} %get-tuple-element.23, f32[2048,32]{1,0:T(8,128)S(1)} %get-tuple-element.24, f32[2048,32]{1,0:T(8,128)S(1)} %get-tuple-element.22, s32[2048]{0:T(1024)S(1)} %bitcast.94), kind=kOutput, calls=%fused_computation.6 | convolution fusion | flops 806617088 | bytes 1187840 | tf_op jit(solution)/shard_map/pa,pb->ab/dot_general | solution.py:309
  30.7 0.0 copy-start.3
  30.7 2.8 %collective-permute-start = (f32[3,2,16,256]{3,2,1,0:T(8,128)S(1)}, f32[3,2,16,256]{3,2,1,0:T(8,128)S(1)}, u32[]{:S(2)}, u32[]{:S(2)}) collective-permute-start(f32[3,2,16,256]{3,2,1,0:T(8,128)S(1)} %bitcast.78), channel_id=1, source_target_pairs={{0,8},{8,16},{16,24},{24,32},{32,40},{40,48},{48,56},{56,64},{64,7... | collective-permute-start | bytes 294920 | tf_op jit(solution)/shard_map/ppermute | solution.py:270
  33.5 1.9 %collective-permute-start.1 = (f32[3,2,16,256]{3,2,1,0:T(8,128)S(1)}, f32[3,2,16,256]{3,2,1,0:T(8,128)S(1)}, u32[]{:S(2)}, u32[]{:S(2)}) collective-permute-start(f32[3,2,16,256]{3,2,1,0:T(8,128)S(1)} %bitcast.79), channel_id=1, source_target_pairs={{8,0},{16,8},{24,16},{32,24},{40,32},{48,40},{56,48},{64,56},{72,6... | collective-permute-start | bytes 294920 | tf_op jit(solution)/shard_map/ppermute | solution.py:270
  35.4 0.0 collective-permute-done
  35.4 4.0 %collective-permute-done.1 = f32[3,2,16,256]{3,2,1,0:T(8,128)S(1)} collective-permute-done((f32[3,2,16,256]{3,2,1,0:T(8,128)S(1)}, f32[3,2,16,256]{3,2,1,0:T(8,128)S(1)}, u32[]{:S(2)}, u32[]{:S(2)}) %collective-permute-start.1) | collective-permute-done | bytes 98336 | tf_op jit(solution)/shard_map/ppermute | solution.py:270
  39.4 0.1 fusion.33
  39.5 4.0 %collective-permute-start.2 = (f32[3,3,2,16,256]{4,3,2,1,0:T(8,128)S(1)}, f32[3,3,2,16,256]{4,3,2,1,0:T(8,128)S(1)}, u32[]{:S(2)}, u32[]{:S(2)}) collective-permute-start(f32[3,3,2,16,256]{4,3,2,1,0:T(8,128)S(1)} %get-tuple-element.7), channel_id=1, source_target_pairs={{0,1},{1,2},{2,3},{3,4},{4,5},{5,6},{6,7},{8,9},{9,10},{10,11},{11... | collective-permute-start | bytes 884744 | tf_op jit(solution)/shard_map/ppermute | solution.py:270
  43.5 1.3 collective-permute-start.3
  44.8 0.6 reshape.55.tab_ref
  45.4 2.6 %collective-permute-done.2 = f32[3,3,2,16,256]{4,3,2,1,0:T(8,128)S(1)} collective-permute-done((f32[3,3,2,16,256]{4,3,2,1,0:T(8,128)S(1)}, f32[3,3,2,16,256]{4,3,2,1,0:T(8,128)S(1)}, u32[]{:S(2)}, u32[]{:S(2)}) %collective-permute-start.2) | collective-permute-done | bytes 294944 | tf_op jit(solution)/shard_map/ppermute | solution.py:270
  48.1 4.5 %collective-permute-done.3 = f32[3,3,2,16,256]{4,3,2,1,0:T(8,128)S(1)} collective-permute-done((f32[3,3,2,16,256]{4,3,2,1,0:T(8,128)S(1)}, f32[3,3,2,16,256]{4,3,2,1,0:T(8,128)S(1)}, u32[]{:S(2)}, u32[]{:S(2)}) %collective-permute-start.3) | collective-permute-done | bytes 294944 | tf_op jit(solution)/shard_map/ppermute | solution.py:270
  52.5 0.1 pad_maximum_fusion
  52.6 1.0 concatenate.25.src_ref
  53.6 1.9 %shard_map.68.rest_0_.refs_0_ = f32[2,16,256]{2,1,0:T(8,128)} custom-call(s32[54]{0:T(128)} %reshape.55.tab_ref, f32[3,19,16,256]{3,2,1,0:T(8,128)} %concatenate.25.src_ref), custom_call_target="tpu_custom_call" | custom-call | flops 163840 | bytes 966872 | tf_op jit(solution)/shard_map/pallas_call | solution.py:258
  55.6 5.1 %collective-permute-start.4 = (f32[2,16,256]{2,1,0:T(8,128)}, f32[2,16,256]{2,1,0:T(8,128)S(1)}, u32[]{:S(2)}, u32[]{:S(2)}) collective-permute-start(f32[2,16,256]{2,1,0:T(8,128)} %shard_map.68.rest_0_.refs_0_), channel_id=1, source_target_pairs={{0,8},{8,16},{16,24},{24,32},{32,40},{40,48},{48,56},{56,64},{64,7... | collective-permute-start | bytes 98312 | tf_op jit(solution)/shard_map/ppermute | solution.py:270
  60.6 1.9 %collective-permute-start.5 = (f32[2,16,256]{2,1,0:T(8,128)}, f32[2,16,256]{2,1,0:T(8,128)S(1)}, u32[]{:S(2)}, u32[]{:S(2)}) collective-permute-start(f32[2,16,256]{2,1,0:T(8,128)} %shard_map.68.rest_0_.refs_0_), channel_id=1, source_target_pairs={{8,0},{16,8},{24,16},{32,24},{40,32},{48,40},{56,48},{64,56},{72,6... | collective-permute-start | bytes 98312 | tf_op jit(solution)/shard_map/ppermute | solution.py:270
  62.6 0.0 collective-permute-done.4
  62.6 3.5 %collective-permute-done.5 = f32[2,16,256]{2,1,0:T(8,128)S(1)} collective-permute-done((f32[2,16,256]{2,1,0:T(8,128)}, f32[2,16,256]{2,1,0:T(8,128)S(1)}, u32[]{:S(2)}, u32[]{:S(2)}) %collective-permute-start.5) | collective-permute-done | bytes 32800 | tf_op jit(solution)/shard_map/ppermute | solution.py:270
  66.1 0.8 fusion.32
  66.9 4.0 %collective-permute-start.6 = (f32[3,2,16,256]{3,2,1,0:T(8,128)S(1)}, f32[3,2,16,256]{3,2,1,0:T(8,128)S(1)}, u32[]{:S(2)}, u32[]{:S(2)}) collective-permute-start(f32[3,2,16,256]{3,2,1,0:T(8,128)S(1)} %get-tuple-element.13), channel_id=1, source_target_pairs={{0,1},{1,2},{2,3},{3,4},{4,5},{5,6},{6,7},{8,9},{9,10},{10,11},{11... | collective-permute-start | bytes 294920 | tf_op jit(solution)/shard_map/ppermute | solution.py:270
  70.9 1.3 collective-permute-start.7
  72.2 0.6 fusion.20
  72.8 5.3 %collective-permute-done.7 = f32[3,2,16,256]{3,2,1,0:T(8,128)S(1)} collective-permute-done((f32[3,2,16,256]{3,2,1,0:T(8,128)S(1)}, f32[3,2,16,256]{3,2,1,0:T(8,128)S(1)}, u32[]{:S(2)}, u32[]{:S(2)}) %collective-permute-start.7) | collective-permute-done | bytes 98336 | tf_op jit(solution)/shard_map/ppermute | solution.py:270
  78.1 0.7 concatenate.26.src_ref
  78.9 2.3 %shard_map.69.rest_0_.refs_1_ = f32[2,16,256]{2,1,0:T(8,128)} custom-call(s32[54]{0:T(128)} %reshape.55.tab_ref, f32[19,16,256]{2,1,0:T(8,128)} %concatenate.26.src_ref, f32[2,16,256]{2,1,0:T(8,128)} %bitcast.72), custom_call_target="tpu_custom_call" | custom-call | flops 491520 | bytes 377048 | tf_op jit(solution)/shard_map/pallas_call | solution.py:258
  81.2 3.6 %collective-permute-start.8 = (f32[2,16,256]{2,1,0:T(8,128)}, f32[2,16,256]{2,1,0:T(8,128)S(1)}, u32[]{:S(2)}, u32[]{:S(2)}) collective-permute-start(f32[2,16,256]{2,1,0:T(8,128)} %shard_map.69.rest_0_.refs_1_), channel_id=1, source_target_pairs={{0,8},{8,16},{16,24},{24,32},{32,40},{40,48},{48,56},{56,64},{64,7... | collective-permute-start | bytes 98312 | tf_op jit(solution)/shard_map/ppermute | solution.py:270
  84.8 1.9 %collective-permute-start.9 = (f32[2,16,256]{2,1,0:T(8,128)}, f32[2,16,256]{2,1,0:T(8,128)S(1)}, u32[]{:S(2)}, u32[]{:S(2)}) collective-permute-start(f32[2,16,256]{2,1,0:T(8,128)} %shard_map.69.rest_0_.refs_1_), channel_id=1, source_target_pairs={{8,0},{16,8},{24,16},{32,24},{40,32},{48,40},{56,48},{64,56},{72,6... | collective-permute-start | bytes 98312 | tf_op jit(solution)/shard_map/ppermute | solution.py:270
  86.7 0.0 collective-permute-done.8
  86.7 3.5 %collective-permute-done.9 = f32[2,16,256]{2,1,0:T(8,128)S(1)} collective-permute-done((f32[2,16,256]{2,1,0:T(8,128)}, f32[2,16,256]{2,1,0:T(8,128)S(1)}, u32[]{:S(2)}, u32[]{:S(2)}) %collective-permute-start.9) | collective-permute-done | bytes 32800 | tf_op jit(solution)/shard_map/ppermute | solution.py:270
  90.2 0.8 fusion.31
  91.0 5.1 %collective-permute-start.10 = (f32[3,2,16,256]{3,2,1,0:T(8,128)S(1)}, f32[3,2,16,256]{3,2,1,0:T(8,128)S(1)}, u32[]{:S(2)}, u32[]{:S(2)}) collective-permute-start(f32[3,2,16,256]{3,2,1,0:T(8,128)S(1)} %get-tuple-element.11), channel_id=1, source_target_pairs={{0,1},{1,2},{2,3},{3,4},{4,5},{5,6},{6,7},{8,9},{9,10},{10,11},{11... | collective-permute-start | bytes 294920 | tf_op jit(solution)/shard_map/ppermute | solution.py:270
  96.1 1.3 collective-permute-start.11
  97.4 0.3 collective-permute-done.10
  97.7 3.7 %collective-permute-done.11 = f32[3,2,16,256]{3,2,1,0:T(8,128)S(1)} collective-permute-done((f32[3,2,16,256]{3,2,1,0:T(8,128)S(1)}, f32[3,2,16,256]{3,2,1,0:T(8,128)S(1)}, u32[]{:S(2)}, u32[]{:S(2)}) %collective-permute-start.11) | collective-permute-done | bytes 98336 | tf_op jit(solution)/shard_map/ppermute | solution.py:270
  101.5 0.7 concatenate.27.src_ref
  102.2 2.4 %shard_map.70.refs_2_ = f32[2,16,256]{2,1,0:T(8,128)} custom-call(s32[54]{0:T(128)} %reshape.55.tab_ref, f32[19,16,256]{2,1,0:T(8,128)} %concatenate.27.src_ref, f32[2,16,256]{2,1,0:T(8,128)} %bitcast.73, f32[2,16,256]{2,1,0:T(8,128)} %shard_map.68.rest_0_.refs_0_), custom_call_target="tpu_custom_call" | custom-call | flops 491520 | bytes 409816 | tf_op jit(solution)/shard_map/pallas_call | solution.py:258
  104.6 3.4 %collective-permute-start.12 = (f32[2,16,256]{2,1,0:T(8,128)}, f32[2,16,256]{2,1,0:T(8,128)S(1)}, u32[]{:S(2)}, u32[]{:S(2)}) collective-permute-start(f32[2,16,256]{2,1,0:T(8,128)} %shard_map.70.refs_2_), channel_id=1, source_target_pairs={{0,8},{8,16},{16,24},{24,32},{32,40},{40,48},{48,56},{56,64},{64,7... | collective-permute-start | bytes 98312 | tf_op jit(solution)/shard_map/ppermute | solution.py:270
  108.1 1.9 %collective-permute-start.13 = (f32[2,16,256]{2,1,0:T(8,128)}, f32[2,16,256]{2,1,0:T(8,128)S(1)}, u32[]{:S(2)}, u32[]{:S(2)}) collective-permute-start(f32[2,16,256]{2,1,0:T(8,128)} %shard_map.70.refs_2_), channel_id=1, source_target_pairs={{8,0},{16,8},{24,16},{32,24},{40,32},{48,40},{56,48},{64,56},{72,6... | collective-permute-start | bytes 98312 | tf_op jit(solution)/shard_map/ppermute | solution.py:270
  110.0 3.5 %collective-permute-done.13 = f32[2,16,256]{2,1,0:T(8,128)S(1)} collective-permute-done((f32[2,16,256]{2,1,0:T(8,128)}, f32[2,16,256]{2,1,0:T(8,128)S(1)}, u32[]{:S(2)}, u32[]{:S(2)}) %collective-permute-start.13) | collective-permute-done | bytes 32800 | tf_op jit(solution)/shard_map/ppermute | solution.py:270
  113.5 0.8 fusion.30
  114.3 3.4 %collective-permute-start.14 = (f32[3,2,16,256]{3,2,1,0:T(8,128)S(1)}, f32[3,2,16,256]{3,2,1,0:T(8,128)S(1)}, u32[]{:S(2)}, u32[]{:S(2)}) collective-permute-start(f32[3,2,16,256]{3,2,1,0:T(8,128)S(1)} %get-tuple-element.9), channel_id=1, source_target_pairs={{0,1},{1,2},{2,3},{3,4},{4,5},{5,6},{6,7},{8,9},{9,10},{10,11},{11... | collective-permute-start | bytes 294920 | tf_op jit(solution)/shard_map/ppermute | solution.py:270
  117.6 1.3 collective-permute-start.15
  118.9 0.3 collective-permute-done.14
  119.3 3.7 %collective-permute-done.15 = f32[3,2,16,256]{3,2,1,0:T(8,128)S(1)} collective-permute-done((f32[3,2,16,256]{3,2,1,0:T(8,128)S(1)}, f32[3,2,16,256]{3,2,1,0:T(8,128)S(1)}, u32[]{:S(2)}, u32[]{:S(2)}) %collective-permute-start.15) | collective-permute-done | bytes 98336 | tf_op jit(solution)/shard_map/ppermute | solution.py:270
  123.1 0.7 concatenate.28.src_ref
  123.8 2.4 %shard_map.71.refs_3_ = f32[2,16,256]{2,1,0:T(8,128)} custom-call(s32[54]{0:T(128)} %reshape.55.tab_ref, f32[19,16,256]{2,1,0:T(8,128)} %concatenate.28.src_ref, f32[2,16,256]{2,1,0:T(8,128)} %bitcast.74, f32[2,16,256]{2,1,0:T(8,128)} %shard_map.69.rest_0_.refs_1_), custom_call_target="tpu_custom_call" | custom-call | flops 491520 | bytes 409816 | tf_op jit(solution)/shard_map/pallas_call | solution.py:258
  126.2 2.1 %shard_map.72 = f32[1,32]{1,0:T(1,128)} custom-call(f32[2,16,256]{2,1,0:T(8,128)} %shard_map.68.rest_0_.refs_0_, f32[2,16,256]{2,1,0:T(8,128)} %shard_map.69.rest_0_.refs_1_, f32[2,16,256]{2,1,0:T(8,128)} %shard_map.70.refs_2_, f32[2,16,256]{2,1,0:T(8,128)} %shard_map.71.refs_3_), custom_call_target="tpu_custom_call" | custom-call | tf_op jit(solution)/shard_map/pallas_call | solution.py:330
  128.2 0.8 broadcast_in_dim.10
  129.0 37.0 %all_to_all.15 = f32[512,1,32]{2,1,0:T(1,128)S(1)} all-to-all(f32[512,1,32]{2,1,0:T(1,128)S(1)} %broadcast_in_dim.10), channel_id=1, replica_groups=mesh['wide'=64,'narrow'=8] {'wide','narrow'}, dimensions={0} | all-to-all | bytes 131072 | tf_op jit(solution)/shard_map/all_to_all | solution.py:333
  166.0 0.7 copy.30
  166.7 2.1 %shard_map.73 = (f32[2,4096]{1,0:T(2,128)}, f32[2,4096]{1,0:T(2,128)}) custom-call(f32[32,512]{1,0:T(8,128)} %bitcast.83, f32[2,16,256]{2,1,0:T(8,128)} %shard_map.68.rest_0_.refs_0_, f32[2,16,256]{2,1,0:T(8,128)} %shard_map.69.rest_0_.refs_1_, f32[2,16,256]{2,1,0:T(8,128)} %shard_map.70.refs_2_, f32[2,16,256]{2,1,0:T(8,128)} %shard_map.71.refs_3_), custom_call_target="tpu_custom_call" | custom-call | tf_op jit(solution)/shard_map/pallas_call | solution.py:335
  (23 shorter events, 0.2 us)
Async XLA Ops:
  0.6 2.1 %copy-start.1 = (s32[1024,1]{0,1:T(1,128)S(1)}, s32[1024,1]{0,1:T(1,128)}, u32[]{:S(2)}) copy-start(s32[1024,1]{0,1:T(1,128)} %param.5) | copy-start | bytes 12292
  0.6 2.1 %copy-start.2 = (s32[1024]{0:T(1024)S(1)}, s32[1024]{0:T(1024)}, u32[]{:S(2)}) copy-start(s32[1024]{0:T(1024)} %param.6) | copy-start | bytes 12292
  0.7 2.1 %copy-start = (f32[3,1024]{1,0:T(4,128)S(1)}, f32[3,1024]{1,0:T(4,128)}, u32[]{:S(2)}) copy-start(f32[3,1024]{1,0:T(4,128)} %param.7) | copy-start | bytes 36868
  30.7 14.1 %copy-start.3 = (s32[1,1,2,27]{3,2,1,0:T(2,128)S(1)}, s32[1,1,2,27]{3,2,1,0:T(2,128)}, u32[]{:S(2)}) copy-start(s32[1,1,2,27]{3,2,1,0:T(2,128)} %param.9) | copy-start | bytes 652
  30.7 4.7 %collective-permute-start = (f32[3,2,16,256]{3,2,1,0:T(8,128)S(1)}, f32[3,2,16,256]{3,2,1,0:T(8,128)S(1)}, u32[]{:S(2)}, u32[]{:S(2)}) collective-permute-start(f32[3,2,16,256]{3,2,1,0:T(8,128)S(1)} %bitcast.78), channel_id=1, source_target_pairs={{0,8},{8,16},{16,24},{24,32},{32,40},{40,48},{48,56},{56,64},{64,7... | collective-permute-start | bytes 294920 | tf_op jit(solution)/shard_map/ppermute | solution.py:270
  33.5 5.9 %collective-permute-start.1 = (f32[3,2,16,256]{3,2,1,0:T(8,128)S(1)}, f32[3,2,16,256]{3,2,1,0:T(8,128)S(1)}, u32[]{:S(2)}, u32[]{:S(2)}) collective-permute-start(f32[3,2,16,256]{3,2,1,0:T(8,128)S(1)} %bitcast.79), channel_id=1, source_target_pairs={{8,0},{16,8},{24,16},{32,24},{40,32},{48,40},{56,48},{64,56},{72,6... | collective-permute-start | bytes 294920 | tf_op jit(solution)/shard_map/ppermute | solution.py:270
  39.5 8.5 %collective-permute-start.2 = (f32[3,3,2,16,256]{4,3,2,1,0:T(8,128)S(1)}, f32[3,3,2,16,256]{4,3,2,1,0:T(8,128)S(1)}, u32[]{:S(2)}, u32[]{:S(2)}) collective-permute-start(f32[3,3,2,16,256]{4,3,2,1,0:T(8,128)S(1)} %get-tuple-element.7), channel_id=1, source_target_pairs={{0,1},{1,2},{2,3},{3,4},{4,5},{5,6},{6,7},{8,9},{9,10},{10,11},{11... | collective-permute-start | bytes 884744 | tf_op jit(solution)/shard_map/ppermute | solution.py:270
  43.5 9.0 %collective-permute-start.3 = (f32[3,3,2,16,256]{4,3,2,1,0:T(8,128)S(1)}, f32[3,3,2,16,256]{4,3,2,1,0:T(8,128)S(1)}, u32[]{:S(2)}, u32[]{:S(2)}) collective-permute-start(f32[3,3,2,16,256]{4,3,2,1,0:T(8,128)S(1)} %get-tuple-element.7), channel_id=1, source_target_pairs={{1,0},{2,1},{3,2},{4,3},{5,4},{6,5},{7,6},{9,8},{10,9},{11,10},{12... | collective-permute-start | bytes 884744 | tf_op jit(solution)/shard_map/ppermute | solution.py:270
  55.6 7.0 %collective-permute-start.4 = (f32[2,16,256]{2,1,0:T(8,128)}, f32[2,16,256]{2,1,0:T(8,128)S(1)}, u32[]{:S(2)}, u32[]{:S(2)}) collective-permute-start(f32[2,16,256]{2,1,0:T(8,128)} %shard_map.68.rest_0_.refs_0_), channel_id=1, source_target_pairs={{0,8},{8,16},{16,24},{24,32},{32,40},{40,48},{48,56},{56,64},{64,7... | collective-permute-start | bytes 98312 | tf_op jit(solution)/shard_map/ppermute | solution.py:270
  60.6 5.4 %collective-permute-start.5 = (f32[2,16,256]{2,1,0:T(8,128)}, f32[2,16,256]{2,1,0:T(8,128)S(1)}, u32[]{:S(2)}, u32[]{:S(2)}) collective-permute-start(f32[2,16,256]{2,1,0:T(8,128)} %shard_map.68.rest_0_.refs_0_), channel_id=1, source_target_pairs={{8,0},{16,8},{24,16},{32,24},{40,32},{48,40},{56,48},{64,56},{72,6... | collective-permute-start | bytes 98312 | tf_op jit(solution)/shard_map/ppermute | solution.py:270
  66.9 5.9 %collective-permute-start.6 = (f32[3,2,16,256]{3,2,1,0:T(8,128)S(1)}, f32[3,2,16,256]{3,2,1,0:T(8,128)S(1)}, u32[]{:S(2)}, u32[]{:S(2)}) collective-permute-start(f32[3,2,16,256]{3,2,1,0:T(8,128)S(1)} %get-tuple-element.13), channel_id=1, source_target_pairs={{0,1},{1,2},{2,3},{3,4},{4,5},{5,6},{6,7},{8,9},{9,10},{10,11},{11... | collective-permute-start | bytes 294920 | tf_op jit(solution)/shard_map/ppermute | solution.py:270
  70.9 7.2 %collective-permute-start.7 = (f32[3,2,16,256]{3,2,1,0:T(8,128)S(1)}, f32[3,2,16,256]{3,2,1,0:T(8,128)S(1)}, u32[]{:S(2)}, u32[]{:S(2)}) collective-permute-start(f32[3,2,16,256]{3,2,1,0:T(8,128)S(1)} %get-tuple-element.13), channel_id=1, source_target_pairs={{1,0},{2,1},{3,2},{4,3},{5,4},{6,5},{7,6},{9,8},{10,9},{11,10},{12... | collective-permute-start | bytes 294920 | tf_op jit(solution)/shard_map/ppermute | solution.py:270
  81.2 5.5 %collective-permute-start.8 = (f32[2,16,256]{2,1,0:T(8,128)}, f32[2,16,256]{2,1,0:T(8,128)S(1)}, u32[]{:S(2)}, u32[]{:S(2)}) collective-permute-start(f32[2,16,256]{2,1,0:T(8,128)} %shard_map.69.rest_0_.refs_1_), channel_id=1, source_target_pairs={{0,8},{8,16},{16,24},{24,32},{32,40},{40,48},{48,56},{56,64},{64,7... | collective-permute-start | bytes 98312 | tf_op jit(solution)/shard_map/ppermute | solution.py:270
  84.8 5.4 %collective-permute-start.9 = (f32[2,16,256]{2,1,0:T(8,128)}, f32[2,16,256]{2,1,0:T(8,128)S(1)}, u32[]{:S(2)}, u32[]{:S(2)}) collective-permute-start(f32[2,16,256]{2,1,0:T(8,128)} %shard_map.69.rest_0_.refs_1_), channel_id=1, source_target_pairs={{8,0},{16,8},{24,16},{32,24},{40,32},{48,40},{56,48},{64,56},{72,6... | collective-permute-start | bytes 98312 | tf_op jit(solution)/shard_map/ppermute | solution.py:270
  91.0 6.7 %collective-permute-start.10 = (f32[3,2,16,256]{3,2,1,0:T(8,128)S(1)}, f32[3,2,16,256]{3,2,1,0:T(8,128)S(1)}, u32[]{:S(2)}, u32[]{:S(2)}) collective-permute-start(f32[3,2,16,256]{3,2,1,0:T(8,128)S(1)} %get-tuple-element.11), channel_id=1, source_target_pairs={{0,1},{1,2},{2,3},{3,4},{4,5},{5,6},{6,7},{8,9},{9,10},{10,11},{11... | collective-permute-start | bytes 294920 | tf_op jit(solution)/shard_map/ppermute | solution.py:270
  96.1 5.4 %collective-permute-start.11 = (f32[3,2,16,256]{3,2,1,0:T(8,128)S(1)}, f32[3,2,16,256]{3,2,1,0:T(8,128)S(1)}, u32[]{:S(2)}, u32[]{:S(2)}) collective-permute-start(f32[3,2,16,256]{3,2,1,0:T(8,128)S(1)} %get-tuple-element.11), channel_id=1, source_target_pairs={{1,0},{2,1},{3,2},{4,3},{5,4},{6,5},{7,6},{9,8},{10,9},{11,10},{12... | collective-permute-start | bytes 294920 | tf_op jit(solution)/shard_map/ppermute | solution.py:270
  104.6 5.4 %collective-permute-start.12 = (f32[2,16,256]{2,1,0:T(8,128)}, f32[2,16,256]{2,1,0:T(8,128)S(1)}, u32[]{:S(2)}, u32[]{:S(2)}) collective-permute-start(f32[2,16,256]{2,1,0:T(8,128)} %shard_map.70.refs_2_), channel_id=1, source_target_pairs={{0,8},{8,16},{16,24},{24,32},{32,40},{40,48},{48,56},{56,64},{64,7... | collective-permute-start | bytes 98312 | tf_op jit(solution)/shard_map/ppermute | solution.py:270
  108.1 5.4 %collective-permute-start.13 = (f32[2,16,256]{2,1,0:T(8,128)}, f32[2,16,256]{2,1,0:T(8,128)S(1)}, u32[]{:S(2)}, u32[]{:S(2)}) collective-permute-start(f32[2,16,256]{2,1,0:T(8,128)} %shard_map.70.refs_2_), channel_id=1, source_target_pairs={{8,0},{16,8},{24,16},{32,24},{40,32},{48,40},{56,48},{64,56},{72,6... | collective-permute-start | bytes 98312 | tf_op jit(solution)/shard_map/ppermute | solution.py:270
  114.3 5.0 %collective-permute-start.14 = (f32[3,2,16,256]{3,2,1,0:T(8,128)S(1)}, f32[3,2,16,256]{3,2,1,0:T(8,128)S(1)}, u32[]{:S(2)}, u32[]{:S(2)}) collective-permute-start(f32[3,2,16,256]{3,2,1,0:T(8,128)S(1)} %get-tuple-element.9), channel_id=1, source_target_pairs={{0,1},{1,2},{2,3},{3,4},{4,5},{5,6},{6,7},{8,9},{9,10},{10,11},{11... | collective-permute-start | bytes 294920 | tf_op jit(solution)/shard_map/ppermute | solution.py:270
  117.6 5.4 %collective-permute-start.15 = (f32[3,2,16,256]{3,2,1,0:T(8,128)S(1)}, f32[3,2,16,256]{3,2,1,0:T(8,128)S(1)}, u32[]{:S(2)}, u32[]{:S(2)}) collective-permute-start(f32[3,2,16,256]{3,2,1,0:T(8,128)S(1)} %get-tuple-element.9), channel_id=1, source_target_pairs={{1,0},{2,1},{3,2},{4,3},{5,4},{6,5},{7,6},{9,8},{10,9},{11,10},{12... | collective-permute-start | bytes 294920 | tf_op jit(solution)/shard_map/ppermute | solution.py:270

commit v12 on v11

--- a/solution.py
+++ b/solution.py
@@ -305,11 +305,14 @@
     cell_yz = cell & (LANES - 1)
     bx_hot = (brick_x[:, None] == jnp.arange(bricks * ROWS, dtype=jnp.int32)[None, :]).astype(jnp.float32)
     yz_hot = (cell_yz[:, None] == jnp.arange(LANES, dtype=jnp.int32)[None, :]).astype(jnp.float32)
-    weighted = jnp.concatenate([bx_hot * got[:, 1:2], bx_hot * got[:, 2:3], bx_hot * got[:, 3:4], bx_hot], axis=1)
-    splatted = jnp.einsum("pa,pb->ab", weighted, yz_hot, precision=HIGHEST, preferred_element_type=jnp.float32)
-    splatted = splatted.reshape(4, bricks, ROWS, LANES)
-    vector_field = splatted[:3]
-    diagonal = 14.5 + 2.0 * splatted[3]
+    parts = _bf16_parts(got[:, 1:4])
+    weighted = jnp.concatenate([bx_hot * p[:, c : c + 1] for p in parts for c in range(3)] + [bx_hot], axis=1)
+    splatted = jnp.einsum(
+        "pa,pb->ab", weighted.astype(jnp.bfloat16), yz_hot.astype(jnp.bfloat16), preferred_element_type=jnp.float32
+    )
+    splatted = splatted.reshape(10, bricks, ROWS, LANES)
+    vector_field = (splatted[0:3] + splatted[3:6]) + splatted[6:9]
+    diagonal = 14.5 + 2.0 * splatted[9]
 
     shape = (bricks, ROWS, LANES)
     right_side = _local_call(_divergence_kernel, shape, [table, halo(vector_field)], 20 * bricks * 4096)

time: 170 us -> 182 us (1.071)
  local copies, waits for them, and re-layouts: 6.55 us -> 13.8 us
  other arithmetic: 5.38 us -> 9.75 us
    concatenate x0 -> x1, local copies, waits for them, and re-layouts: none -> 7.24 us  [shards(): jnp.concatenate([bx_hot * p[:, c:c + 1] for p in parts for c in range(3)]...]
    another operation x1 -> x3, other arithmetic: 0.02 us -> 5.84 us
where the time goes in v12:
time: 182 us; the launch traced here: 181 us
  blocking collectives  57.7 us (32%)
  starting transfers between devices  44.1 us (24%)
  waiting for transfers between devices  35 us (19%)
  local copies, waits for them, and re-layouts  13.8 us (8%)
  Pallas kernels  13.3 us (7%)
  other arithmetic  9.75 us (5%)
  matrix products  5.14 us (3%)
    ppermute x16, starting transfers between devices, _shift(): return lax.ppermute(field, axis, pairs)  44.1 us
    all_to_all x1, blocking collectives, shards(): lax.all_to_all(jnp.broadcast_to(payload, (devices, 32)), ('wide', 'narrow...  36.9 us
    ppermute x16, waiting for transfers between devices, _shift(): return lax.ppermute(field, axis, pairs)  35 us
    all_to_all x1, blocking collectives, shards(): lax.all_to_all(send.reshape(owners, CAP, 4), 'wide', 0, 0, tiled=True)  20.8 us
    pallas_call x4, Pallas kernels, _local_call(): pl.pallas_call(kernel, out_shape=jax.ShapeDtypeStruct(out_shape, jnp.floa...  9.05 us
    concatenate x1, local copies, waits for them, and re-layouts, shards(): jnp.concatenate([bx_hot * p[:, c:c + 1] for p in parts for c in range(3)]...  7.24 us
    another operation x3, other arithmetic  5.84 us
  transfers between devices with their start and end apart: 16, of which 11 were waited for; matrix products, arithmetic and copies ran while one was open for 1% of the time, Pallas kernels for 0%

profile of v12, /device:TPU:1, one launch (start us, length us, event | category | flops | bytes accessed | tf_op | source)
XLA Modules:
  0.0 180.6 jit_solution(4725775058205795482)
XLA Ops:
  1.3 1.4 fusion.4
  2.8 1.5 fusion
  4.3 0.1 reshape.88
  4.4 0.1 copy.32
  4.5 0.1 reshape.96
  4.6 20.8 %all_to_all.14 = f32[64,1,128]{2,1,0:T(1,128)S(1)} all-to-all(f32[64,1,128]{2,1,0:T(1,128)S(1)} %reshape.96), channel_id=1, replica_groups=mesh['wide'=64,'narrow'=8] {'wide'}, dimensions={0} | all-to-all | bytes 65536 | tf_op jit(solution)/shard_map/all_to_all | solution.py:301
  25.4 0.5 broadcast.55
  25.9 0.7 reduce
  26.6 0.1 reshape.97
  26.8 0.1 reshape.89
  27.0 1.1 convert_convert_fusion.2
  28.1 4.7 %select_convert_fusion = (bf16[2048,32]{1,0:T(8,128)(2,1)S(1)}, bf16[2048,32]{1,0:T(8,128)(2,1)S(1)}, bf16[2048,32]{1,0:T(8,128)(2,1)S(1)}, bf16[2048,32]{1,0:T(...) fusion(f32[2048]{0:T(1024)S(1)} %bitcast.101, ...), kind=kLoop, calls=%fused_computation.12 | loop fusion | flops 655360 | bytes 1261568 | tf_op jit(solution)/shard_map/convert.8
  32.8 7.2 %concatenate.25 = bf16[2048,320]{1,0:T(8,128)(2,1)} concatenate(bf16[2048,32]{1,0:T(8,128)(2,1)} %get-tuple-element.39, bf16[2048,32]{1,0:T(8,128)(2,1)} %get-tuple-element.38, bf16[2048,32]{1,0:T(8,128)(2,1)} %get-tuple-element.37, bf16[2048,32]{1,0:T(8,128)(2,1)S(1)} %get-tuple-element.36, bf16[2048,32]{1,0:T(8,128)(2,1)S(1)} %get-tuple-element.35, ...), dimensions={1} | concatenate | bytes 2621440 | tf_op jit(solution)/shard_map/concatenate | solution.py:309
  40.1 2.3 %fusion.5 = f32[320,256]{1,0:T(8,128)S(1)} fusion(bf16[2048,320]{1,0:T(8,128)(2,1)} %concatenate.25, s32[2048]{0:T(1024)S(1)} %bitcast.118), kind=kOutput, calls=%fused_computation.9 | convolution fusion | flops 337117184 | bytes 1646592 | tf_op jit(solution)/shard_map/pa,pb->ab/dot_general | solution.py:310
  42.4 2.8 %collective-permute-start = (f32[3,2,16,256]{3,2,1,0:T(8,128)S(1)}, f32[3,2,16,256]{3,2,1,0:T(8,128)S(1)}, u32[]{:S(2)}, u32[]{:S(2)}) collective-permute-start(f32[3,2,16,256]{3,2,1,0:T(8,128)S(1)} %bitcast.85), channel_id=1, source_target_pairs={{0,8},{8,16},{16,24},{24,32},{32,40},{40,48},{48,56},{56,64},{64,7... | collective-permute-start | bytes 294920 | tf_op jit(solution)/shard_map/ppermute | solution.py:270
  45.2 1.9 %collective-permute-start.1 = (f32[3,2,16,256]{3,2,1,0:T(8,128)S(1)}, f32[3,2,16,256]{3,2,1,0:T(8,128)S(1)}, u32[]{:S(2)}, u32[]{:S(2)}) collective-permute-start(f32[3,2,16,256]{3,2,1,0:T(8,128)S(1)} %bitcast.86), channel_id=1, source_target_pairs={{8,0},{16,8},{24,16},{32,24},{40,32},{48,40},{56,48},{64,56},{72,6... | collective-permute-start | bytes 294920 | tf_op jit(solution)/shard_map/ppermute | solution.py:270
  47.1 0.0 collective-permute-done
  47.1 4.0 %collective-permute-done.1 = f32[3,2,16,256]{3,2,1,0:T(8,128)S(1)} collective-permute-done((f32[3,2,16,256]{3,2,1,0:T(8,128)S(1)}, f32[3,2,16,256]{3,2,1,0:T(8,128)S(1)}, u32[]{:S(2)}, u32[]{:S(2)}) %collective-permute-start.1) | collective-permute-done | bytes 98336 | tf_op jit(solution)/shard_map/ppermute | solution.py:270
  51.1 0.1 fusion.22
  51.2 4.0 %collective-permute-start.2 = (f32[3,3,2,16,256]{4,3,2,1,0:T(8,128)S(1)}, f32[3,3,2,16,256]{4,3,2,1,0:T(8,128)S(1)}, u32[]{:S(2)}, u32[]{:S(2)}) collective-permute-start(f32[3,3,2,16,256]{4,3,2,1,0:T(8,128)S(1)} %get-tuple-element.7), channel_id=1, source_target_pairs={{0,1},{1,2},{2,3},{3,4},{4,5},{5,6},{6,7},{8,9},{9,10},{10,11},{11... | collective-permute-start | bytes 884744 | tf_op jit(solution)/shard_map/ppermute | solution.py:270
  55.2 1.3 collective-permute-start.3
  56.5 0.6 reshape.87.tab_ref
  57.1 2.6 %collective-permute-done.2 = f32[3,3,2,16,256]{4,3,2,1,0:T(8,128)S(1)} collective-permute-done((f32[3,3,2,16,256]{4,3,2,1,0:T(8,128)S(1)}, f32[3,3,2,16,256]{4,3,2,1,0:T(8,128)S(1)}, u32[]{:S(2)}, u32[]{:S(2)}) %collective-permute-start.2) | collective-permute-done | bytes 294944 | tf_op jit(solution)/shard_map/ppermute | solution.py:270
  59.8 4.5 %collective-permute-done.3 = f32[3,3,2,16,256]{4,3,2,1,0:T(8,128)S(1)} collective-permute-done((f32[3,3,2,16,256]{4,3,2,1,0:T(8,128)S(1)}, f32[3,3,2,16,256]{4,3,2,1,0:T(8,128)S(1)}, u32[]{:S(2)}, u32[]{:S(2)}) %collective-permute-start.3) | collective-permute-done | bytes 294944 | tf_op jit(solution)/shard_map/ppermute | solution.py:270
  64.2 0.1 pad_maximum_fusion
  64.3 1.0 concatenate.26.src_ref
  65.3 1.9 %shard_map.68.rest_0_.refs_0_ = f32[2,16,256]{2,1,0:T(8,128)} custom-call(s32[54]{0:T(128)} %reshape.87.tab_ref, f32[3,19,16,256]{3,2,1,0:T(8,128)} %concatenate.26.src_ref), custom_call_target="tpu_custom_call" | custom-call | flops 163840 | bytes 966872 | tf_op jit(solution)/shard_map/pallas_call | solution.py:258
  67.3 5.1 %collective-permute-start.4 = (f32[2,16,256]{2,1,0:T(8,128)}, f32[2,16,256]{2,1,0:T(8,128)S(1)}, u32[]{:S(2)}, u32[]{:S(2)}) collective-permute-start(f32[2,16,256]{2,1,0:T(8,128)} %shard_map.68.rest_0_.refs_0_), channel_id=1, source_target_pairs={{0,8},{8,16},{16,24},{24,32},{32,40},{40,48},{48,56},{56,64},{64,7... | collective-permute-start | bytes 98312 | tf_op jit(solution)/shard_map/ppermute | solution.py:270
  72.3 1.9 %collective-permute-start.5 = (f32[2,16,256]{2,1,0:T(8,128)}, f32[2,16,256]{2,1,0:T(8,128)S(1)}, u32[]{:S(2)}, u32[]{:S(2)}) collective-permute-start(f32[2,16,256]{2,1,0:T(8,128)} %shard_map.68.rest_0_.refs_0_), channel_id=1, source_target_pairs={{8,0},{16,8},{24,16},{32,24},{40,32},{48,40},{56,48},{64,56},{72,6... | collective-permute-start | bytes 98312 | tf_op jit(solution)/shard_map/ppermute | solution.py:270
  74.3 0.0 collective-permute-done.4
  74.3 3.5 %collective-permute-done.5 = f32[2,16,256]{2,1,0:T(8,128)S(1)} collective-permute-done((f32[2,16,256]{2,1,0:T(8,128)}, f32[2,16,256]{2,1,0:T(8,128)S(1)}, u32[]{:S(2)}, u32[]{:S(2)}) %collective-permute-start.5) | collective-permute-done | bytes 32800 | tf_op jit(solution)/shard_map/ppermute | solution.py:270
  77.8 0.8 fusion.21
  78.6 4.0 %collective-permute-start.6 = (f32[3,2,16,256]{3,2,1,0:T(8,128)S(1)}, f32[3,2,16,256]{3,2,1,0:T(8,128)S(1)}, u32[]{:S(2)}, u32[]{:S(2)}) collective-permute-start(f32[3,2,16,256]{3,2,1,0:T(8,128)S(1)} %get-tuple-element.13), channel_id=1, source_target_pairs={{0,1},{1,2},{2,3},{3,4},{4,5},{5,6},{6,7},{8,9},{9,10},{10,11},{11... | collective-permute-start | bytes 294920 | tf_op jit(solution)/shard_map/ppermute | solution.py:270
  82.6 1.3 collective-permute-start.7
  83.9 0.6 fusion.9
  84.5 5.3 %collective-permute-done.7 = f32[3,2,16,256]{3,2,1,0:T(8,128)S(1)} collective-permute-done((f32[3,2,16,256]{3,2,1,0:T(8,128)S(1)}, f32[3,2,16,256]{3,2,1,0:T(8,128)S(1)}, u32[]{:S(2)}, u32[]{:S(2)}) %collective-permute-start.7) | collective-permute-done | bytes 98336 | tf_op jit(solution)/shard_map/ppermute | solution.py:270
  89.8 0.7 concatenate.27.src_ref
  90.6 2.4 %shard_map.69.rest_0_.refs_1_ = f32[2,16,256]{2,1,0:T(8,128)} custom-call(s32[54]{0:T(128)} %reshape.87.tab_ref, f32[19,16,256]{2,1,0:T(8,128)} %concatenate.27.src_ref, f32[2,16,256]{2,1,0:T(8,128)} %bitcast.79), custom_call_target="tpu_custom_call" | custom-call | flops 491520 | bytes 377048 | tf_op jit(solution)/shard_map/pallas_call | solution.py:258
  92.9 3.6 %collective-permute-start.8 = (f32[2,16,256]{2,1,0:T(8,128)}, f32[2,16,256]{2,1,0:T(8,128)S(1)}, u32[]{:S(2)}, u32[]{:S(2)}) collective-permute-start(f32[2,16,256]{2,1,0:T(8,128)} %shard_map.69.rest_0_.refs_1_), channel_id=1, source_target_pairs={{0,8},{8,16},{16,24},{24,32},{32,40},{40,48},{48,56},{56,64},{64,7... | collective-permute-start | bytes 98312 | tf_op jit(solution)/shard_map/ppermute | solution.py:270
  96.5 1.9 %collective-permute-start.9 = (f32[2,16,256]{2,1,0:T(8,128)}, f32[2,16,256]{2,1,0:T(8,128)S(1)}, u32[]{:S(2)}, u32[]{:S(2)}) collective-permute-start(f32[2,16,256]{2,1,0:T(8,128)} %shard_map.69.rest_0_.refs_1_), channel_id=1, source_target_pairs={{8,0},{16,8},{24,16},{32,24},{40,32},{48,40},{56,48},{64,56},{72,6... | collective-permute-start | bytes 98312 | tf_op jit(solution)/shard_map/ppermute | solution.py:270
  98.4 0.0 collective-permute-done.8
  98.4 3.5 %collective-permute-done.9 = f32[2,16,256]{2,1,0:T(8,128)S(1)} collective-permute-done((f32[2,16,256]{2,1,0:T(8,128)}, f32[2,16,256]{2,1,0:T(8,128)S(1)}, u32[]{:S(2)}, u32[]{:S(2)}) %collective-permute-start.9) | collective-permute-done | bytes 32800 | tf_op jit(solution)/shard_map/ppermute | solution.py:270
  102.0 0.8 fusion.20
  102.7 5.1 %collective-permute-start.10 = (f32[3,2,16,256]{3,2,1,0:T(8,128)S(1)}, f32[3,2,16,256]{3,2,1,0:T(8,128)S(1)}, u32[]{:S(2)}, u32[]{:S(2)}) collective-permute-start(f32[3,2,16,256]{3,2,1,0:T(8,128)S(1)} %get-tuple-element.11), channel_id=1, source_target_pairs={{0,1},{1,2},{2,3},{3,4},{4,5},{5,6},{6,7},{8,9},{9,10},{10,11},{11... | collective-permute-start | bytes 294920 | tf_op jit(solution)/shard_map/ppermute | solution.py:270
  107.8 1.3 collective-permute-start.11
  109.1 0.3 collective-permute-done.10
  109.4 3.7 %collective-permute-done.11 = f32[3,2,16,256]{3,2,1,0:T(8,128)S(1)} collective-permute-done((f32[3,2,16,256]{3,2,1,0:T(8,128)S(1)}, f32[3,2,16,256]{3,2,1,0:T(8,128)S(1)}, u32[]{:S(2)}, u32[]{:S(2)}) %collective-permute-start.11) | collective-permute-done | bytes 98336 | tf_op jit(solution)/shard_map/ppermute | solution.py:270
  113.2 0.7 concatenate.28.src_ref
  114.0 2.4 %shard_map.70.refs_2_ = f32[2,16,256]{2,1,0:T(8,128)} custom-call(s32[54]{0:T(128)} %reshape.87.tab_ref, f32[19,16,256]{2,1,0:T(8,128)} %concatenate.28.src_ref, f32[2,16,256]{2,1,0:T(8,128)} %bitcast.80, f32[2,16,256]{2,1,0:T(8,128)} %shard_map.68.rest_0_.refs_0_), custom_call_target="tpu_custom_call" | custom-call | flops 491520 | bytes 409816 | tf_op jit(solution)/shard_map/pallas_call | solution.py:258
  116.3 3.4 %collective-permute-start.12 = (f32[2,16,256]{2,1,0:T(8,128)}, f32[2,16,256]{2,1,0:T(8,128)S(1)}, u32[]{:S(2)}, u32[]{:S(2)}) collective-permute-start(f32[2,16,256]{2,1,0:T(8,128)} %shard_map.70.refs_2_), channel_id=1, source_target_pairs={{0,8},{8,16},{16,24},{24,32},{32,40},{40,48},{48,56},{56,64},{64,7... | collective-permute-start | bytes 98312 | tf_op jit(solution)/shard_map/ppermute | solution.py:270
  119.8 1.9 %collective-permute-start.13 = (f32[2,16,256]{2,1,0:T(8,128)}, f32[2,16,256]{2,1,0:T(8,128)S(1)}, u32[]{:S(2)}, u32[]{:S(2)}) collective-permute-start(f32[2,16,256]{2,1,0:T(8,128)} %shard_map.70.refs_2_), channel_id=1, source_target_pairs={{8,0},{16,8},{24,16},{32,24},{40,32},{48,40},{56,48},{64,56},{72,6... | collective-permute-start | bytes 98312 | tf_op jit(solution)/shard_map/ppermute | solution.py:270
  121.7 3.5 %collective-permute-done.13 = f32[2,16,256]{2,1,0:T(8,128)S(1)} collective-permute-done((f32[2,16,256]{2,1,0:T(8,128)}, f32[2,16,256]{2,1,0:T(8,128)S(1)}, u32[]{:S(2)}, u32[]{:S(2)}) %collective-permute-start.13) | collective-permute-done | bytes 32800 | tf_op jit(solution)/shard_map/ppermute | solution.py:270
  125.2 0.8 fusion.19
  126.0 3.4 %collective-permute-start.14 = (f32[3,2,16,256]{3,2,1,0:T(8,128)S(1)}, f32[3,2,16,256]{3,2,1,0:T(8,128)S(1)}, u32[]{:S(2)}, u32[]{:S(2)}) collective-permute-start(f32[3,2,16,256]{3,2,1,0:T(8,128)S(1)} %get-tuple-element.9), channel_id=1, source_target_pairs={{0,1},{1,2},{2,3},{3,4},{4,5},{5,6},{6,7},{8,9},{9,10},{10,11},{11... | collective-permute-start | bytes 294920 | tf_op jit(solution)/shard_map/ppermute | solution.py:270
  129.4 1.3 collective-permute-start.15
  130.7 0.3 collective-permute-done.14
  131.0 3.7 %collective-permute-done.15 = f32[3,2,16,256]{3,2,1,0:T(8,128)S(1)} collective-permute-done((f32[3,2,16,256]{3,2,1,0:T(8,128)S(1)}, f32[3,2,16,256]{3,2,1,0:T(8,128)S(1)}, u32[]{:S(2)}, u32[]{:S(2)}) %collective-permute-start.15) | collective-permute-done | bytes 98336 | tf_op jit(solution)/shard_map/ppermute | solution.py:270
  134.8 0.7 concatenate.29.src_ref
  135.5 2.4 %shard_map.71.refs_3_ = f32[2,16,256]{2,1,0:T(8,128)} custom-call(s32[54]{0:T(128)} %reshape.87.tab_ref, f32[19,16,256]{2,1,0:T(8,128)} %concatenate.29.src_ref, f32[2,16,256]{2,1,0:T(8,128)} %bitcast.81, f32[2,16,256]{2,1,0:T(8,128)} %shard_map.69.rest_0_.refs_1_), custom_call_target="tpu_custom_call" | custom-call | flops 491520 | bytes 409816 | tf_op jit(solution)/shard_map/pallas_call | solution.py:258
  137.9 2.1 %shard_map.72 = f32[1,32]{1,0:T(1,128)} custom-call(f32[2,16,256]{2,1,0:T(8,128)} %shard_map.68.rest_0_.refs_0_, f32[2,16,256]{2,1,0:T(8,128)} %shard_map.69.rest_0_.refs_1_, f32[2,16,256]{2,1,0:T(8,128)} %shard_map.70.refs_2_, f32[2,16,256]{2,1,0:T(8,128)} %shard_map.71.refs_3_), custom_call_target="tpu_custom_call" | custom-call | tf_op jit(solution)/shard_map/pallas_call | solution.py:333
  140.0 0.8 broadcast_in_dim.10
  140.8 36.9 %all_to_all.15 = f32[512,1,32]{2,1,0:T(1,128)S(1)} all-to-all(f32[512,1,32]{2,1,0:T(1,128)S(1)} %broadcast_in_dim.10), channel_id=1, replica_groups=mesh['wide'=64,'narrow'=8] {'wide','narrow'}, dimensions={0} | all-to-all | bytes 131072 | tf_op jit(solution)/shard_map/all_to_all | solution.py:336
  177.7 0.7 copy.30
  178.4 2.1 %shard_map.73 = (f32[2,4096]{1,0:T(2,128)}, f32[2,4096]{1,0:T(2,128)}) custom-call(f32[32,512]{1,0:T(8,128)} %bitcast.90, f32[2,16,256]{2,1,0:T(8,128)} %shard_map.68.rest_0_.refs_0_, f32[2,16,256]{2,1,0:T(8,128)} %shard_map.69.rest_0_.refs_1_, f32[2,16,256]{2,1,0:T(8,128)} %shard_map.70.refs_2_, f32[2,16,256]{2,1,0:T(8,128)} %shard_map.71.refs_3_), custom_call_target="tpu_custom_call" | custom-call | tf_op jit(solution)/shard_map/pallas_call | solution.py:338
  (26 shorter events, 0.3 us)
Async XLA Ops:
  0.6 2.1 %copy-start.1 = (s32[1024,1]{0,1:T(1,128)S(1)}, s32[1024,1]{0,1:T(1,128)}, u32[]{:S(2)}) copy-start(s32[1024,1]{0,1:T(1,128)} %param.5) | copy-start | bytes 12292
  0.6 2.1 %copy-start.2 = (s32[1024]{0:T(1024)S(1)}, s32[1024]{0:T(1024)}, u32[]{:S(2)}) copy-start(s32[1024]{0:T(1024)} %param.6) | copy-start | bytes 12292
  0.7 2.1 %copy-start = (f32[3,1024]{1,0:T(4,128)S(1)}, f32[3,1024]{1,0:T(4,128)}, u32[]{:S(2)}) copy-start(f32[3,1024]{1,0:T(4,128)} %param.7) | copy-start | bytes 36868
  40.1 16.5 %copy-start.3 = (s32[1,1,2,27]{3,2,1,0:T(2,128)S(1)}, s32[1,1,2,27]{3,2,1,0:T(2,128)}, u32[]{:S(2)}) copy-start(s32[1,1,2,27]{3,2,1,0:T(2,128)} %param.9) | copy-start | bytes 652
  42.4 4.7 %collective-permute-start = (f32[3,2,16,256]{3,2,1,0:T(8,128)S(1)}, f32[3,2,16,256]{3,2,1,0:T(8,128)S(1)}, u32[]{:S(2)}, u32[]{:S(2)}) collective-permute-start(f32[3,2,16,256]{3,2,1,0:T(8,128)S(1)} %bitcast.85), channel_id=1, source_target_pairs={{0,8},{8,16},{16,24},{24,32},{32,40},{40,48},{48,56},{56,64},{64,7... | collective-permute-start | bytes 294920 | tf_op jit(solution)/shard_map/ppermute | solution.py:270
  45.2 5.9 %collective-permute-start.1 = (f32[3,2,16,256]{3,2,1,0:T(8,128)S(1)}, f32[3,2,16,256]{3,2,1,0:T(8,128)S(1)}, u32[]{:S(2)}, u32[]{:S(2)}) collective-permute-start(f32[3,2,16,256]{3,2,1,0:T(8,128)S(1)} %bitcast.86), channel_id=1, source_target_pairs={{8,0},{16,8},{24,16},{32,24},{40,32},{48,40},{56,48},{64,56},{72,6... | collective-permute-start | bytes 294920 | tf_op jit(solution)/shard_map/ppermute | solution.py:270
  51.2 8.5 %collective-permute-start.2 = (f32[3,3,2,16,256]{4,3,2,1,0:T(8,128)S(1)}, f32[3,3,2,16,256]{4,3,2,1,0:T(8,128)S(1)}, u32[]{:S(2)}, u32[]{:S(2)}) collective-permute-start(f32[3,3,2,16,256]{4,3,2,1,0:T(8,128)S(1)} %get-tuple-element.7), channel_id=1, source_target_pairs={{0,1},{1,2},{2,3},{3,4},{4,5},{5,6},{6,7},{8,9},{9,10},{10,11},{11... | collective-permute-start | bytes 884744 | tf_op jit(solution)/shard_map/ppermute | solution.py:270
  55.2 9.0 %collective-permute-start.3 = (f32[3,3,2,16,256]{4,3,2,1,0:T(8,128)S(1)}, f32[3,3,2,16,256]{4,3,2,1,0:T(8,128)S(1)}, u32[]{:S(2)}, u32[]{:S(2)}) collective-permute-start(f32[3,3,2,16,256]{4,3,2,1,0:T(8,128)S(1)} %get-tuple-element.7), channel_id=1, source_target_pairs={{1,0},{2,1},{3,2},{4,3},{5,4},{6,5},{7,6},{9,8},{10,9},{11,10},{12... | collective-permute-start | bytes 884744 | tf_op jit(solution)/shard_map/ppermute | solution.py:270
  67.3 7.0 %collective-permute-start.4 = (f32[2,16,256]{2,1,0:T(8,128)}, f32[2,16,256]{2,1,0:T(8,128)S(1)}, u32[]{:S(2)}, u32[]{:S(2)}) collective-permute-start(f32[2,16,256]{2,1,0:T(8,128)} %shard_map.68.rest_0_.refs_0_), channel_id=1, source_target_pairs={{0,8},{8,16},{16,24},{24,32},{32,40},{40,48},{48,56},{56,64},{64,7... | collective-permute-start | bytes 98312 | tf_op jit(solution)/shard_map/ppermute | solution.py:270
  72.3 5.4 %collective-permute-start.5 = (f32[2,16,256]{2,1,0:T(8,128)}, f32[2,16,256]{2,1,0:T(8,128)S(1)}, u32[]{:S(2)}, u32[]{:S(2)}) collective-permute-start(f32[2,16,256]{2,1,0:T(8,128)} %shard_map.68.rest_0_.refs_0_), channel_id=1, source_target_pairs={{8,0},{16,8},{24,16},{32,24},{40,32},{48,40},{56,48},{64,56},{72,6... | collective-permute-start | bytes 98312 | tf_op jit(solution)/shard_map/ppermute | solution.py:270
  78.6 5.9 %collective-permute-start.6 = (f32[3,2,16,256]{3,2,1,0:T(8,128)S(1)}, f32[3,2,16,256]{3,2,1,0:T(8,128)S(1)}, u32[]{:S(2)}, u32[]{:S(2)}) collective-permute-start(f32[3,2,16,256]{3,2,1,0:T(8,128)S(1)} %get-tuple-element.13), channel_id=1, source_target_pairs={{0,1},{1,2},{2,3},{3,4},{4,5},{5,6},{6,7},{8,9},{9,10},{10,11},{11... | collective-permute-start | bytes 294920 | tf_op jit(solution)/shard_map/ppermute | solution.py:270
  82.6 7.2 %collective-permute-start.7 = (f32[3,2,16,256]{3,2,1,0:T(8,128)S(1)}, f32[3,2,16,256]{3,2,1,0:T(8,128)S(1)}, u32[]{:S(2)}, u32[]{:S(2)}) collective-permute-start(f32[3,2,16,256]{3,2,1,0:T(8,128)S(1)} %get-tuple-element.13), channel_id=1, source_target_pairs={{1,0},{2,1},{3,2},{4,3},{5,4},{6,5},{7,6},{9,8},{10,9},{11,10},{12... | collective-permute-start | bytes 294920 | tf_op jit(solution)/shard_map/ppermute | solution.py:270
  92.9 5.5 %collective-permute-start.8 = (f32[2,16,256]{2,1,0:T(8,128)}, f32[2,16,256]{2,1,0:T(8,128)S(1)}, u32[]{:S(2)}, u32[]{:S(2)}) collective-permute-start(f32[2,16,256]{2,1,0:T(8,128)} %shard_map.69.rest_0_.refs_1_), channel_id=1, source_target_pairs={{0,8},{8,16},{16,24},{24,32},{32,40},{40,48},{48,56},{56,64},{64,7... | collective-permute-start | bytes 98312 | tf_op jit(solution)/shard_map/ppermute | solution.py:270
  96.5 5.4 %collective-permute-start.9 = (f32[2,16,256]{2,1,0:T(8,128)}, f32[2,16,256]{2,1,0:T(8,128)S(1)}, u32[]{:S(2)}, u32[]{:S(2)}) collective-permute-start(f32[2,16,256]{2,1,0:T(8,128)} %shard_map.69.rest_0_.refs_1_), channel_id=1, source_target_pairs={{8,0},{16,8},{24,16},{32,24},{40,32},{48,40},{56,48},{64,56},{72,6... | collective-permute-start | bytes 98312 | tf_op jit(solution)/shard_map/ppermute | solution.py:270
  102.7 6.7 %collective-permute-start.10 = (f32[3,2,16,256]{3,2,1,0:T(8,128)S(1)}, f32[3,2,16,256]{3,2,1,0:T(8,128)S(1)}, u32[]{:S(2)}, u32[]{:S(2)}) collective-permute-start(f32[3,2,16,256]{3,2,1,0:T(8,128)S(1)} %get-tuple-element.11), channel_id=1, source_target_pairs={{0,1},{1,2},{2,3},{3,4},{4,5},{5,6},{6,7},{8,9},{9,10},{10,11},{11... | collective-permute-start | bytes 294920 | tf_op jit(solution)/shard_map/ppermute | solution.py:270
  107.8 5.4 %collective-permute-start.11 = (f32[3,2,16,256]{3,2,1,0:T(8,128)S(1)}, f32[3,2,16,256]{3,2,1,0:T(8,128)S(1)}, u32[]{:S(2)}, u32[]{:S(2)}) collective-permute-start(f32[3,2,16,256]{3,2,1,0:T(8,128)S(1)} %get-tuple-element.11), channel_id=1, source_target_pairs={{1,0},{2,1},{3,2},{4,3},{5,4},{6,5},{7,6},{9,8},{10,9},{11,10},{12... | collective-permute-start | bytes 294920 | tf_op jit(solution)/shard_map/ppermute | solution.py:270
  116.3 5.4 %collective-permute-start.12 = (f32[2,16,256]{2,1,0:T(8,128)}, f32[2,16,256]{2,1,0:T(8,128)S(1)}, u32[]{:S(2)}, u32[]{:S(2)}) collective-permute-start(f32[2,16,256]{2,1,0:T(8,128)} %shard_map.70.refs_2_), channel_id=1, source_target_pairs={{0,8},{8,16},{16,24},{24,32},{32,40},{40,48},{48,56},{56,64},{64,7... | collective-permute-start | bytes 98312 | tf_op jit(solution)/shard_map/ppermute | solution.py:270
  119.8 5.4 %collective-permute-start.13 = (f32[2,16,256]{2,1,0:T(8,128)}, f32[2,16,256]{2,1,0:T(8,128)S(1)}, u32[]{:S(2)}, u32[]{:S(2)}) collective-permute-start(f32[2,16,256]{2,1,0:T(8,128)} %shard_map.70.refs_2_), channel_id=1, source_target_pairs={{8,0},{16,8},{24,16},{32,24},{40,32},{48,40},{56,48},{64,56},{72,6... | collective-permute-start | bytes 98312 | tf_op jit(solution)/shard_map/ppermute | solution.py:270
  126.0 5.0 %collective-permute-start.14 = (f32[3,2,16,256]{3,2,1,0:T(8,128)S(1)}, f32[3,2,16,256]{3,2,1,0:T(8,128)S(1)}, u32[]{:S(2)}, u32[]{:S(2)}) collective-permute-start(f32[3,2,16,256]{3,2,1,0:T(8,128)S(1)} %get-tuple-element.9), channel_id=1, source_target_pairs={{0,1},{1,2},{2,3},{3,4},{4,5},{5,6},{6,7},{8,9},{9,10},{10,11},{11... | collective-permute-start | bytes 294920 | tf_op jit(solution)/shard_map/ppermute | solution.py:270
  129.4 5.4 %collective-permute-start.15 = (f32[3,2,16,256]{3,2,1,0:T(8,128)S(1)}, f32[3,2,16,256]{3,2,1,0:T(8,128)S(1)}, u32[]{:S(2)}, u32[]{:S(2)}) collective-permute-start(f32[3,2,16,256]{3,2,1,0:T(8,128)S(1)} %get-tuple-element.9), channel_id=1, source_target_pairs={{1,0},{2,1},{3,2},{4,3},{5,4},{6,5},{7,6},{9,8},{10,9},{11,10},{12... | collective-permute-start | bytes 294920 | tf_op jit(solution)/shard_map/ppermute | solution.py:270

commit v13 on v11

--- a/solution.py
+++ b/solution.py
@@ -290,10 +290,8 @@
     slots = jnp.arange(point_total, dtype=jnp.int32)
     is_live = slots < strip_count[0]
     code = jnp.where(is_live, point_cell + 1, 0).astype(jnp.float32)
-    owner_hot = (owner[:, None] == jnp.arange(owners, dtype=jnp.int32)[None, :]).astype(jnp.bfloat16)
-    earlier = (slots[None, :] < slots[:, None]).astype(jnp.bfloat16)
-    before = jnp.dot(earlier, owner_hot, preferred_element_type=jnp.float32)
-    rank = jnp.sum(before * owner_hot.astype(jnp.float32), axis=1).astype(jnp.int32)
+    owner_hot = (owner[:, None] == jnp.arange(owners, dtype=jnp.int32)[None, :]).astype(jnp.int32)
+    rank = jnp.sum((jnp.cumsum(owner_hot, axis=0) - owner_hot) * owner_hot, axis=1)
     dest = owner * CAP + rank
     payload = jnp.concatenate([code[:, None], normals.T], axis=1)
     place_hot = (jnp.arange(owners * CAP, dtype=jnp.int32)[:, None] == dest[None, :]).astype(jnp.bfloat16)

time: 170 us -> 188 us (1.11)
  other arithmetic: 5.38 us -> 24.4 us
    another operation x1 -> x4, other arithmetic: 0.02 us -> 18.2 us
where the time goes in v13:
time: 188 us; the launch traced here: 187 us
  blocking collectives  57.8 us (31%)
  starting transfers between devices  44.1 us (23%)
  waiting for transfers between devices  35 us (19%)
  other arithmetic  24.4 us (13%)
  Pallas kernels  13.3 us (7%)
  local copies, waits for them, and re-layouts  6.91 us (4%)
  matrix products  3.72 us (2%)
    ppermute x16, starting transfers between devices, _shift(): return lax.ppermute(field, axis, pairs)  44.1 us
    all_to_all x1, blocking collectives, shards(): lax.all_to_all(jnp.broadcast_to(payload, (devices, 32)), ('wide', 'narrow...  37 us
    ppermute x16, waiting for transfers between devices, _shift(): return lax.ppermute(field, axis, pairs)  35 us
    all_to_all x1, blocking collectives, shards(): lax.all_to_all(send.reshape(owners, CAP, 4), 'wide', 0, 0, tiled=True)  20.8 us
    another operation x4, other arithmetic  18.2 us
    pallas_call x4, Pallas kernels, _local_call(): pl.pallas_call(kernel, out_shape=jax.ShapeDtypeStruct(out_shape, jnp.floa...  9.05 us
  transfers between devices with their start and end apart: 16, of which 11 were waited for; matrix products, arithmetic and copies ran while one was open for 1% of the time, Pallas kernels for 0%

profile of v13, /device:TPU:1, one launch (start us, length us, event | category | flops | bytes accessed | tf_op | source)
XLA Modules:
  0.0 186.9 jit_solution(11544990200809371271)
XLA Ops:
  0.6 0.8 fusion.18
  1.4 18.0 %reduce-window.6 = s32[64,8,128]{2,1,0:T(8,128)S(1)} reduce-window(s32[64,8,128]{2,1,0:T(8,128)S(1)} %fusion.18, s32[]{:T(128)} %constant.10.clone.1), window={size=1x1x128 pad=0_0x0_0x127_0}, to_apply=%region_0.1 | reduce-window | flops 8323072 | bytes 524292 | tf_op jit(solution)/shard_map/reduce-window
  19.4 0.1 slice.49
  19.6 0.1 copy.23
  19.8 0.1 copy.24
  19.9 0.1 broadcast_add_fusion
  20.0 0.1 fusion.17
  20.8 1.5 fusion
  22.3 0.1 reshape.72
  22.4 0.1 copy.38
  22.5 0.1 reshape.80
  22.6 20.8 %all_to_all.14 = f32[64,1,128]{2,1,0:T(1,128)S(1)} all-to-all(f32[64,1,128]{2,1,0:T(1,128)S(1)} %reshape.80), channel_id=1, replica_groups=mesh['wide'=64,'narrow'=8] {'wide'}, dimensions={0} | all-to-all | bytes 65536 | tf_op jit(solution)/shard_map/all_to_all | solution.py:299
  43.4 0.5 broadcast.61
  43.9 0.7 reduce
  44.7 0.1 reshape.81
  44.8 0.1 reshape.73
  45.0 0.3 fusion.11
  45.3 1.1 fusion.14
  46.5 2.2 %fusion.2 = f32[128,256]{1,0:T(8,128)S(1)} fusion(f32[2048,32]{1,0:T(8,128)S(1)} %fusion.11, f32[2048,32]{1,0:T(8,128)S(1)} %get-tuple-element.23, f32[2048,32]{1,0:T(8,128)S(1)} %get-tuple-element.24, f32[2048,32]{1,0:T(8,128)S(1)} %get-tuple-element.22, s32[2048]{0:T(1024)S(1)} %bitcast.117), kind=kOutput, calls=%fused_computation.4 | convolution fusion | flops 806617088 | bytes 1187840 | tf_op jit(solution)/shard_map/pa,pb->ab/dot_general | solution.py:307
  48.8 2.8 %collective-permute-start = (f32[3,2,16,256]{3,2,1,0:T(8,128)S(1)}, f32[3,2,16,256]{3,2,1,0:T(8,128)S(1)}, u32[]{:S(2)}, u32[]{:S(2)}) collective-permute-start(f32[3,2,16,256]{3,2,1,0:T(8,128)S(1)} %bitcast.98), channel_id=1, source_target_pairs={{0,8},{8,16},{16,24},{24,32},{32,40},{40,48},{48,56},{56,64},{64,7... | collective-permute-start | bytes 294920 | tf_op jit(solution)/shard_map/ppermute | solution.py:270
  51.5 1.9 %collective-permute-start.1 = (f32[3,2,16,256]{3,2,1,0:T(8,128)S(1)}, f32[3,2,16,256]{3,2,1,0:T(8,128)S(1)}, u32[]{:S(2)}, u32[]{:S(2)}) collective-permute-start(f32[3,2,16,256]{3,2,1,0:T(8,128)S(1)} %bitcast.99), channel_id=1, source_target_pairs={{8,0},{16,8},{24,16},{32,24},{40,32},{48,40},{56,48},{64,56},{72,6... | collective-permute-start | bytes 294920 | tf_op jit(solution)/shard_map/ppermute | solution.py:270
  53.5 4.0 %collective-permute-done.1 = f32[3,2,16,256]{3,2,1,0:T(8,128)S(1)} collective-permute-done((f32[3,2,16,256]{3,2,1,0:T(8,128)S(1)}, f32[3,2,16,256]{3,2,1,0:T(8,128)S(1)}, u32[]{:S(2)}, u32[]{:S(2)}) %collective-permute-start.1) | collective-permute-done | bytes 98336 | tf_op jit(solution)/shard_map/ppermute | solution.py:270
  57.5 4.0 %collective-permute-start.2 = (f32[3,3,2,16,256]{4,3,2,1,0:T(8,128)S(1)}, f32[3,3,2,16,256]{4,3,2,1,0:T(8,128)S(1)}, u32[]{:S(2)}, u32[]{:S(2)}) collective-permute-start(f32[3,3,2,16,256]{4,3,2,1,0:T(8,128)S(1)} %get-tuple-element.7), channel_id=1, source_target_pairs={{0,1},{1,2},{2,3},{3,4},{4,5},{5,6},{6,7},{8,9},{9,10},{10,11},{11... | collective-permute-start | bytes 884744 | tf_op jit(solution)/shard_map/ppermute | solution.py:270
  61.6 1.3 collective-permute-start.3
  62.9 0.6 reshape.70.tab_ref
  63.5 2.6 %collective-permute-done.2 = f32[3,3,2,16,256]{4,3,2,1,0:T(8,128)S(1)} collective-permute-done((f32[3,3,2,16,256]{4,3,2,1,0:T(8,128)S(1)}, f32[3,3,2,16,256]{4,3,2,1,0:T(8,128)S(1)}, u32[]{:S(2)}, u32[]{:S(2)}) %collective-permute-start.2) | collective-permute-done | bytes 294944 | tf_op jit(solution)/shard_map/ppermute | solution.py:270
  66.1 4.5 %collective-permute-done.3 = f32[3,3,2,16,256]{4,3,2,1,0:T(8,128)S(1)} collective-permute-done((f32[3,3,2,16,256]{4,3,2,1,0:T(8,128)S(1)}, f32[3,3,2,16,256]{4,3,2,1,0:T(8,128)S(1)}, u32[]{:S(2)}, u32[]{:S(2)}) %collective-permute-start.3) | collective-permute-done | bytes 294944 | tf_op jit(solution)/shard_map/ppermute | solution.py:270
  70.6 1.0 concatenate.25.src_ref
  71.6 1.9 %shard_map.68.rest_0_.refs_0_ = f32[2,16,256]{2,1,0:T(8,128)} custom-call(s32[54]{0:T(128)} %reshape.70.tab_ref, f32[3,19,16,256]{3,2,1,0:T(8,128)} %concatenate.25.src_ref), custom_call_target="tpu_custom_call" | custom-call | flops 163840 | bytes 966872 | tf_op jit(solution)/shard_map/pallas_call | solution.py:258
  73.6 5.1 %collective-permute-start.4 = (f32[2,16,256]{2,1,0:T(8,128)}, f32[2,16,256]{2,1,0:T(8,128)S(1)}, u32[]{:S(2)}, u32[]{:S(2)}) collective-permute-start(f32[2,16,256]{2,1,0:T(8,128)} %shard_map.68.rest_0_.refs_0_), channel_id=1, source_target_pairs={{0,8},{8,16},{16,24},{24,32},{32,40},{40,48},{48,56},{56,64},{64,7... | collective-permute-start | bytes 98312 | tf_op jit(solution)/shard_map/ppermute | solution.py:270
  78.7 1.9 %collective-permute-start.5 = (f32[2,16,256]{2,1,0:T(8,128)}, f32[2,16,256]{2,1,0:T(8,128)S(1)}, u32[]{:S(2)}, u32[]{:S(2)}) collective-permute-start(f32[2,16,256]{2,1,0:T(8,128)} %shard_map.68.rest_0_.refs_0_), channel_id=1, source_target_pairs={{8,0},{16,8},{24,16},{32,24},{40,32},{48,40},{56,48},{64,56},{72,6... | collective-permute-start | bytes 98312 | tf_op jit(solution)/shard_map/ppermute | solution.py:270
  80.6 3.5 %collective-permute-done.5 = f32[2,16,256]{2,1,0:T(8,128)S(1)} collective-permute-done((f32[2,16,256]{2,1,0:T(8,128)}, f32[2,16,256]{2,1,0:T(8,128)S(1)}, u32[]{:S(2)}, u32[]{:S(2)}) %collective-permute-start.5) | collective-permute-done | bytes 32800 | tf_op jit(solution)/shard_map/ppermute | solution.py:270
  84.1 0.8 fusion.31
  84.9 4.0 %collective-permute-start.6 = (f32[3,2,16,256]{3,2,1,0:T(8,128)S(1)}, f32[3,2,16,256]{3,2,1,0:T(8,128)S(1)}, u32[]{:S(2)}, u32[]{:S(2)}) collective-permute-start(f32[3,2,16,256]{3,2,1,0:T(8,128)S(1)} %get-tuple-element.13), channel_id=1, source_target_pairs={{0,1},{1,2},{2,3},{3,4},{4,5},{5,6},{6,7},{8,9},{9,10},{10,11},{11... | collective-permute-start | bytes 294920 | tf_op jit(solution)/shard_map/ppermute | solution.py:270
  88.9 1.3 collective-permute-start.7
  90.2 0.6 fusion.19
  90.8 5.3 %collective-permute-done.7 = f32[3,2,16,256]{3,2,1,0:T(8,128)S(1)} collective-permute-done((f32[3,2,16,256]{3,2,1,0:T(8,128)S(1)}, f32[3,2,16,256]{3,2,1,0:T(8,128)S(1)}, u32[]{:S(2)}, u32[]{:S(2)}) %collective-permute-start.7) | collective-permute-done | bytes 98336 | tf_op jit(solution)/shard_map/ppermute | solution.py:270
  96.2 0.7 concatenate.26.src_ref
  96.9 2.4 %shard_map.69.rest_0_.refs_1_ = f32[2,16,256]{2,1,0:T(8,128)} custom-call(s32[54]{0:T(128)} %reshape.70.tab_ref, f32[19,16,256]{2,1,0:T(8,128)} %concatenate.26.src_ref, f32[2,16,256]{2,1,0:T(8,128)} %bitcast.92), custom_call_target="tpu_custom_call" | custom-call | flops 491520 | bytes 377048 | tf_op jit(solution)/shard_map/pallas_call | solution.py:258
  99.3 3.6 %collective-permute-start.8 = (f32[2,16,256]{2,1,0:T(8,128)}, f32[2,16,256]{2,1,0:T(8,128)S(1)}, u32[]{:S(2)}, u32[]{:S(2)}) collective-permute-start(f32[2,16,256]{2,1,0:T(8,128)} %shard_map.69.rest_0_.refs_1_), channel_id=1, source_target_pairs={{0,8},{8,16},{16,24},{24,32},{32,40},{40,48},{48,56},{56,64},{64,7... | collective-permute-start | bytes 98312 | tf_op jit(solution)/shard_map/ppermute | solution.py:270
  102.8 1.9 %collective-permute-start.9 = (f32[2,16,256]{2,1,0:T(8,128)}, f32[2,16,256]{2,1,0:T(8,128)S(1)}, u32[]{:S(2)}, u32[]{:S(2)}) collective-permute-start(f32[2,16,256]{2,1,0:T(8,128)} %shard_map.69.rest_0_.refs_1_), channel_id=1, source_target_pairs={{8,0},{16,8},{24,16},{32,24},{40,32},{48,40},{56,48},{64,56},{72,6... | collective-permute-start | bytes 98312 | tf_op jit(solution)/shard_map/ppermute | solution.py:270
  104.8 3.5 %collective-permute-done.9 = f32[2,16,256]{2,1,0:T(8,128)S(1)} collective-permute-done((f32[2,16,256]{2,1,0:T(8,128)}, f32[2,16,256]{2,1,0:T(8,128)S(1)}, u32[]{:S(2)}, u32[]{:S(2)}) %collective-permute-start.9) | collective-permute-done | bytes 32800 | tf_op jit(solution)/shard_map/ppermute | solution.py:270
  108.3 0.8 fusion.30
  109.1 5.1 %collective-permute-start.10 = (f32[3,2,16,256]{3,2,1,0:T(8,128)S(1)}, f32[3,2,16,256]{3,2,1,0:T(8,128)S(1)}, u32[]{:S(2)}, u32[]{:S(2)}) collective-permute-start(f32[3,2,16,256]{3,2,1,0:T(8,128)S(1)} %get-tuple-element.11), channel_id=1, source_target_pairs={{0,1},{1,2},{2,3},{3,4},{4,5},{5,6},{6,7},{8,9},{9,10},{10,11},{11... | collective-permute-start | bytes 294920 | tf_op jit(solution)/shard_map/ppermute | solution.py:270
  114.1 1.3 collective-permute-start.11
  115.4 0.3 collective-permute-done.10
  115.7 3.7 %collective-permute-done.11 = f32[3,2,16,256]{3,2,1,0:T(8,128)S(1)} collective-permute-done((f32[3,2,16,256]{3,2,1,0:T(8,128)S(1)}, f32[3,2,16,256]{3,2,1,0:T(8,128)S(1)}, u32[]{:S(2)}, u32[]{:S(2)}) %collective-permute-start.11) | collective-permute-done | bytes 98336 | tf_op jit(solution)/shard_map/ppermute | solution.py:270
  119.5 0.7 concatenate.27.src_ref
  120.3 2.4 %shard_map.70.refs_2_ = f32[2,16,256]{2,1,0:T(8,128)} custom-call(s32[54]{0:T(128)} %reshape.70.tab_ref, f32[19,16,256]{2,1,0:T(8,128)} %concatenate.27.src_ref, f32[2,16,256]{2,1,0:T(8,128)} %bitcast.93, f32[2,16,256]{2,1,0:T(8,128)} %shard_map.68.rest_0_.refs_0_), custom_call_target="tpu_custom_call" | custom-call | flops 491520 | bytes 409816 | tf_op jit(solution)/shard_map/pallas_call | solution.py:258
  122.7 3.4 %collective-permute-start.12 = (f32[2,16,256]{2,1,0:T(8,128)}, f32[2,16,256]{2,1,0:T(8,128)S(1)}, u32[]{:S(2)}, u32[]{:S(2)}) collective-permute-start(f32[2,16,256]{2,1,0:T(8,128)} %shard_map.70.refs_2_), channel_id=1, source_target_pairs={{0,8},{8,16},{16,24},{24,32},{32,40},{40,48},{48,56},{56,64},{64,7... | collective-permute-start | bytes 98312 | tf_op jit(solution)/shard_map/ppermute | solution.py:270
  126.1 1.9 %collective-permute-start.13 = (f32[2,16,256]{2,1,0:T(8,128)}, f32[2,16,256]{2,1,0:T(8,128)S(1)}, u32[]{:S(2)}, u32[]{:S(2)}) collective-permute-start(f32[2,16,256]{2,1,0:T(8,128)} %shard_map.70.refs_2_), channel_id=1, source_target_pairs={{8,0},{16,8},{24,16},{32,24},{40,32},{48,40},{56,48},{64,56},{72,6... | collective-permute-start | bytes 98312 | tf_op jit(solution)/shard_map/ppermute | solution.py:270
  128.0 3.5 %collective-permute-done.13 = f32[2,16,256]{2,1,0:T(8,128)S(1)} collective-permute-done((f32[2,16,256]{2,1,0:T(8,128)}, f32[2,16,256]{2,1,0:T(8,128)S(1)}, u32[]{:S(2)}, u32[]{:S(2)}) %collective-permute-start.13) | collective-permute-done | bytes 32800 | tf_op jit(solution)/shard_map/ppermute | solution.py:270
  131.5 0.8 fusion.29
  132.3 3.4 %collective-permute-start.14 = (f32[3,2,16,256]{3,2,1,0:T(8,128)S(1)}, f32[3,2,16,256]{3,2,1,0:T(8,128)S(1)}, u32[]{:S(2)}, u32[]{:S(2)}) collective-permute-start(f32[3,2,16,256]{3,2,1,0:T(8,128)S(1)} %get-tuple-element.9), channel_id=1, source_target_pairs={{0,1},{1,2},{2,3},{3,4},{4,5},{5,6},{6,7},{8,9},{9,10},{10,11},{11... | collective-permute-start | bytes 294920 | tf_op jit(solution)/shard_map/ppermute | solution.py:270
  135.7 1.3 collective-permute-start.15
  137.0 0.3 collective-permute-done.14
  137.3 3.7 %collective-permute-done.15 = f32[3,2,16,256]{3,2,1,0:T(8,128)S(1)} collective-permute-done((f32[3,2,16,256]{3,2,1,0:T(8,128)S(1)}, f32[3,2,16,256]{3,2,1,0:T(8,128)S(1)}, u32[]{:S(2)}, u32[]{:S(2)}) %collective-permute-start.15) | collective-permute-done | bytes 98336 | tf_op jit(solution)/shard_map/ppermute | solution.py:270
  141.1 0.7 concatenate.28.src_ref
  141.8 2.4 %shard_map.71.refs_3_ = f32[2,16,256]{2,1,0:T(8,128)} custom-call(s32[54]{0:T(128)} %reshape.70.tab_ref, f32[19,16,256]{2,1,0:T(8,128)} %concatenate.28.src_ref, f32[2,16,256]{2,1,0:T(8,128)} %bitcast.94, f32[2,16,256]{2,1,0:T(8,128)} %shard_map.69.rest_0_.refs_1_), custom_call_target="tpu_custom_call" | custom-call | flops 491520 | bytes 409816 | tf_op jit(solution)/shard_map/pallas_call | solution.py:258
  144.2 2.1 %shard_map.72 = f32[1,32]{1,0:T(1,128)} custom-call(f32[2,16,256]{2,1,0:T(8,128)} %shard_map.68.rest_0_.refs_0_, f32[2,16,256]{2,1,0:T(8,128)} %shard_map.69.rest_0_.refs_1_, f32[2,16,256]{2,1,0:T(8,128)} %shard_map.70.refs_2_, f32[2,16,256]{2,1,0:T(8,128)} %shard_map.71.refs_3_), custom_call_target="tpu_custom_call" | custom-call | tf_op jit(solution)/shard_map/pallas_call | solution.py:328
  146.3 0.8 broadcast_in_dim.10
  147.1 37.0 %all_to_all.15 = f32[512,1,32]{2,1,0:T(1,128)S(1)} all-to-all(f32[512,1,32]{2,1,0:T(1,128)S(1)} %broadcast_in_dim.10), channel_id=1, replica_groups=mesh['wide'=64,'narrow'=8] {'wide','narrow'}, dimensions={0} | all-to-all | bytes 131072 | tf_op jit(solution)/shard_map/all_to_all | solution.py:331
  184.0 0.7 copy.34
  184.8 2.1 %shard_map.73 = (f32[2,4096]{1,0:T(2,128)}, f32[2,4096]{1,0:T(2,128)}) custom-call(f32[32,512]{1,0:T(8,128)} %bitcast.103, f32[2,16,256]{2,1,0:T(8,128)} %shard_map.68.rest_0_.refs_0_, f32[2,16,256]{2,1,0:T(8,128)} %shard_map.69.rest_0_.refs_1_, f32[2,16,256]{2,1,0:T(8,128)} %shard_map.70.refs_2_, f32[2,16,256]{2,1,0:T(8,128)} %shard_map.71.refs_3_), custom_call_target="tpu_custom_call" | custom-call | tf_op jit(solution)/shard_map/pallas_call | solution.py:333
  (31 shorter events, 0.4 us)
Async XLA Ops:
  0.6 19.4 %copy-start = (s32[1024,1]{0,1:T(1,128)S(1)}, s32[1024,1]{0,1:T(1,128)}, u32[]{:S(2)}) copy-start(s32[1024,1]{0,1:T(1,128)} %param.5) | copy-start | bytes 12292
  1.4 19.3 %copy-start.2 = (s32[1024]{0:T(1024)S(1)}, s32[1024]{0:T(1024)}, u32[]{:S(2)}) copy-start(s32[1024]{0:T(1024)} %param.6) | copy-start | bytes 12292
  1.4 19.3 %copy-start.1 = (f32[3,1024]{1,0:T(4,128)S(1)}, f32[3,1024]{1,0:T(4,128)}, u32[]{:S(2)}) copy-start(f32[3,1024]{1,0:T(4,128)} %param.7) | copy-start | bytes 36868
  48.7 14.1 %copy-start.3 = (s32[1,1,2,27]{3,2,1,0:T(2,128)S(1)}, s32[1,1,2,27]{3,2,1,0:T(2,128)}, u32[]{:S(2)}) copy-start(s32[1,1,2,27]{3,2,1,0:T(2,128)} %param.9) | copy-start | bytes 652
  48.8 4.7 %collective-permute-start = (f32[3,2,16,256]{3,2,1,0:T(8,128)S(1)}, f32[3,2,16,256]{3,2,1,0:T(8,128)S(1)}, u32[]{:S(2)}, u32[]{:S(2)}) collective-permute-start(f32[3,2,16,256]{3,2,1,0:T(8,128)S(1)} %bitcast.98), channel_id=1, source_target_pairs={{0,8},{8,16},{16,24},{24,32},{32,40},{40,48},{48,56},{56,64},{64,7... | collective-permute-start | bytes 294920 | tf_op jit(solution)/shard_map/ppermute | solution.py:270
  51.5 5.9 %collective-permute-start.1 = (f32[3,2,16,256]{3,2,1,0:T(8,128)S(1)}, f32[3,2,16,256]{3,2,1,0:T(8,128)S(1)}, u32[]{:S(2)}, u32[]{:S(2)}) collective-permute-start(f32[3,2,16,256]{3,2,1,0:T(8,128)S(1)} %bitcast.99), channel_id=1, source_target_pairs={{8,0},{16,8},{24,16},{32,24},{40,32},{48,40},{56,48},{64,56},{72,6... | collective-permute-start | bytes 294920 | tf_op jit(solution)/shard_map/ppermute | solution.py:270
  57.5 8.5 %collective-permute-start.2 = (f32[3,3,2,16,256]{4,3,2,1,0:T(8,128)S(1)}, f32[3,3,2,16,256]{4,3,2,1,0:T(8,128)S(1)}, u32[]{:S(2)}, u32[]{:S(2)}) collective-permute-start(f32[3,3,2,16,256]{4,3,2,1,0:T(8,128)S(1)} %get-tuple-element.7), channel_id=1, source_target_pairs={{0,1},{1,2},{2,3},{3,4},{4,5},{5,6},{6,7},{8,9},{9,10},{10,11},{11... | collective-permute-start | bytes 884744 | tf_op jit(solution)/shard_map/ppermute | solution.py:270
  61.6 9.0 %collective-permute-start.3 = (f32[3,3,2,16,256]{4,3,2,1,0:T(8,128)S(1)}, f32[3,3,2,16,256]{4,3,2,1,0:T(8,128)S(1)}, u32[]{:S(2)}, u32[]{:S(2)}) collective-permute-start(f32[3,3,2,16,256]{4,3,2,1,0:T(8,128)S(1)} %get-tuple-element.7), channel_id=1, source_target_pairs={{1,0},{2,1},{3,2},{4,3},{5,4},{6,5},{7,6},{9,8},{10,9},{11,10},{12... | collective-permute-start | bytes 884744 | tf_op jit(solution)/shard_map/ppermute | solution.py:270
  73.6 7.0 %collective-permute-start.4 = (f32[2,16,256]{2,1,0:T(8,128)}, f32[2,16,256]{2,1,0:T(8,128)S(1)}, u32[]{:S(2)}, u32[]{:S(2)}) collective-permute-start(f32[2,16,256]{2,1,0:T(8,128)} %shard_map.68.rest_0_.refs_0_), channel_id=1, source_target_pairs={{0,8},{8,16},{16,24},{24,32},{32,40},{40,48},{48,56},{56,64},{64,7... | collective-permute-start | bytes 98312 | tf_op jit(solution)/shard_map/ppermute | solution.py:270
  78.7 5.4 %collective-permute-start.5 = (f32[2,16,256]{2,1,0:T(8,128)}, f32[2,16,256]{2,1,0:T(8,128)S(1)}, u32[]{:S(2)}, u32[]{:S(2)}) collective-permute-start(f32[2,16,256]{2,1,0:T(8,128)} %shard_map.68.rest_0_.refs_0_), channel_id=1, source_target_pairs={{8,0},{16,8},{24,16},{32,24},{40,32},{48,40},{56,48},{64,56},{72,6... | collective-permute-start | bytes 98312 | tf_op jit(solution)/shard_map/ppermute | solution.py:270
  84.9 5.9 %collective-permute-start.6 = (f32[3,2,16,256]{3,2,1,0:T(8,128)S(1)}, f32[3,2,16,256]{3,2,1,0:T(8,128)S(1)}, u32[]{:S(2)}, u32[]{:S(2)}) collective-permute-start(f32[3,2,16,256]{3,2,1,0:T(8,128)S(1)} %get-tuple-element.13), channel_id=1, source_target_pairs={{0,1},{1,2},{2,3},{3,4},{4,5},{5,6},{6,7},{8,9},{9,10},{10,11},{11... | collective-permute-start | bytes 294920 | tf_op jit(solution)/shard_map/ppermute | solution.py:270
  88.9 7.2 %collective-permute-start.7 = (f32[3,2,16,256]{3,2,1,0:T(8,128)S(1)}, f32[3,2,16,256]{3,2,1,0:T(8,128)S(1)}, u32[]{:S(2)}, u32[]{:S(2)}) collective-permute-start(f32[3,2,16,256]{3,2,1,0:T(8,128)S(1)} %get-tuple-element.13), channel_id=1, source_target_pairs={{1,0},{2,1},{3,2},{4,3},{5,4},{6,5},{7,6},{9,8},{10,9},{11,10},{12... | collective-permute-start | bytes 294920 | tf_op jit(solution)/shard_map/ppermute | solution.py:270
  99.3 5.5 %collective-permute-start.8 = (f32[2,16,256]{2,1,0:T(8,128)}, f32[2,16,256]{2,1,0:T(8,128)S(1)}, u32[]{:S(2)}, u32[]{:S(2)}) collective-permute-start(f32[2,16,256]{2,1,0:T(8,128)} %shard_map.69.rest_0_.refs_1_), channel_id=1, source_target_pairs={{0,8},{8,16},{16,24},{24,32},{32,40},{40,48},{48,56},{56,64},{64,7... | collective-permute-start | bytes 98312 | tf_op jit(solution)/shard_map/ppermute | solution.py:270
  102.8 5.4 %collective-permute-start.9 = (f32[2,16,256]{2,1,0:T(8,128)}, f32[2,16,256]{2,1,0:T(8,128)S(1)}, u32[]{:S(2)}, u32[]{:S(2)}) collective-permute-start(f32[2,16,256]{2,1,0:T(8,128)} %shard_map.69.rest_0_.refs_1_), channel_id=1, source_target_pairs={{8,0},{16,8},{24,16},{32,24},{40,32},{48,40},{56,48},{64,56},{72,6... | collective-permute-start | bytes 98312 | tf_op jit(solution)/shard_map/ppermute | solution.py:270
  109.1 6.7 %collective-permute-start.10 = (f32[3,2,16,256]{3,2,1,0:T(8,128)S(1)}, f32[3,2,16,256]{3,2,1,0:T(8,128)S(1)}, u32[]{:S(2)}, u32[]{:S(2)}) collective-permute-start(f32[3,2,16,256]{3,2,1,0:T(8,128)S(1)} %get-tuple-element.11), channel_id=1, source_target_pairs={{0,1},{1,2},{2,3},{3,4},{4,5},{5,6},{6,7},{8,9},{9,10},{10,11},{11... | collective-permute-start | bytes 294920 | tf_op jit(solution)/shard_map/ppermute | solution.py:270
  114.1 5.4 %collective-permute-start.11 = (f32[3,2,16,256]{3,2,1,0:T(8,128)S(1)}, f32[3,2,16,256]{3,2,1,0:T(8,128)S(1)}, u32[]{:S(2)}, u32[]{:S(2)}) collective-permute-start(f32[3,2,16,256]{3,2,1,0:T(8,128)S(1)} %get-tuple-element.11), channel_id=1, source_target_pairs={{1,0},{2,1},{3,2},{4,3},{5,4},{6,5},{7,6},{9,8},{10,9},{11,10},{12... | collective-permute-start | bytes 294920 | tf_op jit(solution)/shard_map/ppermute | solution.py:270
  122.7 5.4 %collective-permute-start.12 = (f32[2,16,256]{2,1,0:T(8,128)}, f32[2,16,256]{2,1,0:T(8,128)S(1)}, u32[]{:S(2)}, u32[]{:S(2)}) collective-permute-start(f32[2,16,256]{2,1,0:T(8,128)} %shard_map.70.refs_2_), channel_id=1, source_target_pairs={{0,8},{8,16},{16,24},{24,32},{32,40},{40,48},{48,56},{56,64},{64,7... | collective-permute-start | bytes 98312 | tf_op jit(solution)/shard_map/ppermute | solution.py:270
  126.1 5.4 %collective-permute-start.13 = (f32[2,16,256]{2,1,0:T(8,128)}, f32[2,16,256]{2,1,0:T(8,128)S(1)}, u32[]{:S(2)}, u32[]{:S(2)}) collective-permute-start(f32[2,16,256]{2,1,0:T(8,128)} %shard_map.70.refs_2_), channel_id=1, source_target_pairs={{8,0},{16,8},{24,16},{32,24},{40,32},{48,40},{56,48},{64,56},{72,6... | collective-permute-start | bytes 98312 | tf_op jit(solution)/shard_map/ppermute | solution.py:270
  132.3 5.0 %collective-permute-start.14 = (f32[3,2,16,256]{3,2,1,0:T(8,128)S(1)}, f32[3,2,16,256]{3,2,1,0:T(8,128)S(1)}, u32[]{:S(2)}, u32[]{:S(2)}) collective-permute-start(f32[3,2,16,256]{3,2,1,0:T(8,128)S(1)} %get-tuple-element.9), channel_id=1, source_target_pairs={{0,1},{1,2},{2,3},{3,4},{4,5},{5,6},{6,7},{8,9},{9,10},{10,11},{11... | collective-permute-start | bytes 294920 | tf_op jit(solution)/shard_map/ppermute | solution.py:270
  135.7 5.4 %collective-permute-start.15 = (f32[3,2,16,256]{3,2,1,0:T(8,128)S(1)}, f32[3,2,16,256]{3,2,1,0:T(8,128)S(1)}, u32[]{:S(2)}, u32[]{:S(2)}) collective-permute-start(f32[3,2,16,256]{3,2,1,0:T(8,128)S(1)} %get-tuple-element.9), channel_id=1, source_target_pairs={{1,0},{2,1},{3,2},{4,3},{5,4},{6,5},{7,6},{9,8},{10,9},{11,10},{12... | collective-permute-start | bytes 294920 | tf_op jit(solution)/shard_map/ppermute | solution.py:270

commit v14 on v11

--- a/solution.py
+++ b/solution.py
@@ -220,14 +220,16 @@
 
         planes = {}
         for ex in (-1, 0, 1):
+            face = {-1: slice(ROWS - 1, ROWS), 0: slice(0, ROWS), 1: slice(0, 1)}[ex]
             lines = {}
             for ey in (-1, 0, 1):
-                c = brick(ex, ey, 0)
-                lo, hi = _neighbour_z(c, brick(ex, ey, -1), brick(ex, ey, 1), z)
+                c, m, p = (brick(ex, ey, ez)[face] for ez in (0, -1, 1))
+                lo, hi = _neighbour_z(c, m, p, z[face])
                 lines[ey] = c + 0.5 * (lo + hi)
-            lo, hi = _neighbour_y(lines[0], lines[-1], lines[1], y)
+            lo, hi = _neighbour_y(lines[0], lines[-1], lines[1], y[face])
             planes[ex] = lines[0] + 0.5 * (lo + hi)
-        lo, hi = _neighbour_x(planes[0], planes[-1], planes[1], row)
+        lo = jnp.where(row == 0, planes[-1], pltpu.roll(planes[0], 1, 0))
+        hi = jnp.where(row == ROWS - 1, planes[1], pltpu.roll(planes[0], ROWS - 1, 0))
         smoothed = planes[0] + 0.5 * (lo + hi)
         image = ((diag_ref[b] + (2.0 - shift)) * own - 2.0 * smoothed) * scale
         out_ref[b] = 2.0 * image - previous[0][b] if previous else image

time: 170 us -> 170 us (level)
  no operation moved by 1% of the time
where the time goes in v14:
time: 170 us; the launch traced here: 168 us
  blocking collectives  57.7 us (34%)
  starting transfers between devices  44.1 us (26%)
  waiting for transfers between devices  35 us (21%)
  Pallas kernels  12.8 us (8%)
  local copies, waits for them, and re-layouts  6.55 us (4%)
  other arithmetic  5.38 us (3%)
  matrix products  5.08 us (3%)
  between operations  1.72 us (1%)
    ppermute x16, starting transfers between devices, _shift(): return lax.ppermute(field, axis, pairs)  44.1 us
    all_to_all x1, blocking collectives, shards(): lax.all_to_all(jnp.broadcast_to(payload, (devices, 32)), ('wide', 'narrow...  37 us
    ppermute x16, waiting for transfers between devices, _shift(): return lax.ppermute(field, axis, pairs)  35 us
    all_to_all x1, blocking collectives, shards(): lax.all_to_all(send.reshape(owners, CAP, 4), 'wide', 0, 0, tiled=True)  20.8 us
    pallas_call x4, Pallas kernels, _local_call(): pl.pallas_call(kernel, out_shape=jax.ShapeDtypeStruct(out_shape, jnp.floa...  8.59 us
  transfers between devices with their start and end apart: 16, of which 11 were waited for; matrix products, arithmetic and copies ran while one was open for 1% of the time, Pallas kernels for 0%

profile of v14, /device:TPU:1, one launch (start us, length us, event | category | flops | bytes accessed | tf_op | source)
XLA Modules:
  0.0 168.4 jit_solution(3669656003713294406)
XLA Ops:
  1.3 1.4 fusion.5
  2.8 1.5 fusion
  4.3 0.1 reshape.56
  4.4 0.1 copy.32
  4.5 0.1 reshape.64
  4.6 20.8 %all_to_all.14 = f32[64,1,128]{2,1,0:T(1,128)S(1)} all-to-all(f32[64,1,128]{2,1,0:T(1,128)S(1)} %reshape.64), channel_id=1, replica_groups=mesh['wide'=64,'narrow'=8] {'wide'}, dimensions={0} | all-to-all | bytes 65536 | tf_op jit(solution)/shard_map/all_to_all | solution.py:303
  25.4 0.5 broadcast.43
  25.9 0.7 reduce
  26.6 0.1 reshape.65
  26.8 0.1 reshape.57
  27.0 0.3 fusion.14
  27.3 1.1 fusion.17
  28.4 2.2 %fusion.3 = f32[128,256]{1,0:T(8,128)S(1)} fusion(f32[2048,32]{1,0:T(8,128)S(1)} %fusion.14, f32[2048,32]{1,0:T(8,128)S(1)} %get-tuple-element.23, f32[2048,32]{1,0:T(8,128)S(1)} %get-tuple-element.24, f32[2048,32]{1,0:T(8,128)S(1)} %get-tuple-element.22, s32[2048]{0:T(1024)S(1)} %bitcast.94), kind=kOutput, calls=%fused_computation.6 | convolution fusion | flops 806617088 | bytes 1187840 | tf_op jit(solution)/shard_map/pa,pb->ab/dot_general | solution.py:311
  30.7 0.0 copy-start.3
  30.7 2.8 %collective-permute-start = (f32[3,2,16,256]{3,2,1,0:T(8,128)S(1)}, f32[3,2,16,256]{3,2,1,0:T(8,128)S(1)}, u32[]{:S(2)}, u32[]{:S(2)}) collective-permute-start(f32[3,2,16,256]{3,2,1,0:T(8,128)S(1)} %bitcast.78), channel_id=1, source_target_pairs={{0,8},{8,16},{16,24},{24,32},{32,40},{40,48},{48,56},{56,64},{64,7... | collective-permute-start | bytes 294920 | tf_op jit(solution)/shard_map/ppermute | solution.py:272
  33.5 1.9 %collective-permute-start.1 = (f32[3,2,16,256]{3,2,1,0:T(8,128)S(1)}, f32[3,2,16,256]{3,2,1,0:T(8,128)S(1)}, u32[]{:S(2)}, u32[]{:S(2)}) collective-permute-start(f32[3,2,16,256]{3,2,1,0:T(8,128)S(1)} %bitcast.79), channel_id=1, source_target_pairs={{8,0},{16,8},{24,16},{32,24},{40,32},{48,40},{56,48},{64,56},{72,6... | collective-permute-start | bytes 294920 | tf_op jit(solution)/shard_map/ppermute | solution.py:272
  35.4 0.0 collective-permute-done
  35.4 4.0 %collective-permute-done.1 = f32[3,2,16,256]{3,2,1,0:T(8,128)S(1)} collective-permute-done((f32[3,2,16,256]{3,2,1,0:T(8,128)S(1)}, f32[3,2,16,256]{3,2,1,0:T(8,128)S(1)}, u32[]{:S(2)}, u32[]{:S(2)}) %collective-permute-start.1) | collective-permute-done | bytes 98336 | tf_op jit(solution)/shard_map/ppermute | solution.py:272
  39.4 0.1 fusion.33
  39.5 4.0 %collective-permute-start.2 = (f32[3,3,2,16,256]{4,3,2,1,0:T(8,128)S(1)}, f32[3,3,2,16,256]{4,3,2,1,0:T(8,128)S(1)}, u32[]{:S(2)}, u32[]{:S(2)}) collective-permute-start(f32[3,3,2,16,256]{4,3,2,1,0:T(8,128)S(1)} %get-tuple-element.7), channel_id=1, source_target_pairs={{0,1},{1,2},{2,3},{3,4},{4,5},{5,6},{6,7},{8,9},{9,10},{10,11},{11... | collective-permute-start | bytes 884744 | tf_op jit(solution)/shard_map/ppermute | solution.py:272
  43.5 1.3 collective-permute-start.3
  44.8 0.6 reshape.55.tab_ref
  45.4 2.6 %collective-permute-done.2 = f32[3,3,2,16,256]{4,3,2,1,0:T(8,128)S(1)} collective-permute-done((f32[3,3,2,16,256]{4,3,2,1,0:T(8,128)S(1)}, f32[3,3,2,16,256]{4,3,2,1,0:T(8,128)S(1)}, u32[]{:S(2)}, u32[]{:S(2)}) %collective-permute-start.2) | collective-permute-done | bytes 294944 | tf_op jit(solution)/shard_map/ppermute | solution.py:272
  48.1 4.5 %collective-permute-done.3 = f32[3,3,2,16,256]{4,3,2,1,0:T(8,128)S(1)} collective-permute-done((f32[3,3,2,16,256]{4,3,2,1,0:T(8,128)S(1)}, f32[3,3,2,16,256]{4,3,2,1,0:T(8,128)S(1)}, u32[]{:S(2)}, u32[]{:S(2)}) %collective-permute-start.3) | collective-permute-done | bytes 294944 | tf_op jit(solution)/shard_map/ppermute | solution.py:272
  52.5 0.1 pad_maximum_fusion
  52.6 1.0 concatenate.25.src_ref
  53.6 1.9 %shard_map.68.rest_0_.refs_0_ = f32[2,16,256]{2,1,0:T(8,128)} custom-call(s32[54]{0:T(128)} %reshape.55.tab_ref, f32[3,19,16,256]{3,2,1,0:T(8,128)} %concatenate.25.src_ref), custom_call_target="tpu_custom_call" | custom-call | flops 163840 | bytes 966872 | tf_op jit(solution)/shard_map/pallas_call | solution.py:260
  55.6 5.1 %collective-permute-start.4 = (f32[2,16,256]{2,1,0:T(8,128)}, f32[2,16,256]{2,1,0:T(8,128)S(1)}, u32[]{:S(2)}, u32[]{:S(2)}) collective-permute-start(f32[2,16,256]{2,1,0:T(8,128)} %shard_map.68.rest_0_.refs_0_), channel_id=1, source_target_pairs={{0,8},{8,16},{16,24},{24,32},{32,40},{40,48},{48,56},{56,64},{64,7... | collective-permute-start | bytes 98312 | tf_op jit(solution)/shard_map/ppermute | solution.py:272
  60.6 1.9 %collective-permute-start.5 = (f32[2,16,256]{2,1,0:T(8,128)}, f32[2,16,256]{2,1,0:T(8,128)S(1)}, u32[]{:S(2)}, u32[]{:S(2)}) collective-permute-start(f32[2,16,256]{2,1,0:T(8,128)} %shard_map.68.rest_0_.refs_0_), channel_id=1, source_target_pairs={{8,0},{16,8},{24,16},{32,24},{40,32},{48,40},{56,48},{64,56},{72,6... | collective-permute-start | bytes 98312 | tf_op jit(solution)/shard_map/ppermute | solution.py:272
  62.6 0.0 collective-permute-done.4
  62.6 3.5 %collective-permute-done.5 = f32[2,16,256]{2,1,0:T(8,128)S(1)} collective-permute-done((f32[2,16,256]{2,1,0:T(8,128)}, f32[2,16,256]{2,1,0:T(8,128)S(1)}, u32[]{:S(2)}, u32[]{:S(2)}) %collective-permute-start.5) | collective-permute-done | bytes 32800 | tf_op jit(solution)/shard_map/ppermute | solution.py:272
  66.1 0.8 fusion.32
  66.9 4.0 %collective-permute-start.6 = (f32[3,2,16,256]{3,2,1,0:T(8,128)S(1)}, f32[3,2,16,256]{3,2,1,0:T(8,128)S(1)}, u32[]{:S(2)}, u32[]{:S(2)}) collective-permute-start(f32[3,2,16,256]{3,2,1,0:T(8,128)S(1)} %get-tuple-element.13), channel_id=1, source_target_pairs={{0,1},{1,2},{2,3},{3,4},{4,5},{5,6},{6,7},{8,9},{9,10},{10,11},{11... | collective-permute-start | bytes 294920 | tf_op jit(solution)/shard_map/ppermute | solution.py:272
  70.9 1.3 collective-permute-start.7
  72.2 0.6 fusion.20
  72.8 5.3 %collective-permute-done.7 = f32[3,2,16,256]{3,2,1,0:T(8,128)S(1)} collective-permute-done((f32[3,2,16,256]{3,2,1,0:T(8,128)S(1)}, f32[3,2,16,256]{3,2,1,0:T(8,128)S(1)}, u32[]{:S(2)}, u32[]{:S(2)}) %collective-permute-start.7) | collective-permute-done | bytes 98336 | tf_op jit(solution)/shard_map/ppermute | solution.py:272
  78.1 0.7 concatenate.26.src_ref
  78.9 2.2 %shard_map.69.rest_0_.refs_1_ = f32[2,16,256]{2,1,0:T(8,128)} custom-call(s32[54]{0:T(128)} %reshape.55.tab_ref, f32[19,16,256]{2,1,0:T(8,128)} %concatenate.26.src_ref, f32[2,16,256]{2,1,0:T(8,128)} %bitcast.72), custom_call_target="tpu_custom_call" | custom-call | flops 491520 | bytes 377048 | tf_op jit(solution)/shard_map/pallas_call | solution.py:260
  81.1 3.6 %collective-permute-start.8 = (f32[2,16,256]{2,1,0:T(8,128)}, f32[2,16,256]{2,1,0:T(8,128)S(1)}, u32[]{:S(2)}, u32[]{:S(2)}) collective-permute-start(f32[2,16,256]{2,1,0:T(8,128)} %shard_map.69.rest_0_.refs_1_), channel_id=1, source_target_pairs={{0,8},{8,16},{16,24},{24,32},{32,40},{40,48},{48,56},{56,64},{64,7... | collective-permute-start | bytes 98312 | tf_op jit(solution)/shard_map/ppermute | solution.py:272
  84.6 1.9 %collective-permute-start.9 = (f32[2,16,256]{2,1,0:T(8,128)}, f32[2,16,256]{2,1,0:T(8,128)S(1)}, u32[]{:S(2)}, u32[]{:S(2)}) collective-permute-start(f32[2,16,256]{2,1,0:T(8,128)} %shard_map.69.rest_0_.refs_1_), channel_id=1, source_target_pairs={{8,0},{16,8},{24,16},{32,24},{40,32},{48,40},{56,48},{64,56},{72,6... | collective-permute-start | bytes 98312 | tf_op jit(solution)/shard_map/ppermute | solution.py:272
  86.6 0.0 collective-permute-done.8
  86.6 3.5 %collective-permute-done.9 = f32[2,16,256]{2,1,0:T(8,128)S(1)} collective-permute-done((f32[2,16,256]{2,1,0:T(8,128)}, f32[2,16,256]{2,1,0:T(8,128)S(1)}, u32[]{:S(2)}, u32[]{:S(2)}) %collective-permute-start.9) | collective-permute-done | bytes 32800 | tf_op jit(solution)/shard_map/ppermute | solution.py:272
  90.1 0.8 fusion.31
  90.9 5.1 %collective-permute-start.10 = (f32[3,2,16,256]{3,2,1,0:T(8,128)S(1)}, f32[3,2,16,256]{3,2,1,0:T(8,128)S(1)}, u32[]{:S(2)}, u32[]{:S(2)}) collective-permute-start(f32[3,2,16,256]{3,2,1,0:T(8,128)S(1)} %get-tuple-element.11), channel_id=1, source_target_pairs={{0,1},{1,2},{2,3},{3,4},{4,5},{5,6},{6,7},{8,9},{9,10},{10,11},{11... | collective-permute-start | bytes 294920 | tf_op jit(solution)/shard_map/ppermute | solution.py:272
  95.9 1.3 collective-permute-start.11
  97.2 0.3 collective-permute-done.10
  97.5 3.7 %collective-permute-done.11 = f32[3,2,16,256]{3,2,1,0:T(8,128)S(1)} collective-permute-done((f32[3,2,16,256]{3,2,1,0:T(8,128)S(1)}, f32[3,2,16,256]{3,2,1,0:T(8,128)S(1)}, u32[]{:S(2)}, u32[]{:S(2)}) %collective-permute-start.11) | collective-permute-done | bytes 98336 | tf_op jit(solution)/shard_map/ppermute | solution.py:272
  101.3 0.7 concatenate.27.src_ref
  102.1 2.2 %shard_map.70.refs_2_ = f32[2,16,256]{2,1,0:T(8,128)} custom-call(s32[54]{0:T(128)} %reshape.55.tab_ref, f32[19,16,256]{2,1,0:T(8,128)} %concatenate.27.src_ref, f32[2,16,256]{2,1,0:T(8,128)} %bitcast.73, f32[2,16,256]{2,1,0:T(8,128)} %shard_map.68.rest_0_.refs_0_), custom_call_target="tpu_custom_call" | custom-call | flops 491520 | bytes 409816 | tf_op jit(solution)/shard_map/pallas_call | solution.py:260
  104.3 3.4 %collective-permute-start.12 = (f32[2,16,256]{2,1,0:T(8,128)}, f32[2,16,256]{2,1,0:T(8,128)S(1)}, u32[]{:S(2)}, u32[]{:S(2)}) collective-permute-start(f32[2,16,256]{2,1,0:T(8,128)} %shard_map.70.refs_2_), channel_id=1, source_target_pairs={{0,8},{8,16},{16,24},{24,32},{32,40},{40,48},{48,56},{56,64},{64,7... | collective-permute-start | bytes 98312 | tf_op jit(solution)/shard_map/ppermute | solution.py:272
  107.8 1.9 %collective-permute-start.13 = (f32[2,16,256]{2,1,0:T(8,128)}, f32[2,16,256]{2,1,0:T(8,128)S(1)}, u32[]{:S(2)}, u32[]{:S(2)}) collective-permute-start(f32[2,16,256]{2,1,0:T(8,128)} %shard_map.70.refs_2_), channel_id=1, source_target_pairs={{8,0},{16,8},{24,16},{32,24},{40,32},{48,40},{56,48},{64,56},{72,6... | collective-permute-start | bytes 98312 | tf_op jit(solution)/shard_map/ppermute | solution.py:272
  109.7 3.5 %collective-permute-done.13 = f32[2,16,256]{2,1,0:T(8,128)S(1)} collective-permute-done((f32[2,16,256]{2,1,0:T(8,128)}, f32[2,16,256]{2,1,0:T(8,128)S(1)}, u32[]{:S(2)}, u32[]{:S(2)}) %collective-permute-start.13) | collective-permute-done | bytes 32800 | tf_op jit(solution)/shard_map/ppermute | solution.py:272
  113.2 0.8 fusion.30
  114.0 3.4 %collective-permute-start.14 = (f32[3,2,16,256]{3,2,1,0:T(8,128)S(1)}, f32[3,2,16,256]{3,2,1,0:T(8,128)S(1)}, u32[]{:S(2)}, u32[]{:S(2)}) collective-permute-start(f32[3,2,16,256]{3,2,1,0:T(8,128)S(1)} %get-tuple-element.9), channel_id=1, source_target_pairs={{0,1},{1,2},{2,3},{3,4},{4,5},{5,6},{6,7},{8,9},{9,10},{10,11},{11... | collective-permute-start | bytes 294920 | tf_op jit(solution)/shard_map/ppermute | solution.py:272
  117.3 1.3 collective-permute-start.15
  118.6 0.3 collective-permute-done.14
  119.0 3.7 %collective-permute-done.15 = f32[3,2,16,256]{3,2,1,0:T(8,128)S(1)} collective-permute-done((f32[3,2,16,256]{3,2,1,0:T(8,128)S(1)}, f32[3,2,16,256]{3,2,1,0:T(8,128)S(1)}, u32[]{:S(2)}, u32[]{:S(2)}) %collective-permute-start.15) | collective-permute-done | bytes 98336 | tf_op jit(solution)/shard_map/ppermute | solution.py:272
  122.8 0.7 concatenate.28.src_ref
  123.5 2.2 %shard_map.71.refs_3_ = f32[2,16,256]{2,1,0:T(8,128)} custom-call(s32[54]{0:T(128)} %reshape.55.tab_ref, f32[19,16,256]{2,1,0:T(8,128)} %concatenate.28.src_ref, f32[2,16,256]{2,1,0:T(8,128)} %bitcast.74, f32[2,16,256]{2,1,0:T(8,128)} %shard_map.69.rest_0_.refs_1_), custom_call_target="tpu_custom_call" | custom-call | flops 491520 | bytes 409816 | tf_op jit(solution)/shard_map/pallas_call | solution.py:260
  125.7 2.1 %shard_map.72 = f32[1,32]{1,0:T(1,128)} custom-call(f32[2,16,256]{2,1,0:T(8,128)} %shard_map.68.rest_0_.refs_0_, f32[2,16,256]{2,1,0:T(8,128)} %shard_map.69.rest_0_.refs_1_, f32[2,16,256]{2,1,0:T(8,128)} %shard_map.70.refs_2_, f32[2,16,256]{2,1,0:T(8,128)} %shard_map.71.refs_3_), custom_call_target="tpu_custom_call" | custom-call | tf_op jit(solution)/shard_map/pallas_call | solution.py:332
  127.8 0.8 broadcast_in_dim.10
  128.6 37.0 %all_to_all.15 = f32[512,1,32]{2,1,0:T(1,128)S(1)} all-to-all(f32[512,1,32]{2,1,0:T(1,128)S(1)} %broadcast_in_dim.10), channel_id=1, replica_groups=mesh['wide'=64,'narrow'=8] {'wide','narrow'}, dimensions={0} | all-to-all | bytes 131072 | tf_op jit(solution)/shard_map/all_to_all | solution.py:335
  165.5 0.7 copy.30
  166.3 2.1 %shard_map.73 = (f32[2,4096]{1,0:T(2,128)}, f32[2,4096]{1,0:T(2,128)}) custom-call(f32[32,512]{1,0:T(8,128)} %bitcast.83, f32[2,16,256]{2,1,0:T(8,128)} %shard_map.68.rest_0_.refs_0_, f32[2,16,256]{2,1,0:T(8,128)} %shard_map.69.rest_0_.refs_1_, f32[2,16,256]{2,1,0:T(8,128)} %shard_map.70.refs_2_, f32[2,16,256]{2,1,0:T(8,128)} %shard_map.71.refs_3_), custom_call_target="tpu_custom_call" | custom-call | tf_op jit(solution)/shard_map/pallas_call | solution.py:337
  (23 shorter events, 0.2 us)
Async XLA Ops:
  0.6 2.1 %copy-start.1 = (s32[1024,1]{0,1:T(1,128)S(1)}, s32[1024,1]{0,1:T(1,128)}, u32[]{:S(2)}) copy-start(s32[1024,1]{0,1:T(1,128)} %param.5) | copy-start | bytes 12292
  0.6 2.1 %copy-start.2 = (s32[1024]{0:T(1024)S(1)}, s32[1024]{0:T(1024)}, u32[]{:S(2)}) copy-start(s32[1024]{0:T(1024)} %param.6) | copy-start | bytes 12292
  0.7 2.1 %copy-start = (f32[3,1024]{1,0:T(4,128)S(1)}, f32[3,1024]{1,0:T(4,128)}, u32[]{:S(2)}) copy-start(f32[3,1024]{1,0:T(4,128)} %param.7) | copy-start | bytes 36868
  30.7 14.1 %copy-start.3 = (s32[1,1,2,27]{3,2,1,0:T(2,128)S(1)}, s32[1,1,2,27]{3,2,1,0:T(2,128)}, u32[]{:S(2)}) copy-start(s32[1,1,2,27]{3,2,1,0:T(2,128)} %param.9) | copy-start | bytes 652
  30.7 4.7 %collective-permute-start = (f32[3,2,16,256]{3,2,1,0:T(8,128)S(1)}, f32[3,2,16,256]{3,2,1,0:T(8,128)S(1)}, u32[]{:S(2)}, u32[]{:S(2)}) collective-permute-start(f32[3,2,16,256]{3,2,1,0:T(8,128)S(1)} %bitcast.78), channel_id=1, source_target_pairs={{0,8},{8,16},{16,24},{24,32},{32,40},{40,48},{48,56},{56,64},{64,7... | collective-permute-start | bytes 294920 | tf_op jit(solution)/shard_map/ppermute | solution.py:272
  33.5 5.9 %collective-permute-start.1 = (f32[3,2,16,256]{3,2,1,0:T(8,128)S(1)}, f32[3,2,16,256]{3,2,1,0:T(8,128)S(1)}, u32[]{:S(2)}, u32[]{:S(2)}) collective-permute-start(f32[3,2,16,256]{3,2,1,0:T(8,128)S(1)} %bitcast.79), channel_id=1, source_target_pairs={{8,0},{16,8},{24,16},{32,24},{40,32},{48,40},{56,48},{64,56},{72,6... | collective-permute-start | bytes 294920 | tf_op jit(solution)/shard_map/ppermute | solution.py:272
  39.5 8.5 %collective-permute-start.2 = (f32[3,3,2,16,256]{4,3,2,1,0:T(8,128)S(1)}, f32[3,3,2,16,256]{4,3,2,1,0:T(8,128)S(1)}, u32[]{:S(2)}, u32[]{:S(2)}) collective-permute-start(f32[3,3,2,16,256]{4,3,2,1,0:T(8,128)S(1)} %get-tuple-element.7), channel_id=1, source_target_pairs={{0,1},{1,2},{2,3},{3,4},{4,5},{5,6},{6,7},{8,9},{9,10},{10,11},{11... | collective-permute-start | bytes 884744 | tf_op jit(solution)/shard_map/ppermute | solution.py:272
  43.5 9.0 %collective-permute-start.3 = (f32[3,3,2,16,256]{4,3,2,1,0:T(8,128)S(1)}, f32[3,3,2,16,256]{4,3,2,1,0:T(8,128)S(1)}, u32[]{:S(2)}, u32[]{:S(2)}) collective-permute-start(f32[3,3,2,16,256]{4,3,2,1,0:T(8,128)S(1)} %get-tuple-element.7), channel_id=1, source_target_pairs={{1,0},{2,1},{3,2},{4,3},{5,4},{6,5},{7,6},{9,8},{10,9},{11,10},{12... | collective-permute-start | bytes 884744 | tf_op jit(solution)/shard_map/ppermute | solution.py:272
  55.6 7.0 %collective-permute-start.4 = (f32[2,16,256]{2,1,0:T(8,128)}, f32[2,16,256]{2,1,0:T(8,128)S(1)}, u32[]{:S(2)}, u32[]{:S(2)}) collective-permute-start(f32[2,16,256]{2,1,0:T(8,128)} %shard_map.68.rest_0_.refs_0_), channel_id=1, source_target_pairs={{0,8},{8,16},{16,24},{24,32},{32,40},{40,48},{48,56},{56,64},{64,7... | collective-permute-start | bytes 98312 | tf_op jit(solution)/shard_map/ppermute | solution.py:272
  60.6 5.4 %collective-permute-start.5 = (f32[2,16,256]{2,1,0:T(8,128)}, f32[2,16,256]{2,1,0:T(8,128)S(1)}, u32[]{:S(2)}, u32[]{:S(2)}) collective-permute-start(f32[2,16,256]{2,1,0:T(8,128)} %shard_map.68.rest_0_.refs_0_), channel_id=1, source_target_pairs={{8,0},{16,8},{24,16},{32,24},{40,32},{48,40},{56,48},{64,56},{72,6... | collective-permute-start | bytes 98312 | tf_op jit(solution)/shard_map/ppermute | solution.py:272
  66.9 5.9 %collective-permute-start.6 = (f32[3,2,16,256]{3,2,1,0:T(8,128)S(1)}, f32[3,2,16,256]{3,2,1,0:T(8,128)S(1)}, u32[]{:S(2)}, u32[]{:S(2)}) collective-permute-start(f32[3,2,16,256]{3,2,1,0:T(8,128)S(1)} %get-tuple-element.13), channel_id=1, source_target_pairs={{0,1},{1,2},{2,3},{3,4},{4,5},{5,6},{6,7},{8,9},{9,10},{10,11},{11... | collective-permute-start | bytes 294920 | tf_op jit(solution)/shard_map/ppermute | solution.py:272
  70.9 7.2 %collective-permute-start.7 = (f32[3,2,16,256]{3,2,1,0:T(8,128)S(1)}, f32[3,2,16,256]{3,2,1,0:T(8,128)S(1)}, u32[]{:S(2)}, u32[]{:S(2)}) collective-permute-start(f32[3,2,16,256]{3,2,1,0:T(8,128)S(1)} %get-tuple-element.13), channel_id=1, source_target_pairs={{1,0},{2,1},{3,2},{4,3},{5,4},{6,5},{7,6},{9,8},{10,9},{11,10},{12... | collective-permute-start | bytes 294920 | tf_op jit(solution)/shard_map/ppermute | solution.py:272
  81.1 5.5 %collective-permute-start.8 = (f32[2,16,256]{2,1,0:T(8,128)}, f32[2,16,256]{2,1,0:T(8,128)S(1)}, u32[]{:S(2)}, u32[]{:S(2)}) collective-permute-start(f32[2,16,256]{2,1,0:T(8,128)} %shard_map.69.rest_0_.refs_1_), channel_id=1, source_target_pairs={{0,8},{8,16},{16,24},{24,32},{32,40},{40,48},{48,56},{56,64},{64,7... | collective-permute-start | bytes 98312 | tf_op jit(solution)/shard_map/ppermute | solution.py:272
  84.6 5.4 %collective-permute-start.9 = (f32[2,16,256]{2,1,0:T(8,128)}, f32[2,16,256]{2,1,0:T(8,128)S(1)}, u32[]{:S(2)}, u32[]{:S(2)}) collective-permute-start(f32[2,16,256]{2,1,0:T(8,128)} %shard_map.69.rest_0_.refs_1_), channel_id=1, source_target_pairs={{8,0},{16,8},{24,16},{32,24},{40,32},{48,40},{56,48},{64,56},{72,6... | collective-permute-start | bytes 98312 | tf_op jit(solution)/shard_map/ppermute | solution.py:272
  90.9 6.7 %collective-permute-start.10 = (f32[3,2,16,256]{3,2,1,0:T(8,128)S(1)}, f32[3,2,16,256]{3,2,1,0:T(8,128)S(1)}, u32[]{:S(2)}, u32[]{:S(2)}) collective-permute-start(f32[3,2,16,256]{3,2,1,0:T(8,128)S(1)} %get-tuple-element.11), channel_id=1, source_target_pairs={{0,1},{1,2},{2,3},{3,4},{4,5},{5,6},{6,7},{8,9},{9,10},{10,11},{11... | collective-permute-start | bytes 294920 | tf_op jit(solution)/shard_map/ppermute | solution.py:272
  95.9 5.4 %collective-permute-start.11 = (f32[3,2,16,256]{3,2,1,0:T(8,128)S(1)}, f32[3,2,16,256]{3,2,1,0:T(8,128)S(1)}, u32[]{:S(2)}, u32[]{:S(2)}) collective-permute-start(f32[3,2,16,256]{3,2,1,0:T(8,128)S(1)} %get-tuple-element.11), channel_id=1, source_target_pairs={{1,0},{2,1},{3,2},{4,3},{5,4},{6,5},{7,6},{9,8},{10,9},{11,10},{12... | collective-permute-start | bytes 294920 | tf_op jit(solution)/shard_map/ppermute | solution.py:272
  104.3 5.4 %collective-permute-start.12 = (f32[2,16,256]{2,1,0:T(8,128)}, f32[2,16,256]{2,1,0:T(8,128)S(1)}, u32[]{:S(2)}, u32[]{:S(2)}) collective-permute-start(f32[2,16,256]{2,1,0:T(8,128)} %shard_map.70.refs_2_), channel_id=1, source_target_pairs={{0,8},{8,16},{16,24},{24,32},{32,40},{40,48},{48,56},{56,64},{64,7... | collective-permute-start | bytes 98312 | tf_op jit(solution)/shard_map/ppermute | solution.py:272
  107.8 5.4 %collective-permute-start.13 = (f32[2,16,256]{2,1,0:T(8,128)}, f32[2,16,256]{2,1,0:T(8,128)S(1)}, u32[]{:S(2)}, u32[]{:S(2)}) collective-permute-start(f32[2,16,256]{2,1,0:T(8,128)} %shard_map.70.refs_2_), channel_id=1, source_target_pairs={{8,0},{16,8},{24,16},{32,24},{40,32},{48,40},{56,48},{64,56},{72,6... | collective-permute-start | bytes 98312 | tf_op jit(solution)/shard_map/ppermute | solution.py:272
  114.0 5.0 %collective-permute-start.14 = (f32[3,2,16,256]{3,2,1,0:T(8,128)S(1)}, f32[3,2,16,256]{3,2,1,0:T(8,128)S(1)}, u32[]{:S(2)}, u32[]{:S(2)}) collective-permute-start(f32[3,2,16,256]{3,2,1,0:T(8,128)S(1)} %get-tuple-element.9), channel_id=1, source_target_pairs={{0,1},{1,2},{2,3},{3,4},{4,5},{5,6},{6,7},{8,9},{9,10},{10,11},{11... | collective-permute-start | bytes 294920 | tf_op jit(solution)/shard_map/ppermute | solution.py:272
  117.3 5.4 %collective-permute-start.15 = (f32[3,2,16,256]{3,2,1,0:T(8,128)S(1)}, f32[3,2,16,256]{3,2,1,0:T(8,128)S(1)}, u32[]{:S(2)}, u32[]{:S(2)}) collective-permute-start(f32[3,2,16,256]{3,2,1,0:T(8,128)S(1)} %get-tuple-element.9), channel_id=1, source_target_pairs={{1,0},{2,1},{3,2},{4,3},{5,4},{6,5},{7,6},{9,8},{10,9},{11,10},{12... | collective-permute-start | bytes 294920 | tf_op jit(solution)/shard_map/ppermute | solution.py:272
